TPU v7x, 32 devices: a whole 2x2x4 slice. The times are simulated.
32 devices in a mesh: groups: 2 (over y), ctx: 4 (over z), head: 4 (over x, core).
Axes of the slice: x: 2, y: 2, z: 4, core: 2. Of those that a mesh axis runs over, the one named last changes fastest.
Arguments:
- hidden_in: bfloat16 [4096, 4096], P(('groups', 'ctx'), 'head'), parts along dimension 0, may hold values from -6 to 6
- attn_gain: float32 [4096], replicated, may hold values from 0.5 to 12, as said below
- w_query: bfloat16 [4096, 2048], P(None, 'head'), may hold values from -0.09375 to 0.09375
- w_keys: bfloat16 [4096, 1024], P(None, 'head'), may hold values from -0.09375 to 0.09375
- w_values: bfloat16 [4096, 1024], P(None, 'head'), may hold values from -0.09375 to 0.09375
- wo_attn: bfloat16 [2048, 4096], P('head'), may hold values from -0.125 to 0.125
- lin_gain: float32 [4096], replicated, may hold values from 0.5 to 1.5
- w_feature: bfloat16 [4096, 256], P(None, 'head'), may hold values from -0.09375 to 0.09375
- wv_linear: bfloat16 [4096, 2048], P(None, 'head'), may hold values from -0.09375 to 0.09375
- out_gain: float32 [8, 256], P('head'), may hold values from 0.5 to 1.5
- wo_linear: bfloat16 [2048, 4096], P('head'), may hold values from -0.125 to 0.125
- entry_state: float32 [16, 273, 256], P(('groups', 'head')), parts along dimension 0, may hold values from -180 to 180
Outputs:
- mixed: bfloat16 [4096, 4096], P(('groups', 'ctx'), 'head'), parts along dimension 0
There are 2 independent parts, one for each index of `groups`. A program takes and returns all parts, laid end to end along the dimension named above; an argument that names none is the same for every part. Nothing has to cross between parts.
Inputs may be any that keep to these rules, and one draw needn't show every extreme that they name: `attn_gain`: a positive gain for every feature.
All inputs are finite; a program needn't handle non-finite values.
Results may differ from a plain program's by a relative error of at most 0.008.
The roundings to bfloat16 on the way count: a program that leaves them out, or rounds other values in their place, can miss the bound.
Values may be sent and summed in bfloat16 or wider, within the bound.
No kernel may reach another device: no remote copies, remote signals or barrier semaphores. Data moves between devices by JAX's collectives and lax.ppermute only.
A program may use at most 128 MiB of HBM per device.

v0:
```python
import math

import jax
import jax.numpy as jnp
from jax import lax
from jax.sharding import PartitionSpec as P

HEAD = 128
WINDOW = 64
FEAT = 16
VDIM = 256


def from_behind(value, axis, by):
    devices = lax.axis_size(axis)
    pairs = [(i, i + by) for i in range(devices) if 0 <= i + by < devices]
    return lax.ppermute(value, axis, pairs)


def norm_rows(values, gain):
    wide = values.astype(jnp.float32)
    scale = lax.rsqrt(jnp.mean(wide * wide, axis=-1, keepdims=True) + 1e-05)
    return (wide * scale * gain).astype(jnp.bfloat16)


def taylor(inputs):
    width = inputs.shape[-1]
    outer = (inputs[..., :, None] * inputs[..., None, :]).reshape(
        inputs.shape[:-1] + (width * width,)
    )
    ones = jnp.ones(inputs.shape[:-1] + (1,), jnp.float32)
    return jnp.concatenate(
        [ones, inputs / width**0.25, outer / (math.sqrt(2.0) * math.sqrt(width))], axis=-1
    )


def body(
    hidden_in,
    attn_gain,
    w_query,
    w_keys,
    w_values,
    wo_attn,
    lin_gain,
    w_feature,
    wv_linear,
    out_gain,
    wo_linear,
    entry_state,
):
    tok_rows = hidden_in.shape[0]
    whole = lax.all_gather(hidden_in, "head", axis=1, tiled=True)
    normed = norm_rows(whole, attn_gain)
    query = jnp.dot(normed, w_query, preferred_element_type=jnp.float32).astype(jnp.bfloat16)
    keys = jnp.dot(normed, w_keys, preferred_element_type=jnp.float32).astype(jnp.bfloat16)
    values = jnp.dot(normed, w_values, preferred_element_type=jnp.float32).astype(jnp.bfloat16)
    kv_cols = keys.shape[1]
    kv_heads = kv_cols // HEAD
    group = query.shape[1] // HEAD // kv_heads
    kv_pair = jnp.concatenate([keys, values], axis=1)
    rim = from_behind(kv_pair[tok_rows - WINDOW :], "ctx", 1)
    kv_all = jnp.concatenate([rim, kv_pair], axis=0)
    key_all = kv_all[:, :kv_cols].reshape(tok_rows + WINDOW, kv_heads, HEAD)
    value_all = kv_all[:, kv_cols:].reshape(tok_rows + WINDOW, kv_heads, HEAD)
    query_heads = query.reshape(tok_rows, kv_heads, group, HEAD)
    scores = jnp.einsum(
        "tkgd,skd->kgts", query_heads, key_all, preferred_element_type=jnp.float32
    ) / math.sqrt(HEAD)
    start = lax.axis_index("ctx") * tok_rows
    qpos = start + jnp.arange(tok_rows, dtype=jnp.int32)
    kpos = start - WINDOW + jnp.arange(tok_rows + WINDOW, dtype=jnp.int32)
    visible = (
        (kpos[None, :] <= qpos[:, None])
        & (kpos[None, :] > qpos[:, None] - WINDOW)
        & (kpos[None, :] >= 0)
    )
    scores = jnp.where(visible, scores, -jnp.inf)
    top = jnp.max(scores, axis=-1, keepdims=True)
    expd = jnp.exp(scores - top)
    probs = (expd / jnp.sum(expd, axis=-1, keepdims=True)).astype(jnp.bfloat16)
    attended = jnp.einsum("kgts,skd->tkgd", probs, value_all, preferred_element_type=jnp.float32)
    attended = attended.astype(jnp.bfloat16).reshape(tok_rows, -1)
    terms = jnp.dot(attended, wo_attn, preferred_element_type=jnp.float32)
    partial_out = lax.psum_scatter(terms, "head", scatter_dimension=1, tiled=True)
    after_window = (hidden_in.astype(jnp.float32) + partial_out).astype(jnp.bfloat16)
    after_whole = lax.all_gather(after_window, "head", axis=1, tiled=True)
    normed2 = norm_rows(after_whole, lin_gain)
    feats = jnp.dot(normed2, w_feature, preferred_element_type=jnp.float32)
    lin_heads = feats.shape[1] // (2 * FEAT)
    feats = feats.reshape(tok_rows, lin_heads, 2, FEAT)
    query_feat = feats[:, :, 0, :]
    key_feat = feats[:, :, 1, :]
    lvalues = (
        jnp.dot(normed2, wv_linear, preferred_element_type=jnp.float32)
        .astype(jnp.bfloat16)
        .reshape(tok_rows, lin_heads, VDIM)
    )
    phi_query = taylor(query_feat)
    phi_key = taylor(key_feat)
    highest = lax.Precision.HIGHEST
    local_state = jnp.einsum(
        "thf,thv->hfv", phi_key, lvalues.astype(jnp.float32), precision=highest
    )
    ctx_count = lax.axis_size("ctx")
    every = (
        lax.all_gather(local_state.astype(jnp.bfloat16), "ctx", axis=0, tiled=True)
        .astype(local_state.dtype)
        .reshape((ctx_count,) + local_state.shape)
    )
    earlier = (jnp.arange(ctx_count, dtype=jnp.int32) < lax.axis_index("ctx")).astype(jnp.float32)
    prior = jnp.einsum("c,chfv->hfv", earlier, every, precision=highest)
    carried = entry_state + prior
    cross = jnp.einsum("thf,hfv->thv", phi_query, carried, precision=highest)
    sims = jnp.einsum("thf,shf->hts", query_feat, key_feat, precision=highest) / math.sqrt(FEAT)
    causal = jnp.arange(tok_rows)[:, None] >= jnp.arange(tok_rows)[None, :]
    weights = jnp.where(causal[None], 1.0 + sims + 0.5 * sims * sims, 0.0).astype(jnp.bfloat16)
    intra = jnp.einsum("hts,shv->thv", weights, lvalues, preferred_element_type=jnp.float32)
    lin_out = cross + intra
    scale = lax.rsqrt(jnp.mean(lin_out * lin_out, axis=-1, keepdims=True) + 1e-05)
    lin_normed = (
        (lin_out * scale * out_gain[None]).astype(jnp.bfloat16).reshape(tok_rows, lin_heads * VDIM)
    )
    lin_terms = jnp.dot(lin_normed, wo_linear, preferred_element_type=jnp.float32)
    lin_part = lax.psum_scatter(lin_terms, "head", scatter_dimension=1, tiled=True)
    return (after_window.astype(jnp.float32) + lin_part).astype(jnp.bfloat16)


def solution(mesh):
    in_specs = (
        P(("groups", "ctx"), "head"),
        P(),
        P(None, "head"),
        P(None, "head"),
        P(None, "head"),
        P("head", None),
        P(),
        P(None, "head"),
        P(None, "head"),
        P("head", None),
        P("head", None),
        P(("groups", "head"), None, None),
    )
    out_specs = P(("groups", "ctx"), "head")
    return jax.shard_map(body, mesh=mesh, in_specs=in_specs, out_specs=out_specs, check_vma=False)
```

profile of v0, /device:TPU:24, one launch (start us, length us, event | category | flops | bytes accessed | tf_op | source)
XLA Modules:
  0.0 314.2 jit_solution(14720713540210426157)
XLA Ops:
  7.7 36.7 %all-gather.4.cloned.1.call-done = bf16[512,4096]{1,0:T(8,128)(2,1)} async-done(((bf16[512,1024]{1,0:T(8,128)(2,1)}), bf16[512,4096]{1,0:T(8,128)(2,1)}) %all-gather.4.cloned.1.call-update) | async-done | bytes 4194320 | tf_op jit(solution)/shard_map/all_gather | solution.py:52
  44.4 3.2 %fusion.1 = f32[512]{0:T(512)S(1)} fusion(bf16[512,4096]{1,0:T(8,128)(2,1)} %all-gather.4.cloned.1.call-done), kind=kLoop, calls=%fused_computation.5 | loop fusion | flops 6290944 | bytes 4196352 | tf_op jit(solution)/shard_map/reduce_sum | solution.py:22
  47.9 1.6 convolution_convert_fusion.3
  49.5 1.6 convolution_convert_fusion.4
  52.7 2.6 convolution_convert_fusion.1
  55.4 3.4 %collective-permute-done = bf16[64,512]{0,1:T(8,128)(2,1)S(1)} collective-permute-done((bf16[64,512]{0,1:T(8,128)(2,1)S(1)}, bf16[64,512]{0,1:T(8,128)(2,1)S(1)}, u32[]{:S(2)}, u32[]{:S(2)}) %collective-permute-start) | collective-permute-done | bytes 65568 | tf_op jit(solution)/shard_map/ppermute | solution.py:17
  59.2 3.9 %fusion.43 = (f32[2,2,512]{2,1,0:T(2,128)S(1)}, f32[2,2,512,576]{2,3,1,0:T(8,128)}) fusion(pred[512,576]{0,1:T(8,128)(4,1)S(1)} %and_and_fusion, bf16[576,2,128,1]{0,2,3,1:T(8,128)(2,1)S(1)} %bitcast.82, bf16[512,2,2,128]{0,3,2,1:T(8,128)(2,1)S(1)} %bitcast.84), kind=kOutput, calls=%fused_computation.74 | convolution fusion | flops 306709056 | bytes 5840896 | tf_op jit(solution)/shard_map/sub | solution.py:79
  63.1 3.1 fusion.13
  66.7 5.7 %fusion.44 = f32[512,4096]{1,0:T(8,128)} fusion(bf16[512,512]{0,1:T(8,128)(2,1)S(1)} %bitcast.75, bf16[512,4096]{1,0:T(8,128)(2,1)S(1)} %copy-done.3), kind=kOutput, calls=%fused_computation.75 | convolution fusion | flops 2147483648 | bytes 13107200 | tf_op jit(solution)/shard_map/dot_general | solution.py:83
  72.5 71.8 %reduce-scatter.3.cloned.1.call-done = f32[512,1024]{1,0:T(8,128)} async-done(((f32[512,4096]{1,0:T(8,128)}), f32[512,1024]{1,0:T(8,128)}) %reduce-scatter.3.cloned.1.call-update) | async-done | bytes 2097168 | tf_op jit(solution)/shard_map/reduce_scatter | solution.py:84
  144.3 2.9 add_convert_fusion.1
  147.5 34.4 %all-gather.6.cloned.1.call-done = bf16[512,4096]{1,0:T(8,128)(2,1)} async-done(((bf16[512,1024]{1,0:T(8,128)(2,1)}), bf16[512,4096]{1,0:T(8,128)(2,1)}) %all-gather.6.cloned.1.call-update) | async-done | bytes 4194320 | tf_op jit(solution)/shard_map/all_gather | solution.py:86
  181.9 3.2 %fusion.4 = f32[512]{0:T(512)S(1)} fusion(bf16[512,4096]{1,0:T(8,128)(2,1)} %all-gather.6.cloned.1.call-done), kind=kLoop, calls=%fused_computation.8 | loop fusion | flops 6290944 | bytes 4196352 | tf_op jit(solution)/shard_map/reduce_sum | solution.py:22
  185.3 1.5 fusion.15
  187.5 2.6 convolution_convert_fusion
  190.2 1.5 convolution_convert_fusion.2
  192.2 2.3 select_convert_fusion
  194.6 25.4 %all-gather.8.cloned.1.call-done = bf16[8,273,256]{2,1,0:T(8,128)(2,1)} async-done(((bf16[2,273,256]{2,1,0:T(8,128)(2,1)}), bf16[8,273,256]{2,1,0:T(8,128)(2,1)}) %all-gather.8.cloned.1.call-update) | async-done | bytes 1118224 | tf_op jit(solution)/shard_map/all_gather | solution.py:106
  220.0 2.0 fusion.26
  222.0 1.5 bitcast_add_fusion
  223.5 2.0 fusion.21
  226.2 5.7 %fusion.45 = f32[512,4096]{1,0:T(8,128)} fusion(bf16[512,512]{0,1:T(8,128)(2,1)S(1)} %bitcast.73, bf16[512,4096]{1,0:T(8,128)(2,1)S(1)} %copy-done.4), kind=kOutput, calls=%fused_computation.76 | convolution fusion | flops 2147483648 | bytes 13107200 | tf_op jit(solution)/shard_map/dot_general | solution.py:123
  231.9 72.8 %reduce-scatter.5.cloned.1.call-done = f32[512,1024]{1,0:T(8,128)} async-done(((f32[512,4096]{1,0:T(8,128)}), f32[512,1024]{1,0:T(8,128)}) %reduce-scatter.5.cloned.1.call-update) | async-done | bytes 2097168 | tf_op jit(solution)/shard_map/reduce_scatter | solution.py:124
  304.7 2.9 add_convert_fusion
  (63 shorter events, 6.3 us)
Async XLA Ops:
  6.5 41.1 %copy-start = (bf16[4096,256]{1,0:T(8,128)(2,1)S(1)}, bf16[4096,256]{1,0:T(8,128)(2,1)}, u32[]{:S(2)}) copy-start(bf16[4096,256]{1,0:T(8,128)(2,1)} %param.16) | copy-start | bytes 6291460
  6.5 41.1 %copy-start.15 = (f32[4096]{0:T(1024)S(1)}, f32[4096]{0:T(1024)}, u32[]{:S(2)}) copy-start(f32[4096]{0:T(1024)} %param.13) | copy-start | bytes 49156
  6.5 37.9 %all-gather.4.cloned.1.call-start = ((), (), s32[]{:S(2)}) async-start(), calls=%async_computation.2 | async-start | bytes 5242880 | tf_op jit(solution)/shard_map/all_gather | solution.py:52
  7.3 137.1 %reduce-scatter.3.cloned.1.call-start = ((), (), s32[]{:S(2)}) async-start(), calls=%async_computation.3 | async-start | bytes 10485760 | tf_op jit(solution)/shard_map/reduce_scatter | solution.py:84
  44.4 3.4 %copy-start.5 = (bf16[512,4096]{1,0:T(8,128)(2,1)S(1)}, bf16[512,4096]{1,0:T(8,128)(2,1)}, u32[]{:S(2)}) copy-start(bf16[512,4096]{1,0:T(8,128)(2,1)} %all-gather.4.cloned.1.call-done) | copy-start | bytes 12582916
  47.9 1.6 copy-start.13
  49.5 3.2 %copy-start.11 = (bf16[4096,512]{1,0:T(8,128)(2,1)S(1)}, bf16[4096,512]{1,0:T(8,128)(2,1)}, u32[]{:S(2)}) copy-start(bf16[4096,512]{1,0:T(8,128)(2,1)} %param.14) | copy-start | bytes 12582916
  51.2 7.5 %collective-permute-start = (bf16[64,512]{0,1:T(8,128)(2,1)S(1)}, bf16[64,512]{0,1:T(8,128)(2,1)S(1)}, u32[]{:S(2)}, u32[]{:S(2)}) collective-permute-start(bf16[64,512]{0,1:T(8,128)(2,1)S(1)} %pad_maximum_fusion), channel_id=1, source_target_pairs={{0,4},{4,8},{8,12},{1,5},{5,9},{9,13},{2,6},{6,10},{10,14},{3,7},{... | collective-permute-start | bytes 196616 | tf_op jit(solution)/shard_map/ppermute | solution.py:17
  63.1 3.6 %copy-start.3 = (bf16[512,4096]{1,0:T(8,128)(2,1)S(1)}, bf16[512,4096]{1,0:T(8,128)(2,1)}, u32[]{:S(2)}) copy-start(bf16[512,4096]{1,0:T(8,128)(2,1)} %param.17) | copy-start | bytes 12582916
  72.4 71.9 %copy-start.7 = (bf16[512,1024]{1,0:T(8,128)(2,1)S(1)}, bf16[512,1024]{1,0:T(8,128)(2,1)}, u32[]{:S(2)}) copy-start(bf16[512,1024]{1,0:T(8,128)(2,1)} %param.12) | copy-start | bytes 3145732
  72.4 112.7 %copy-start.14 = (bf16[4096,64]{0,1:T(8,128)(2,1)S(1)}, bf16[4096,64]{0,1:T(8,128)(2,1)}, u32[]{:S(2)}) copy-start(bf16[4096,64]{0,1:T(8,128)(2,1)} %param.19) | copy-start | bytes 1572868
  72.4 112.7 %copy-start.16 = (f32[4096]{0:T(1024)S(1)}, f32[4096]{0:T(1024)}, u32[]{:S(2)}) copy-start(f32[4096]{0:T(1024)} %param.18) | copy-start | bytes 49156
  72.5 109.4 %all-gather.6.cloned.1.call-start = ((), (), s32[]{:S(2)}) async-start(), calls=%async_computation.4 | async-start | bytes 5242880 | tf_op jit(solution)/shard_map/all_gather | solution.py:86
  147.2 72.7 %all-gather.8.cloned.1.call-start = ((), (), s32[]{:S(2)}) async-start(), calls=%async_computation.5 | async-start | bytes 1433600 | tf_op jit(solution)/shard_map/all_gather | solution.py:106
  181.9 3.4 %copy-start.6 = (bf16[512,4096]{1,0:T(8,128)(2,1)S(1)}, bf16[512,4096]{1,0:T(8,128)(2,1)}, u32[]{:S(2)}) copy-start(bf16[512,4096]{1,0:T(8,128)(2,1)} %all-gather.6.cloned.1.call-done) | copy-start | bytes 12582916
  185.3 2.2 copy-start.12
  190.1 29.8 %copy-start.8 = (bf16[512,512]{0,1:T(8,128)(2,1)}, bf16[512,512]{0,1:T(8,128)(2,1)S(1)}, u32[]{:S(2)}) copy-start(bf16[512,512]{0,1:T(8,128)(2,1)S(1)} %convolution_convert_fusion) | copy-start | bytes 1572868
  191.7 113.0 %reduce-scatter.5.cloned.1.call-start = ((), (), s32[]{:S(2)}) async-start(), calls=%async_computation.6 | async-start | bytes 10485760 | tf_op jit(solution)/shard_map/reduce_scatter | solution.py:124
  221.9 3.6 %copy-start.9 = (bf16[512,512]{0,1:T(8,128)(2,1)S(1)}, bf16[512,512]{0,1:T(8,128)(2,1)}, u32[]{:S(2)}) copy-start(bf16[512,512]{0,1:T(8,128)(2,1)} %copy-done.8) | copy-start | bytes 1572868
  222.0 4.1 %copy-start.10 = (f32[2,256]{1,0:T(2,128)S(1)}, f32[2,256]{1,0:T(2,128)}, u32[]{:S(2)}) copy-start(f32[2,256]{1,0:T(2,128)} %param.21) | copy-start | bytes 6148
  223.5 2.7 copy-start.4
  231.9 72.8 %copy-start.2 = (bf16[512,1024]{1,0:T(8,128)(2,1)S(1)}, bf16[512,1024]{1,0:T(8,128)(2,1)}, u32[]{:S(2)}) copy-start(bf16[512,1024]{1,0:T(8,128)(2,1)} %add_convert_fusion.1) | copy-start | bytes 3145732
  231.9 75.7 %copy-start.1 = (bf16[4096,256]{1,0:T(8,128)(2,1)S(1)}, bf16[4096,256]{1,0:T(8,128)(2,1)}, u32[]{:S(2)}) copy-start(bf16[4096,256]{1,0:T(8,128)(2,1)} %param.16) | copy-start | bytes 6291460
Sparse Core Ops, SparseCore 0:
  8.9 35.4 all-gather.3
  72.6 71.7 reduce-scatter.2
  147.4 34.4 all-gather.5
  191.8 28.1 all-gather.7
  232.0 72.6 reduce-scatter.4
where the time goes:
time: 316 us; the launch traced here: 314 us
  waiting for transfers between devices  245 us (78%)
  matrix products  36.6 us (12%)
  other arithmetic  15.1 us (5%)
  between operations  13.5 us (4%)
    reduce_scatter x1, waiting for transfers between devices, body(): lax.psum_scatter(lin_terms, 'head', scatter_dimension=1, tiled=True)  72.8 us
    reduce_scatter x1, waiting for transfers between devices, body(): lax.psum_scatter(terms, 'head', scatter_dimension=1, tiled=True)  71.8 us
    all_gather x1, waiting for transfers between devices, body(): whole = lax.all_gather(hidden_in, 'head', axis=1, tiled=True)  36.7 us
    all_gather x1, waiting for transfers between devices, body(): after_whole = lax.all_gather(after_window, 'head', axis=1, tiled=True)  34.4 us
    all_gather x1, waiting for transfers between devices, body(): lax.all_gather(local_state.astype(jnp.bfloat16), 'ctx', axis=0, tiled=True)  25.4 us
    reduce_sum x2, other arithmetic, norm_rows(): scale = lax.rsqrt(jnp.mean(wide * wide, axis=-1, keepdims=True) + 1e-05)  6.46 us
  transfers between devices with their start and end apart: 6, of which 6 were waited for; matrix products, arithmetic and copies ran while one was open for 2% of the time, Pallas kernels for 0%

commit v1 on v0

--- a/solution.py
+++ b/solution.py
@@ -15,6 +15,71 @@
     devices = lax.axis_size(axis)
     pairs = [(i, i + by) for i in range(devices) if 0 <= i + by < devices]
     return lax.ppermute(value, axis, pairs)
+
+
+def head_layout():
+    devices = lax.axis_size("head")
+    return devices, devices // 2
+
+
+def core_swap(value):
+    devices = lax.axis_size("head")
+    return lax.ppermute(value, "head", [(h, h ^ 1) for h in range(devices)])
+
+
+def chip_shift(value, by):
+    devices, chips = head_layout()
+    pairs = [(h, ((h // 2 + by) % chips) * 2 + h % 2) for h in range(devices)]
+    return lax.ppermute(value, "head", pairs)
+
+
+def head_reduce_scatter(terms):
+    rows, cols = terms.shape
+    devices, chips = head_layout()
+    me = lax.axis_index("head")
+    core, chip = me % 2, me // 2
+    split = terms.reshape(rows, chips, 2, cols // devices)
+    mine = lax.dynamic_index_in_dim(split, core, axis=2, keepdims=False)
+    other = lax.dynamic_index_in_dim(split, 1 - core, axis=2, keepdims=False)
+    on_chip = mine + core_swap(other)
+    if chips == 1:
+        return on_chip[:, 0]
+    acc = lax.dynamic_index_in_dim(on_chip, (chip + chips - 1) % chips, axis=1, keepdims=False)
+    for step in range(chips - 1):
+        got = chip_shift(acc, 1)
+        index = (chip + 2 * chips - step - 2) % chips
+        acc = got + lax.dynamic_index_in_dim(on_chip, index, axis=1, keepdims=False)
+    return acc
+
+
+def head_all_gather(piece):
+    rows, cols = piece.shape
+    devices, chips = head_layout()
+    me = lax.axis_index("head")
+    core, chip = me % 2, me // 2
+    chip_buf = jnp.zeros((rows, chips, cols), piece.dtype)
+    chip_buf = lax.dynamic_update_index_in_dim(chip_buf, piece, chip, axis=1)
+    cur = piece
+    for step in range(chips - 1):
+        cur = chip_shift(cur, 1)
+        chip_buf = lax.dynamic_update_index_in_dim(
+            chip_buf, cur, (chip + 2 * chips - step - 1) % chips, axis=1
+        )
+    partner = core_swap(chip_buf)
+    whole = jnp.zeros((rows, chips, 2, cols), piece.dtype)
+    whole = lax.dynamic_update_index_in_dim(whole, chip_buf, core, axis=2)
+    whole = lax.dynamic_update_index_in_dim(whole, partner, 1 - core, axis=2)
+    return whole.reshape(rows, devices * cols)
+
+
+def earlier_sum(local):
+    count = lax.axis_size("ctx")
+    sent = local.astype(jnp.bfloat16)
+    total = jnp.zeros(local.shape, jnp.float32)
+    for by in range(1, count):
+        pairs = [(i, i + by) for i in range(count - by)]
+        total = total + lax.ppermute(sent, "ctx", pairs).astype(jnp.float32)
+    return total
 
 
 def norm_rows(values, gain):
@@ -49,7 +114,7 @@
     entry_state,
 ):
     tok_rows = hidden_in.shape[0]
-    whole = lax.all_gather(hidden_in, "head", axis=1, tiled=True)
+    whole = head_all_gather(hidden_in)
     normed = norm_rows(whole, attn_gain)
     query = jnp.dot(normed, w_query, preferred_element_type=jnp.float32).astype(jnp.bfloat16)
     keys = jnp.dot(normed, w_keys, preferred_element_type=jnp.float32).astype(jnp.bfloat16)
@@ -81,9 +146,9 @@
     attended = jnp.einsum("kgts,skd->tkgd", probs, value_all, preferred_element_type=jnp.float32)
     attended = attended.astype(jnp.bfloat16).reshape(tok_rows, -1)
     terms = jnp.dot(attended, wo_attn, preferred_element_type=jnp.float32)
-    partial_out = lax.psum_scatter(terms, "head", scatter_dimension=1, tiled=True)
+    partial_out = head_reduce_scatter(terms)
     after_window = (hidden_in.astype(jnp.float32) + partial_out).astype(jnp.bfloat16)
-    after_whole = lax.all_gather(after_window, "head", axis=1, tiled=True)
+    after_whole = head_all_gather(after_window)
     normed2 = norm_rows(after_whole, lin_gain)
     feats = jnp.dot(normed2, w_feature, preferred_element_type=jnp.float32)
     lin_heads = feats.shape[1] // (2 * FEAT)
@@ -101,14 +166,7 @@
     local_state = jnp.einsum(
         "thf,thv->hfv", phi_key, lvalues.astype(jnp.float32), precision=highest
     )
-    ctx_count = lax.axis_size("ctx")
-    every = (
-        lax.all_gather(local_state.astype(jnp.bfloat16), "ctx", axis=0, tiled=True)
-        .astype(local_state.dtype)
-        .reshape((ctx_count,) + local_state.shape)
-    )
-    earlier = (jnp.arange(ctx_count, dtype=jnp.int32) < lax.axis_index("ctx")).astype(jnp.float32)
-    prior = jnp.einsum("c,chfv->hfv", earlier, every, precision=highest)
+    prior = earlier_sum(local_state)
     carried = entry_state + prior
     cross = jnp.einsum("thf,hfv->thv", phi_query, carried, precision=highest)
     sims = jnp.einsum("thf,shf->hts", query_feat, key_feat, precision=highest) / math.sqrt(FEAT)
@@ -121,7 +179,7 @@
         (lin_out * scale * out_gain[None]).astype(jnp.bfloat16).reshape(tok_rows, lin_heads * VDIM)
     )
     lin_terms = jnp.dot(lin_normed, wo_linear, preferred_element_type=jnp.float32)
-    lin_part = lax.psum_scatter(lin_terms, "head", scatter_dimension=1, tiled=True)
+    lin_part = head_reduce_scatter(lin_terms)
     return (after_window.astype(jnp.float32) + lin_part).astype(jnp.bfloat16)
 
 

time: 316 us -> 277 us (0.88)
  waiting for transfers between devices: 245 us -> 173 us
  local copies, waits for them, and re-layouts: 1.57 us -> 47.3 us
  between operations: 13.5 us -> 0.51 us
  matrix products: 36.6 us -> 25.8 us
  starting transfers between devices: 2.12 us -> 11.9 us
    ppermute x0 -> x11, waiting for transfers between devices: none -> 169 us  [the longest x4 132 us: chip_shift(): return lax.ppermute(value, 'head', pairs)]
    reduce_scatter x2 -> x0, waiting for transfers between devices: 145 us -> none  [the longest x1 72.8 us: body(): lax.psum_scatter(lin_terms, 'head', scatter_dimension=1, tiled=True)]
    all_gather x3 -> x0, waiting for transfers between devices: 96.5 us -> none  [the longest x1 36.7 us: body(): whole = lax.all_gather(hidden_in, 'head', axis=1, tiled=True)]
    dynamic_slice x0 -> x6, local copies, waits for them, and re-layouts: none -> 13.2 us  [the longest x4 8.44 us: head_reduce_scatter(): acc = got + lax.dynamic_index_in_dim(on_chip, index, axis=1, keepdims=False)]
    dot_general x0 -> x2, local copies, waits for them, and re-layouts: none -> 12.9 us  [the longest x1 6.48 us: body(): terms = jnp.dot(attended, wo_attn, preferred_element_type=jnp.float32)]
    ppermute x0 -> x11, starting transfers between devices: none -> 10.5 us  [the longest x4 6.06 us: chip_shift(): return lax.ppermute(value, 'head', pairs)]
    dynamic_update_slice x0 -> x7, local copies, waits for them, and re-layouts: none -> 9.08 us  [the longest x2 3.62 us: head_all_gather(): whole = lax.dynamic_update_index_in_dim(whole, partner, 1 - core, axis=2)]
    reduce_sum x2, other arithmetic: 6.46 us -> 1.89 us  [norm_rows(): scale = lax.rsqrt(jnp.mean(wide * wide, axis=-1, keepdims=True) + 1e-05)]
  transfers between devices with their start and end apart: 6 -> 12, of which waited for: 6 -> 9; matrix products, arithmetic and copies ran while one was open for 2% -> 10% of each run, Pallas kernels for 0% -> 0%
where the time goes in v1:
time: 277 us
  waiting for transfers between devices  173 us (62%)
  local copies, waits for them, and re-layouts  47.3 us (17%)
  matrix products  25.8 us (9%)
  other arithmetic  18.2 us (7%)
  starting transfers between devices  11.9 us (4%)
    ppermute x4, waiting for transfers between devices, chip_shift(): return lax.ppermute(value, 'head', pairs)  132 us
    ppermute x3, waiting for transfers between devices, earlier_sum(): total = total + lax.ppermute(sent, 'ctx', pairs).astype(jnp.float32)  22.3 us
    ppermute x4, waiting for transfers between devices, core_swap(): return lax.ppermute(value, 'head', [(h, h ^ 1) for h in range(devices)])  14.6 us
    dynamic_slice x4, local copies, waits for them, and re-layouts, head_reduce_scatter(): acc = got + lax.dynamic_index_in_dim(on_chip, index, axis=1, keepdims=False)  8.44 us
    dot_general x1, local copies, waits for them, and re-layouts, body(): terms = jnp.dot(attended, wo_attn, preferred_element_type=jnp.float32)  6.48 us
    dot_general x1, local copies, waits for them, and re-layouts, body(): jnp.dot(lin_normed, wo_linear, preferred_element_type=jnp.float32)  6.46 us
    ppermute x4, starting transfers between devices, chip_shift(): return lax.ppermute(value, 'head', pairs)  6.06 us
    add x2, other arithmetic, head_reduce_scatter(): on_chip = mine + core_swap(other)  5.76 us
  transfers between devices with their start and end apart: 12, of which 9 were waited for; matrix products, arithmetic and copies ran while one was open for 10% of the time, Pallas kernels for 0%

profile of v1, /device:TPU:24, one launch (start us, length us, event | category | flops | bytes accessed | tf_op | source)
XLA Modules:
  0.0 276.7 jit_solution(10208983978334083080)
XLA Ops:
  5.7 21.0 %collective-permute-done = bf16[512,1024]{0,1:T(8,128)(2,1)} collective-permute-done((bf16[512,1024]{0,1:T(8,128)(2,1)S(1)}, bf16[512,1024]{0,1:T(8,128)(2,1)}, u32[]{:S(2)}, u32[]{:S(2)}) %collective-permute-start) | collective-permute-done | bytes 1048608 | tf_op jit(solution)/shard_map/ppermute | solution.py:33
  29.0 6.5 %copy.78 = bf16[4096,512]{1,0:T(8,128)(2,1)} copy(bf16[4096,512]{0,1:T(8,128)(2,1)} %bitcast.141) | data formatting | bytes 8388608 | tf_op jit(solution)/shard_map/dot_general | solution.py:148
  46.4 2.4 convolution_convert_fusion.1
  48.8 3.9 %collective-permute-done.2 = bf16[64,512]{0,1:T(8,128)(2,1)S(1)} collective-permute-done((bf16[64,512]{0,1:T(8,128)(2,1)S(1)}, bf16[64,512]{0,1:T(8,128)(2,1)S(1)}, u32[]{:S(2)}, u32[]{:S(2)}) %collective-permute-start.2) | collective-permute-done | bytes 65568 | tf_op jit(solution)/shard_map/ppermute | solution.py:17
  53.1 3.9 %fusion.39 = (f32[2,2,512]{2,1,0:T(2,128)S(1)}, f32[2,2,512,576]{2,3,1,0:T(8,128)}) fusion(pred[512,576]{0,1:T(8,128)(4,1)S(1)} %and_and_fusion, bf16[576,2,128,1]{0,2,3,1:T(8,128)(2,1)S(1)} %bitcast.151, bf16[512,2,2,128]{0,3,2,1:T(8,128)(2,1)S(1)} %bitcast.153), kind=kOutput, calls=%fused_computation.90 | convolution fusion | flops 306709056 | bytes 5840896 | tf_op jit(solution)/shard_map/sub | solution.py:144
  57.0 3.1 %fusion.15 = bf16[2,128,2,512]{3,1,2,0:T(8,128)(2,1)S(1)} fusion(bf16[576,2,128,1]{0,2,3,1:T(8,128)(2,1)S(1)} %bitcast.150, f32[2,2,512,576]{2,3,1,0:T(8,128)} %get-tuple-element.18, f32[2,2,512]{2,1,0:T(2,128)S(1)} %get-tuple-element.17), kind=kOutput, calls=%fused_computation.37 | convolution fusion | flops 304611328 | bytes 5545984 | tf_op jit(solution)/shard_map/kgts,skd->tkgd/dot_general | solution.py:146
  60.6 2.4 fusion.40
  63.1 2.8 %dynamic-slice_bitcast_fusion.1 = f32[512,2,1024]{2,0,1:T(8,128)} fusion(f32[512,2,2,1024]{3,0,2,1:T(8,128)S(1)} %fusion.40, s32[]{:T(128)S(6)} %select_n.84), kind=kLoop, calls=%fused_computation.16 | loop fusion | bytes 8388612 | tf_op jit(solution)/shard_map/jit(dynamic_index_in_dim)/squeeze | solution.py:43
  67.6 7.5 %collective-permute-done.3 = f32[512,2,1024]{2,0,1:T(8,128)} collective-permute-done((f32[512,2,1024]{2,0,1:T(8,128)}, f32[512,2,1024]{2,0,1:T(8,128)}, u32[]{:S(2)}, u32[]{:S(2)}) %collective-permute-start.3) | collective-permute-done | bytes 4194336 | tf_op jit(solution)/shard_map/ppermute | solution.py:27
  75.1 4.4 %bitcast_add_fusion.1 = f32[512,2,1024]{2,0,1:T(8,128)S(1)} fusion(f32[512,2,1024]{2,0,1:T(8,128)} %collective-permute-done.3, f32[512,2,2,1024]{3,0,2,1:T(8,128)} %copy-done.2, s32[]{:T(128)S(6)} %select_n.83), kind=kLoop, calls=%fused_computation.14 | loop fusion | flops 1048576 | bytes 12582916 | tf_op jit(solution)/shard_map/add | solution.py:44
  81.1 2.9 %copy.51 = f32[512,1,1024]{0,2,1:T(8,128)} copy(f32[512,1,1024]{2,0,1:T(8,128)} %get-tuple-element.10) | data formatting | bytes 4194304 | tf_op jit(solution)/shard_map/jit(dynamic_index_in_dim)/dynamic_slice | solution.py:47
  87.3 44.7 %collective-permute-done.4 = f32[512,1024]{0,1:T(8,128)} collective-permute-done((f32[512,1024]{0,1:T(8,128)}, f32[512,1024]{0,1:T(8,128)}, u32[]{:S(2)}, u32[]{:S(2)}) %collective-permute-start.4) | collective-permute-done | bytes 2097184 | tf_op jit(solution)/shard_map/ppermute | solution.py:33
  132.1 2.9 %bitcast_dynamic-update-slice_fusion.5 = (bf16[512,2,1024]{0,2,1:T(8,128)(2,1)S(1)}, bf16[512,1024]{0,1:T(8,128)(2,1)S(1)}) fusion(bf16[512,2,1024]{0,2,1:T(8,128)(2,1)S(1)} %broadcast.118, s32[]{:T(128)S(6)} %select_n.79, f32[512,1024]{0,1:T(8,128)} %collective-permute-done.4, f32[512,1,1024]{0,2,1:T(8,128)} %copy.52, bf16[512,1024]{0,1:T(8,128)(2,1)S(1)} %copy.42), kind=kLoop, calls=%fused_computation.51 | loop fusion | flops 2097152 | bytes 7340036 | tf_op jit(solution)/shard_map/jit(dynamic_update_index_in_dim)/dynamic_update_slice | solution.py:61
  136.6 22.9 %collective-permute-done.5 = bf16[512,1024]{0,1:T(8,128)(2,1)S(1)} collective-permute-done((bf16[512,1024]{0,1:T(8,128)(2,1)S(1)}, bf16[512,1024]{0,1:T(8,128)(2,1)S(1)}, u32[]{:S(2)}, u32[]{:S(2)}) %collective-permute-start.5) | collective-permute-done | bytes 1048608 | tf_op jit(solution)/shard_map/ppermute | solution.py:33
  159.7 6.5 %copy.85 = bf16[4096,512]{1,0:T(8,128)(2,1)} copy(bf16[4096,512]{0,1:T(8,128)(2,1)} %bitcast.142) | data formatting | bytes 8388608 | tf_op jit(solution)/shard_map/dot_general | solution.py:181
  173.8 2.4 convolution_convert_fusion
  181.3 2.3 select_convert_fusion
  184.3 4.1 %collective-permute-done.7 = bf16[2,273,256]{2,1,0:T(8,128)(2,1)S(1)} collective-permute-done((bf16[2,273,256]{2,1,0:T(8,128)(2,1)S(1)}, bf16[2,273,256]{2,1,0:T(8,128)(2,1)S(1)}, u32[]{:S(2)}, u32[]{:S(2)}) %collective-permute-start.7) | collective-permute-done | bytes 279584 | tf_op jit(solution)/shard_map/ppermute | solution.py:81
  188.4 18.2 %collective-permute-done.8 = bf16[2,273,256]{2,1,0:T(8,128)(2,1)S(1)} collective-permute-done((bf16[2,273,256]{2,1,0:T(8,128)(2,1)S(1)}, bf16[2,273,256]{2,1,0:T(8,128)(2,1)S(1)}, u32[]{:S(2)}, u32[]{:S(2)}) %collective-permute-start.8) | collective-permute-done | bytes 279584 | tf_op jit(solution)/shard_map/ppermute | solution.py:81
  209.0 2.4 fusion.43
  212.1 7.1 %collective-permute-done.10 = f32[512,2,1024]{2,0,1:T(8,128)S(1)} collective-permute-done((f32[512,2,1024]{2,0,1:T(8,128)S(1)}, f32[512,2,1024]{2,0,1:T(8,128)S(1)}, u32[]{:S(2)}, u32[]{:S(2)}) %collective-permute-start.10) | collective-permute-done | bytes 4194336 | tf_op jit(solution)/shard_map/ppermute | solution.py:27
  225.8 3.1 %copy.64 = f32[512,1,1024]{0,2,1:T(8,128)} copy(f32[512,1,1024]{2,0,1:T(8,128)} %get-tuple-element.7) | data formatting | bytes 4194304 | tf_op jit(solution)/shard_map/jit(dynamic_index_in_dim)/dynamic_slice | solution.py:51
  228.9 43.4 %collective-permute-done.11 = f32[512,1024]{0,1:T(8,128)} collective-permute-done((f32[512,1024]{0,1:T(8,128)}, f32[512,1024]{0,1:T(8,128)}, u32[]{:S(2)}, u32[]{:S(2)}) %collective-permute-start.11) | collective-permute-done | bytes 2097184 | tf_op jit(solution)/shard_map/ppermute | solution.py:33
  272.3 3.1 %fusion.11 = bf16[512,1024]{0,1:T(8,128)(2,1)S(1)} fusion(f32[512,1024]{0,1:T(8,128)} %collective-permute-done.11, f32[512,1,1024]{0,2,1:T(8,128)} %copy.64, bf16[512,1024]{0,1:T(8,128)(2,1)} %copy-done.5), kind=kLoop, calls=%fused_computation.27 | loop fusion | flops 2097152 | bytes 6291456 | tf_op jit(solution)/shard_map/convert_element_type | solution.py:183
  (91 shorter events, 52.3 us)
Async XLA Ops:
  0.0 41.9 %copy-start = (bf16[4096,256]{1,0:T(8,128)(2,1)S(1)}, bf16[4096,256]{1,0:T(8,128)(2,1)}, u32[]{:S(2)}) copy-start(bf16[4096,256]{1,0:T(8,128)(2,1)} %param.16) | copy-start | bytes 6291460
  1.7 25.1 %collective-permute-start = (bf16[512,1024]{0,1:T(8,128)(2,1)S(1)}, bf16[512,1024]{0,1:T(8,128)(2,1)}, u32[]{:S(2)}, u32[]{:S(2)}) collective-permute-start(bf16[512,1024]{0,1:T(8,128)(2,1)S(1)} %copy.42), channel_id=1, source_target_pairs={{0,2},{1,3},{2,0},{3,1},{4,6},{5,7},{6,4},{7,5},{8,10},{9,11},{10,... | collective-permute-start | bytes 3145736 | tf_op jit(solution)/shard_map/ppermute | solution.py:33
  29.0 9.0 %collective-permute-start.1 = (bf16[512,2,1024]{0,2,1:T(8,128)(2,1)}, bf16[512,2,1024]{0,2,1:T(8,128)(2,1)}, u32[]{:S(2)}, u32[]{:S(2)}) collective-permute-start(bf16[512,2,1024]{0,2,1:T(8,128)(2,1)} %bitcast_dynamic-update-slice_fusion.6), channel_id=1, source_target_pairs={{0,1},{1,0},{2,3},{3,2},{4,5},{5,4},{6,7},{7,6},{8,9},{9,8},{10,11... | collective-permute-start | bytes 6291464 | tf_op jit(solution)/shard_map/ppermute | solution.py:27
  38.0 2.8 %copy-start.8 = (f32[4096]{0:T(1024)S(1)}, f32[4096]{0:T(1024)}, u32[]{:S(2)}) copy-start(f32[4096]{0:T(1024)} %param.13) | copy-start | bytes 49156
  43.5 2.9 %copy-start.10 = (bf16[4096,512]{1,0:T(8,128)(2,1)S(1)}, bf16[4096,512]{1,0:T(8,128)(2,1)}, u32[]{:S(2)}) copy-start(bf16[4096,512]{1,0:T(8,128)(2,1)} %param.14) | copy-start | bytes 12582916
  44.9 7.8 %collective-permute-start.2 = (bf16[64,512]{0,1:T(8,128)(2,1)S(1)}, bf16[64,512]{0,1:T(8,128)(2,1)S(1)}, u32[]{:S(2)}, u32[]{:S(2)}) collective-permute-start(bf16[64,512]{0,1:T(8,128)(2,1)S(1)} %pad_maximum_fusion), channel_id=1, source_target_pairs={{0,4},{4,8},{8,12},{1,5},{5,9},{9,13},{2,6},{6,10},{10,14},{3,7},{... | collective-permute-start | bytes 196616 | tf_op jit(solution)/shard_map/ppermute | solution.py:17
  57.0 3.6 %copy-start.4 = (bf16[4096,512]{1,0:T(8,128)(2,1)S(1)}, bf16[4096,512]{1,0:T(8,128)(2,1)}, u32[]{:S(2)}) copy-start(bf16[4096,512]{1,0:T(8,128)(2,1)} %copy.78) | copy-start | bytes 12582916
  63.1 4.5 %copy-start.2 = (f32[512,2,2,1024]{3,0,2,1:T(8,128)}, f32[512,2,2,1024]{3,0,2,1:T(8,128)S(1)}, u32[]{:S(2)}) copy-start(f32[512,2,2,1024]{3,0,2,1:T(8,128)S(1)} %fusion.40) | copy-start | bytes 25165828
  67.5 7.5 %collective-permute-start.3 = (f32[512,2,1024]{2,0,1:T(8,128)}, f32[512,2,1024]{2,0,1:T(8,128)}, u32[]{:S(2)}, u32[]{:S(2)}) collective-permute-start(f32[512,2,1024]{2,0,1:T(8,128)} %dynamic-slice_bitcast_fusion.1), channel_id=1, source_target_pairs={{0,1},{1,0},{2,3},{3,2},{4,5},{5,4},{6,7},{7,6},{8,9},{9,8},{10,11... | collective-permute-start | bytes 12582920 | tf_op jit(solution)/shard_map/ppermute | solution.py:27
  84.0 48.0 %collective-permute-start.4 = (f32[512,1024]{0,1:T(8,128)}, f32[512,1024]{0,1:T(8,128)}, u32[]{:S(2)}, u32[]{:S(2)}) collective-permute-start(f32[512,1024]{0,1:T(8,128)} %bitcast.144), channel_id=1, source_target_pairs={{0,2},{1,3},{2,0},{3,1},{4,6},{5,7},{6,4},{7,5},{8,10},{9,11},{10,... | collective-permute-start | bytes 6291464 | tf_op jit(solution)/shard_map/ppermute | solution.py:33
  132.1 27.6 %copy-start.7 = (f32[4096]{0:T(1024)S(1)}, f32[4096]{0:T(1024)}, u32[]{:S(2)}) copy-start(f32[4096]{0:T(1024)} %param.18) | copy-start | bytes 49156
  135.0 24.6 %copy-start.5 = (bf16[512,1024]{0,1:T(8,128)(2,1)}, bf16[512,1024]{0,1:T(8,128)(2,1)S(1)}, u32[]{:S(2)}) copy-start(bf16[512,1024]{0,1:T(8,128)(2,1)S(1)} %get-tuple-element.6) | copy-start | bytes 3145732
  135.0 24.4 %collective-permute-start.5 = (bf16[512,1024]{0,1:T(8,128)(2,1)S(1)}, bf16[512,1024]{0,1:T(8,128)(2,1)S(1)}, u32[]{:S(2)}, u32[]{:S(2)}) collective-permute-start(bf16[512,1024]{0,1:T(8,128)(2,1)S(1)} %get-tuple-element.6), channel_id=1, source_target_pairs={{0,2},{1,3},{2,0},{3,1},{4,6},{5,7},{6,4},{7,5},{8,10},{9,11},{10,... | collective-permute-start | bytes 3145736 | tf_op jit(solution)/shard_map/ppermute | solution.py:33
  159.6 7.2 %collective-permute-start.6 = (bf16[512,2,1024]{0,2,1:T(8,128)(2,1)S(1)}, bf16[512,2,1024]{0,2,1:T(8,128)(2,1)}, u32[]{:S(2)}, u32[]{:S(2)}) collective-permute-start(bf16[512,2,1024]{0,2,1:T(8,128)(2,1)S(1)} %bitcast_dynamic-update-slice_fusion.4), channel_id=1, source_target_pairs={{0,1},{1,0},{2,3},{3,2},{4,5},{5,4},{6,7},{7,6},{8,9},{9,8},{10,11... | collective-permute-start | bytes 6291464 | tf_op jit(solution)/shard_map/ppermute | solution.py:27
  171.6 2.2 copy-start.11
  177.0 29.6 %copy-start.6 = (f32[2,273,256]{2,0,1:T(2,128)S(1)}, f32[2,273,256]{2,0,1:T(2,128)}, u32[]{:S(2)}) copy-start(f32[2,273,256]{2,0,1:T(2,128)} %param.23) | copy-start | bytes 1677316
  177.0 11.4 %collective-permute-start.7 = (bf16[2,273,256]{2,1,0:T(8,128)(2,1)S(1)}, bf16[2,273,256]{2,1,0:T(8,128)(2,1)S(1)}, u32[]{:S(2)}, u32[]{:S(2)}) collective-permute-start(bf16[2,273,256]{2,1,0:T(8,128)(2,1)S(1)} %convolution_convert_fusion.2), channel_id=1, source_target_pairs={{0,4},{4,8},{8,12},{1,5},{5,9},{9,13},{2,6},{6,10},{10,14},{3,7},{... | collective-permute-start | bytes 838664 | tf_op jit(solution)/shard_map/ppermute | solution.py:81
  178.4 28.1 %collective-permute-start.8 = (bf16[2,273,256]{2,1,0:T(8,128)(2,1)S(1)}, bf16[2,273,256]{2,1,0:T(8,128)(2,1)S(1)}, u32[]{:S(2)}, u32[]{:S(2)}) collective-permute-start(bf16[2,273,256]{2,1,0:T(8,128)(2,1)S(1)} %convolution_convert_fusion.2), channel_id=1, source_target_pairs={{0,8},{4,12},{1,9},{5,13},{2,10},{6,14},{3,11},{7,15},{16,24},{20,... | collective-permute-start | bytes 838664 | tf_op jit(solution)/shard_map/ppermute | solution.py:81
  179.7 26.8 %collective-permute-start.9 = (bf16[2,273,256]{2,1,0:T(8,128)(2,1)S(1)}, bf16[2,273,256]{2,1,0:T(8,128)(2,1)S(1)}, u32[]{:S(2)}, u32[]{:S(2)}) collective-permute-start(bf16[2,273,256]{2,1,0:T(8,128)(2,1)S(1)} %convolution_convert_fusion.2), channel_id=1, source_target_pairs={{0,12},{1,13},{2,14},{3,15},{16,28},{17,29},{18,30},{19,31}} | collective-permute-start | bytes 838664 | tf_op jit(solution)/shard_map/ppermute | solution.py:81
  183.6 25.1 %copy-start.9 = (f32[2,256]{1,0:T(2,128)S(1)}, f32[2,256]{1,0:T(2,128)}, u32[]{:S(2)}) copy-start(f32[2,256]{1,0:T(2,128)} %param.21) | copy-start | bytes 6148
  183.8 25.2 %copy-start.3 = (bf16[4096,512]{1,0:T(8,128)(2,1)S(1)}, bf16[4096,512]{1,0:T(8,128)(2,1)}, u32[]{:S(2)}) copy-start(bf16[4096,512]{1,0:T(8,128)(2,1)} %copy.85) | copy-start | bytes 12582916
  212.0 7.2 %collective-permute-start.10 = (f32[512,2,1024]{2,0,1:T(8,128)S(1)}, f32[512,2,1024]{2,0,1:T(8,128)S(1)}, u32[]{:S(2)}, u32[]{:S(2)}) collective-permute-start(f32[512,2,1024]{2,0,1:T(8,128)S(1)} %dynamic-slice_bitcast_fusion), channel_id=1, source_target_pairs={{0,1},{1,0},{2,3},{3,2},{4,5},{5,4},{6,7},{7,6},{8,9},{9,8},{10,11... | collective-permute-start | bytes 12582920 | tf_op jit(solution)/shard_map/ppermute | solution.py:27
  224.3 48.0 %collective-permute-start.11 = (f32[512,1024]{0,1:T(8,128)}, f32[512,1024]{0,1:T(8,128)}, u32[]{:S(2)}, u32[]{:S(2)}) collective-permute-start(f32[512,1024]{0,1:T(8,128)} %bitcast.145), channel_id=1, source_target_pairs={{0,2},{1,3},{2,0},{3,1},{4,6},{5,7},{6,4},{7,5},{8,10},{9,11},{10,... | collective-permute-start | bytes 6291464 | tf_op jit(solution)/shard_map/ppermute | solution.py:33
  225.8 50.9 %copy-start.1 = (bf16[4096,256]{1,0:T(8,128)(2,1)S(1)}, bf16[4096,256]{1,0:T(8,128)(2,1)}, u32[]{:S(2)}) copy-start(bf16[4096,256]{1,0:T(8,128)(2,1)} %param.16) | copy-start | bytes 6291460
  (2 other events, 2.7 us)

commit v2 on v1

v2 whole, which is shorter than its diff:
```python
import math

import jax
import jax.numpy as jnp
from jax import lax
from jax.sharding import PartitionSpec as P

HEAD = 128
WINDOW = 64
FEAT = 16
VDIM = 256


def from_behind(value, axis, by):
    devices = lax.axis_size(axis)
    pairs = [(i, i + by) for i in range(devices) if 0 <= i + by < devices]
    return lax.ppermute(value, axis, pairs)


def head_layout():
    devices = lax.axis_size("head")
    return devices, devices // 2


def core_swap(value):
    devices = lax.axis_size("head")
    return lax.ppermute(value, "head", [(h, h ^ 1) for h in range(devices)])


def chip_shift(value, by):
    devices, chips = head_layout()
    pairs = [(h, ((h // 2 + by) % chips) * 2 + h % 2) for h in range(devices)]
    return lax.ppermute(value, "head", pairs)


def head_reduce_scatter(lhs, weight):
    devices, chips = head_layout()
    me = lax.axis_index("head")
    core, chip = me % 2, me // 2
    width = weight.shape[1] // devices

    def block(which, offset):
        col = (((chip + offset) % chips) * 2 + which) * width
        cols = lax.dynamic_slice_in_dim(weight, col, width, axis=1)
        return jnp.dot(lhs, cols, preferred_element_type=jnp.float32)

    order = [chips - 1 - j for j in range(chips)]
    on_chip = {}
    for offset in order:
        on_chip[offset] = block(core, offset) + core_swap(block(1 - core, offset))
    acc = on_chip[chips - 1]
    for step in range(chips - 1):
        got = chip_shift(acc.astype(jnp.bfloat16), 1).astype(jnp.float32)
        acc = got + on_chip[(chips - step - 2) % chips]
    return acc


def head_all_gather(piece):
    rows, cols = piece.shape
    devices, chips = head_layout()
    me = lax.axis_index("head")
    core, chip = me % 2, me // 2
    chip_buf = jnp.zeros((rows, chips, cols), piece.dtype)
    chip_buf = lax.dynamic_update_index_in_dim(chip_buf, piece, chip, axis=1)
    cur = piece
    for step in range(chips - 1):
        cur = chip_shift(cur, 1)
        chip_buf = lax.dynamic_update_index_in_dim(
            chip_buf, cur, (chip + 2 * chips - step - 1) % chips, axis=1
        )
    partner = core_swap(chip_buf)
    whole = jnp.zeros((rows, chips, 2, cols), piece.dtype)
    whole = lax.dynamic_update_index_in_dim(whole, chip_buf, core, axis=2)
    whole = lax.dynamic_update_index_in_dim(whole, partner, 1 - core, axis=2)
    return whole.reshape(rows, devices * cols)


def earlier_sum(local):
    count = lax.axis_size("ctx")
    sent = local.astype(jnp.bfloat16)
    total = jnp.zeros(local.shape, jnp.float32)
    for by in range(1, count):
        pairs = [(i, i + by) for i in range(count - by)]
        total = total + lax.ppermute(sent, "ctx", pairs).astype(jnp.float32)
    return total


def norm_rows(values, gain):
    wide = values.astype(jnp.float32)
    scale = lax.rsqrt(jnp.mean(wide * wide, axis=-1, keepdims=True) + 1e-05)
    return (wide * scale * gain).astype(jnp.bfloat16)


def taylor(inputs):
    width = inputs.shape[-1]
    outer = (inputs[..., :, None] * inputs[..., None, :]).reshape(
        inputs.shape[:-1] + (width * width,)
    )
    ones = jnp.ones(inputs.shape[:-1] + (1,), jnp.float32)
    return jnp.concatenate(
        [ones, inputs / width**0.25, outer / (math.sqrt(2.0) * math.sqrt(width))], axis=-1
    )


CHUNKS = 2


def body(
    hidden_in,
    attn_gain,
    w_query,
    w_keys,
    w_values,
    wo_attn,
    lin_gain,
    w_feature,
    wv_linear,
    out_gain,
    wo_linear,
    entry_state,
):
    tok_rows = hidden_in.shape[0]
    size = tok_rows // CHUNKS
    kv_cols = w_keys.shape[1]
    kv_heads = kv_cols // HEAD
    group = w_query.shape[1] // HEAD // kv_heads
    hidden_parts = [hidden_in[i * size : (i + 1) * size] for i in range(CHUNKS)]

    query_parts, kv_parts = [], []
    for part in hidden_parts:
        normed = norm_rows(head_all_gather(part), attn_gain)
        query_parts.append(
            jnp.dot(normed, w_query, preferred_element_type=jnp.float32).astype(jnp.bfloat16)
        )
        keys = jnp.dot(normed, w_keys, preferred_element_type=jnp.float32).astype(jnp.bfloat16)
        values = jnp.dot(normed, w_values, preferred_element_type=jnp.float32).astype(jnp.bfloat16)
        kv_parts.append(jnp.concatenate([keys, values], axis=1))
    rim = from_behind(kv_parts[-1][size - WINDOW :], "ctx", 1)
    kv_all = jnp.concatenate([rim] + kv_parts, axis=0)
    start = lax.axis_index("ctx") * tok_rows

    after_parts, after_whole_parts = [], []
    for i in range(CHUNKS):
        kv_win = kv_all[i * size : i * size + size + WINDOW]
        key_win = kv_win[:, :kv_cols].reshape(size + WINDOW, kv_heads, HEAD)
        value_win = kv_win[:, kv_cols:].reshape(size + WINDOW, kv_heads, HEAD)
        query_heads = query_parts[i].reshape(size, kv_heads, group, HEAD)
        scores = jnp.einsum(
            "tkgd,skd->kgts", query_heads, key_win, preferred_element_type=jnp.float32
        ) / math.sqrt(HEAD)
        qpos = start + i * size + jnp.arange(size, dtype=jnp.int32)
        kpos = start + i * size - WINDOW + jnp.arange(size + WINDOW, dtype=jnp.int32)
        visible = (
            (kpos[None, :] <= qpos[:, None])
            & (kpos[None, :] > qpos[:, None] - WINDOW)
            & (kpos[None, :] >= 0)
        )
        scores = jnp.where(visible, scores, -jnp.inf)
        top = jnp.max(scores, axis=-1, keepdims=True)
        expd = jnp.exp(scores - top)
        probs = (expd / jnp.sum(expd, axis=-1, keepdims=True)).astype(jnp.bfloat16)
        attended = jnp.einsum(
            "kgts,skd->tkgd", probs, value_win, preferred_element_type=jnp.float32
        )
        attended = attended.astype(jnp.bfloat16).reshape(size, -1)
        partial_out = head_reduce_scatter(attended, wo_attn)
        after_window = (hidden_parts[i].astype(jnp.float32) + partial_out).astype(jnp.bfloat16)
        after_parts.append(after_window)
        after_whole_parts.append(head_all_gather(after_window))

    qf_parts, kf_parts, lv_parts = [], [], []
    for i in range(CHUNKS):
        normed2 = norm_rows(after_whole_parts[i], lin_gain)
        feats = jnp.dot(normed2, w_feature, preferred_element_type=jnp.float32)
        lin_heads = feats.shape[1] // (2 * FEAT)
        feats = feats.reshape(size, lin_heads, 2, FEAT)
        qf_parts.append(feats[:, :, 0, :])
        kf_parts.append(feats[:, :, 1, :])
        lv_parts.append(
            jnp.dot(normed2, wv_linear, preferred_element_type=jnp.float32)
            .astype(jnp.bfloat16)
            .reshape(size, lin_heads, VDIM)
        )
    key_feat = jnp.concatenate(kf_parts, axis=0)
    lvalues = jnp.concatenate(lv_parts, axis=0)
    lin_heads = key_feat.shape[1]
    highest = lax.Precision.HIGHEST
    phi_key = taylor(key_feat)
    local_state = jnp.einsum(
        "thf,thv->hfv", phi_key, lvalues.astype(jnp.float32), precision=highest
    )
    carried = entry_state + earlier_sum(local_state)

    outs = []
    for i in range(CHUNKS):
        query_feat = qf_parts[i]
        phi_query = taylor(query_feat)
        cross = jnp.einsum("thf,hfv->thv", phi_query, carried, precision=highest)
        sims = jnp.einsum(
            "thf,shf->hts", query_feat, key_feat, precision=highest
        ) / math.sqrt(FEAT)
        causal = (i * size + jnp.arange(size))[:, None] >= jnp.arange(tok_rows)[None, :]
        weights = jnp.where(causal[None], 1.0 + sims + 0.5 * sims * sims, 0.0).astype(jnp.bfloat16)
        intra = jnp.einsum("hts,shv->thv", weights, lvalues, preferred_element_type=jnp.float32)
        lin_out = cross + intra
        scale = lax.rsqrt(jnp.mean(lin_out * lin_out, axis=-1, keepdims=True) + 1e-05)
        lin_normed = (
            (lin_out * scale * out_gain[None]).astype(jnp.bfloat16).reshape(size, lin_heads * VDIM)
        )
        lin_part = head_reduce_scatter(lin_normed, wo_linear)
        outs.append((after_parts[i].astype(jnp.float32) + lin_part).astype(jnp.bfloat16))
    return jnp.concatenate(outs, axis=0)


def solution(mesh):
    in_specs = (
        P(("groups", "ctx"), "head"),
        P(),
        P(None, "head"),
        P(None, "head"),
        P(None, "head"),
        P("head", None),
        P(),
        P(None, "head"),
        P(None, "head"),
        P("head", None),
        P("head", None),
        P(("groups", "head"), None, None),
    )
    out_specs = P(("groups", "ctx"), "head")
    return jax.shard_map(body, mesh=mesh, in_specs=in_specs, out_specs=out_specs, check_vma=False)
```

time: 277 us -> 195 us (0.70)
  waiting for transfers between devices: 173 us -> 85.4 us
  matrix products: 25.8 us -> 47.6 us
  local copies, waits for them, and re-layouts: 47.3 us -> 33.7 us
  other arithmetic: 18.2 us -> 8.26 us
  starting transfers between devices: 11.9 us -> 17.8 us
    ppermute x4 -> x8, waiting for transfers between devices: 132 us -> 61.6 us  [chip_shift(): return lax.ppermute(value, 'head', pairs)]
    dot_general x3 -> x18, matrix products: 7.92 us -> 27 us  [the longest x16 23.8 us: block(): return jnp.dot(lhs, cols, preferred_element_type=jnp.float32)]
    ppermute x4 -> x12, waiting for transfers between devices: 14.6 us -> 0.1 us  [core_swap(): return lax.ppermute(value, 'head', [(h, h ^ 1) for h in range(devices)])]
    dynamic_slice x6 -> x0, local copies, waits for them, and re-layouts: 13.2 us -> none  [the longest x4 8.44 us: head_reduce_scatter(): acc = got + lax.dynamic_index_in_dim(on_chip, index, axis=1, keepdims=False)]
    dot_general x2 -> x0, local copies, waits for them, and re-layouts: 12.9 us -> none  [the longest x1 6.48 us: body(): terms = jnp.dot(attended, wo_attn, preferred_element_type=jnp.float32)]
    broadcast_in_dim x0 -> x8, local copies, waits for them, and re-layouts: none -> 8.99 us  [the longest x4 5.55 us: head_all_gather(): lax.dynamic_update_index_in_dim(chip_buf, cur, (chip + 2 * chips - step -...]
    add x4 -> x5, other arithmetic: 5.77 us -> 0.03 us  [the longest x2 0.01 us: body(): qpos = start + i * size + jnp.arange(size, dtype=jnp.int32)]
    ppermute x1, waiting for transfers between devices: 3.94 us -> 0.01 us  [from_behind(): return lax.ppermute(value, axis, pairs)]
  transfers between devices with their start and end apart: 12 -> 24, of which waited for: 9 -> 11; matrix products, arithmetic and copies ran while one was open for 10% -> 31% of each run, Pallas kernels for 0% -> 0%
where the time goes in v2:
time: 195 us; the launch traced here: 193 us
  waiting for transfers between devices  85.4 us (44%)
  matrix products  47.6 us (24%)
  local copies, waits for them, and re-layouts  33.7 us (17%)
  starting transfers between devices  17.8 us (9%)
  other arithmetic  8.26 us (4%)
    ppermute x8, waiting for transfers between devices, chip_shift(): return lax.ppermute(value, 'head', pairs)  61.6 us
    dot_general x16, matrix products, block(): return jnp.dot(lhs, cols, preferred_element_type=jnp.float32)  23.8 us
    ppermute x3, waiting for transfers between devices, earlier_sum(): total = total + lax.ppermute(sent, 'ctx', pairs).astype(jnp.float32)  23.7 us
    ppermute x8, starting transfers between devices, chip_shift(): return lax.ppermute(value, 'head', pairs)  9.77 us
    broadcast_in_dim x4, local copies, waits for them, and re-layouts, head_all_gather(): lax.dynamic_update_index_in_dim(chip_buf, cur, (chip + 2 * chips - step -...  5.55 us
    unnamed x29, local copies, waits for them, and re-layouts  5.1 us
    dynamic_update_slice x4, local copies, waits for them, and re-layouts, head_all_gather(): lax.dynamic_update_index_in_dim(chip_buf, cur, (chip + 2 * chips - step -...  4.61 us
    ppermute x3, starting transfers between devices, earlier_sum(): total = total + lax.ppermute(sent, 'ctx', pairs).astype(jnp.float32)  4.1 us
  transfers between devices with their start and end apart: 24, of which 11 were waited for; matrix products, arithmetic and copies ran while one was open for 31% of the time, Pallas kernels for 0%

profile of v2, /device:TPU:24, one launch (start us, length us, event | category | flops | bytes accessed | tf_op | source)
XLA Modules:
  0.0 193.5 jit_solution(8731388461503611028)
XLA Ops:
  0.0 2.6 %fusion.109 = (bf16[256,1024]{1,0:T(8,128)(2,1)}, bf16[256,1,1024]{2,0,1:T(8,128)(2,1)S(1)}, bf16[256,1,1024]{2,0,1:T(8,128)(2,1)}, bf16[256,1024]{1,0:T(8,128)(2,1)}) fusion(bf16[512,1024]{1,0:T(8,128)(2,1)} %param.12), kind=kLoop, calls=%fused_computation.195 | loop fusion | bytes 3145728 | tf_op jit(solution)/shard_map/slice | solution.py:127
  7.0 10.7 %collective-permute-done.3 = bf16[256,1024]{1,0:T(8,128)(2,1)} collective-permute-done((bf16[256,1024]{1,0:T(8,128)(2,1)}, bf16[256,1024]{1,0:T(8,128)(2,1)}, u32[]{:S(2)}, u32[]{:S(2)}) %collective-permute-start.3) | collective-permute-done | bytes 524320 | tf_op jit(solution)/shard_map/ppermute | solution.py:33
  17.7 2.1 %copy.61 = bf16[256,1,1024]{0,2,1:T(8,128)(2,1)} copy(bf16[256,1,1024]{2,0,1:T(8,128)(2,1)} %bitcast.7) | data formatting | bytes 1048576 | tf_op jit(solution)/shard_map/jit(dynamic_update_index_in_dim)/broadcast_in_dim | solution.py:68
  21.0 2.0 %copy.57 = bf16[256,1,1024]{0,2,1:T(8,128)(2,1)} copy(bf16[256,1,1024]{2,0,1:T(8,128)(2,1)} %get-tuple-element.7) | data formatting | bytes 1048576 | tf_op jit(solution)/shard_map/jit(dynamic_update_index_in_dim)/broadcast_in_dim | solution.py:64
  24.1 1.9 constant_dynamic-update-slice_fusion.7
  26.1 1.7 collective-permute-done
  27.8 2.0 %copy.58 = bf16[256,1,1024]{0,2,1:T(8,128)(2,1)} copy(bf16[256,1,1024]{2,0,1:T(8,128)(2,1)} %bitcast.1) | data formatting | bytes 1048576 | tf_op jit(solution)/shard_map/jit(dynamic_update_index_in_dim)/broadcast_in_dim | solution.py:68
  29.9 1.9 constant_dynamic-update-slice_fusion.6
  50.6 2.7 %fusion.54 = f32[256,1024]{1,0:T(8,128)} fusion(bf16[256,512]{0,1:T(8,128)(2,1)S(1)} %bitcast.206, bf16[512,4096]{1,0:T(8,128)(2,1)} %param.17, s32[]{:T(128)S(6)} %select_n.152), kind=kOutput, calls=%fused_computation.97 | convolution fusion | flops 268435456 | bytes 2359300 | tf_op jit(solution)/shard_map/dot_general | solution.py:45
  57.5 2.7 %fusion.56 = f32[256,1024]{1,0:T(8,128)} fusion(bf16[256,512]{0,1:T(8,128)(2,1)S(1)} %bitcast.210, bf16[512,4096]{1,0:T(8,128)(2,1)} %param.17, s32[]{:T(128)S(6)} %select_n.152), kind=kOutput, calls=%fused_computation.99 | convolution fusion | flops 268435456 | bytes 2359300 | tf_op jit(solution)/shard_map/dot_general | solution.py:45
  60.2 2.7 %fusion.44 = f32[256,1024]{1,0:T(8,128)} fusion(bf16[256,512]{0,1:T(8,128)(2,1)S(1)} %bitcast.207, bf16[512,4096]{1,0:T(8,128)(2,1)} %param.17, s32[]{:T(128)S(6)} %select_n.155), kind=kOutput, calls=%fused_computation.91 | convolution fusion | flops 268435456 | bytes 2359300 | tf_op jit(solution)/shard_map/dot_general | solution.py:45
  63.4 2.5 %fusion.19 = bf16[256,1024]{1,0:T(8,128)(2,1)} fusion(f32[256,1024]{1,0:T(8,128)S(1)} %collective-permute-done.10, bf16[256,512]{0,1:T(8,128)(2,1)S(1)} %bitcast.208, bf16[512,4096]{1,0:T(8,128)(2,1)} %param.17, s32[]{:T(128)S(6)} %select_n.151), kind=kOutput, calls=%fused_computation.41 | convolution fusion | flops 268959744 | bytes 2883588 | tf_op jit(solution)/shard_map/dot_general | solution.py:45
  67.4 2.7 %fusion.46 = f32[256,1024]{1,0:T(8,128)} fusion(bf16[256,512]{0,1:T(8,128)(2,1)S(1)} %bitcast.211, bf16[512,4096]{1,0:T(8,128)(2,1)} %param.17, s32[]{:T(128)S(6)} %select_n.155), kind=kOutput, calls=%fused_computation.93 | convolution fusion | flops 268435456 | bytes 2359300 | tf_op jit(solution)/shard_map/dot_general | solution.py:45
  70.0 2.5 %fusion.18 = bf16[256,1024]{1,0:T(8,128)(2,1)} fusion(f32[256,1024]{1,0:T(8,128)S(1)} %collective-permute-done.5, bf16[256,512]{0,1:T(8,128)(2,1)S(1)} %bitcast.212, bf16[512,4096]{1,0:T(8,128)(2,1)} %param.17, s32[]{:T(128)S(6)} %select_n.151), kind=kOutput, calls=%fused_computation.40 | convolution fusion | flops 268959744 | bytes 2883588 | tf_op jit(solution)/shard_map/dot_general | solution.py:45
  73.1 7.8 %collective-permute-done.11 = bf16[256,1024]{1,0:T(8,128)(2,1)S(1)} collective-permute-done((bf16[256,1024]{1,0:T(8,128)(2,1)}, bf16[256,1024]{1,0:T(8,128)(2,1)S(1)}, u32[]{:S(2)}, u32[]{:S(2)}) %collective-permute-start.11) | collective-permute-done | bytes 524320 | tf_op jit(solution)/shard_map/ppermute | solution.py:33
  80.9 2.1 %add_convert_fusion.2 = bf16[256,1024]{1,0:T(8,128)(2,1)S(1)} fusion(bf16[256,1024]{1,0:T(8,128)(2,1)S(1)} %collective-permute-done.11, f32[256,1024]{1,0:T(8,128)} %collective-permute-done.12, bf16[256,512]{0,1:T(8,128)(2,1)S(1)} %bitcast.209, bf16[512,4096]{1,0:T(8,128)(2,1)} %param.17, s32[]{:T(128)S(6)} %select_n.154, bf16[512,1024]{1,0:T(8,128)(2,1)S(1)} %copy-done.3), kind=kOutput, calls=%fused_computation.77 | convolution fusion | flops 270008320 | bytes 3932164 | tf_op jit(solution)/shard_map/dot_general | solution.py:45
  85.9 6.4 %collective-permute-done.6 = bf16[256,1024]{1,0:T(8,128)(2,1)} collective-permute-done((bf16[256,1024]{1,0:T(8,128)(2,1)}, bf16[256,1024]{1,0:T(8,128)(2,1)}, u32[]{:S(2)}, u32[]{:S(2)}) %collective-permute-start.6) | collective-permute-done | bytes 524320 | tf_op jit(solution)/shard_map/ppermute | solution.py:33
  92.2 2.2 %add_convert_fusion.3 = bf16[256,1024]{1,0:T(8,128)(2,1)S(1)} fusion(bf16[256,1024]{1,0:T(8,128)(2,1)} %collective-permute-done.6, f32[256,1024]{1,0:T(8,128)} %collective-permute-done.7, bf16[256,512]{0,1:T(8,128)(2,1)S(1)} %bitcast.213, bf16[512,4096]{1,0:T(8,128)(2,1)} %param.17, s32[]{:T(128)S(6)} %select_n.154, bf16[512,1024]{1,0:T(8,128)(2,1)S(1)} %copy-done.3), kind=kOutput, calls=%fused_computation.78 | convolution fusion | flops 270008320 | bytes 3932164 | tf_op jit(solution)/shard_map/dot_general | solution.py:45
  96.0 7.4 %collective-permute-done.13 = bf16[256,1024]{1,0:T(8,128)(2,1)} collective-permute-done((bf16[256,1024]{1,0:T(8,128)(2,1)S(1)}, bf16[256,1024]{1,0:T(8,128)(2,1)}, u32[]{:S(2)}, u32[]{:S(2)}) %collective-permute-start.13) | collective-permute-done | bytes 524320 | tf_op jit(solution)/shard_map/ppermute | solution.py:33
  107.8 5.8 %collective-permute-done.8 = bf16[256,1024]{1,0:T(8,128)(2,1)S(1)} collective-permute-done((bf16[256,1024]{1,0:T(8,128)(2,1)S(1)}, bf16[256,1024]{1,0:T(8,128)(2,1)S(1)}, u32[]{:S(2)}, u32[]{:S(2)}) %collective-permute-start.8) | collective-permute-done | bytes 524320 | tf_op jit(solution)/shard_map/ppermute | solution.py:33
  135.4 4.1 %collective-permute-done.15 = bf16[2,273,256]{2,1,0:T(8,128)(2,1)S(1)} collective-permute-done((bf16[2,273,256]{2,1,0:T(8,128)(2,1)S(1)}, bf16[2,273,256]{2,1,0:T(8,128)(2,1)S(1)}, u32[]{:S(2)}, u32[]{:S(2)}) %collective-permute-start.15) | collective-permute-done | bytes 279584 | tf_op jit(solution)/shard_map/ppermute | solution.py:84
  139.5 19.6 %collective-permute-done.16 = bf16[2,273,256]{2,1,0:T(8,128)(2,1)S(1)} collective-permute-done((bf16[2,273,256]{2,1,0:T(8,128)(2,1)S(1)}, bf16[2,273,256]{2,1,0:T(8,128)(2,1)S(1)}, u32[]{:S(2)}, u32[]{:S(2)}) %collective-permute-start.16) | collective-permute-done | bytes 279584 | tf_op jit(solution)/shard_map/ppermute | solution.py:84
  169.7 11.8 %collective-permute-done.19 = bf16[256,1024]{1,0:T(8,128)(2,1)S(1)} collective-permute-done((bf16[256,1024]{1,0:T(8,128)(2,1)S(1)}, bf16[256,1024]{1,0:T(8,128)(2,1)S(1)}, u32[]{:S(2)}, u32[]{:S(2)}) %collective-permute-start.19) | collective-permute-done | bytes 524320 | tf_op jit(solution)/shard_map/ppermute | solution.py:33
  182.0 9.9 %collective-permute-done.22 = bf16[256,1024]{1,0:T(8,128)(2,1)S(1)} collective-permute-done((bf16[256,1024]{1,0:T(8,128)(2,1)S(1)}, bf16[256,1024]{1,0:T(8,128)(2,1)S(1)}, u32[]{:S(2)}, u32[]{:S(2)}) %collective-permute-start.22) | collective-permute-done | bytes 524320 | tf_op jit(solution)/shard_map/ppermute | solution.py:33
  (165 shorter events, 75.0 us)
Async XLA Ops:
  2.6 15.1 %collective-permute-start.3 = (bf16[256,1024]{1,0:T(8,128)(2,1)}, bf16[256,1024]{1,0:T(8,128)(2,1)}, u32[]{:S(2)}, u32[]{:S(2)}) collective-permute-start(bf16[256,1024]{1,0:T(8,128)(2,1)} %get-tuple-element.8), channel_id=1, source_target_pairs={{0,2},{1,3},{2,0},{3,1},{4,6},{5,7},{6,4},{7,5},{8,10},{9,11},{10,... | collective-permute-start | bytes 1572872 | tf_op jit(solution)/shard_map/ppermute | solution.py:33
  4.1 23.7 %collective-permute-start = (bf16[256,1024]{1,0:T(8,128)(2,1)}, bf16[256,1024]{1,0:T(8,128)(2,1)}, u32[]{:S(2)}, u32[]{:S(2)}) collective-permute-start(bf16[256,1024]{1,0:T(8,128)(2,1)} %get-tuple-element.5), channel_id=1, source_target_pairs={{0,2},{1,3},{2,0},{3,1},{4,6},{5,7},{6,4},{7,5},{8,10},{9,11},{10,... | collective-permute-start | bytes 1572872 | tf_op jit(solution)/shard_map/ppermute | solution.py:33
  20.9 12.6 %collective-permute-start.4 = (bf16[256,2,1024]{0,2,1:T(8,128)(2,1)S(1)}, bf16[256,2,1024]{0,2,1:T(8,128)(2,1)}, u32[]{:S(2)}, u32[]{:S(2)}) collective-permute-start(bf16[256,2,1024]{0,2,1:T(8,128)(2,1)S(1)} %constant_dynamic-update-slice_fusion.4), channel_id=1, source_target_pairs={{0,1},{1,0},{2,3},{3,2},{4,5},{5,4},{6,7},{7,6},{8,9},{9,8},{10,11... | collective-permute-start | bytes 3145736 | tf_op jit(solution)/shard_map/ppermute | solution.py:27
  31.8 3.6 %collective-permute-start.1 = (bf16[256,2,1024]{0,2,1:T(8,128)(2,1)}, bf16[256,2,1024]{0,2,1:T(8,128)(2,1)S(1)}, u32[]{:S(2)}, u32[]{:S(2)}) collective-permute-start(bf16[256,2,1024]{0,2,1:T(8,128)(2,1)} %constant_dynamic-update-slice_fusion.6), channel_id=1, source_target_pairs={{0,1},{1,0},{2,3},{3,2},{4,5},{5,4},{6,7},{7,6},{8,9},{9,8},{10,11... | collective-permute-start | bytes 3145736 | tf_op jit(solution)/shard_map/ppermute | solution.py:27
  45.5 8.5 %collective-permute-start.2 = (bf16[64,512]{0,1:T(8,128)(2,1)S(1)}, bf16[64,512]{0,1:T(8,128)(2,1)S(1)}, u32[]{:S(2)}, u32[]{:S(2)}) collective-permute-start(bf16[64,512]{0,1:T(8,128)(2,1)S(1)} %pad_maximum_fusion.3), channel_id=1, source_target_pairs={{0,4},{4,8},{8,12},{1,5},{5,9},{9,13},{2,6},{6,10},{10,14},{3,7},{... | collective-permute-start | bytes 196616 | tf_op jit(solution)/shard_map/ppermute | solution.py:17
  53.4 10.0 %collective-permute-start.10 = (f32[256,1024]{1,0:T(8,128)}, f32[256,1024]{1,0:T(8,128)S(1)}, u32[]{:S(2)}, u32[]{:S(2)}) collective-permute-start(f32[256,1024]{1,0:T(8,128)} %fusion.54), channel_id=1, source_target_pairs={{0,1},{1,0},{2,3},{3,2},{4,5},{5,4},{6,7},{7,6},{8,9},{9,8},{10,11... | collective-permute-start | bytes 3145736 | tf_op jit(solution)/shard_map/ppermute | solution.py:27
  60.2 9.9 %collective-permute-start.5 = (f32[256,1024]{1,0:T(8,128)}, f32[256,1024]{1,0:T(8,128)S(1)}, u32[]{:S(2)}, u32[]{:S(2)}) collective-permute-start(f32[256,1024]{1,0:T(8,128)} %fusion.56), channel_id=1, source_target_pairs={{0,1},{1,0},{2,3},{3,2},{4,5},{5,4},{6,7},{7,6},{8,9},{9,8},{10,11... | collective-permute-start | bytes 3145736 | tf_op jit(solution)/shard_map/ppermute | solution.py:27
  62.9 10.2 %collective-permute-start.12 = (f32[256,1024]{1,0:T(8,128)}, f32[256,1024]{1,0:T(8,128)}, u32[]{:S(2)}, u32[]{:S(2)}) collective-permute-start(f32[256,1024]{1,0:T(8,128)} %fusion.44), channel_id=1, source_target_pairs={{0,1},{1,0},{2,3},{3,2},{4,5},{5,4},{6,7},{7,6},{8,9},{9,8},{10,11... | collective-permute-start | bytes 3145736 | tf_op jit(solution)/shard_map/ppermute | solution.py:27
  65.9 15.0 %collective-permute-start.11 = (bf16[256,1024]{1,0:T(8,128)(2,1)}, bf16[256,1024]{1,0:T(8,128)(2,1)S(1)}, u32[]{:S(2)}, u32[]{:S(2)}) collective-permute-start(bf16[256,1024]{1,0:T(8,128)(2,1)} %fusion.19), channel_id=1, source_target_pairs={{0,2},{1,3},{2,0},{3,1},{4,6},{5,7},{6,4},{7,5},{8,10},{9,11},{10,... | collective-permute-start | bytes 1572872 | tf_op jit(solution)/shard_map/ppermute | solution.py:33
  70.0 14.9 %collective-permute-start.7 = (f32[256,1024]{1,0:T(8,128)}, f32[256,1024]{1,0:T(8,128)}, u32[]{:S(2)}, u32[]{:S(2)}) collective-permute-start(f32[256,1024]{1,0:T(8,128)} %fusion.46), channel_id=1, source_target_pairs={{0,1},{1,0},{2,3},{3,2},{4,5},{5,4},{6,7},{7,6},{8,9},{9,8},{10,11... | collective-permute-start | bytes 3145736 | tf_op jit(solution)/shard_map/ppermute | solution.py:27
  72.5 19.7 %collective-permute-start.6 = (bf16[256,1024]{1,0:T(8,128)(2,1)}, bf16[256,1024]{1,0:T(8,128)(2,1)}, u32[]{:S(2)}, u32[]{:S(2)}) collective-permute-start(bf16[256,1024]{1,0:T(8,128)(2,1)} %fusion.18), channel_id=1, source_target_pairs={{0,2},{1,3},{2,0},{3,1},{4,6},{5,7},{6,4},{7,5},{8,10},{9,11},{10,... | collective-permute-start | bytes 1572872 | tf_op jit(solution)/shard_map/ppermute | solution.py:33
  83.0 20.5 %collective-permute-start.13 = (bf16[256,1024]{1,0:T(8,128)(2,1)S(1)}, bf16[256,1024]{1,0:T(8,128)(2,1)}, u32[]{:S(2)}, u32[]{:S(2)}) collective-permute-start(bf16[256,1024]{1,0:T(8,128)(2,1)S(1)} %add_convert_fusion.2), channel_id=1, source_target_pairs={{0,2},{1,3},{2,0},{3,1},{4,6},{5,7},{6,4},{7,5},{8,10},{9,11},{10,... | collective-permute-start | bytes 1572872 | tf_op jit(solution)/shard_map/ppermute | solution.py:33
  94.5 19.2 %collective-permute-start.8 = (bf16[256,1024]{1,0:T(8,128)(2,1)S(1)}, bf16[256,1024]{1,0:T(8,128)(2,1)S(1)}, u32[]{:S(2)}, u32[]{:S(2)}) collective-permute-start(bf16[256,1024]{1,0:T(8,128)(2,1)S(1)} %add_convert_fusion.3), channel_id=1, source_target_pairs={{0,2},{1,3},{2,0},{3,1},{4,6},{5,7},{6,4},{7,5},{8,10},{9,11},{10,... | collective-permute-start | bytes 1572872 | tf_op jit(solution)/shard_map/ppermute | solution.py:33
  105.5 11.3 %collective-permute-start.14 = (bf16[256,2,1024]{0,2,1:T(8,128)(2,1)}, bf16[256,2,1024]{0,2,1:T(8,128)(2,1)}, u32[]{:S(2)}, u32[]{:S(2)}) collective-permute-start(bf16[256,2,1024]{0,2,1:T(8,128)(2,1)} %constant_dynamic-update-slice_fusion), channel_id=1, source_target_pairs={{0,1},{1,0},{2,3},{3,2},{4,5},{5,4},{6,7},{7,6},{8,9},{9,8},{10,11... | collective-permute-start | bytes 3145736 | tf_op jit(solution)/shard_map/ppermute | solution.py:27
  114.7 4.0 %collective-permute-start.9 = (bf16[256,2,1024]{0,2,1:T(8,128)(2,1)}, bf16[256,2,1024]{0,2,1:T(8,128)(2,1)S(1)}, u32[]{:S(2)}, u32[]{:S(2)}) collective-permute-start(bf16[256,2,1024]{0,2,1:T(8,128)(2,1)} %constant_dynamic-update-slice_fusion.2), channel_id=1, source_target_pairs={{0,1},{1,0},{2,3},{3,2},{4,5},{5,4},{6,7},{7,6},{8,9},{9,8},{10,11... | collective-permute-start | bytes 3145736 | tf_op jit(solution)/shard_map/ppermute | solution.py:27
  127.9 11.6 %collective-permute-start.15 = (bf16[2,273,256]{2,1,0:T(8,128)(2,1)S(1)}, bf16[2,273,256]{2,1,0:T(8,128)(2,1)S(1)}, u32[]{:S(2)}, u32[]{:S(2)}) collective-permute-start(bf16[2,273,256]{2,1,0:T(8,128)(2,1)S(1)} %convolution_convert_fusion), channel_id=1, source_target_pairs={{0,4},{4,8},{8,12},{1,5},{5,9},{9,13},{2,6},{6,10},{10,14},{3,7},{... | collective-permute-start | bytes 838664 | tf_op jit(solution)/shard_map/ppermute | solution.py:84
  129.2 29.9 %collective-permute-start.16 = (bf16[2,273,256]{2,1,0:T(8,128)(2,1)S(1)}, bf16[2,273,256]{2,1,0:T(8,128)(2,1)S(1)}, u32[]{:S(2)}, u32[]{:S(2)}) collective-permute-start(bf16[2,273,256]{2,1,0:T(8,128)(2,1)S(1)} %convolution_convert_fusion), channel_id=1, source_target_pairs={{0,8},{4,12},{1,9},{5,13},{2,10},{6,14},{3,11},{7,15},{16,24},{20,... | collective-permute-start | bytes 838664 | tf_op jit(solution)/shard_map/ppermute | solution.py:84
  130.5 28.6 %collective-permute-start.17 = (bf16[2,273,256]{2,1,0:T(8,128)(2,1)S(1)}, bf16[2,273,256]{2,1,0:T(8,128)(2,1)S(1)}, u32[]{:S(2)}, u32[]{:S(2)}) collective-permute-start(bf16[2,273,256]{2,1,0:T(8,128)(2,1)S(1)} %convolution_convert_fusion), channel_id=1, source_target_pairs={{0,12},{1,13},{2,14},{3,15},{16,28},{17,29},{18,30},{19,31}} | collective-permute-start | bytes 838664 | tf_op jit(solution)/shard_map/ppermute | solution.py:84
  163.5 2.7 %collective-permute-start.18 = (f32[256,1024]{1,0:T(8,128)S(1)}, f32[256,1024]{1,0:T(8,128)S(1)}, u32[]{:S(2)}, u32[]{:S(2)}) collective-permute-start(f32[256,1024]{1,0:T(8,128)S(1)} %fusion.40), channel_id=1, source_target_pairs={{0,1},{1,0},{2,3},{3,2},{4,5},{5,4},{6,7},{7,6},{8,9},{9,8},{10,11... | collective-permute-start | bytes 3145736 | tf_op jit(solution)/shard_map/ppermute | solution.py:27
  164.0 4.2 %collective-permute-start.21 = (f32[256,1024]{1,0:T(8,128)S(1)}, f32[256,1024]{1,0:T(8,128)S(1)}, u32[]{:S(2)}, u32[]{:S(2)}) collective-permute-start(f32[256,1024]{1,0:T(8,128)S(1)} %fusion.38), channel_id=1, source_target_pairs={{0,1},{1,0},{2,3},{3,2},{4,5},{5,4},{6,7},{7,6},{8,9},{9,8},{10,11... | collective-permute-start | bytes 3145736 | tf_op jit(solution)/shard_map/ppermute | solution.py:27
  165.0 4.7 %collective-permute-start.20 = (f32[256,1024]{1,0:T(8,128)S(1)}, f32[256,1024]{1,0:T(8,128)S(1)}, u32[]{:S(2)}, u32[]{:S(2)}) collective-permute-start(f32[256,1024]{1,0:T(8,128)S(1)} %fusion.30), channel_id=1, source_target_pairs={{0,1},{1,0},{2,3},{3,2},{4,5},{5,4},{6,7},{7,6},{8,9},{9,8},{10,11... | collective-permute-start | bytes 3145736 | tf_op jit(solution)/shard_map/ppermute | solution.py:27
  165.6 16.4 %collective-permute-start.23 = (f32[256,1024]{1,0:T(8,128)S(1)}, f32[256,1024]{1,0:T(8,128)S(1)}, u32[]{:S(2)}, u32[]{:S(2)}) collective-permute-start(f32[256,1024]{1,0:T(8,128)S(1)} %fusion.28), channel_id=1, source_target_pairs={{0,1},{1,0},{2,3},{3,2},{4,5},{5,4},{6,7},{7,6},{8,9},{9,8},{10,11... | collective-permute-start | bytes 3145736 | tf_op jit(solution)/shard_map/ppermute | solution.py:27
  166.7 14.8 %collective-permute-start.19 = (bf16[256,1024]{1,0:T(8,128)(2,1)S(1)}, bf16[256,1024]{1,0:T(8,128)(2,1)S(1)}, u32[]{:S(2)}, u32[]{:S(2)}) collective-permute-start(bf16[256,1024]{1,0:T(8,128)(2,1)S(1)} %fusion.20), channel_id=1, source_target_pairs={{0,2},{1,3},{2,0},{3,1},{4,6},{5,7},{6,4},{7,5},{8,10},{9,11},{10,... | collective-permute-start | bytes 1572872 | tf_op jit(solution)/shard_map/ppermute | solution.py:33
  168.7 23.2 %collective-permute-start.22 = (bf16[256,1024]{1,0:T(8,128)(2,1)S(1)}, bf16[256,1024]{1,0:T(8,128)(2,1)S(1)}, u32[]{:S(2)}, u32[]{:S(2)}) collective-permute-start(bf16[256,1024]{1,0:T(8,128)(2,1)S(1)} %fusion.21), channel_id=1, source_target_pairs={{0,2},{1,3},{2,0},{3,1},{4,6},{5,7},{6,4},{7,5},{8,10},{9,11},{10,... | collective-permute-start | bytes 1572872 | tf_op jit(solution)/shard_map/ppermute | solution.py:33
  (14 other events, 125.9 us)

commit v3 on v2

--- a/solution.py
+++ b/solution.py
@@ -55,24 +55,33 @@
     return acc
 
 
-def head_all_gather(piece):
-    rows, cols = piece.shape
+def gather_sources():
     devices, chips = head_layout()
     me = lax.axis_index("head")
     core, chip = me % 2, me // 2
-    chip_buf = jnp.zeros((rows, chips, cols), piece.dtype)
-    chip_buf = lax.dynamic_update_index_in_dim(chip_buf, piece, chip, axis=1)
-    cur = piece
+    ring = [((chip + chips - step - 1) % chips) * 2 for step in range(chips - 1)]
+    return [me] + [r + core for r in ring] + [me ^ 1] + [r + 1 - core for r in ring]
+
+
+def head_all_gather(piece):
+    devices, chips = head_layout()
+    pieces = [piece, None]
+    pieces[1] = core_swap(piece)
+    ring, cur = [], piece
     for step in range(chips - 1):
         cur = chip_shift(cur, 1)
-        chip_buf = lax.dynamic_update_index_in_dim(
-            chip_buf, cur, (chip + 2 * chips - step - 1) % chips, axis=1
-        )
-    partner = core_swap(chip_buf)
-    whole = jnp.zeros((rows, chips, 2, cols), piece.dtype)
-    whole = lax.dynamic_update_index_in_dim(whole, chip_buf, core, axis=2)
-    whole = lax.dynamic_update_index_in_dim(whole, partner, 1 - core, axis=2)
-    return whole.reshape(rows, devices * cols)
+        ring.append(cur)
+    forwarded = [core_swap(r) for r in ring]
+    return jnp.concatenate([piece] + ring + [pieces[1]] + forwarded, axis=1)
+
+
+def gathered_rows(weight):
+    devices, chips = head_layout()
+    block = weight.shape[0] // devices
+    return jnp.concatenate(
+        [lax.dynamic_slice_in_dim(weight, src * block, block, axis=0) for src in gather_sources()],
+        axis=0,
+    )
 
 
 def earlier_sum(local):
@@ -125,6 +134,13 @@
     kv_heads = kv_cols // HEAD
     group = w_query.shape[1] // HEAD // kv_heads
     hidden_parts = [hidden_in[i * size : (i + 1) * size] for i in range(CHUNKS)]
+    attn_gain = gathered_rows(attn_gain)
+    w_query = gathered_rows(w_query)
+    w_keys = gathered_rows(w_keys)
+    w_values = gathered_rows(w_values)
+    lin_gain = gathered_rows(lin_gain)
+    w_feature = gathered_rows(w_feature)
+    wv_linear = gathered_rows(wv_linear)
 
     query_parts, kv_parts = [], []
     for part in hidden_parts:

time: 195 us -> 193 us (0.990)
  local copies, waits for them, and re-layouts: 33.7 us -> 9.21 us
  matrix products: 47.6 us -> 58.4 us
  waiting for transfers between devices: 85.4 us -> 94.4 us
    dynamic_update_slice x16 -> x0, local copies, waits for them, and re-layouts: 14 us -> none  [the longest x4 4.61 us: head_all_gather(): lax.dynamic_update_index_in_dim(chip_buf, cur, (chip + 2 * chips - step -...]
    broadcast_in_dim x8 -> x0, local copies, waits for them, and re-layouts: 8.99 us -> none  [the longest x4 5.55 us: head_all_gather(): lax.dynamic_update_index_in_dim(chip_buf, cur, (chip + 2 * chips - step -...]
    ppermute x8, waiting for transfers between devices: 61.6 us -> 69.1 us  [chip_shift(): return lax.ppermute(value, 'head', pairs)]
    dynamic_slice x0 -> x6, local copies, waits for them, and re-layouts: none -> 5.82 us  [gathered_rows(): lax.dynamic_slice_in_dim(weight, src * block, block, axis=0)]
    unnamed x29 -> x51, local copies, waits for them, and re-layouts: 5.1 us -> 0.97 us
    dot_general x2, matrix products: 1.98 us -> 5.84 us  [body(): jnp.dot(normed, w_keys, preferred_element_type=jnp.float32)]
    convert_element_type x3 -> x0, other arithmetic: 3.37 us -> none  [norm_rows(): return (wide * scale * gain).astype(jnp.bfloat16)]
    dot_general x2, matrix products: 2.52 us -> 5.84 us  [body(): jnp.dot(normed, w_query, preferred_element_type=jnp.float32)]
  transfers between devices with their start and end apart: 24 -> 28, of which waited for: 11 -> 12; matrix products, arithmetic and copies ran while one was open for 31% -> 23% of each run, Pallas kernels for 0% -> 0%
where the time goes in v3:
time: 193 us; the launch traced here: 192 us
  waiting for transfers between devices  94.4 us (49%)
  matrix products  58.4 us (30%)
  starting transfers between devices  18.7 us (10%)
  other arithmetic  10.2 us (5%)
  local copies, waits for them, and re-layouts  9.21 us (5%)
    ppermute x8, waiting for transfers between devices, chip_shift(): return lax.ppermute(value, 'head', pairs)  69.1 us
    dot_general x16, matrix products, block(): return jnp.dot(lhs, cols, preferred_element_type=jnp.float32)  23.2 us
    ppermute x3, waiting for transfers between devices, earlier_sum(): total = total + lax.ppermute(sent, 'ctx', pairs).astype(jnp.float32)  22 us
    ppermute x8, starting transfers between devices, chip_shift(): return lax.ppermute(value, 'head', pairs)  9.92 us
    dot_general x2, matrix products, body(): jnp.dot(normed, w_query, preferred_element_type=jnp.float32)  5.84 us
    dot_general x2, matrix products, body(): jnp.dot(normed, w_keys, preferred_element_type=jnp.float32)  5.84 us
    dynamic_slice x6, local copies, waits for them, and re-layouts, gathered_rows(): lax.dynamic_slice_in_dim(weight, src * block, block, axis=0)  5.82 us
    dot_general x2, matrix products, body(): jnp.dot(normed, w_values, preferred_element_type=jnp.float32)  5.1 us
  transfers between devices with their start and end apart: 28, of which 12 were waited for; matrix products, arithmetic and copies ran while one was open for 23% of the time, Pallas kernels for 0%

profile of v3, /device:TPU:24, one launch (start us, length us, event | category | flops | bytes accessed | tf_op | source)
XLA Modules:
  0.0 191.8 jit_solution(4728218286339747866)
XLA Ops:
  4.4 2.6 %constant_dynamic-slice_fusion.11 = (bf16[1024,512]{1,0:T(8,128)(2,1)S(1)}, bf16[1024,512]{1,0:T(8,128)(2,1)S(1)}, bf16[1024,512]{1,0:T(8,128)(2,1)S(1)}, bf16[1024,512]{1,0:T(8,128)(2,1)S(1)}) fusion(bf16[4096,512]{1,0:T(8,128)(2,1)} %param.14, s32[]{:T(128)S(6)} %select_n.163, s32[]{:T(128)S(6)} %select_n.167, s32[]{:T(128)S(6)} %select_n.169, ...), kind=kLoop, calls=%fused_computation.177 | loop fusion | bytes 8388624 | tf_op jit(solution)/shard_map/dynamic_slice | solution.py:82
  10.0 6.2 %collective-permute-done = bf16[256,1024]{1,0:T(8,128)(2,1)} collective-permute-done((bf16[256,1024]{1,0:T(8,128)(2,1)S(1)}, bf16[256,1024]{1,0:T(8,128)(2,1)}, u32[]{:S(2)}, u32[]{:S(2)}) %collective-permute-start) | collective-permute-done | bytes 524320 | tf_op jit(solution)/shard_map/ppermute | solution.py:33
  17.8 8.5 %collective-permute-done.4 = bf16[256,1024]{1,0:T(8,128)(2,1)} collective-permute-done((bf16[256,1024]{1,0:T(8,128)(2,1)S(1)}, bf16[256,1024]{1,0:T(8,128)(2,1)}, u32[]{:S(2)}, u32[]{:S(2)}) %collective-permute-start.4) | collective-permute-done | bytes 524320 | tf_op jit(solution)/shard_map/ppermute | solution.py:33
  28.3 3.2 %convolution_convert_fusion.4 = bf16[256,512]{1,0:T(8,128)(2,1)} fusion(bf16[1024,512]{1,0:T(8,128)(2,1)S(1)} %get-tuple-element.7, bf16[1024,512]{1,0:T(8,128)(2,1)S(1)} %get-tuple-element.8, bf16[1024,512]{1,0:T(8,128)(2,1)S(1)} %get-tuple-element.6, bf16[1024,512]{1,0:T(8,128)(2,1)S(1)} %get-tuple-element.5, f32[4096]{0:T(1024)S(1)} %pad_maximum_fusion.24, ...), kind=kOutput, calls=%fused_computation.62 | convolution fusion | flops 1102184448 | bytes 6571008 | tf_op jit(solution)/shard_map/dot_general | solution.py:149
  34.5 3.3 %convolution_convert_fusion.10 = bf16[256,256]{0,1:T(8,128)(2,1)S(1)} fusion(bf16[1024,256]{1,0:T(8,128)(2,1)} %get-tuple-element.56, bf16[1024,256]{1,0:T(8,128)(2,1)} %get-tuple-element.55, bf16[1024,256]{1,0:T(8,128)(2,1)} %get-tuple-element.57, bf16[1024,256]{1,0:T(8,128)(2,1)} %get-tuple-element.58, f32[4096]{0:T(1024)S(1)} %pad_maximum_fusion.24, ...), kind=kOutput, calls=%fused_computation.68 | convolution fusion | flops 556859392 | bytes 4342784 | tf_op jit(solution)/shard_map/dot_general | solution.py:151
  37.8 2.5 %convolution_convert_fusion.9 = bf16[256,256]{0,1:T(8,128)(2,1)S(1)} fusion(bf16[1024,256]{1,0:T(8,128)(2,1)S(1)} %copy-done.12, bf16[1024,256]{1,0:T(8,128)(2,1)S(1)} %copy-done.13, bf16[1024,256]{1,0:T(8,128)(2,1)S(1)} %copy-done.11, bf16[1024,256]{1,0:T(8,128)(2,1)S(1)} %copy-done.10, f32[4096]{0:T(1024)S(1)} %pad_maximum_fusion.24, ...), kind=kOutput, calls=%fused_computation.67 | convolution fusion | flops 556859392 | bytes 4342784 | tf_op jit(solution)/shard_map/dot_general | solution.py:152
  40.5 2.6 %convolution_convert_fusion.8 = bf16[256,256]{0,1:T(8,128)(2,1)S(1)} fusion(bf16[1024,256]{1,0:T(8,128)(2,1)S(1)} %copy-done.15, bf16[1024,256]{1,0:T(8,128)(2,1)S(1)} %copy-done.14, bf16[1024,256]{1,0:T(8,128)(2,1)S(1)} %copy-done.16, bf16[1024,256]{1,0:T(8,128)(2,1)S(1)} %copy-done.17, f32[256]{0:T(256)S(1)} %add_rsqrt_fusion.4, ...), kind=kOutput, calls=%fused_computation.66 | convolution fusion | flops 556859392 | bytes 4342784 | tf_op jit(solution)/shard_map/dot_general | solution.py:151
  43.1 2.6 %convolution_convert_fusion.7 = bf16[256,256]{0,1:T(8,128)(2,1)S(1)} fusion(bf16[1024,256]{1,0:T(8,128)(2,1)S(1)} %copy-done.12, bf16[1024,256]{1,0:T(8,128)(2,1)S(1)} %copy-done.13, bf16[1024,256]{1,0:T(8,128)(2,1)S(1)} %copy-done.11, bf16[1024,256]{1,0:T(8,128)(2,1)S(1)} %copy-done.10, f32[256]{0:T(256)S(1)} %add_rsqrt_fusion.4, ...), kind=kOutput, calls=%fused_computation.65 | convolution fusion | flops 556859392 | bytes 4342784 | tf_op jit(solution)/shard_map/dot_general | solution.py:152
  46.6 3.2 %fusion.140 = (f32[2,2,256]{2,1,0:T(2,128)}, f32[2,2,256,320]{2,3,1,0:T(8,128)}) fusion(bf16[320,2,128,1]{0,2,3,1:T(8,128)(2,1)S(1)} %bitcast.134, pred[256,320]{0,1:T(8,128)(4,1)} %and_and_fusion, bf16[256,2,2,128]{3,2,1,0:T(2,128)(2,1)S(1)} %reshape.193), kind=kOutput, calls=%fused_computation.225 | convolution fusion | flops 85197120 | bytes 1822720 | tf_op jit(solution)/shard_map/sub | solution.py:176
  51.6 2.7 %fusion.58 = f32[256,1024]{1,0:T(8,128)} fusion(bf16[256,512]{0,1:T(8,128)(2,1)S(1)} %bitcast.120, bf16[512,4096]{1,0:T(8,128)(2,1)} %param.17, s32[]{:T(128)S(6)} %select_n.171), kind=kOutput, calls=%fused_computation.99 | convolution fusion | flops 268435456 | bytes 2359300 | tf_op jit(solution)/shard_map/dot_general | solution.py:45
  56.2 2.6 %convolution_convert_fusion.6 = bf16[256,512]{1,0:T(8,128)(2,1)S(1)} fusion(bf16[1024,512]{1,0:T(8,128)(2,1)S(1)} %copy-done.7, bf16[1024,512]{1,0:T(8,128)(2,1)S(1)} %copy-done.9, bf16[1024,512]{1,0:T(8,128)(2,1)S(1)} %get-tuple-element.6, bf16[1024,512]{1,0:T(8,128)(2,1)S(1)} %get-tuple-element.5, f32[256]{0:T(256)S(1)} %copy-done.24, ...), kind=kOutput, calls=%fused_computation.64 | convolution fusion | flops 1102184448 | bytes 6571008 | tf_op jit(solution)/shard_map/dot_general | solution.py:149
  59.0 3.2 %collective-permute-done.3 = bf16[64,512]{0,1:T(8,128)(2,1)} collective-permute-done((bf16[64,512]{0,1:T(8,128)(2,1)S(1)}, bf16[64,512]{0,1:T(8,128)(2,1)}, u32[]{:S(2)}, u32[]{:S(2)}) %collective-permute-start.3) | collective-permute-done | bytes 65568 | tf_op jit(solution)/shard_map/ppermute | solution.py:17
  65.1 2.7 %fusion.60 = f32[256,1024]{1,0:T(8,128)} fusion(bf16[256,512]{0,1:T(8,128)(2,1)S(1)} %bitcast.124, bf16[512,4096]{1,0:T(8,128)(2,1)} %param.17, s32[]{:T(128)S(6)} %select_n.171), kind=kOutput, calls=%fused_computation.101 | convolution fusion | flops 268435456 | bytes 2359300 | tf_op jit(solution)/shard_map/dot_general | solution.py:45
  67.8 2.7 %fusion.48 = f32[256,1024]{1,0:T(8,128)} fusion(bf16[256,512]{0,1:T(8,128)(2,1)S(1)} %bitcast.121, bf16[512,4096]{1,0:T(8,128)(2,1)} %param.17, s32[]{:T(128)S(6)} %select_n.174), kind=kOutput, calls=%fused_computation.93 | convolution fusion | flops 268435456 | bytes 2359300 | tf_op jit(solution)/shard_map/dot_general | solution.py:45
  71.0 2.8 %fusion.23 = bf16[256,1024]{1,0:T(8,128)(2,1)} fusion(f32[256,1024]{1,0:T(8,128)} %collective-permute-done.13, bf16[256,512]{0,1:T(8,128)(2,1)S(1)} %bitcast.122, bf16[512,4096]{1,0:T(8,128)(2,1)} %param.17, s32[]{:T(128)S(6)} %select_n.167), kind=kOutput, calls=%fused_computation.51 | convolution fusion | flops 268959744 | bytes 2883588 | tf_op jit(solution)/shard_map/dot_general | solution.py:45
  75.3 2.7 %fusion.50 = f32[256,1024]{1,0:T(8,128)} fusion(bf16[256,512]{0,1:T(8,128)(2,1)S(1)} %bitcast.125, bf16[512,4096]{1,0:T(8,128)(2,1)} %param.17, s32[]{:T(128)S(6)} %select_n.174), kind=kOutput, calls=%fused_computation.95 | convolution fusion | flops 268435456 | bytes 2359300 | tf_op jit(solution)/shard_map/dot_general | solution.py:45
  80.5 8.3 %collective-permute-done.14 = bf16[256,1024]{1,0:T(8,128)(2,1)S(1)} collective-permute-done((bf16[256,1024]{1,0:T(8,128)(2,1)}, bf16[256,1024]{1,0:T(8,128)(2,1)S(1)}, u32[]{:S(2)}, u32[]{:S(2)}) %collective-permute-start.14) | collective-permute-done | bytes 524320 | tf_op jit(solution)/shard_map/ppermute | solution.py:33
  92.6 7.5 %collective-permute-done.8 = bf16[256,1024]{1,0:T(8,128)(2,1)S(1)} collective-permute-done((bf16[256,1024]{1,0:T(8,128)(2,1)S(1)}, bf16[256,1024]{1,0:T(8,128)(2,1)S(1)}, u32[]{:S(2)}, u32[]{:S(2)}) %collective-permute-start.8) | collective-permute-done | bytes 524320 | tf_op jit(solution)/shard_map/ppermute | solution.py:33
  103.7 7.6 %collective-permute-done.16 = bf16[256,1024]{1,0:T(8,128)(2,1)S(1)} collective-permute-done((bf16[256,1024]{1,0:T(8,128)(2,1)S(1)}, bf16[256,1024]{1,0:T(8,128)(2,1)S(1)}, u32[]{:S(2)}, u32[]{:S(2)}) %collective-permute-start.16) | collective-permute-done | bytes 524320 | tf_op jit(solution)/shard_map/ppermute | solution.py:33
  112.3 9.4 %collective-permute-done.10 = bf16[256,1024]{1,0:T(8,128)(2,1)S(1)} collective-permute-done((bf16[256,1024]{1,0:T(8,128)(2,1)S(1)}, bf16[256,1024]{1,0:T(8,128)(2,1)S(1)}, u32[]{:S(2)}, u32[]{:S(2)}) %collective-permute-start.10) | collective-permute-done | bytes 524320 | tf_op jit(solution)/shard_map/ppermute | solution.py:33
  135.7 3.8 %collective-permute-done.19 = bf16[2,273,256]{2,1,0:T(8,128)(2,1)S(1)} collective-permute-done((bf16[2,273,256]{2,1,0:T(8,128)(2,1)S(1)}, bf16[2,273,256]{2,1,0:T(8,128)(2,1)S(1)}, u32[]{:S(2)}, u32[]{:S(2)}) %collective-permute-start.19) | collective-permute-done | bytes 279584 | tf_op jit(solution)/shard_map/ppermute | solution.py:93
  139.5 18.2 %collective-permute-done.20 = bf16[2,273,256]{2,1,0:T(8,128)(2,1)S(1)} collective-permute-done((bf16[2,273,256]{2,1,0:T(8,128)(2,1)S(1)}, bf16[2,273,256]{2,1,0:T(8,128)(2,1)S(1)}, u32[]{:S(2)}, u32[]{:S(2)}) %collective-permute-start.20) | collective-permute-done | bytes 279584 | tf_op jit(solution)/shard_map/ppermute | solution.py:93
  168.0 11.8 %collective-permute-done.23 = bf16[256,1024]{1,0:T(8,128)(2,1)S(1)} collective-permute-done((bf16[256,1024]{1,0:T(8,128)(2,1)S(1)}, bf16[256,1024]{1,0:T(8,128)(2,1)S(1)}, u32[]{:S(2)}, u32[]{:S(2)}) %collective-permute-start.23) | collective-permute-done | bytes 524320 | tf_op jit(solution)/shard_map/ppermute | solution.py:33
  180.3 9.9 %collective-permute-done.26 = bf16[256,1024]{1,0:T(8,128)(2,1)S(1)} collective-permute-done((bf16[256,1024]{1,0:T(8,128)(2,1)S(1)}, bf16[256,1024]{1,0:T(8,128)(2,1)S(1)}, u32[]{:S(2)}, u32[]{:S(2)}) %collective-permute-start.26) | collective-permute-done | bytes 524320 | tf_op jit(solution)/shard_map/ppermute | solution.py:33
  (168 shorter events, 60.5 us)
Async XLA Ops:
  1.3 15.0 %collective-permute-start = (bf16[256,1024]{1,0:T(8,128)(2,1)S(1)}, bf16[256,1024]{1,0:T(8,128)(2,1)}, u32[]{:S(2)}, u32[]{:S(2)}) collective-permute-start(bf16[256,1024]{1,0:T(8,128)(2,1)S(1)} %get-tuple-element.21), channel_id=1, source_target_pairs={{0,2},{1,3},{2,0},{3,1},{4,6},{5,7},{6,4},{7,5},{8,10},{9,11},{10,... | collective-permute-start | bytes 1572872 | tf_op jit(solution)/shard_map/ppermute | solution.py:33
  2.8 23.5 %collective-permute-start.1 = (bf16[256,1024]{1,0:T(8,128)(2,1)S(1)}, bf16[256,1024]{1,0:T(8,128)(2,1)}, u32[]{:S(2)}, u32[]{:S(2)}) collective-permute-start(bf16[256,1024]{1,0:T(8,128)(2,1)S(1)} %get-tuple-element.21), channel_id=1, source_target_pairs={{0,1},{1,0},{2,3},{3,2},{4,5},{5,4},{6,7},{7,6},{8,9},{9,8},{10,11... | collective-permute-start | bytes 1572872 | tf_op jit(solution)/shard_map/ppermute | solution.py:27
  2.8 23.5 %collective-permute-start.4 = (bf16[256,1024]{1,0:T(8,128)(2,1)S(1)}, bf16[256,1024]{1,0:T(8,128)(2,1)}, u32[]{:S(2)}, u32[]{:S(2)}) collective-permute-start(bf16[256,1024]{1,0:T(8,128)(2,1)S(1)} %get-tuple-element.22), channel_id=1, source_target_pairs={{0,2},{1,3},{2,0},{3,1},{4,6},{5,7},{6,4},{7,5},{8,10},{9,11},{10,... | collective-permute-start | bytes 1572872 | tf_op jit(solution)/shard_map/ppermute | solution.py:33
  3.4 29.1 %collective-permute-start.5 = (bf16[256,1024]{1,0:T(8,128)(2,1)S(1)}, bf16[256,1024]{1,0:T(8,128)(2,1)}, u32[]{:S(2)}, u32[]{:S(2)}) collective-permute-start(bf16[256,1024]{1,0:T(8,128)(2,1)S(1)} %get-tuple-element.22), channel_id=1, source_target_pairs={{0,1},{1,0},{2,3},{3,2},{4,5},{5,4},{6,7},{7,6},{8,9},{9,8},{10,11... | collective-permute-start | bytes 1572872 | tf_op jit(solution)/shard_map/ppermute | solution.py:27
  16.3 10.1 %collective-permute-start.2 = (bf16[256,1024]{1,0:T(8,128)(2,1)}, bf16[256,1024]{1,0:T(8,128)(2,1)S(1)}, u32[]{:S(2)}, u32[]{:S(2)}) collective-permute-start(bf16[256,1024]{1,0:T(8,128)(2,1)} %collective-permute-done), channel_id=1, source_target_pairs={{0,1},{1,0},{2,3},{3,2},{4,5},{5,4},{6,7},{7,6},{8,9},{9,8},{10,11... | collective-permute-start | bytes 1572872 | tf_op jit(solution)/shard_map/ppermute | solution.py:27
  26.3 6.2 %collective-permute-start.6 = (bf16[256,1024]{1,0:T(8,128)(2,1)}, bf16[256,1024]{1,0:T(8,128)(2,1)}, u32[]{:S(2)}, u32[]{:S(2)}) collective-permute-start(bf16[256,1024]{1,0:T(8,128)(2,1)} %collective-permute-done.4), channel_id=1, source_target_pairs={{0,1},{1,0},{2,3},{3,2},{4,5},{5,4},{6,7},{7,6},{8,9},{9,8},{10,11... | collective-permute-start | bytes 1572872 | tf_op jit(solution)/shard_map/ppermute | solution.py:27
  54.3 16.8 %collective-permute-start.13 = (f32[256,1024]{1,0:T(8,128)}, f32[256,1024]{1,0:T(8,128)}, u32[]{:S(2)}, u32[]{:S(2)}) collective-permute-start(f32[256,1024]{1,0:T(8,128)} %fusion.58), channel_id=1, source_target_pairs={{0,1},{1,0},{2,3},{3,2},{4,5},{5,4},{6,7},{7,6},{8,9},{9,8},{10,11... | collective-permute-start | bytes 3145736 | tf_op jit(solution)/shard_map/ppermute | solution.py:27
  54.7 7.4 %collective-permute-start.3 = (bf16[64,512]{0,1:T(8,128)(2,1)S(1)}, bf16[64,512]{0,1:T(8,128)(2,1)}, u32[]{:S(2)}, u32[]{:S(2)}) collective-permute-start(bf16[64,512]{0,1:T(8,128)(2,1)S(1)} %pad_maximum_fusion.20), channel_id=1, source_target_pairs={{0,4},{4,8},{8,12},{1,5},{5,9},{9,13},{2,6},{6,10},{10,14},{3,7},{... | collective-permute-start | bytes 196616 | tf_op jit(solution)/shard_map/ppermute | solution.py:17
  67.8 10.3 %collective-permute-start.7 = (f32[256,1024]{1,0:T(8,128)}, f32[256,1024]{1,0:T(8,128)S(1)}, u32[]{:S(2)}, u32[]{:S(2)}) collective-permute-start(f32[256,1024]{1,0:T(8,128)} %fusion.60), channel_id=1, source_target_pairs={{0,1},{1,0},{2,3},{3,2},{4,5},{5,4},{6,7},{7,6},{8,9},{9,8},{10,11... | collective-permute-start | bytes 3145736 | tf_op jit(solution)/shard_map/ppermute | solution.py:27
  70.5 10.0 %collective-permute-start.15 = (f32[256,1024]{1,0:T(8,128)}, f32[256,1024]{1,0:T(8,128)}, u32[]{:S(2)}, u32[]{:S(2)}) collective-permute-start(f32[256,1024]{1,0:T(8,128)} %fusion.48), channel_id=1, source_target_pairs={{0,1},{1,0},{2,3},{3,2},{4,5},{5,4},{6,7},{7,6},{8,9},{9,8},{10,11... | collective-permute-start | bytes 3145736 | tf_op jit(solution)/shard_map/ppermute | solution.py:27
  73.8 15.0 %collective-permute-start.14 = (bf16[256,1024]{1,0:T(8,128)(2,1)}, bf16[256,1024]{1,0:T(8,128)(2,1)S(1)}, u32[]{:S(2)}, u32[]{:S(2)}) collective-permute-start(bf16[256,1024]{1,0:T(8,128)(2,1)} %fusion.23), channel_id=1, source_target_pairs={{0,2},{1,3},{2,0},{3,1},{4,6},{5,7},{6,4},{7,5},{8,10},{9,11},{10,... | collective-permute-start | bytes 1572872 | tf_op jit(solution)/shard_map/ppermute | solution.py:33
  78.0 14.6 %collective-permute-start.9 = (f32[256,1024]{1,0:T(8,128)}, f32[256,1024]{1,0:T(8,128)}, u32[]{:S(2)}, u32[]{:S(2)}) collective-permute-start(f32[256,1024]{1,0:T(8,128)} %fusion.50), channel_id=1, source_target_pairs={{0,1},{1,0},{2,3},{3,2},{4,5},{5,4},{6,7},{7,6},{8,9},{9,8},{10,11... | collective-permute-start | bytes 3145736 | tf_op jit(solution)/shard_map/ppermute | solution.py:27
  79.9 20.1 %collective-permute-start.8 = (bf16[256,1024]{1,0:T(8,128)(2,1)S(1)}, bf16[256,1024]{1,0:T(8,128)(2,1)S(1)}, u32[]{:S(2)}, u32[]{:S(2)}) collective-permute-start(bf16[256,1024]{1,0:T(8,128)(2,1)S(1)} %fusion.22), channel_id=1, source_target_pairs={{0,2},{1,3},{2,0},{3,1},{4,6},{5,7},{6,4},{7,5},{8,10},{9,11},{10,... | collective-permute-start | bytes 1572872 | tf_op jit(solution)/shard_map/ppermute | solution.py:33
  90.9 20.4 %collective-permute-start.16 = (bf16[256,1024]{1,0:T(8,128)(2,1)S(1)}, bf16[256,1024]{1,0:T(8,128)(2,1)S(1)}, u32[]{:S(2)}, u32[]{:S(2)}) collective-permute-start(bf16[256,1024]{1,0:T(8,128)(2,1)S(1)} %add_convert_fusion.2), channel_id=1, source_target_pairs={{0,2},{1,3},{2,0},{3,1},{4,6},{5,7},{6,4},{7,5},{8,10},{9,11},{10,... | collective-permute-start | bytes 1572872 | tf_op jit(solution)/shard_map/ppermute | solution.py:33
  92.5 29.2 %collective-permute-start.17 = (bf16[256,1024]{1,0:T(8,128)(2,1)S(1)}, bf16[256,1024]{1,0:T(8,128)(2,1)S(1)}, u32[]{:S(2)}, u32[]{:S(2)}) collective-permute-start(bf16[256,1024]{1,0:T(8,128)(2,1)S(1)} %add_convert_fusion.2), channel_id=1, source_target_pairs={{0,1},{1,0},{2,3},{3,2},{4,5},{5,4},{6,7},{7,6},{8,9},{9,8},{10,11... | collective-permute-start | bytes 1572872 | tf_op jit(solution)/shard_map/ppermute | solution.py:27
  102.1 19.6 %collective-permute-start.10 = (bf16[256,1024]{1,0:T(8,128)(2,1)S(1)}, bf16[256,1024]{1,0:T(8,128)(2,1)S(1)}, u32[]{:S(2)}, u32[]{:S(2)}) collective-permute-start(bf16[256,1024]{1,0:T(8,128)(2,1)S(1)} %add_convert_fusion.3), channel_id=1, source_target_pairs={{0,2},{1,3},{2,0},{3,1},{4,6},{5,7},{6,4},{7,5},{8,10},{9,11},{10,... | collective-permute-start | bytes 1572872 | tf_op jit(solution)/shard_map/ppermute | solution.py:33
  111.3 10.4 %collective-permute-start.18 = (bf16[256,1024]{1,0:T(8,128)(2,1)S(1)}, bf16[256,1024]{1,0:T(8,128)(2,1)S(1)}, u32[]{:S(2)}, u32[]{:S(2)}) collective-permute-start(bf16[256,1024]{1,0:T(8,128)(2,1)S(1)} %collective-permute-done.16), channel_id=1, source_target_pairs={{0,1},{1,0},{2,3},{3,2},{4,5},{5,4},{6,7},{7,6},{8,9},{9,8},{10,11... | collective-permute-start | bytes 1572872 | tf_op jit(solution)/shard_map/ppermute | solution.py:27
  111.7 12.7 %collective-permute-start.11 = (bf16[256,1024]{1,0:T(8,128)(2,1)S(1)}, bf16[256,1024]{1,0:T(8,128)(2,1)S(1)}, u32[]{:S(2)}, u32[]{:S(2)}) collective-permute-start(bf16[256,1024]{1,0:T(8,128)(2,1)S(1)} %add_convert_fusion.3), channel_id=1, source_target_pairs={{0,1},{1,0},{2,3},{3,2},{4,5},{5,4},{6,7},{7,6},{8,9},{9,8},{10,11... | collective-permute-start | bytes 1572872 | tf_op jit(solution)/shard_map/ppermute | solution.py:27
  128.1 11.4 %collective-permute-start.19 = (bf16[2,273,256]{2,1,0:T(8,128)(2,1)S(1)}, bf16[2,273,256]{2,1,0:T(8,128)(2,1)S(1)}, u32[]{:S(2)}, u32[]{:S(2)}) collective-permute-start(bf16[2,273,256]{2,1,0:T(8,128)(2,1)S(1)} %convolution_convert_fusion), channel_id=1, source_target_pairs={{0,4},{4,8},{8,12},{1,5},{5,9},{9,13},{2,6},{6,10},{10,14},{3,7},{... | collective-permute-start | bytes 838664 | tf_op jit(solution)/shard_map/ppermute | solution.py:93
  129.6 28.1 %collective-permute-start.20 = (bf16[2,273,256]{2,1,0:T(8,128)(2,1)S(1)}, bf16[2,273,256]{2,1,0:T(8,128)(2,1)S(1)}, u32[]{:S(2)}, u32[]{:S(2)}) collective-permute-start(bf16[2,273,256]{2,1,0:T(8,128)(2,1)S(1)} %convolution_convert_fusion), channel_id=1, source_target_pairs={{0,8},{4,12},{1,9},{5,13},{2,10},{6,14},{3,11},{7,15},{16,24},{20,... | collective-permute-start | bytes 838664 | tf_op jit(solution)/shard_map/ppermute | solution.py:93
  130.9 26.8 %collective-permute-start.21 = (bf16[2,273,256]{2,1,0:T(8,128)(2,1)S(1)}, bf16[2,273,256]{2,1,0:T(8,128)(2,1)S(1)}, u32[]{:S(2)}, u32[]{:S(2)}) collective-permute-start(bf16[2,273,256]{2,1,0:T(8,128)(2,1)S(1)} %convolution_convert_fusion), channel_id=1, source_target_pairs={{0,12},{1,13},{2,14},{3,15},{16,28},{17,29},{18,30},{19,31}} | collective-permute-start | bytes 838664 | tf_op jit(solution)/shard_map/ppermute | solution.py:93
  163.9 16.5 %collective-permute-start.27 = (f32[256,1024]{1,0:T(8,128)S(1)}, f32[256,1024]{1,0:T(8,128)S(1)}, u32[]{:S(2)}, u32[]{:S(2)}) collective-permute-start(f32[256,1024]{1,0:T(8,128)S(1)} %fusion.32), channel_id=1, source_target_pairs={{0,1},{1,0},{2,3},{3,2},{4,5},{5,4},{6,7},{7,6},{8,9},{9,8},{10,11... | collective-permute-start | bytes 3145736 | tf_op jit(solution)/shard_map/ppermute | solution.py:27
  164.9 14.8 %collective-permute-start.23 = (bf16[256,1024]{1,0:T(8,128)(2,1)S(1)}, bf16[256,1024]{1,0:T(8,128)(2,1)S(1)}, u32[]{:S(2)}, u32[]{:S(2)}) collective-permute-start(bf16[256,1024]{1,0:T(8,128)(2,1)S(1)} %fusion.24), channel_id=1, source_target_pairs={{0,2},{1,3},{2,0},{3,1},{4,6},{5,7},{6,4},{7,5},{8,10},{9,11},{10,... | collective-permute-start | bytes 1572872 | tf_op jit(solution)/shard_map/ppermute | solution.py:33
  167.0 23.2 %collective-permute-start.26 = (bf16[256,1024]{1,0:T(8,128)(2,1)S(1)}, bf16[256,1024]{1,0:T(8,128)(2,1)S(1)}, u32[]{:S(2)}, u32[]{:S(2)}) collective-permute-start(bf16[256,1024]{1,0:T(8,128)(2,1)S(1)} %fusion.25), channel_id=1, source_target_pairs={{0,2},{1,3},{2,0},{3,1},{4,6},{5,7},{6,4},{7,5},{8,10},{9,11},{10,... | collective-permute-start | bytes 1572872 | tf_op jit(solution)/shard_map/ppermute | solution.py:33
  (29 other events, 274.3 us)

commit v4 on v3

--- a/solution.py
+++ b/solution.py
@@ -27,10 +27,17 @@
     return lax.ppermute(value, "head", [(h, h ^ 1) for h in range(devices)])
 
 
+LINK = []
+
+
 def chip_shift(value, by):
     devices, chips = head_layout()
     pairs = [(h, ((h // 2 + by) % chips) * 2 + h % 2) for h in range(devices)]
-    return lax.ppermute(value, "head", pairs)
+    if LINK:
+        value, _ = lax.optimization_barrier((value, LINK[-1]))
+    moved = lax.ppermute(value, "head", pairs)
+    LINK.append(moved)
+    return moved
 
 
 def head_reduce_scatter(lhs, weight):
@@ -128,6 +135,7 @@
     wo_linear,
     entry_state,
 ):
+    LINK.clear()
     tok_rows = hidden_in.shape[0]
     size = tok_rows // CHUNKS
     kv_cols = w_keys.shape[1]
@@ -155,8 +163,8 @@
     kv_all = jnp.concatenate([rim] + kv_parts, axis=0)
     start = lax.axis_index("ctx") * tok_rows
 
-    after_parts, after_whole_parts = [], []
-    for i in range(CHUNKS):
+    partial_parts = [None] * CHUNKS
+    for i in reversed(range(CHUNKS)):
         kv_win = kv_all[i * size : i * size + size + WINDOW]
         key_win = kv_win[:, :kv_cols].reshape(size + WINDOW, kv_heads, HEAD)
         value_win = kv_win[:, kv_cols:].reshape(size + WINDOW, kv_heads, HEAD)
@@ -179,10 +187,12 @@
             "kgts,skd->tkgd", probs, value_win, preferred_element_type=jnp.float32
         )
         attended = attended.astype(jnp.bfloat16).reshape(size, -1)
-        partial_out = head_reduce_scatter(attended, wo_attn)
-        after_window = (hidden_parts[i].astype(jnp.float32) + partial_out).astype(jnp.bfloat16)
-        after_parts.append(after_window)
-        after_whole_parts.append(head_all_gather(after_window))
+        partial_parts[i] = head_reduce_scatter(attended, wo_attn)
+    after_parts, after_whole_parts = [None] * CHUNKS, [None] * CHUNKS
+    for i in reversed(range(CHUNKS)):
+        after_window = (hidden_parts[i].astype(jnp.float32) + partial_parts[i]).astype(jnp.bfloat16)
+        after_parts[i] = after_window
+        after_whole_parts[i] = head_all_gather(after_window)
 
     qf_parts, kf_parts, lv_parts = [], [], []
     for i in range(CHUNKS):

time: 193 us -> 196 us (1.016)
  the two profiles are of different devices: /device:TPU:24 before, /device:TPU:22 now
where the time goes in v4:
time: 196 us; the launch traced here: 195 us
  waiting for transfers between devices  107 us (55%)
  matrix products  53.4 us (27%)
  starting transfers between devices  14.2 us (7%)
  local copies, waits for them, and re-layouts  10.7 us (5%)
  other arithmetic  9.34 us (5%)
    ppermute x8, waiting for transfers between devices, chip_shift(): moved = lax.ppermute(value, 'head', pairs)  83.3 us
    ppermute x3, waiting for transfers between devices, earlier_sum(): total = total + lax.ppermute(sent, 'ctx', pairs).astype(jnp.float32)  21.8 us
    dot_general x16, matrix products, block(): return jnp.dot(lhs, cols, preferred_element_type=jnp.float32)  20.5 us
    dynamic_slice x5, local copies, waits for them, and re-layouts, gathered_rows(): lax.dynamic_slice_in_dim(weight, src * block, block, axis=0)  7.51 us
    dot_general x2, matrix products, body(): jnp.dot(normed, w_values, preferred_element_type=jnp.float32)  5.69 us
    dot_general x2, matrix products, body(): jnp.dot(normed, w_keys, preferred_element_type=jnp.float32)  5.09 us
    dot_general x2, matrix products, body(): jnp.dot(normed, w_query, preferred_element_type=jnp.float32)  4.98 us
    reduce_sum x4, other arithmetic, norm_rows(): scale = lax.rsqrt(jnp.mean(wide * wide, axis=-1, keepdims=True) + 1e-05)  4.57 us
  transfers between devices with their start and end apart: 28, of which 12 were waited for; matrix products, arithmetic and copies ran while one was open for 28% of the time, Pallas kernels for 0%

profile of v4, /device:TPU:22, one launch (start us, length us, event | category | flops | bytes accessed | tf_op | source)
XLA Modules:
  0.0 195.2 jit_solution(4016563293735867560)
XLA Ops:
  3.6 2.6 %constant_dynamic-slice_fusion.11 = (bf16[1024,512]{1,0:T(8,128)(2,1)S(1)}, bf16[1024,512]{1,0:T(8,128)(2,1)S(1)}, bf16[1024,512]{1,0:T(8,128)(2,1)S(1)}, bf16[1024,512]{1,0:T(8,128)(2,1)S(1)}) fusion(bf16[4096,512]{1,0:T(8,128)(2,1)} %param.14, s32[]{:T(128)S(6)} %select_n.163, s32[]{:T(128)S(6)} %select_n.167, s32[]{:T(128)S(6)} %select_n.169, ...), kind=kLoop, calls=%fused_computation.177 | loop fusion | bytes 8388624 | tf_op jit(solution)/shard_map/dynamic_slice | solution.py:89
  9.2 6.6 %collective-permute-done = bf16[256,1024]{1,0:T(8,128)(2,1)} collective-permute-done((bf16[256,1024]{1,0:T(8,128)(2,1)S(1)}, bf16[256,1024]{1,0:T(8,128)(2,1)}, u32[]{:S(2)}, u32[]{:S(2)}) %collective-permute-start) | collective-permute-done | bytes 524320 | tf_op jit(solution)/shard_map/ppermute | solution.py:38
  19.9 2.5 %convolution_convert_fusion.6 = bf16[256,512]{1,0:T(8,128)(2,1)S(1)} fusion(bf16[1024,512]{1,0:T(8,128)(2,1)S(1)} %get-tuple-element.21, bf16[1024,512]{1,0:T(8,128)(2,1)S(1)} %get-tuple-element.22, bf16[1024,512]{1,0:T(8,128)(2,1)S(1)} %get-tuple-element.20, bf16[1024,512]{1,0:T(8,128)(2,1)S(1)} %get-tuple-element.19, f32[256]{0:T(256)S(1)} %add_rsqrt_fusion.4, ...), kind=kOutput, calls=%fused_computation.64 | convolution fusion | flops 1102184448 | bytes 6571008 | tf_op jit(solution)/shard_map/dot_general | solution.py:157
  23.2 8.7 %collective-permute-done.1 = bf16[256,1024]{1,0:T(8,128)(2,1)} collective-permute-done((bf16[256,1024]{1,0:T(8,128)(2,1)S(1)}, bf16[256,1024]{1,0:T(8,128)(2,1)}, u32[]{:S(2)}, u32[]{:S(2)}) %collective-permute-start.1) | collective-permute-done | bytes 524320 | tf_op jit(solution)/shard_map/ppermute | solution.py:38
  31.9 3.3 %convolution_convert_fusion.7 = bf16[256,256]{0,1:T(8,128)(2,1)S(1)} fusion(bf16[1024,256]{1,0:T(8,128)(2,1)} %get-tuple-element.33, bf16[1024,256]{1,0:T(8,128)(2,1)} %get-tuple-element.34, bf16[1024,256]{1,0:T(8,128)(2,1)} %get-tuple-element.32, bf16[1024,256]{1,0:T(8,128)(2,1)} %get-tuple-element.31, f32[256]{0:T(256)S(1)} %add_rsqrt_fusion.4, ...), kind=kOutput, calls=%fused_computation.65 | convolution fusion | flops 556859392 | bytes 4342784 | tf_op jit(solution)/shard_map/dot_general | solution.py:160
  35.2 2.5 %convolution_convert_fusion.8 = bf16[256,256]{0,1:T(8,128)(2,1)S(1)} fusion(bf16[1024,256]{1,0:T(8,128)(2,1)S(1)} %copy-done.12, bf16[1024,256]{1,0:T(8,128)(2,1)S(1)} %copy-done.11, bf16[1024,256]{1,0:T(8,128)(2,1)S(1)} %copy-done.13, bf16[1024,256]{1,0:T(8,128)(2,1)S(1)} %copy-done.14, f32[256]{0:T(256)S(1)} %add_rsqrt_fusion.4, ...), kind=kOutput, calls=%fused_computation.66 | convolution fusion | flops 556859392 | bytes 4342784 | tf_op jit(solution)/shard_map/dot_general | solution.py:159
  39.6 2.4 %convolution_convert_fusion.9 = bf16[256,256]{0,1:T(8,128)(2,1)S(1)} fusion(bf16[1024,256]{1,0:T(8,128)(2,1)S(1)} %copy-done.17, bf16[1024,256]{1,0:T(8,128)(2,1)S(1)} %copy-done.18, bf16[1024,256]{1,0:T(8,128)(2,1)S(1)} %copy-done.16, bf16[1024,256]{1,0:T(8,128)(2,1)S(1)} %copy-done.15, f32[4096]{0:T(1024)S(1)} %pad_maximum_fusion.24, ...), kind=kOutput, calls=%fused_computation.67 | convolution fusion | flops 556859392 | bytes 4342784 | tf_op jit(solution)/shard_map/dot_general | solution.py:160
  42.0 2.5 %convolution_convert_fusion.10 = bf16[256,256]{0,1:T(8,128)(2,1)S(1)} fusion(bf16[1024,256]{1,0:T(8,128)(2,1)S(1)} %copy-done.12, bf16[1024,256]{1,0:T(8,128)(2,1)S(1)} %copy-done.11, bf16[1024,256]{1,0:T(8,128)(2,1)S(1)} %copy-done.13, bf16[1024,256]{1,0:T(8,128)(2,1)S(1)} %copy-done.14, f32[4096]{0:T(1024)S(1)} %pad_maximum_fusion.24, ...), kind=kOutput, calls=%fused_computation.68 | convolution fusion | flops 556859392 | bytes 4342784 | tf_op jit(solution)/shard_map/dot_general | solution.py:159
  44.7 3.7 %collective-permute-start.4 = (bf16[64,512]{0,1:T(8,128)(2,1)S(1)}, bf16[64,512]{0,1:T(8,128)(2,1)}, u32[]{:S(2)}, u32[]{:S(2)}) collective-permute-start(bf16[64,512]{0,1:T(8,128)(2,1)S(1)} %pad_maximum_fusion.20), channel_id=1, source_target_pairs={{0,4},{4,8},{8,12},{1,5},{5,9},{9,13},{2,6},{6,10},{10,14},{3,7},{... | collective-permute-start | bytes 196616 | tf_op jit(solution)/shard_map/ppermute | solution.py:17
  48.4 2.5 %convolution_convert_fusion.4 = bf16[256,512]{1,0:T(8,128)(2,1)S(1)} fusion(bf16[1024,512]{1,0:T(8,128)(2,1)S(1)} %copy-done.8, bf16[1024,512]{1,0:T(8,128)(2,1)S(1)} %copy-done.10, bf16[1024,512]{1,0:T(8,128)(2,1)S(1)} %get-tuple-element.20, bf16[1024,512]{1,0:T(8,128)(2,1)S(1)} %get-tuple-element.19, f32[4096]{0:T(1024)S(1)} %pad_maximum_fusion.24, ...), kind=kOutput, calls=%fused_computation.62 | convolution fusion | flops 1102184448 | bytes 6571008 | tf_op jit(solution)/shard_map/dot_general | solution.py:157
  51.2 2.6 %fusion.140 = (f32[2,2,256]{2,1,0:T(2,128)S(1)}, f32[2,2,256,320]{2,3,1,0:T(8,128)}) fusion(bf16[320,2,128,1]{0,2,3,1:T(8,128)(2,1)S(1)} %bitcast.134, pred[256,320]{0,1:T(8,128)(4,1)} %and_and_fusion, bf16[256,2,2,128]{3,2,1,0:T(2,128)(2,1)S(1)} %reshape.192), kind=kOutput, calls=%fused_computation.225 | convolution fusion | flops 85197120 | bytes 1822720 | tf_op jit(solution)/shard_map/sub | solution.py:184
  55.5 2.7 %fusion.58 = f32[256,1024]{1,0:T(8,128)} fusion(bf16[256,512]{0,1:T(8,128)(2,1)S(1)} %bitcast.124, bf16[512,4096]{1,0:T(8,128)(2,1)} %param.17, s32[]{:T(128)S(6)} %select_n.171), kind=kOutput, calls=%fused_computation.99 | convolution fusion | flops 268435456 | bytes 2359300 | tf_op jit(solution)/shard_map/dot_general | solution.py:52
  60.5 2.7 %fusion.60 = f32[256,1024]{1,0:T(8,128)} fusion(bf16[256,512]{0,1:T(8,128)(2,1)S(1)} %bitcast.120, bf16[512,4096]{1,0:T(8,128)(2,1)} %param.17, s32[]{:T(128)S(6)} %select_n.171), kind=kOutput, calls=%fused_computation.101 | convolution fusion | flops 268435456 | bytes 2359300 | tf_op jit(solution)/shard_map/dot_general | solution.py:52
  63.5 2.7 %fusion.48 = f32[256,1024]{1,0:T(8,128)} fusion(bf16[256,512]{0,1:T(8,128)(2,1)S(1)} %bitcast.125, bf16[512,4096]{1,0:T(8,128)(2,1)} %param.17, s32[]{:T(128)S(6)} %select_n.175), kind=kOutput, calls=%fused_computation.93 | convolution fusion | flops 268435456 | bytes 2359300 | tf_op jit(solution)/shard_map/dot_general | solution.py:52
  66.4 2.6 %fusion.23 = bf16[256,1024]{1,0:T(8,128)(2,1)} fusion(f32[256,1024]{1,0:T(8,128)S(1)} %collective-permute-done.8, bf16[256,512]{0,1:T(8,128)(2,1)S(1)} %bitcast.126, bf16[512,4096]{1,0:T(8,128)(2,1)} %param.17, s32[]{:T(128)S(6)} %select_n.167), kind=kOutput, calls=%fused_computation.51 | convolution fusion | flops 268959744 | bytes 2883588 | tf_op jit(solution)/shard_map/dot_general | solution.py:52
  69.5 2.2 %fusion.22 = bf16[256,1024]{1,0:T(8,128)(2,1)S(1)} fusion(f32[256,1024]{1,0:T(8,128)} %collective-permute-done.7, bf16[256,512]{0,1:T(8,128)(2,1)S(1)} %bitcast.121, bf16[512,4096]{1,0:T(8,128)(2,1)} %param.17, s32[]{:T(128)S(6)} %select_n.167), kind=kOutput, calls=%fused_computation.50 | convolution fusion | flops 268959744 | bytes 2883588 | tf_op jit(solution)/shard_map/dot_general | solution.py:52
  71.7 11.5 %collective-permute-done.9 = bf16[256,1024]{1,0:T(8,128)(2,1)S(1)} collective-permute-done((bf16[256,1024]{1,0:T(8,128)(2,1)}, bf16[256,1024]{1,0:T(8,128)(2,1)S(1)}, u32[]{:S(2)}, u32[]{:S(2)}) %collective-permute-start.9) | collective-permute-done | bytes 524320 | tf_op jit(solution)/shard_map/ppermute | solution.py:38
  88.4 8.1 %collective-permute-done.10 = bf16[256,1024]{1,0:T(8,128)(2,1)S(1)} collective-permute-done((bf16[256,1024]{1,0:T(8,128)(2,1)S(1)}, bf16[256,1024]{1,0:T(8,128)(2,1)S(1)}, u32[]{:S(2)}, u32[]{:S(2)}) %collective-permute-start.10) | collective-permute-done | bytes 524320 | tf_op jit(solution)/shard_map/ppermute | solution.py:38
  97.5 11.3 %collective-permute-done.13 = bf16[256,1024]{1,0:T(8,128)(2,1)S(1)} collective-permute-done((bf16[256,1024]{1,0:T(8,128)(2,1)S(1)}, bf16[256,1024]{1,0:T(8,128)(2,1)S(1)}, u32[]{:S(2)}, u32[]{:S(2)}) %collective-permute-start.13) | collective-permute-done | bytes 524320 | tf_op jit(solution)/shard_map/ppermute | solution.py:38
  111.2 12.6 %collective-permute-done.14 = bf16[256,1024]{1,0:T(8,128)(2,1)S(1)} collective-permute-done((bf16[256,1024]{1,0:T(8,128)(2,1)S(1)}, bf16[256,1024]{1,0:T(8,128)(2,1)S(1)}, u32[]{:S(2)}, u32[]{:S(2)}) %collective-permute-start.14) | collective-permute-done | bytes 524320 | tf_op jit(solution)/shard_map/ppermute | solution.py:38
  137.4 9.9 %collective-permute-done.20 = bf16[2,273,256]{2,1,0:T(8,128)(2,1)S(1)} collective-permute-done((bf16[2,273,256]{2,1,0:T(8,128)(2,1)S(1)}, bf16[2,273,256]{2,1,0:T(8,128)(2,1)S(1)}, u32[]{:S(2)}, u32[]{:S(2)}) %collective-permute-start.20) | collective-permute-done | bytes 279584 | tf_op jit(solution)/shard_map/ppermute | solution.py:100
  147.3 11.9 %collective-permute-done.19 = bf16[2,273,256]{2,1,0:T(8,128)(2,1)S(1)} collective-permute-done((bf16[2,273,256]{2,1,0:T(8,128)(2,1)S(1)}, bf16[2,273,256]{2,1,0:T(8,128)(2,1)S(1)}, u32[]{:S(2)}, u32[]{:S(2)}) %collective-permute-start.19) | collective-permute-done | bytes 279584 | tf_op jit(solution)/shard_map/ppermute | solution.py:100
  168.0 12.4 %collective-permute-done.23 = bf16[256,1024]{1,0:T(8,128)(2,1)S(1)} collective-permute-done((bf16[256,1024]{1,0:T(8,128)(2,1)S(1)}, bf16[256,1024]{1,0:T(8,128)(2,1)S(1)}, u32[]{:S(2)}, u32[]{:S(2)}) %collective-permute-start.23) | collective-permute-done | bytes 524320 | tf_op jit(solution)/shard_map/ppermute | solution.py:38
  181.5 12.1 %collective-permute-done.26 = bf16[256,1024]{1,0:T(8,128)(2,1)S(1)} collective-permute-done((bf16[256,1024]{1,0:T(8,128)(2,1)S(1)}, bf16[256,1024]{1,0:T(8,128)(2,1)S(1)}, u32[]{:S(2)}, u32[]{:S(2)}) %collective-permute-start.26) | collective-permute-done | bytes 524320 | tf_op jit(solution)/shard_map/ppermute | solution.py:38
  (173 shorter events, 51.8 us)
Async XLA Ops:
  1.3 16.7 %collective-permute-start.5 = (bf16[256,1024]{1,0:T(8,128)(2,1)S(1)}, bf16[256,1024]{1,0:T(8,128)(2,1)}, u32[]{:S(2)}, u32[]{:S(2)}) collective-permute-start(bf16[256,1024]{1,0:T(8,128)(2,1)S(1)} %get-tuple-element.36), channel_id=1, source_target_pairs={{0,1},{1,0},{2,3},{3,2},{4,5},{5,4},{6,7},{7,6},{8,9},{9,8},{10,11... | collective-permute-start | bytes 1572872 | tf_op jit(solution)/shard_map/ppermute | solution.py:27
  1.4 14.4 %collective-permute-start = (bf16[256,1024]{1,0:T(8,128)(2,1)S(1)}, bf16[256,1024]{1,0:T(8,128)(2,1)}, u32[]{:S(2)}, u32[]{:S(2)}) collective-permute-start(bf16[256,1024]{1,0:T(8,128)(2,1)S(1)} %get-tuple-element.36), channel_id=1, source_target_pairs={{0,2},{1,3},{2,0},{3,1},{4,6},{5,7},{6,4},{7,5},{8,10},{9,11},{10,... | collective-permute-start | bytes 1572872 | tf_op jit(solution)/shard_map/ppermute | solution.py:38
  2.0 35.8 %collective-permute-start.2 = (bf16[256,1024]{1,0:T(8,128)(2,1)S(1)}, bf16[256,1024]{1,0:T(8,128)(2,1)}, u32[]{:S(2)}, u32[]{:S(2)}) collective-permute-start(bf16[256,1024]{1,0:T(8,128)(2,1)S(1)} %get-tuple-element.12), channel_id=1, source_target_pairs={{0,1},{1,0},{2,3},{3,2},{4,5},{5,4},{6,7},{7,6},{8,9},{9,8},{10,11... | collective-permute-start | bytes 1572872 | tf_op jit(solution)/shard_map/ppermute | solution.py:27
  17.4 14.4 %collective-permute-start.1 = (bf16[256,1024]{1,0:T(8,128)(2,1)S(1)}, bf16[256,1024]{1,0:T(8,128)(2,1)}, u32[]{:S(2)}, u32[]{:S(2)}) collective-permute-start(bf16[256,1024]{1,0:T(8,128)(2,1)S(1)} %get-tuple-element.12), channel_id=1, source_target_pairs={{0,2},{1,3},{2,0},{3,1},{4,6},{5,7},{6,4},{7,5},{8,10},{9,11},{10,... | collective-permute-start | bytes 1572872 | tf_op jit(solution)/shard_map/ppermute | solution.py:38
  31.8 6.0 %collective-permute-start.3 = (bf16[256,1024]{1,0:T(8,128)(2,1)}, bf16[256,1024]{1,0:T(8,128)(2,1)S(1)}, u32[]{:S(2)}, u32[]{:S(2)}) collective-permute-start(bf16[256,1024]{1,0:T(8,128)(2,1)} %collective-permute-done.1), channel_id=1, source_target_pairs={{0,1},{1,0},{2,3},{3,2},{4,5},{5,4},{6,7},{7,6},{8,9},{9,8},{10,11... | collective-permute-start | bytes 1572872 | tf_op jit(solution)/shard_map/ppermute | solution.py:27
  44.7 13.7 %collective-permute-start.4 = (bf16[64,512]{0,1:T(8,128)(2,1)S(1)}, bf16[64,512]{0,1:T(8,128)(2,1)}, u32[]{:S(2)}, u32[]{:S(2)}) collective-permute-start(bf16[64,512]{0,1:T(8,128)(2,1)S(1)} %pad_maximum_fusion.20), channel_id=1, source_target_pairs={{0,4},{4,8},{8,12},{1,5},{5,9},{9,13},{2,6},{6,10},{10,14},{3,7},{... | collective-permute-start | bytes 196616 | tf_op jit(solution)/shard_map/ppermute | solution.py:17
  58.1 8.2 %collective-permute-start.8 = (f32[256,1024]{1,0:T(8,128)}, f32[256,1024]{1,0:T(8,128)S(1)}, u32[]{:S(2)}, u32[]{:S(2)}) collective-permute-start(f32[256,1024]{1,0:T(8,128)} %fusion.58), channel_id=1, source_target_pairs={{0,1},{1,0},{2,3},{3,2},{4,5},{5,4},{6,7},{7,6},{8,9},{9,8},{10,11... | collective-permute-start | bytes 3145736 | tf_op jit(solution)/shard_map/ppermute | solution.py:27
  63.2 6.3 %collective-permute-start.7 = (f32[256,1024]{1,0:T(8,128)}, f32[256,1024]{1,0:T(8,128)}, u32[]{:S(2)}, u32[]{:S(2)}) collective-permute-start(f32[256,1024]{1,0:T(8,128)} %fusion.60), channel_id=1, source_target_pairs={{0,1},{1,0},{2,3},{3,2},{4,5},{5,4},{6,7},{7,6},{8,9},{9,8},{10,11... | collective-permute-start | bytes 3145736 | tf_op jit(solution)/shard_map/ppermute | solution.py:27
  66.2 20.5 %collective-permute-start.12 = (f32[256,1024]{1,0:T(8,128)}, f32[256,1024]{1,0:T(8,128)}, u32[]{:S(2)}, u32[]{:S(2)}) collective-permute-start(f32[256,1024]{1,0:T(8,128)} %fusion.48), channel_id=1, source_target_pairs={{0,1},{1,0},{2,3},{3,2},{4,5},{5,4},{6,7},{7,6},{8,9},{9,8},{10,11... | collective-permute-start | bytes 3145736 | tf_op jit(solution)/shard_map/ppermute | solution.py:27
  69.0 14.3 %collective-permute-start.9 = (bf16[256,1024]{1,0:T(8,128)(2,1)}, bf16[256,1024]{1,0:T(8,128)(2,1)S(1)}, u32[]{:S(2)}, u32[]{:S(2)}) collective-permute-start(bf16[256,1024]{1,0:T(8,128)(2,1)} %fusion.23), channel_id=1, source_target_pairs={{0,2},{1,3},{2,0},{3,1},{4,6},{5,7},{6,4},{7,5},{8,10},{9,11},{10,... | collective-permute-start | bytes 1572872 | tf_op jit(solution)/shard_map/ppermute | solution.py:38
  83.2 13.3 %collective-permute-start.10 = (bf16[256,1024]{1,0:T(8,128)(2,1)S(1)}, bf16[256,1024]{1,0:T(8,128)(2,1)S(1)}, u32[]{:S(2)}, u32[]{:S(2)}) collective-permute-start(bf16[256,1024]{1,0:T(8,128)(2,1)S(1)} %fusion.22), channel_id=1, source_target_pairs={{0,2},{1,3},{2,0},{3,1},{4,6},{5,7},{6,4},{7,5},{8,10},{9,11},{10,... | collective-permute-start | bytes 1572872 | tf_op jit(solution)/shard_map/ppermute | solution.py:38
  85.4 23.4 %collective-permute-start.11 = (f32[256,1024]{1,0:T(8,128)S(1)}, f32[256,1024]{1,0:T(8,128)S(1)}, u32[]{:S(2)}, u32[]{:S(2)}) collective-permute-start(f32[256,1024]{1,0:T(8,128)S(1)} %fusion.50), channel_id=1, source_target_pairs={{0,1},{1,0},{2,3},{3,2},{4,5},{5,4},{6,7},{7,6},{8,9},{9,8},{10,11... | collective-permute-start | bytes 3145736 | tf_op jit(solution)/shard_map/ppermute | solution.py:27
  96.5 12.3 %collective-permute-start.13 = (bf16[256,1024]{1,0:T(8,128)(2,1)S(1)}, bf16[256,1024]{1,0:T(8,128)(2,1)S(1)}, u32[]{:S(2)}, u32[]{:S(2)}) collective-permute-start(bf16[256,1024]{1,0:T(8,128)(2,1)S(1)} %add_convert_fusion.2), channel_id=1, source_target_pairs={{0,2},{1,3},{2,0},{3,1},{4,6},{5,7},{6,4},{7,5},{8,10},{9,11},{10,... | collective-permute-start | bytes 1572872 | tf_op jit(solution)/shard_map/ppermute | solution.py:38
  97.4 12.8 %collective-permute-start.17 = (bf16[256,1024]{1,0:T(8,128)(2,1)S(1)}, bf16[256,1024]{1,0:T(8,128)(2,1)S(1)}, u32[]{:S(2)}, u32[]{:S(2)}) collective-permute-start(bf16[256,1024]{1,0:T(8,128)(2,1)S(1)} %add_convert_fusion.2), channel_id=1, source_target_pairs={{0,1},{1,0},{2,3},{3,2},{4,5},{5,4},{6,7},{7,6},{8,9},{9,8},{10,11... | collective-permute-start | bytes 1572872 | tf_op jit(solution)/shard_map/ppermute | solution.py:27
  109.4 14.4 %collective-permute-start.14 = (bf16[256,1024]{1,0:T(8,128)(2,1)S(1)}, bf16[256,1024]{1,0:T(8,128)(2,1)S(1)}, u32[]{:S(2)}, u32[]{:S(2)}) collective-permute-start(bf16[256,1024]{1,0:T(8,128)(2,1)S(1)} %add_convert_fusion.3), channel_id=1, source_target_pairs={{0,2},{1,3},{2,0},{3,1},{4,6},{5,7},{6,4},{7,5},{8,10},{9,11},{10,... | collective-permute-start | bytes 1572872 | tf_op jit(solution)/shard_map/ppermute | solution.py:38
  110.0 16.1 %collective-permute-start.15 = (bf16[256,1024]{1,0:T(8,128)(2,1)S(1)}, bf16[256,1024]{1,0:T(8,128)(2,1)S(1)}, u32[]{:S(2)}, u32[]{:S(2)}) collective-permute-start(bf16[256,1024]{1,0:T(8,128)(2,1)S(1)} %add_convert_fusion.3), channel_id=1, source_target_pairs={{0,1},{1,0},{2,3},{3,2},{4,5},{5,4},{6,7},{7,6},{8,9},{9,8},{10,11... | collective-permute-start | bytes 1572872 | tf_op jit(solution)/shard_map/ppermute | solution.py:27
  130.0 7.4 %collective-permute-start.21 = (bf16[2,273,256]{2,1,0:T(8,128)(2,1)S(1)}, bf16[2,273,256]{2,1,0:T(8,128)(2,1)S(1)}, u32[]{:S(2)}, u32[]{:S(2)}) collective-permute-start(bf16[2,273,256]{2,1,0:T(8,128)(2,1)S(1)} %convolution_convert_fusion), channel_id=1, source_target_pairs={{0,12},{1,13},{2,14},{3,15},{16,28},{17,29},{18,30},{19,31}} | collective-permute-start | bytes 838664 | tf_op jit(solution)/shard_map/ppermute | solution.py:100
  130.8 16.5 %collective-permute-start.20 = (bf16[2,273,256]{2,1,0:T(8,128)(2,1)S(1)}, bf16[2,273,256]{2,1,0:T(8,128)(2,1)S(1)}, u32[]{:S(2)}, u32[]{:S(2)}) collective-permute-start(bf16[2,273,256]{2,1,0:T(8,128)(2,1)S(1)} %convolution_convert_fusion), channel_id=1, source_target_pairs={{0,8},{4,12},{1,9},{5,13},{2,10},{6,14},{3,11},{7,15},{16,24},{20,... | collective-permute-start | bytes 838664 | tf_op jit(solution)/shard_map/ppermute | solution.py:100
  132.1 27.1 %collective-permute-start.19 = (bf16[2,273,256]{2,1,0:T(8,128)(2,1)S(1)}, bf16[2,273,256]{2,1,0:T(8,128)(2,1)S(1)}, u32[]{:S(2)}, u32[]{:S(2)}) collective-permute-start(bf16[2,273,256]{2,1,0:T(8,128)(2,1)S(1)} %convolution_convert_fusion), channel_id=1, source_target_pairs={{0,4},{4,8},{8,12},{1,5},{5,9},{9,13},{2,6},{6,10},{10,14},{3,7},{... | collective-permute-start | bytes 838664 | tf_op jit(solution)/shard_map/ppermute | solution.py:100
  163.8 3.7 %collective-permute-start.25 = (f32[256,1024]{1,0:T(8,128)S(1)}, f32[256,1024]{1,0:T(8,128)S(1)}, u32[]{:S(2)}, u32[]{:S(2)}) collective-permute-start(f32[256,1024]{1,0:T(8,128)S(1)} %fusion.42), channel_id=1, source_target_pairs={{0,1},{1,0},{2,3},{3,2},{4,5},{5,4},{6,7},{7,6},{8,9},{9,8},{10,11... | collective-permute-start | bytes 3145736 | tf_op jit(solution)/shard_map/ppermute | solution.py:27
  164.8 16.2 %collective-permute-start.24 = (f32[256,1024]{1,0:T(8,128)S(1)}, f32[256,1024]{1,0:T(8,128)S(1)}, u32[]{:S(2)}, u32[]{:S(2)}) collective-permute-start(f32[256,1024]{1,0:T(8,128)S(1)} %fusion.34), channel_id=1, source_target_pairs={{0,1},{1,0},{2,3},{3,2},{4,5},{5,4},{6,7},{7,6},{8,9},{9,8},{10,11... | collective-permute-start | bytes 3145736 | tf_op jit(solution)/shard_map/ppermute | solution.py:27
  166.4 14.0 %collective-permute-start.23 = (bf16[256,1024]{1,0:T(8,128)(2,1)S(1)}, bf16[256,1024]{1,0:T(8,128)(2,1)S(1)}, u32[]{:S(2)}, u32[]{:S(2)}) collective-permute-start(bf16[256,1024]{1,0:T(8,128)(2,1)S(1)} %fusion.24), channel_id=1, source_target_pairs={{0,2},{1,3},{2,0},{3,1},{4,6},{5,7},{6,4},{7,5},{8,10},{9,11},{10,... | collective-permute-start | bytes 1572872 | tf_op jit(solution)/shard_map/ppermute | solution.py:38
  167.5 14.0 %collective-permute-start.27 = (f32[256,1024]{1,0:T(8,128)S(1)}, f32[256,1024]{1,0:T(8,128)S(1)}, u32[]{:S(2)}, u32[]{:S(2)}) collective-permute-start(f32[256,1024]{1,0:T(8,128)S(1)} %fusion.32), channel_id=1, source_target_pairs={{0,1},{1,0},{2,3},{3,2},{4,5},{5,4},{6,7},{7,6},{8,9},{9,8},{10,11... | collective-permute-start | bytes 3145736 | tf_op jit(solution)/shard_map/ppermute | solution.py:27
  180.5 13.1 %collective-permute-start.26 = (bf16[256,1024]{1,0:T(8,128)(2,1)S(1)}, bf16[256,1024]{1,0:T(8,128)(2,1)S(1)}, u32[]{:S(2)}, u32[]{:S(2)}) collective-permute-start(bf16[256,1024]{1,0:T(8,128)(2,1)S(1)} %fusion.25), channel_id=1, source_target_pairs={{0,2},{1,3},{2,0},{3,1},{4,6},{5,7},{6,4},{7,5},{8,10},{9,11},{10,... | collective-permute-start | bytes 1572872 | tf_op jit(solution)/shard_map/ppermute | solution.py:38
  (32 other events, 294.7 us)

commit v5 on v4

--- a/solution.py
+++ b/solution.py
@@ -150,21 +150,24 @@
     w_feature = gathered_rows(w_feature)
     wv_linear = gathered_rows(wv_linear)
 
+    tail = from_behind(hidden_in[tok_rows - WINDOW :], "ctx", 1)
     query_parts, kv_parts = [], []
-    for part in hidden_parts:
+    for i, part in enumerate(hidden_parts):
+        if i == 0:
+            part = jnp.concatenate([tail, part], axis=0)
         normed = norm_rows(head_all_gather(part), attn_gain)
+        query_rows = normed[WINDOW:] if i == 0 else normed
         query_parts.append(
-            jnp.dot(normed, w_query, preferred_element_type=jnp.float32).astype(jnp.bfloat16)
+            jnp.dot(query_rows, w_query, preferred_element_type=jnp.float32).astype(jnp.bfloat16)
         )
         keys = jnp.dot(normed, w_keys, preferred_element_type=jnp.float32).astype(jnp.bfloat16)
         values = jnp.dot(normed, w_values, preferred_element_type=jnp.float32).astype(jnp.bfloat16)
         kv_parts.append(jnp.concatenate([keys, values], axis=1))
-    rim = from_behind(kv_parts[-1][size - WINDOW :], "ctx", 1)
-    kv_all = jnp.concatenate([rim] + kv_parts, axis=0)
+    kv_all = jnp.concatenate(kv_parts, axis=0)
     start = lax.axis_index("ctx") * tok_rows
 
     partial_parts = [None] * CHUNKS
-    for i in reversed(range(CHUNKS)):
+    for i in range(CHUNKS):
         kv_win = kv_all[i * size : i * size + size + WINDOW]
         key_win = kv_win[:, :kv_cols].reshape(size + WINDOW, kv_heads, HEAD)
         value_win = kv_win[:, kv_cols:].reshape(size + WINDOW, kv_heads, HEAD)
@@ -189,7 +192,7 @@
         attended = attended.astype(jnp.bfloat16).reshape(size, -1)
         partial_parts[i] = head_reduce_scatter(attended, wo_attn)
     after_parts, after_whole_parts = [None] * CHUNKS, [None] * CHUNKS
-    for i in reversed(range(CHUNKS)):
+    for i in range(CHUNKS):
         after_window = (hidden_parts[i].astype(jnp.float32) + partial_parts[i]).astype(jnp.bfloat16)
         after_parts[i] = after_window
         after_whole_parts[i] = head_all_gather(after_window)

time: 196 us -> 212 us (1.082)
  the two profiles are of different devices: /device:TPU:22 before, /device:TPU:24 now
where the time goes in v5:
time: 212 us; the launch traced here: 211 us
  waiting for transfers between devices  109 us (51%)
  matrix products  52.5 us (25%)
  starting transfers between devices  20 us (9%)
  local copies, waits for them, and re-layouts  15.9 us (8%)
  other arithmetic  12.3 us (6%)
    ppermute x8, waiting for transfers between devices, chip_shift(): moved = lax.ppermute(value, 'head', pairs)  82 us
    ppermute x3, waiting for transfers between devices, earlier_sum(): total = total + lax.ppermute(sent, 'ctx', pairs).astype(jnp.float32)  23.3 us
    dot_general x16, matrix products, block(): return jnp.dot(lhs, cols, preferred_element_type=jnp.float32)  20.5 us
    ppermute x8, starting transfers between devices, chip_shift(): moved = lax.ppermute(value, 'head', pairs)  12.1 us
    dynamic_slice x5, local copies, waits for them, and re-layouts, gathered_rows(): lax.dynamic_slice_in_dim(weight, src * block, block, axis=0)  7.66 us
    dot_general x2, matrix products, body(): jnp.dot(query_rows, w_query, preferred_element_type=jnp.float32)  7.33 us
    reduce_sum x4, other arithmetic, norm_rows(): scale = lax.rsqrt(jnp.mean(wide * wide, axis=-1, keepdims=True) + 1e-05)  6.43 us
    dot_general x2, matrix products, body(): jnp.dot(normed, w_keys, preferred_element_type=jnp.float32)  4.8 us
  transfers between devices with their start and end apart: 28, of which 13 were waited for; matrix products, arithmetic and copies ran while one was open for 33% of the time, Pallas kernels for 0%

profile of v5, /device:TPU:24, one launch (start us, length us, event | category | flops | bytes accessed | tf_op | source)
XLA Modules:
  0.0 210.9 jit_solution(16966051320963618426)
XLA Ops:
  2.2 2.1 fusion.147
  5.8 2.2 %collective-permute-done = bf16[64,1024]{1,0:T(8,128)(2,1)S(1)} collective-permute-done((bf16[64,1024]{1,0:T(8,128)(2,1)S(1)}, bf16[64,1024]{1,0:T(8,128)(2,1)S(1)}, u32[]{:S(2)}, u32[]{:S(2)}) %collective-permute-start) | collective-permute-done | bytes 131104 | tf_op jit(solution)/shard_map/ppermute | solution.py:17
  9.7 4.4 %constant_dynamic-slice_fusion.11 = (bf16[1024,512]{1,0:T(8,128)(2,1)}, bf16[1024,512]{1,0:T(8,128)(2,1)}, bf16[1024,512]{1,0:T(8,128)(2,1)}, bf16[1024,512]{1,0:T(8,128)(2,1)}) fusion(bf16[4096,512]{1,0:T(8,128)(2,1)} %param.14, s32[]{:T(128)S(6)} %select_n.163, s32[]{:T(128)S(6)} %select_n.167, s32[]{:T(128)S(6)} %select_n.169, s32[]{:T(128)S(6)} %select_n.168), kind=kLoop, calls=%fused_computation.182 | loop fusion | bytes 8388624 | tf_op jit(solution)/shard_map/dynamic_slice | solution.py:89
  15.7 8.1 %collective-permute-done.1 = bf16[320,1024]{1,0:T(8,128)(2,1)S(1)} collective-permute-done((bf16[320,1024]{1,0:T(8,128)(2,1)S(1)}, bf16[320,1024]{1,0:T(8,128)(2,1)S(1)}, u32[]{:S(2)}, u32[]{:S(2)}) %collective-permute-start.1) | collective-permute-done | bytes 655392 | tf_op jit(solution)/shard_map/ppermute | solution.py:38
  26.9 11.5 %collective-permute-done.5 = bf16[256,1024]{1,0:T(8,128)(2,1)} collective-permute-done((bf16[256,1024]{1,0:T(8,128)(2,1)}, bf16[256,1024]{1,0:T(8,128)(2,1)}, u32[]{:S(2)}, u32[]{:S(2)}) %collective-permute-start.5) | collective-permute-done | bytes 524320 | tf_op jit(solution)/shard_map/ppermute | solution.py:38
  38.4 3.4 %fusion.2 = f32[320]{0:T(512)S(1)} fusion(bf16[320,1024]{1,0:T(8,128)(2,1)S(1)} %collective-permute-done.3, bf16[320,1024]{1,0:T(8,128)(2,1)S(1)} %collective-permute-done.2, bf16[320,1024]{1,0:T(8,128)(2,1)S(1)} %collective-permute-done.1, bf16[256,1024]{1,0:T(8,128)(2,1)S(1)} %get-tuple-element.36, bf16[64,1024]{1,0:T(8,128)(2,1)S(1)} %collective-permute-done), kind=kLoop, calls=%fused_computation.10 | loop fusion | flops 15728320 | bytes 2622720 | tf_op jit(solution)/shard_map/reduce_sum | solution.py:106
  45.2 2.4 %convolution_convert_fusion.6 = bf16[320,256]{1,0:T(8,128)(2,1)S(1)} fusion(bf16[320,4096]{1,0:T(8,128)(2,1)S(1)} %fusion.4, bf16[1024,256]{1,0:T(8,128)(2,1)} %get-tuple-element.33, bf16[1024,256]{1,0:T(8,128)(2,1)} %get-tuple-element.34, bf16[1024,256]{1,0:T(8,128)(2,1)} %get-tuple-element.32, bf16[1024,256]{1,0:T(8,128)(2,1)} %get-tuple-element.31), kind=kOutput, calls=%fused_computation.67 | convolution fusion | flops 679559168 | bytes 4882432 | tf_op jit(solution)/shard_map/dot_general | solution.py:163
  48.3 3.4 %fusion.30 = bf16[256,512]{1,0:T(8,128)(2,1)S(1)} fusion(bf16[320,4096]{1,0:T(8,128)(2,1)S(1)} %fusion.4, bf16[1024,512]{1,0:T(8,128)(2,1)} %get-tuple-element.21, bf16[1024,512]{1,0:T(8,128)(2,1)} %get-tuple-element.22, bf16[1024,512]{1,0:T(8,128)(2,1)} %get-tuple-element.20, bf16[1024,512]{1,0:T(8,128)(2,1)} %get-tuple-element.19), kind=kOutput, calls=%fused_computation.61 | convolution fusion | flops 1090650112 | bytes 6553600 | tf_op jit(solution)/shard_map/dot_general | solution.py:161
  54.8 2.7 %fusion.65 = f32[256,1024]{1,0:T(8,128)} fusion(bf16[256,512]{0,1:T(8,128)(2,1)S(1)} %bitcast.102, bf16[512,4096]{1,0:T(8,128)(2,1)} %param.17, s32[]{:T(128)S(6)} %select_n.171), kind=kOutput, calls=%fused_computation.103 | convolution fusion | flops 268435456 | bytes 2359300 | tf_op jit(solution)/shard_map/dot_general | solution.py:52
  58.0 2.0 fusion.5
  60.1 2.4 %convolution_convert_fusion.9 = bf16[256,256]{1,0:T(8,128)(2,1)S(1)} fusion(bf16[1024,256]{1,0:T(8,128)(2,1)S(1)} %copy-done.24, bf16[1024,256]{1,0:T(8,128)(2,1)S(1)} %copy-done.25, bf16[1024,256]{1,0:T(8,128)(2,1)S(1)} %copy-done.23, bf16[1024,256]{1,0:T(8,128)(2,1)S(1)} %copy-done.22, f32[4096]{0:T(1024)S(1)} %pad_maximum_fusion.24, ...), kind=kOutput, calls=%fused_computation.70 | convolution fusion | flops 556859392 | bytes 4342784 | tf_op jit(solution)/shard_map/dot_general | solution.py:163
  62.6 2.5 %convolution_convert_fusion.8 = bf16[256,256]{1,0:T(8,128)(2,1)S(1)} fusion(bf16[1024,256]{1,0:T(8,128)(2,1)S(1)} %copy-done.17, bf16[1024,256]{1,0:T(8,128)(2,1)S(1)} %copy-done.15, bf16[1024,256]{1,0:T(8,128)(2,1)S(1)} %copy-done.19, bf16[1024,256]{1,0:T(8,128)(2,1)S(1)} %copy-done.21, f32[4096]{0:T(1024)S(1)} %pad_maximum_fusion.24, ...), kind=kOutput, calls=%fused_computation.69 | convolution fusion | flops 556859392 | bytes 4342784 | tf_op jit(solution)/shard_map/dot_general | solution.py:164
  67.5 3.9 %convolution_convert_fusion.4 = bf16[256,512]{1,0:T(8,128)(2,1)} fusion(bf16[1024,512]{1,0:T(8,128)(2,1)S(1)} %copy-done.9, bf16[1024,512]{1,0:T(8,128)(2,1)} %get-tuple-element.22, bf16[1024,512]{1,0:T(8,128)(2,1)S(1)} %copy-done.8, bf16[1024,512]{1,0:T(8,128)(2,1)S(1)} %copy-done.7, f32[4096]{0:T(1024)S(1)} %pad_maximum_fusion.24, ...), kind=kOutput, calls=%fused_computation.65 | convolution fusion | flops 1102184448 | bytes 6571008 | tf_op jit(solution)/shard_map/dot_general | solution.py:161
  75.3 2.7 %fusion.63 = f32[256,1024]{1,0:T(8,128)} fusion(bf16[256,512]{0,1:T(8,128)(2,1)S(1)} %bitcast.106, bf16[512,4096]{1,0:T(8,128)(2,1)} %param.17, s32[]{:T(128)S(6)} %select_n.171), kind=kOutput, calls=%fused_computation.101 | convolution fusion | flops 268435456 | bytes 2359300 | tf_op jit(solution)/shard_map/dot_general | solution.py:52
  78.0 2.7 %fusion.55 = f32[256,1024]{1,0:T(8,128)} fusion(bf16[256,512]{0,1:T(8,128)(2,1)S(1)} %bitcast.103, bf16[512,4096]{1,0:T(8,128)(2,1)} %param.17, s32[]{:T(128)S(6)} %select_n.174), kind=kOutput, calls=%fused_computation.97 | convolution fusion | flops 268435456 | bytes 2359300 | tf_op jit(solution)/shard_map/dot_general | solution.py:52
  81.2 2.8 %fusion.24 = bf16[256,1024]{1,0:T(8,128)(2,1)} fusion(f32[256,1024]{1,0:T(8,128)} %collective-permute-done.4, bf16[256,512]{0,1:T(8,128)(2,1)S(1)} %bitcast.104, bf16[512,4096]{1,0:T(8,128)(2,1)} %param.17, s32[]{:T(128)S(6)} %select_n.167), kind=kOutput, calls=%fused_computation.52 | convolution fusion | flops 268959744 | bytes 2883588 | tf_op jit(solution)/shard_map/dot_general | solution.py:52
  87.5 10.7 %collective-permute-done.6 = bf16[256,1024]{1,0:T(8,128)(2,1)S(1)} collective-permute-done((bf16[256,1024]{1,0:T(8,128)(2,1)}, bf16[256,1024]{1,0:T(8,128)(2,1)S(1)}, u32[]{:S(2)}, u32[]{:S(2)}) %collective-permute-start.6) | collective-permute-done | bytes 524320 | tf_op jit(solution)/shard_map/ppermute | solution.py:38
  103.2 8.1 %collective-permute-done.11 = bf16[256,1024]{1,0:T(8,128)(2,1)S(1)} collective-permute-done((bf16[256,1024]{1,0:T(8,128)(2,1)S(1)}, bf16[256,1024]{1,0:T(8,128)(2,1)S(1)}, u32[]{:S(2)}, u32[]{:S(2)}) %collective-permute-start.11) | collective-permute-done | bytes 524320 | tf_op jit(solution)/shard_map/ppermute | solution.py:38
  113.3 10.2 %collective-permute-done.12 = bf16[256,1024]{1,0:T(8,128)(2,1)S(1)} collective-permute-done((bf16[256,1024]{1,0:T(8,128)(2,1)S(1)}, bf16[256,1024]{1,0:T(8,128)(2,1)S(1)}, u32[]{:S(2)}, u32[]{:S(2)}) %collective-permute-start.12) | collective-permute-done | bytes 524320 | tf_op jit(solution)/shard_map/ppermute | solution.py:38
  127.8 10.9 %collective-permute-done.16 = bf16[256,1024]{1,0:T(8,128)(2,1)S(1)} collective-permute-done((bf16[256,1024]{1,0:T(8,128)(2,1)S(1)}, bf16[256,1024]{1,0:T(8,128)(2,1)S(1)}, u32[]{:S(2)}, u32[]{:S(2)}) %collective-permute-start.16) | collective-permute-done | bytes 524320 | tf_op jit(solution)/shard_map/ppermute | solution.py:38
  151.6 3.7 %collective-permute-done.19 = bf16[2,273,256]{2,1,0:T(8,128)(2,1)S(1)} collective-permute-done((bf16[2,273,256]{2,1,0:T(8,128)(2,1)S(1)}, bf16[2,273,256]{2,1,0:T(8,128)(2,1)S(1)}, u32[]{:S(2)}, u32[]{:S(2)}) %collective-permute-start.19) | collective-permute-done | bytes 279584 | tf_op jit(solution)/shard_map/ppermute | solution.py:100
  155.3 19.6 %collective-permute-done.20 = bf16[2,273,256]{2,1,0:T(8,128)(2,1)S(1)} collective-permute-done((bf16[2,273,256]{2,1,0:T(8,128)(2,1)S(1)}, bf16[2,273,256]{2,1,0:T(8,128)(2,1)S(1)}, u32[]{:S(2)}, u32[]{:S(2)}) %collective-permute-start.20) | collective-permute-done | bytes 279584 | tf_op jit(solution)/shard_map/ppermute | solution.py:100
  184.7 11.4 %collective-permute-done.23 = bf16[256,1024]{1,0:T(8,128)(2,1)S(1)} collective-permute-done((bf16[256,1024]{1,0:T(8,128)(2,1)S(1)}, bf16[256,1024]{1,0:T(8,128)(2,1)S(1)}, u32[]{:S(2)}, u32[]{:S(2)}) %collective-permute-start.23) | collective-permute-done | bytes 524320 | tf_op jit(solution)/shard_map/ppermute | solution.py:38
  198.2 11.1 %collective-permute-done.26 = bf16[256,1024]{1,0:T(8,128)(2,1)S(1)} collective-permute-done((bf16[256,1024]{1,0:T(8,128)(2,1)S(1)}, bf16[256,1024]{1,0:T(8,128)(2,1)S(1)}, u32[]{:S(2)}, u32[]{:S(2)}) %collective-permute-start.26) | collective-permute-done | bytes 524320 | tf_op jit(solution)/shard_map/ppermute | solution.py:38
  (189 shorter events, 64.9 us)
Async XLA Ops:
  0.9 7.1 %collective-permute-start = (bf16[64,1024]{1,0:T(8,128)(2,1)S(1)}, bf16[64,1024]{1,0:T(8,128)(2,1)S(1)}, u32[]{:S(2)}, u32[]{:S(2)}) collective-permute-start(bf16[64,1024]{1,0:T(8,128)(2,1)S(1)} %slice.34), channel_id=1, source_target_pairs={{0,4},{4,8},{8,12},{1,5},{5,9},{9,13},{2,6},{6,10},{10,14},{3,7},{... | collective-permute-start | bytes 393224 | tf_op jit(solution)/shard_map/ppermute | solution.py:17
  4.3 53.7 %collective-permute-start.8 = (bf16[256,1024]{1,0:T(8,128)(2,1)}, bf16[256,1024]{1,0:T(8,128)(2,1)}, u32[]{:S(2)}, u32[]{:S(2)}) collective-permute-start(bf16[256,1024]{1,0:T(8,128)(2,1)} %get-tuple-element.12), channel_id=1, source_target_pairs={{0,1},{1,0},{2,3},{3,2},{4,5},{5,4},{6,7},{7,6},{8,9},{9,8},{10,11... | collective-permute-start | bytes 1572872 | tf_op jit(solution)/shard_map/ppermute | solution.py:27
  8.1 15.7 %collective-permute-start.1 = (bf16[320,1024]{1,0:T(8,128)(2,1)S(1)}, bf16[320,1024]{1,0:T(8,128)(2,1)S(1)}, u32[]{:S(2)}, u32[]{:S(2)}) collective-permute-start(bf16[320,1024]{1,0:T(8,128)(2,1)S(1)} %pad_maximum_fusion.13), channel_id=1, source_target_pairs={{0,2},{1,3},{2,0},{3,1},{4,6},{5,7},{6,4},{7,5},{8,10},{9,11},{10,... | collective-permute-start | bytes 1966088 | tf_op jit(solution)/shard_map/ppermute | solution.py:38
  15.6 22.8 %collective-permute-start.2 = (bf16[320,1024]{1,0:T(8,128)(2,1)S(1)}, bf16[320,1024]{1,0:T(8,128)(2,1)S(1)}, u32[]{:S(2)}, u32[]{:S(2)}) collective-permute-start(bf16[320,1024]{1,0:T(8,128)(2,1)S(1)} %pad_maximum_fusion.13), channel_id=1, source_target_pairs={{0,1},{1,0},{2,3},{3,2},{4,5},{5,4},{6,7},{7,6},{8,9},{9,8},{10,11... | collective-permute-start | bytes 1966088 | tf_op jit(solution)/shard_map/ppermute | solution.py:27
  23.8 14.7 %collective-permute-start.3 = (bf16[320,1024]{1,0:T(8,128)(2,1)S(1)}, bf16[320,1024]{1,0:T(8,128)(2,1)S(1)}, u32[]{:S(2)}, u32[]{:S(2)}) collective-permute-start(bf16[320,1024]{1,0:T(8,128)(2,1)S(1)} %collective-permute-done.1), channel_id=1, source_target_pairs={{0,1},{1,0},{2,3},{3,2},{4,5},{5,4},{6,7},{7,6},{8,9},{9,8},{10,11... | collective-permute-start | bytes 1966088 | tf_op jit(solution)/shard_map/ppermute | solution.py:27
  23.8 14.7 %collective-permute-start.5 = (bf16[256,1024]{1,0:T(8,128)(2,1)}, bf16[256,1024]{1,0:T(8,128)(2,1)}, u32[]{:S(2)}, u32[]{:S(2)}) collective-permute-start(bf16[256,1024]{1,0:T(8,128)(2,1)} %get-tuple-element.12), channel_id=1, source_target_pairs={{0,2},{1,3},{2,0},{3,1},{4,6},{5,7},{6,4},{7,5},{8,10},{9,11},{10,... | collective-permute-start | bytes 1572872 | tf_op jit(solution)/shard_map/ppermute | solution.py:38
  38.4 19.5 %collective-permute-start.9 = (bf16[256,1024]{1,0:T(8,128)(2,1)}, bf16[256,1024]{1,0:T(8,128)(2,1)}, u32[]{:S(2)}, u32[]{:S(2)}) collective-permute-start(bf16[256,1024]{1,0:T(8,128)(2,1)} %collective-permute-done.5), channel_id=1, source_target_pairs={{0,1},{1,0},{2,3},{3,2},{4,5},{5,4},{6,7},{7,6},{8,9},{9,8},{10,11... | collective-permute-start | bytes 1572872 | tf_op jit(solution)/shard_map/ppermute | solution.py:27
  57.5 23.7 %collective-permute-start.4 = (f32[256,1024]{1,0:T(8,128)}, f32[256,1024]{1,0:T(8,128)}, u32[]{:S(2)}, u32[]{:S(2)}) collective-permute-start(f32[256,1024]{1,0:T(8,128)} %fusion.65), channel_id=1, source_target_pairs={{0,1},{1,0},{2,3},{3,2},{4,5},{5,4},{6,7},{7,6},{8,9},{9,8},{10,11... | collective-permute-start | bytes 3145736 | tf_op jit(solution)/shard_map/ppermute | solution.py:27
  78.0 7.6 %collective-permute-start.10 = (f32[256,1024]{1,0:T(8,128)}, f32[256,1024]{1,0:T(8,128)S(1)}, u32[]{:S(2)}, u32[]{:S(2)}) collective-permute-start(f32[256,1024]{1,0:T(8,128)} %fusion.63), channel_id=1, source_target_pairs={{0,1},{1,0},{2,3},{3,2},{4,5},{5,4},{6,7},{7,6},{8,9},{9,8},{10,11... | collective-permute-start | bytes 3145736 | tf_op jit(solution)/shard_map/ppermute | solution.py:27
  80.7 20.7 %collective-permute-start.7 = (f32[256,1024]{1,0:T(8,128)}, f32[256,1024]{1,0:T(8,128)}, u32[]{:S(2)}, u32[]{:S(2)}) collective-permute-start(f32[256,1024]{1,0:T(8,128)} %fusion.55), channel_id=1, source_target_pairs={{0,1},{1,0},{2,3},{3,2},{4,5},{5,4},{6,7},{7,6},{8,9},{9,8},{10,11... | collective-permute-start | bytes 3145736 | tf_op jit(solution)/shard_map/ppermute | solution.py:27
  84.0 14.2 %collective-permute-start.6 = (bf16[256,1024]{1,0:T(8,128)(2,1)}, bf16[256,1024]{1,0:T(8,128)(2,1)S(1)}, u32[]{:S(2)}, u32[]{:S(2)}) collective-permute-start(bf16[256,1024]{1,0:T(8,128)(2,1)} %fusion.24), channel_id=1, source_target_pairs={{0,2},{1,3},{2,0},{3,1},{4,6},{5,7},{6,4},{7,5},{8,10},{9,11},{10,... | collective-permute-start | bytes 1572872 | tf_op jit(solution)/shard_map/ppermute | solution.py:38
  98.2 13.1 %collective-permute-start.11 = (bf16[256,1024]{1,0:T(8,128)(2,1)S(1)}, bf16[256,1024]{1,0:T(8,128)(2,1)S(1)}, u32[]{:S(2)}, u32[]{:S(2)}) collective-permute-start(bf16[256,1024]{1,0:T(8,128)(2,1)S(1)} %fusion.25), channel_id=1, source_target_pairs={{0,2},{1,3},{2,0},{3,1},{4,6},{5,7},{6,4},{7,5},{8,10},{9,11},{10,... | collective-permute-start | bytes 1572872 | tf_op jit(solution)/shard_map/ppermute | solution.py:38
  101.4 22.3 %collective-permute-start.15 = (f32[256,1024]{1,0:T(8,128)S(1)}, f32[256,1024]{1,0:T(8,128)S(1)}, u32[]{:S(2)}, u32[]{:S(2)}) collective-permute-start(f32[256,1024]{1,0:T(8,128)S(1)} %fusion.53), channel_id=1, source_target_pairs={{0,1},{1,0},{2,3},{3,2},{4,5},{5,4},{6,7},{7,6},{8,9},{9,8},{10,11... | collective-permute-start | bytes 3145736 | tf_op jit(solution)/shard_map/ppermute | solution.py:27
  111.3 12.2 %collective-permute-start.12 = (bf16[256,1024]{1,0:T(8,128)(2,1)S(1)}, bf16[256,1024]{1,0:T(8,128)(2,1)S(1)}, u32[]{:S(2)}, u32[]{:S(2)}) collective-permute-start(bf16[256,1024]{1,0:T(8,128)(2,1)S(1)} %add_convert_fusion.3), channel_id=1, source_target_pairs={{0,2},{1,3},{2,0},{3,1},{4,6},{5,7},{6,4},{7,5},{8,10},{9,11},{10,... | collective-permute-start | bytes 1572872 | tf_op jit(solution)/shard_map/ppermute | solution.py:38
  113.2 13.1 %collective-permute-start.13 = (bf16[256,1024]{1,0:T(8,128)(2,1)S(1)}, bf16[256,1024]{1,0:T(8,128)(2,1)S(1)}, u32[]{:S(2)}, u32[]{:S(2)}) collective-permute-start(bf16[256,1024]{1,0:T(8,128)(2,1)S(1)} %add_convert_fusion.3), channel_id=1, source_target_pairs={{0,1},{1,0},{2,3},{3,2},{4,5},{5,4},{6,7},{7,6},{8,9},{9,8},{10,11... | collective-permute-start | bytes 1572872 | tf_op jit(solution)/shard_map/ppermute | solution.py:27
  124.2 15.9 %collective-permute-start.17 = (bf16[256,1024]{1,0:T(8,128)(2,1)S(1)}, bf16[256,1024]{1,0:T(8,128)(2,1)S(1)}, u32[]{:S(2)}, u32[]{:S(2)}) collective-permute-start(bf16[256,1024]{1,0:T(8,128)(2,1)S(1)} %add_convert_fusion.2), channel_id=1, source_target_pairs={{0,1},{1,0},{2,3},{3,2},{4,5},{5,4},{6,7},{7,6},{8,9},{9,8},{10,11... | collective-permute-start | bytes 1572872 | tf_op jit(solution)/shard_map/ppermute | solution.py:27
  124.8 13.9 %collective-permute-start.16 = (bf16[256,1024]{1,0:T(8,128)(2,1)S(1)}, bf16[256,1024]{1,0:T(8,128)(2,1)S(1)}, u32[]{:S(2)}, u32[]{:S(2)}) collective-permute-start(bf16[256,1024]{1,0:T(8,128)(2,1)S(1)} %add_convert_fusion.2), channel_id=1, source_target_pairs={{0,2},{1,3},{2,0},{3,1},{4,6},{5,7},{6,4},{7,5},{8,10},{9,11},{10,... | collective-permute-start | bytes 1572872 | tf_op jit(solution)/shard_map/ppermute | solution.py:38
  144.3 11.1 %collective-permute-start.19 = (bf16[2,273,256]{2,1,0:T(8,128)(2,1)S(1)}, bf16[2,273,256]{2,1,0:T(8,128)(2,1)S(1)}, u32[]{:S(2)}, u32[]{:S(2)}) collective-permute-start(bf16[2,273,256]{2,1,0:T(8,128)(2,1)S(1)} %convolution_convert_fusion), channel_id=1, source_target_pairs={{0,4},{4,8},{8,12},{1,5},{5,9},{9,13},{2,6},{6,10},{10,14},{3,7},{... | collective-permute-start | bytes 838664 | tf_op jit(solution)/shard_map/ppermute | solution.py:100
  145.7 29.2 %collective-permute-start.20 = (bf16[2,273,256]{2,1,0:T(8,128)(2,1)S(1)}, bf16[2,273,256]{2,1,0:T(8,128)(2,1)S(1)}, u32[]{:S(2)}, u32[]{:S(2)}) collective-permute-start(bf16[2,273,256]{2,1,0:T(8,128)(2,1)S(1)} %convolution_convert_fusion), channel_id=1, source_target_pairs={{0,8},{4,12},{1,9},{5,13},{2,10},{6,14},{3,11},{7,15},{16,24},{20,... | collective-permute-start | bytes 838664 | tf_op jit(solution)/shard_map/ppermute | solution.py:100
  147.0 28.0 %collective-permute-start.21 = (bf16[2,273,256]{2,1,0:T(8,128)(2,1)S(1)}, bf16[2,273,256]{2,1,0:T(8,128)(2,1)S(1)}, u32[]{:S(2)}, u32[]{:S(2)}) collective-permute-start(bf16[2,273,256]{2,1,0:T(8,128)(2,1)S(1)} %convolution_convert_fusion), channel_id=1, source_target_pairs={{0,12},{1,13},{2,14},{3,15},{16,28},{17,29},{18,30},{19,31}} | collective-permute-start | bytes 838664 | tf_op jit(solution)/shard_map/ppermute | solution.py:100
  180.5 17.2 %collective-permute-start.24 = (f32[256,1024]{1,0:T(8,128)S(1)}, f32[256,1024]{1,0:T(8,128)S(1)}, u32[]{:S(2)}, u32[]{:S(2)}) collective-permute-start(f32[256,1024]{1,0:T(8,128)S(1)} %fusion.39), channel_id=1, source_target_pairs={{0,1},{1,0},{2,3},{3,2},{4,5},{5,4},{6,7},{7,6},{8,9},{9,8},{10,11... | collective-permute-start | bytes 3145736 | tf_op jit(solution)/shard_map/ppermute | solution.py:27
  182.1 14.0 %collective-permute-start.23 = (bf16[256,1024]{1,0:T(8,128)(2,1)S(1)}, bf16[256,1024]{1,0:T(8,128)(2,1)S(1)}, u32[]{:S(2)}, u32[]{:S(2)}) collective-permute-start(bf16[256,1024]{1,0:T(8,128)(2,1)S(1)} %fusion.26), channel_id=1, source_target_pairs={{0,2},{1,3},{2,0},{3,1},{4,6},{5,7},{6,4},{7,5},{8,10},{9,11},{10,... | collective-permute-start | bytes 1572872 | tf_op jit(solution)/shard_map/ppermute | solution.py:38
  184.2 14.0 %collective-permute-start.27 = (f32[256,1024]{1,0:T(8,128)S(1)}, f32[256,1024]{1,0:T(8,128)S(1)}, u32[]{:S(2)}, u32[]{:S(2)}) collective-permute-start(f32[256,1024]{1,0:T(8,128)S(1)} %fusion.37), channel_id=1, source_target_pairs={{0,1},{1,0},{2,3},{3,2},{4,5},{5,4},{6,7},{7,6},{8,9},{9,8},{10,11... | collective-permute-start | bytes 3145736 | tf_op jit(solution)/shard_map/ppermute | solution.py:27
  196.2 13.1 %collective-permute-start.26 = (bf16[256,1024]{1,0:T(8,128)(2,1)S(1)}, bf16[256,1024]{1,0:T(8,128)(2,1)S(1)}, u32[]{:S(2)}, u32[]{:S(2)}) collective-permute-start(bf16[256,1024]{1,0:T(8,128)(2,1)S(1)} %fusion.27), channel_id=1, source_target_pairs={{0,2},{1,3},{2,0},{3,1},{4,6},{5,7},{6,4},{7,5},{8,10},{9,11},{10,... | collective-permute-start | bytes 1572872 | tf_op jit(solution)/shard_map/ppermute | solution.py:38
  (38 other events, 421.3 us)

commit v6 on v3

--- a/solution.py
+++ b/solution.py
@@ -111,7 +111,7 @@
     )
 
 
-CHUNKS = 2
+CHUNKS = 1
 
 
 def body(

time: 193 us -> 190 us (0.984)
  waiting for transfers between devices: 94.4 us -> 123 us
  matrix products: 58.4 us -> 36.8 us
  starting transfers between devices: 18.7 us -> 13 us
  local copies, waits for them, and re-layouts: 9.21 us -> 5.54 us
    ppermute x8 -> x4, waiting for transfers between devices: 69.1 us -> 91.4 us  [chip_shift(): return lax.ppermute(value, 'head', pairs)]
    dot_general x16 -> x8, matrix products: 23.2 us -> 15.1 us  [block(): return jnp.dot(lhs, cols, preferred_element_type=jnp.float32)]
    convert_element_type x0 -> x3, other arithmetic: none -> 6.56 us  [the longest x1 2.42 us: norm_rows(): return (wide * scale * gain).astype(jnp.bfloat16)]
    ppermute x16 -> x8, waiting for transfers between devices: 0.1 us -> 5.71 us  [core_swap(): return lax.ppermute(value, 'head', [(h, h ^ 1) for h in range(devices)])]
    dot_general x2 -> x1, matrix products: 5.84 us -> 1.31 us  [body(): jnp.dot(normed, w_keys, preferred_element_type=jnp.float32)]
    ppermute x8 -> x4, starting transfers between devices: 9.92 us -> 6.09 us  [chip_shift(): return lax.ppermute(value, 'head', pairs)]
    dot_general x2 -> x1, matrix products: 5.1 us -> 1.31 us  [body(): jnp.dot(normed, w_values, preferred_element_type=jnp.float32)]
    dot_general x2 -> x1, matrix products: 5.84 us -> 2.37 us  [body(): jnp.dot(normed, w_query, preferred_element_type=jnp.float32)]
  transfers between devices with their start and end apart: 28 -> 16, of which waited for: 12 -> 10; matrix products, arithmetic and copies ran while one was open for 23% -> 11% of each run, Pallas kernels for 0% -> 0%
where the time goes in v6:
time: 190 us
  waiting for transfers between devices  123 us (65%)
  matrix products  36.8 us (19%)
  starting transfers between devices  13 us (7%)
  other arithmetic  10.9 us (6%)
  local copies, waits for them, and re-layouts  5.54 us (3%)
    ppermute x4, waiting for transfers between devices, chip_shift(): return lax.ppermute(value, 'head', pairs)  91.4 us
    ppermute x3, waiting for transfers between devices, earlier_sum(): total = total + lax.ppermute(sent, 'ctx', pairs).astype(jnp.float32)  21.9 us
    dot_general x8, matrix products, block(): return jnp.dot(lhs, cols, preferred_element_type=jnp.float32)  15.1 us
    ppermute x4, starting transfers between devices, chip_shift(): return lax.ppermute(value, 'head', pairs)  6.09 us
    ppermute x8, waiting for transfers between devices, core_swap(): return lax.ppermute(value, 'head', [(h, h ^ 1) for h in range(devices)])  5.71 us
    ppermute x3, starting transfers between devices, earlier_sum(): total = total + lax.ppermute(sent, 'ctx', pairs).astype(jnp.float32)  4.27 us
    dynamic_slice x6, local copies, waits for them, and re-layouts, gathered_rows(): lax.dynamic_slice_in_dim(weight, src * block, block, axis=0)  4.02 us
    sub x1, matrix products, body(): expd = jnp.exp(scores - top)  3.95 us
  transfers between devices with their start and end apart: 16, of which 10 were waited for; matrix products, arithmetic and copies ran while one was open for 11% of the time, Pallas kernels for 0%

profile of v6, /device:TPU:24, one launch (start us, length us, event | category | flops | bytes accessed | tf_op | source)
XLA Modules:
  0.0 189.6 jit_solution(3999199710354560572)
XLA Ops:
  1.5 23.6 %collective-permute-done = bf16[512,1024]{1,0:T(8,128)(2,1)S(1)} collective-permute-done((bf16[512,1024]{1,0:T(8,128)(2,1)}, bf16[512,1024]{1,0:T(8,128)(2,1)S(1)}, u32[]{:S(2)}, u32[]{:S(2)}) %collective-permute-start) | collective-permute-done | bytes 1048608 | tf_op jit(solution)/shard_map/ppermute | solution.py:33
  26.0 2.6 %constant_dynamic-slice_fusion.11 = (bf16[1024,512]{1,0:T(8,128)(2,1)S(1)}, bf16[1024,512]{1,0:T(8,128)(2,1)S(1)}, bf16[1024,512]{1,0:T(8,128)(2,1)S(1)}, bf16[1024,512]{1,0:T(8,128)(2,1)S(1)}) fusion(bf16[4096,512]{1,0:T(8,128)(2,1)} %param.14, s32[]{:T(128)S(6)} %select_n.127, s32[]{:T(128)S(6)} %select_n.131, s32[]{:T(128)S(6)} %select_n.133, ...), kind=kLoop, calls=%fused_computation.138 | loop fusion | bytes 8388624 | tf_op jit(solution)/shard_map/dynamic_slice | solution.py:82
  30.7 2.0 %fusion.1 = f32[512]{0:T(512)S(1)} fusion(bf16[512,1024]{1,0:T(8,128)(2,1)} %collective-permute-done.2, bf16[512,1024]{1,0:T(8,128)(2,1)S(1)} %collective-permute-done.1, bf16[512,1024]{1,0:T(8,128)(2,1)S(1)} %collective-permute-done, bf16[512,1024]{1,0:T(8,128)(2,1)S(1)} %copy-done), kind=kLoop, calls=%fused_computation.5 | loop fusion | flops 20971008 | bytes 4196352 | tf_op jit(solution)/shard_map/reduce_sum | solution.py:99
  32.7 2.4 %fusion.3 = bf16[512,4096]{1,0:T(8,128)(2,1)S(1)} fusion(f32[4096]{0:T(1024)S(1)} %pad_maximum_fusion.3, f32[512]{0:T(512)S(1)} %add_rsqrt_fusion.2, bf16[512,1024]{1,0:T(8,128)(2,1)} %collective-permute-done.2, bf16[512,1024]{1,0:T(8,128)(2,1)S(1)} %collective-permute-done.1, bf16[512,1024]{1,0:T(8,128)(2,1)S(1)} %collective-permute-done, ...), kind=kLoop, calls=%fused_computation.7 | loop fusion | flops 23068672 | bytes 8407040 | tf_op jit(solution)/shard_map/convert_element_type | solution.py:100
  39.4 2.4 %fusion.48 = bf16[512,512]{0,1:T(8,128)(2,1)S(1)} fusion(bf16[512,4096]{1,0:T(8,128)(2,1)S(1)} %fusion.3, bf16[1024,512]{1,0:T(8,128)(2,1)S(1)} %get-tuple-element.7, bf16[1024,512]{1,0:T(8,128)(2,1)S(1)} %get-tuple-element.8, bf16[1024,512]{1,0:T(8,128)(2,1)S(1)} %get-tuple-element.6, bf16[1024,512]{1,0:T(8,128)(2,1)S(1)} %get-tuple-element.5), kind=kOutput, calls=%fused_computation.61 | convolution fusion | flops 2164523008 | bytes 8912896 | tf_op jit(solution)/shard_map/dot_general | solution.py:149
  41.8 3.9 %collective-permute-done.3 = bf16[64,512]{0,1:T(8,128)(2,1)S(1)} collective-permute-done((bf16[64,512]{0,1:T(8,128)(2,1)S(1)}, bf16[64,512]{0,1:T(8,128)(2,1)S(1)}, u32[]{:S(2)}, u32[]{:S(2)}) %collective-permute-start.3) | collective-permute-done | bytes 65568 | tf_op jit(solution)/shard_map/ppermute | solution.py:17
  46.0 3.9 %fusion.119 = (f32[2,2,512]{2,1,0:T(2,128)S(1)}, f32[2,2,512,576]{2,3,1,0:T(8,128)}) fusion(pred[512,576]{0,1:T(8,128)(4,1)S(1)} %and_and_fusion, bf16[576,2,128,1]{0,2,3,1:T(8,128)(2,1)S(1)} %bitcast.82, bf16[512,2,2,128]{0,3,2,1:T(8,128)(2,1)S(1)} %bitcast.83), kind=kOutput, calls=%fused_computation.166 | convolution fusion | flops 306709056 | bytes 5840896 | tf_op jit(solution)/shard_map/sub | solution.py:176
  50.0 2.9 %fusion.51 = bf16[2,128,2,512]{3,1,2,0:T(8,128)(2,1)S(1)} fusion(bf16[576,2,128,1]{0,2,3,1:T(8,128)(2,1)S(1)} %bitcast.81, f32[2,2,512,576]{2,3,1,0:T(8,128)} %get-tuple-element.40, f32[2,2,512]{2,1,0:T(2,128)S(1)} %get-tuple-element.39), kind=kOutput, calls=%fused_computation.62 | convolution fusion | flops 304611328 | bytes 5545984 | tf_op jit(solution)/shard_map/kgts,skd->tkgd/dot_general | solution.py:178
  52.9 3.3 %fusion.80 = f32[512,1024]{1,0:T(8,128)} fusion(bf16[512,512]{0,1:T(8,128)(2,1)S(1)} %bitcast.70, bf16[512,4096]{1,0:T(8,128)(2,1)} %param.17, s32[]{:T(128)S(6)} %select_n.135), kind=kOutput, calls=%fused_computation.92 | convolution fusion | flops 536870912 | bytes 3670020 | tf_op jit(solution)/shard_map/dot_general | solution.py:45
  56.2 3.3 %fusion.76 = f32[512,1024]{1,0:T(8,128)} fusion(bf16[512,512]{0,1:T(8,128)(2,1)S(1)} %bitcast.71, bf16[512,4096]{1,0:T(8,128)(2,1)} %param.17, s32[]{:T(128)S(6)} %select_n.138), kind=kOutput, calls=%fused_computation.88 | convolution fusion | flops 536870912 | bytes 3670020 | tf_op jit(solution)/shard_map/dot_general | solution.py:45
  60.7 3.6 %add_convert_fusion.3 = bf16[512,1024]{1,0:T(8,128)(2,1)} fusion(f32[512,1024]{1,0:T(8,128)} %collective-permute-done.4, bf16[512,512]{0,1:T(8,128)(2,1)S(1)} %bitcast.72, bf16[512,4096]{1,0:T(8,128)(2,1)} %param.17, s32[]{:T(128)S(6)} %select_n.131), kind=kOutput, calls=%fused_computation.57 | convolution fusion | flops 537919488 | bytes 4718596 | tf_op jit(solution)/shard_map/dot_general | solution.py:45
  65.8 1.9 %fusion.78 = f32[512,1024]{1,0:T(8,128)S(1)} fusion(bf16[512,512]{0,1:T(8,128)(2,1)S(1)} %bitcast.73, bf16[512,4096]{1,0:T(8,128)(2,1)} %param.17, s32[]{:T(128)S(6)} %select_n.137), kind=kOutput, calls=%fused_computation.90 | convolution fusion | flops 536870912 | bytes 3670020 | tf_op jit(solution)/shard_map/dot_general | solution.py:45
  67.8 21.9 %collective-permute-done.5 = bf16[512,1024]{1,0:T(8,128)(2,1)S(1)} collective-permute-done((bf16[512,1024]{1,0:T(8,128)(2,1)}, bf16[512,1024]{1,0:T(8,128)(2,1)S(1)}, u32[]{:S(2)}, u32[]{:S(2)}) %collective-permute-start.5) | collective-permute-done | bytes 1048608 | tf_op jit(solution)/shard_map/ppermute | solution.py:33
  89.8 2.4 %add_convert_fusion.2 = bf16[512,1024]{1,0:T(8,128)(2,1)S(1)} fusion(f32[512,1024]{1,0:T(8,128)S(1)} %fusion.78, f32[512,1024]{1,0:T(8,128)} %collective-permute-done.6, bf16[512,1024]{1,0:T(8,128)(2,1)S(1)} %collective-permute-done.5, bf16[512,1024]{1,0:T(8,128)(2,1)S(1)} %copy-done), kind=kLoop, calls=%fused_computation.56 | loop fusion | flops 3145728 | bytes 7340032 | tf_op jit(solution)/shard_map/convert_element_type | solution.py:183
  93.7 22.9 %collective-permute-done.7 = bf16[512,1024]{1,0:T(8,128)(2,1)S(1)} collective-permute-done((bf16[512,1024]{1,0:T(8,128)(2,1)S(1)}, bf16[512,1024]{1,0:T(8,128)(2,1)S(1)}, u32[]{:S(2)}, u32[]{:S(2)}) %collective-permute-start.7) | collective-permute-done | bytes 1048608 | tf_op jit(solution)/shard_map/ppermute | solution.py:33
  117.1 2.1 %collective-permute-done.9 = bf16[512,1024]{1,0:T(8,128)(2,1)S(1)} collective-permute-done((bf16[512,1024]{1,0:T(8,128)(2,1)S(1)}, bf16[512,1024]{1,0:T(8,128)(2,1)S(1)}, u32[]{:S(2)}, u32[]{:S(2)}) %collective-permute-start.9) | collective-permute-done | bytes 1048608 | tf_op jit(solution)/shard_map/ppermute | solution.py:27
  122.0 2.6 %fusion.45 = bf16[512,512]{0,1:T(8,128)(2,1)S(1)} fusion(bf16[1024,512]{1,0:T(8,128)(2,1)S(1)} %get-tuple-element.11, bf16[1024,512]{1,0:T(8,128)(2,1)S(1)} %get-tuple-element.12, bf16[1024,512]{1,0:T(8,128)(2,1)S(1)} %get-tuple-element.10, bf16[1024,512]{1,0:T(8,128)(2,1)S(1)} %get-tuple-element.9, f32[4096]{0:T(1024)S(1)} %pad_maximum_fusion.4, ...), kind=kOutput, calls=%fused_computation.60 | convolution fusion | flops 2187591680 | bytes 8931328 | tf_op jit(solution)/shard_map/dot_general | solution.py:196
  129.7 2.3 %select_convert_fusion = bf16[2,512,512]{2,1,0:T(8,128)(2,1)S(1)} fusion(pred[512,512]{1,0:T(8,128)(4,1)S(1)} %iota_compare_fusion, f32[512,2,2,16]{0,3,2,1:T(8,128)S(1)} %bitcast.80), kind=kOutput, calls=%fused_computation.55 | convolution fusion | flops 104333312 | bytes 1441792 | tf_op jit(solution)/shard_map/thf,shf->hts/dot_general | solution.py:215
  132.6 3.9 %collective-permute-done.10 = bf16[2,273,256]{2,1,0:T(8,128)(2,1)S(1)} collective-permute-done((bf16[2,273,256]{2,1,0:T(8,128)(2,1)S(1)}, bf16[2,273,256]{2,1,0:T(8,128)(2,1)S(1)}, u32[]{:S(2)}, u32[]{:S(2)}) %collective-permute-start.10) | collective-permute-done | bytes 279584 | tf_op jit(solution)/shard_map/ppermute | solution.py:93
  136.5 18.0 %collective-permute-done.11 = bf16[2,273,256]{2,1,0:T(8,128)(2,1)S(1)} collective-permute-done((bf16[2,273,256]{2,1,0:T(8,128)(2,1)S(1)}, bf16[2,273,256]{2,1,0:T(8,128)(2,1)S(1)}, u32[]{:S(2)}, u32[]{:S(2)}) %collective-permute-start.11) | collective-permute-done | bytes 279584 | tf_op jit(solution)/shard_map/ppermute | solution.py:93
  154.6 2.2 %multiply_reduce_fusion = (f32[512,2]{0,1:T(2,128)S(1)}, f32[512,2,256]{0,2,1:T(8,128)S(1)}) fusion(f32[2,256,512]{2,1,0:T(8,128)S(1)} %fusion.120, f32[512,2,256]{0,2,1:T(8,128)S(1)} %bitcast.74, f32[512,2,16]{0,2,1:T(8,128)S(1)} %get-tuple-element.28, f32[273]{0:T(512)S(1)} %pad.7.clone, f32[2,273,256]{2,0,1:T(2,128)S(1)} %copy-done.5, ...), kind=kOutput, calls=%fused_computation.84 | convolution fusion | flops 860966912 | bytes 4614212 | tf_op jit(solution)/shard_map/thf,hfv->thv/dot_general | solution.py:214
  159.1 2.9 %collective-permute-done.13 = f32[512,1024]{1,0:T(8,128)S(1)} collective-permute-done((f32[512,1024]{1,0:T(8,128)S(1)}, f32[512,1024]{1,0:T(8,128)S(1)}, u32[]{:S(2)}, u32[]{:S(2)}) %collective-permute-start.13) | collective-permute-done | bytes 2097184 | tf_op jit(solution)/shard_map/ppermute | solution.py:27
  165.0 23.0 %collective-permute-done.14 = bf16[512,1024]{1,0:T(8,128)(2,1)S(1)} collective-permute-done((bf16[512,1024]{1,0:T(8,128)(2,1)S(1)}, bf16[512,1024]{1,0:T(8,128)(2,1)S(1)}, u32[]{:S(2)}, u32[]{:S(2)}) %collective-permute-start.14) | collective-permute-done | bytes 1048608 | tf_op jit(solution)/shard_map/ppermute | solution.py:33
  187.9 1.7 add_convert_fusion
  (75 shorter events, 27.2 us)
Async XLA Ops:
  0.0 25.1 %collective-permute-start = (bf16[512,1024]{1,0:T(8,128)(2,1)}, bf16[512,1024]{1,0:T(8,128)(2,1)S(1)}, u32[]{:S(2)}, u32[]{:S(2)}) collective-permute-start(bf16[512,1024]{1,0:T(8,128)(2,1)} %param.12), channel_id=1, source_target_pairs={{0,2},{1,3},{2,0},{3,1},{4,6},{5,7},{6,4},{7,5},{8,10},{9,11},{10,... | collective-permute-start | bytes 3145736 | tf_op jit(solution)/shard_map/ppermute | solution.py:33
  1.5 28.6 %collective-permute-start.1 = (bf16[512,1024]{1,0:T(8,128)(2,1)}, bf16[512,1024]{1,0:T(8,128)(2,1)S(1)}, u32[]{:S(2)}, u32[]{:S(2)}) collective-permute-start(bf16[512,1024]{1,0:T(8,128)(2,1)} %param.12), channel_id=1, source_target_pairs={{0,1},{1,0},{2,3},{3,2},{4,5},{5,4},{6,7},{7,6},{8,9},{9,8},{10,11... | collective-permute-start | bytes 3145736 | tf_op jit(solution)/shard_map/ppermute | solution.py:27
  25.1 5.0 %collective-permute-start.2 = (bf16[512,1024]{1,0:T(8,128)(2,1)S(1)}, bf16[512,1024]{1,0:T(8,128)(2,1)}, u32[]{:S(2)}, u32[]{:S(2)}) collective-permute-start(bf16[512,1024]{1,0:T(8,128)(2,1)S(1)} %collective-permute-done), channel_id=1, source_target_pairs={{0,1},{1,0},{2,3},{3,2},{4,5},{5,4},{6,7},{7,6},{8,9},{9,8},{10,11... | collective-permute-start | bytes 3145736 | tf_op jit(solution)/shard_map/ppermute | solution.py:27
  26.0 2.9 %copy-start.3 = (bf16[4096,256]{1,0:T(8,128)(2,1)S(1)}, bf16[4096,256]{1,0:T(8,128)(2,1)}, u32[]{:S(2)}) copy-start(bf16[4096,256]{1,0:T(8,128)(2,1)} %param.16) | copy-start | bytes 6291460
  26.0 3.5 %copy-start.4 = (bf16[4096,256]{1,0:T(8,128)(2,1)S(1)}, bf16[4096,256]{1,0:T(8,128)(2,1)}, u32[]{:S(2)}) copy-start(bf16[4096,256]{1,0:T(8,128)(2,1)} %param.15) | copy-start | bytes 6291460
  37.9 7.7 %collective-permute-start.3 = (bf16[64,512]{0,1:T(8,128)(2,1)S(1)}, bf16[64,512]{0,1:T(8,128)(2,1)S(1)}, u32[]{:S(2)}, u32[]{:S(2)}) collective-permute-start(bf16[64,512]{0,1:T(8,128)(2,1)S(1)} %pad_maximum_fusion.2), channel_id=1, source_target_pairs={{0,4},{4,8},{8,12},{1,5},{5,9},{9,13},{2,6},{6,10},{10,14},{3,7},{... | collective-permute-start | bytes 196616 | tf_op jit(solution)/shard_map/ppermute | solution.py:17
  56.2 4.5 %collective-permute-start.4 = (f32[512,1024]{1,0:T(8,128)}, f32[512,1024]{1,0:T(8,128)}, u32[]{:S(2)}, u32[]{:S(2)}) collective-permute-start(f32[512,1024]{1,0:T(8,128)} %fusion.80), channel_id=1, source_target_pairs={{0,1},{1,0},{2,3},{3,2},{4,5},{5,4},{6,7},{7,6},{8,9},{9,8},{10,11... | collective-permute-start | bytes 6291464 | tf_op jit(solution)/shard_map/ppermute | solution.py:27
  59.5 8.3 %collective-permute-start.6 = (f32[512,1024]{1,0:T(8,128)}, f32[512,1024]{1,0:T(8,128)}, u32[]{:S(2)}, u32[]{:S(2)}) collective-permute-start(f32[512,1024]{1,0:T(8,128)} %fusion.76), channel_id=1, source_target_pairs={{0,1},{1,0},{2,3},{3,2},{4,5},{5,4},{6,7},{7,6},{8,9},{9,8},{10,11... | collective-permute-start | bytes 6291464 | tf_op jit(solution)/shard_map/ppermute | solution.py:27
  64.4 25.4 %collective-permute-start.5 = (bf16[512,1024]{1,0:T(8,128)(2,1)}, bf16[512,1024]{1,0:T(8,128)(2,1)S(1)}, u32[]{:S(2)}, u32[]{:S(2)}) collective-permute-start(bf16[512,1024]{1,0:T(8,128)(2,1)} %add_convert_fusion.3), channel_id=1, source_target_pairs={{0,2},{1,3},{2,0},{3,1},{4,6},{5,7},{6,4},{7,5},{8,10},{9,11},{10,... | collective-permute-start | bytes 3145736 | tf_op jit(solution)/shard_map/ppermute | solution.py:33
  67.8 48.8 %copy-start.7 = (f32[4096]{0:T(1024)S(1)}, f32[4096]{0:T(1024)}, u32[]{:S(2)}) copy-start(f32[4096]{0:T(1024)} %param.18) | copy-start | bytes 49156
  67.8 48.9 %copy-start.6 = (bf16[4096,64]{0,1:T(8,128)(2,1)S(1)}, bf16[4096,64]{0,1:T(8,128)(2,1)}, u32[]{:S(2)}) copy-start(bf16[4096,64]{0,1:T(8,128)(2,1)} %param.19) | copy-start | bytes 1572868
  67.8 49.0 %copy-start.2 = (bf16[4096,512]{1,0:T(8,128)(2,1)S(1)}, bf16[4096,512]{1,0:T(8,128)(2,1)}, u32[]{:S(2)}) copy-start(bf16[4096,512]{1,0:T(8,128)(2,1)} %param.20) | copy-start | bytes 12582916
  92.2 24.4 %collective-permute-start.7 = (bf16[512,1024]{1,0:T(8,128)(2,1)S(1)}, bf16[512,1024]{1,0:T(8,128)(2,1)S(1)}, u32[]{:S(2)}, u32[]{:S(2)}) collective-permute-start(bf16[512,1024]{1,0:T(8,128)(2,1)S(1)} %add_convert_fusion.2), channel_id=1, source_target_pairs={{0,2},{1,3},{2,0},{3,1},{4,6},{5,7},{6,4},{7,5},{8,10},{9,11},{10,... | collective-permute-start | bytes 3145736 | tf_op jit(solution)/shard_map/ppermute | solution.py:33
  93.7 23.4 %collective-permute-start.8 = (bf16[512,1024]{1,0:T(8,128)(2,1)S(1)}, bf16[512,1024]{1,0:T(8,128)(2,1)S(1)}, u32[]{:S(2)}, u32[]{:S(2)}) collective-permute-start(bf16[512,1024]{1,0:T(8,128)(2,1)S(1)} %add_convert_fusion.2), channel_id=1, source_target_pairs={{0,1},{1,0},{2,3},{3,2},{4,5},{5,4},{6,7},{7,6},{8,9},{9,8},{10,11... | collective-permute-start | bytes 3145736 | tf_op jit(solution)/shard_map/ppermute | solution.py:27
  116.6 2.7 %collective-permute-start.9 = (bf16[512,1024]{1,0:T(8,128)(2,1)S(1)}, bf16[512,1024]{1,0:T(8,128)(2,1)S(1)}, u32[]{:S(2)}, u32[]{:S(2)}) collective-permute-start(bf16[512,1024]{1,0:T(8,128)(2,1)S(1)} %collective-permute-done.7), channel_id=1, source_target_pairs={{0,1},{1,0},{2,3},{3,2},{4,5},{5,4},{6,7},{7,6},{8,9},{9,8},{10,11... | collective-permute-start | bytes 3145736 | tf_op jit(solution)/shard_map/ppermute | solution.py:27
  125.4 29.2 %copy-start.5 = (f32[2,273,256]{2,0,1:T(2,128)S(1)}, f32[2,273,256]{2,0,1:T(2,128)}, u32[]{:S(2)}) copy-start(f32[2,273,256]{2,0,1:T(2,128)} %param.23) | copy-start | bytes 1677316
  125.4 11.2 %collective-permute-start.10 = (bf16[2,273,256]{2,1,0:T(8,128)(2,1)S(1)}, bf16[2,273,256]{2,1,0:T(8,128)(2,1)S(1)}, u32[]{:S(2)}, u32[]{:S(2)}) collective-permute-start(bf16[2,273,256]{2,1,0:T(8,128)(2,1)S(1)} %convolution_convert_fusion), channel_id=1, source_target_pairs={{0,4},{4,8},{8,12},{1,5},{5,9},{9,13},{2,6},{6,10},{10,14},{3,7},{... | collective-permute-start | bytes 838664 | tf_op jit(solution)/shard_map/ppermute | solution.py:93
  126.8 27.8 %collective-permute-start.11 = (bf16[2,273,256]{2,1,0:T(8,128)(2,1)S(1)}, bf16[2,273,256]{2,1,0:T(8,128)(2,1)S(1)}, u32[]{:S(2)}, u32[]{:S(2)}) collective-permute-start(bf16[2,273,256]{2,1,0:T(8,128)(2,1)S(1)} %convolution_convert_fusion), channel_id=1, source_target_pairs={{0,8},{4,12},{1,9},{5,13},{2,10},{6,14},{3,11},{7,15},{16,24},{20,... | collective-permute-start | bytes 838664 | tf_op jit(solution)/shard_map/ppermute | solution.py:93
  128.1 26.5 %collective-permute-start.12 = (bf16[2,273,256]{2,1,0:T(8,128)(2,1)S(1)}, bf16[2,273,256]{2,1,0:T(8,128)(2,1)S(1)}, u32[]{:S(2)}, u32[]{:S(2)}) collective-permute-start(bf16[2,273,256]{2,1,0:T(8,128)(2,1)S(1)} %convolution_convert_fusion), channel_id=1, source_target_pairs={{0,12},{1,13},{2,14},{3,15},{16,28},{17,29},{18,30},{19,31}} | collective-permute-start | bytes 838664 | tf_op jit(solution)/shard_map/ppermute | solution.py:93
  132.0 24.8 %copy-start.8 = (f32[2,256]{1,0:T(2,128)S(1)}, f32[2,256]{1,0:T(2,128)}, u32[]{:S(2)}) copy-start(f32[2,256]{1,0:T(2,128)} %param.21) | copy-start | bytes 6148
  132.2 24.8 %copy-start.1 = (bf16[512,4096]{1,0:T(8,128)(2,1)S(1)}, bf16[512,4096]{1,0:T(8,128)(2,1)}, u32[]{:S(2)}) copy-start(bf16[512,4096]{1,0:T(8,128)(2,1)} %param.22) | copy-start | bytes 12582916
  157.7 4.2 %collective-permute-start.13 = (f32[512,1024]{1,0:T(8,128)S(1)}, f32[512,1024]{1,0:T(8,128)S(1)}, u32[]{:S(2)}, u32[]{:S(2)}) collective-permute-start(f32[512,1024]{1,0:T(8,128)S(1)} %fusion.73), channel_id=1, source_target_pairs={{0,1},{1,0},{2,3},{3,2},{4,5},{5,4},{6,7},{7,6},{8,9},{9,8},{10,11... | collective-permute-start | bytes 6291464 | tf_op jit(solution)/shard_map/ppermute | solution.py:27
  158.5 6.4 %collective-permute-start.15 = (f32[512,1024]{1,0:T(8,128)S(1)}, f32[512,1024]{1,0:T(8,128)S(1)}, u32[]{:S(2)}, u32[]{:S(2)}) collective-permute-start(f32[512,1024]{1,0:T(8,128)S(1)} %fusion.69), channel_id=1, source_target_pairs={{0,1},{1,0},{2,3},{3,2},{4,5},{5,4},{6,7},{7,6},{8,9},{9,8},{10,11... | collective-permute-start | bytes 6291464 | tf_op jit(solution)/shard_map/ppermute | solution.py:27
  162.7 25.3 %collective-permute-start.14 = (bf16[512,1024]{1,0:T(8,128)(2,1)S(1)}, bf16[512,1024]{1,0:T(8,128)(2,1)S(1)}, u32[]{:S(2)}, u32[]{:S(2)}) collective-permute-start(bf16[512,1024]{1,0:T(8,128)(2,1)S(1)} %add_convert_fusion.1), channel_id=1, source_target_pairs={{0,2},{1,3},{2,0},{3,1},{4,6},{5,7},{6,4},{7,5},{8,10},{9,11},{10,... | collective-permute-start | bytes 3145736 | tf_op jit(solution)/shard_map/ppermute | solution.py:33
  (1 other events, 1.2 us)

commit v7 on v5

--- a/solution.py
+++ b/solution.py
@@ -40,7 +40,14 @@
     return moved
 
 
-def head_reduce_scatter(lhs, weight):
+def after(value, dep):
+    if dep is None:
+        return value
+    value, _ = lax.optimization_barrier((value, dep))
+    return value
+
+
+def head_reduce_scatter(lhs, weight, dep=None):
     devices, chips = head_layout()
     me = lax.axis_index("head")
     core, chip = me % 2, me // 2
@@ -57,7 +64,7 @@
         on_chip[offset] = block(core, offset) + core_swap(block(1 - core, offset))
     acc = on_chip[chips - 1]
     for step in range(chips - 1):
-        got = chip_shift(acc.astype(jnp.bfloat16), 1).astype(jnp.float32)
+        got = after(chip_shift(acc.astype(jnp.bfloat16), 1), dep).astype(jnp.float32)
         acc = got + on_chip[(chips - step - 2) % chips]
     return acc
 
@@ -70,16 +77,23 @@
     return [me] + [r + core for r in ring] + [me ^ 1] + [r + 1 - core for r in ring]
 
 
-def head_all_gather(piece):
-    devices, chips = head_layout()
-    pieces = [piece, None]
-    pieces[1] = core_swap(piece)
+def gather_start(piece):
+    devices, chips = head_layout()
     ring, cur = [], piece
     for step in range(chips - 1):
         cur = chip_shift(cur, 1)
         ring.append(cur)
-    forwarded = [core_swap(r) for r in ring]
-    return jnp.concatenate([piece] + ring + [pieces[1]] + forwarded, axis=1)
+    return piece, core_swap(piece), ring
+
+
+def gather_finish(started, dep=None):
+    piece, partner, ring = started
+    forwarded = [core_swap(after(r, dep)) for r in ring]
+    return jnp.concatenate([piece] + ring + [partner] + forwarded, axis=1)
+
+
+def head_all_gather(piece, dep=None):
+    return gather_finish(gather_start(piece), dep)
 
 
 def gathered_rows(weight):
@@ -151,27 +165,21 @@
     wv_linear = gathered_rows(wv_linear)
 
     tail = from_behind(hidden_in[tok_rows - WINDOW :], "ctx", 1)
-    query_parts, kv_parts = [], []
-    for i, part in enumerate(hidden_parts):
-        if i == 0:
-            part = jnp.concatenate([tail, part], axis=0)
-        normed = norm_rows(head_all_gather(part), attn_gain)
-        query_rows = normed[WINDOW:] if i == 0 else normed
-        query_parts.append(
-            jnp.dot(query_rows, w_query, preferred_element_type=jnp.float32).astype(jnp.bfloat16)
-        )
+    parts = [jnp.concatenate([tail, hidden_parts[0]], axis=0)] + hidden_parts[1:]
+    start = lax.axis_index("ctx") * tok_rows
+
+    def project(whole, first):
+        normed = norm_rows(whole, attn_gain)
+        query_rows = normed[WINDOW:] if first else normed
+        query = jnp.dot(query_rows, w_query, preferred_element_type=jnp.float32).astype(jnp.bfloat16)
         keys = jnp.dot(normed, w_keys, preferred_element_type=jnp.float32).astype(jnp.bfloat16)
         values = jnp.dot(normed, w_values, preferred_element_type=jnp.float32).astype(jnp.bfloat16)
-        kv_parts.append(jnp.concatenate([keys, values], axis=1))
-    kv_all = jnp.concatenate(kv_parts, axis=0)
-    start = lax.axis_index("ctx") * tok_rows
-
-    partial_parts = [None] * CHUNKS
-    for i in range(CHUNKS):
-        kv_win = kv_all[i * size : i * size + size + WINDOW]
+        return query, jnp.concatenate([keys, values], axis=1)
+
+    def attend(i, query, kv_win):
         key_win = kv_win[:, :kv_cols].reshape(size + WINDOW, kv_heads, HEAD)
         value_win = kv_win[:, kv_cols:].reshape(size + WINDOW, kv_heads, HEAD)
-        query_heads = query_parts[i].reshape(size, kv_heads, group, HEAD)
+        query_heads = query.reshape(size, kv_heads, group, HEAD)
         scores = jnp.einsum(
             "tkgd,skd->kgts", query_heads, key_win, preferred_element_type=jnp.float32
         ) / math.sqrt(HEAD)
@@ -189,17 +197,31 @@
         attended = jnp.einsum(
             "kgts,skd->tkgd", probs, value_win, preferred_element_type=jnp.float32
         )
-        attended = attended.astype(jnp.bfloat16).reshape(size, -1)
-        partial_parts[i] = head_reduce_scatter(attended, wo_attn)
-    after_parts, after_whole_parts = [None] * CHUNKS, [None] * CHUNKS
-    for i in range(CHUNKS):
-        after_window = (hidden_parts[i].astype(jnp.float32) + partial_parts[i]).astype(jnp.bfloat16)
-        after_parts[i] = after_window
-        after_whole_parts[i] = head_all_gather(after_window)
-
+        return attended.astype(jnp.bfloat16).reshape(size, -1)
+
+    started = [gather_start(parts[0])]
+    wholes = [gather_finish(started[0])]
+    kv_parts, attended_parts = [], []
+    for i in range(CHUNKS):
+        if i + 1 < CHUNKS:
+            started.append(gather_start(parts[i + 1]))
+        query, kv = project(wholes[i], i == 0)
+        kv_parts.append(kv)
+        if i == 0:
+            kv_win = kv
+        else:
+            kv_win = jnp.concatenate([kv_parts[i - 1][-WINDOW:], kv], axis=0)
+        attended_parts.append(attend(i, query, kv_win))
+        if i + 1 < CHUNKS:
+            wholes.append(gather_finish(started[i + 1], attended_parts[i]))
+
+    after_parts = [None] * CHUNKS
     qf_parts, kf_parts, lv_parts = [], [], []
-    for i in range(CHUNKS):
-        normed2 = norm_rows(after_whole_parts[i], lin_gain)
+    dep = attended_parts[1] if CHUNKS > 1 else None
+    for i in range(CHUNKS):
+        partial = head_reduce_scatter(attended_parts[i], wo_attn, dep)
+        after_parts[i] = (hidden_parts[i].astype(jnp.float32) + partial).astype(jnp.bfloat16)
+        normed2 = norm_rows(head_all_gather(after_parts[i]), lin_gain)
         feats = jnp.dot(normed2, w_feature, preferred_element_type=jnp.float32)
         lin_heads = feats.shape[1] // (2 * FEAT)
         feats = feats.reshape(size, lin_heads, 2, FEAT)
@@ -210,6 +232,7 @@
             .astype(jnp.bfloat16)
             .reshape(size, lin_heads, VDIM)
         )
+        dep = lv_parts[-1]
     key_feat = jnp.concatenate(kf_parts, axis=0)
     lvalues = jnp.concatenate(lv_parts, axis=0)
     lin_heads = key_feat.shape[1]
@@ -220,7 +243,7 @@
     )
     carried = entry_state + earlier_sum(local_state)
 
-    outs = []
+    normed_parts = []
     for i in range(CHUNKS):
         query_feat = qf_parts[i]
         phi_query = taylor(query_feat)
@@ -233,10 +256,13 @@
         intra = jnp.einsum("hts,shv->thv", weights, lvalues, preferred_element_type=jnp.float32)
         lin_out = cross + intra
         scale = lax.rsqrt(jnp.mean(lin_out * lin_out, axis=-1, keepdims=True) + 1e-05)
-        lin_normed = (
+        normed_parts.append(
             (lin_out * scale * out_gain[None]).astype(jnp.bfloat16).reshape(size, lin_heads * VDIM)
         )
-        lin_part = head_reduce_scatter(lin_normed, wo_linear)
+    outs = []
+    for i in range(CHUNKS):
+        dep = normed_parts[i + 1] if i + 1 < CHUNKS else None
+        lin_part = head_reduce_scatter(normed_parts[i], wo_linear, dep)
         outs.append((after_parts[i].astype(jnp.float32) + lin_part).astype(jnp.bfloat16))
     return jnp.concatenate(outs, axis=0)
 

time: 212 us -> 201 us (0.948)
  waiting for transfers between devices: 109 us -> 103 us
  starting transfers between devices: 20 us -> 14.3 us
    ppermute x8, waiting for transfers between devices: 82 us -> 74.3 us  [chip_shift(): moved = lax.ppermute(value, 'head', pairs)]
    ppermute x8, starting transfers between devices: 12.1 us -> 6.56 us  [chip_shift(): moved = lax.ppermute(value, 'head', pairs)]
    reshape x6 -> x4, local copies, waits for them, and re-layouts: 5.07 us -> 2.49 us  [the longest x2 1.08 us: attend(): query_heads = query.reshape(size, kv_heads, group, HEAD)]
  transfers between devices with their start and end apart: 28 -> 28, of which waited for: 13 -> 12; matrix products, arithmetic and copies ran while one was open for 33% -> 36% of each run, Pallas kernels for 0% -> 0%
where the time goes in v7:
time: 201 us; the launch traced here: 200 us
  waiting for transfers between devices  103 us (51%)
  matrix products  53.8 us (27%)
  local copies, waits for them, and re-layouts  14.9 us (7%)
  starting transfers between devices  14.3 us (7%)
  other arithmetic  13.4 us (7%)
    ppermute x8, waiting for transfers between devices, chip_shift(): moved = lax.ppermute(value, 'head', pairs)  74.3 us
    ppermute x3, waiting for transfers between devices, earlier_sum(): total = total + lax.ppermute(sent, 'ctx', pairs).astype(jnp.float32)  22 us
    dot_general x16, matrix products, block(): return jnp.dot(lhs, cols, preferred_element_type=jnp.float32)  19.7 us
    dynamic_slice x5, local copies, waits for them, and re-layouts, gathered_rows(): lax.dynamic_slice_in_dim(weight, src * block, block, axis=0)  7.62 us
    dot_general x2, matrix products, project(): jnp.dot(query_rows, w_query, preferred_element_type=jnp.float32)  6.97 us
    ppermute x8, starting transfers between devices, chip_shift(): moved = lax.ppermute(value, 'head', pairs)  6.56 us
    reduce_sum x4, other arithmetic, norm_rows(): scale = lax.rsqrt(jnp.mean(wide * wide, axis=-1, keepdims=True) + 1e-05)  6.4 us
    dot_general x2, matrix products, project(): jnp.dot(normed, w_keys, preferred_element_type=jnp.float32)  5.79 us
  transfers between devices with their start and end apart: 28, of which 12 were waited for; matrix products, arithmetic and copies ran while one was open for 36% of the time, Pallas kernels for 0%

profile of v7, /device:TPU:24, one launch (start us, length us, event | category | flops | bytes accessed | tf_op | source)
XLA Modules:
  0.0 200.1 jit_solution(1603049413309310911)
XLA Ops:
  2.2 2.1 %fusion.140 = (bf16[256,1024]{1,0:T(8,128)(2,1)}, bf16[256,1024]{1,0:T(8,128)(2,1)S(1)}) fusion(bf16[512,1024]{1,0:T(8,128)(2,1)} %param.12), kind=kLoop, calls=%fused_computation.221 | loop fusion | bytes 2097152 | tf_op jit(solution)/shard_map/slice | solution.py:158
  4.5 3.6 %collective-permute-done = bf16[64,1024]{1,0:T(8,128)(2,1)S(1)} collective-permute-done((bf16[64,1024]{1,0:T(8,128)(2,1)S(1)}, bf16[64,1024]{1,0:T(8,128)(2,1)S(1)}, u32[]{:S(2)}, u32[]{:S(2)}) %collective-permute-start) | collective-permute-done | bytes 131104 | tf_op jit(solution)/shard_map/ppermute | solution.py:17
  11.1 4.4 %constant_dynamic-slice_fusion.11 = (bf16[1024,512]{1,0:T(8,128)(2,1)}, bf16[1024,512]{1,0:T(8,128)(2,1)}, bf16[1024,512]{1,0:T(8,128)(2,1)}, bf16[1024,512]{1,0:T(8,128)(2,1)}) fusion(bf16[4096,512]{1,0:T(8,128)(2,1)} %param.14, s32[]{:T(128)S(6)} %select_n.163, s32[]{:T(128)S(6)} %select_n.167, s32[]{:T(128)S(6)} %select_n.169, s32[]{:T(128)S(6)} %select_n.168), kind=kLoop, calls=%fused_computation.178 | loop fusion | bytes 8388624 | tf_op jit(solution)/shard_map/dynamic_slice | solution.py:103
  15.5 8.2 %collective-permute-done.1 = bf16[320,1024]{1,0:T(8,128)(2,1)S(1)} collective-permute-done((bf16[320,1024]{1,0:T(8,128)(2,1)S(1)}, bf16[320,1024]{1,0:T(8,128)(2,1)S(1)}, u32[]{:S(2)}, u32[]{:S(2)}) %collective-permute-start.1) | collective-permute-done | bytes 655392 | tf_op jit(solution)/shard_map/ppermute | solution.py:38
  28.5 3.4 %fusion.2 = f32[320]{0:T(512)S(1)} fusion(bf16[320,1024]{1,0:T(8,128)(2,1)S(1)} %collective-permute-done.3, bf16[320,1024]{1,0:T(8,128)(2,1)S(1)} %collective-permute-done.2, bf16[320,1024]{1,0:T(8,128)(2,1)S(1)} %collective-permute-done.1, bf16[256,1024]{1,0:T(8,128)(2,1)S(1)} %get-tuple-element.44, bf16[64,1024]{1,0:T(8,128)(2,1)S(1)} %collective-permute-done), kind=kLoop, calls=%fused_computation.10 | loop fusion | flops 15728320 | bytes 2622720 | tf_op jit(solution)/shard_map/reduce_sum | solution.py:120
  35.2 2.4 %convolution_convert_fusion.6 = bf16[320,256]{1,0:T(8,128)(2,1)S(1)} fusion(bf16[320,4096]{1,0:T(8,128)(2,1)S(1)} %fusion.4, bf16[1024,256]{1,0:T(8,128)(2,1)} %get-tuple-element.41, bf16[1024,256]{1,0:T(8,128)(2,1)} %get-tuple-element.42, bf16[1024,256]{1,0:T(8,128)(2,1)} %get-tuple-element.40, bf16[1024,256]{1,0:T(8,128)(2,1)} %get-tuple-element.39), kind=kOutput, calls=%fused_computation.67 | convolution fusion | flops 679559168 | bytes 4882432 | tf_op jit(solution)/shard_map/dot_general | solution.py:175
  38.3 3.4 %fusion.30 = bf16[256,512]{1,0:T(8,128)(2,1)S(1)} fusion(bf16[320,4096]{1,0:T(8,128)(2,1)S(1)} %fusion.4, bf16[1024,512]{1,0:T(8,128)(2,1)} %get-tuple-element.29, bf16[1024,512]{1,0:T(8,128)(2,1)} %get-tuple-element.30, bf16[1024,512]{1,0:T(8,128)(2,1)} %get-tuple-element.28, bf16[1024,512]{1,0:T(8,128)(2,1)} %get-tuple-element.27), kind=kOutput, calls=%fused_computation.61 | convolution fusion | flops 1090650112 | bytes 6553600 | tf_op jit(solution)/shard_map/dot_general | solution.py:174
  47.5 2.8 %fusion.65 = f32[256,1024]{1,0:T(8,128)} fusion(bf16[256,512]{0,1:T(8,128)(2,1)S(1)} %bitcast.112, bf16[512,4096]{1,0:T(8,128)(2,1)} %param.17, s32[]{:T(128)S(6)} %select_n.171), kind=kOutput, calls=%fused_computation.103 | convolution fusion | flops 268435456 | bytes 2359300 | tf_op jit(solution)/shard_map/dot_general | solution.py:59
  50.6 2.7 %fusion.55 = f32[256,1024]{1,0:T(8,128)} fusion(bf16[256,512]{0,1:T(8,128)(2,1)S(1)} %bitcast.113, bf16[512,4096]{1,0:T(8,128)(2,1)} %param.17, s32[]{:T(128)S(6)} %select_n.175), kind=kOutput, calls=%fused_computation.97 | convolution fusion | flops 268435456 | bytes 2359300 | tf_op jit(solution)/shard_map/dot_general | solution.py:59
  53.4 2.0 %fusion.5 = f32[256]{0:T(256)S(1)} fusion(bf16[256,1024]{1,0:T(8,128)(2,1)} %collective-permute-done.8, bf16[256,1024]{1,0:T(8,128)(2,1)} %collective-permute-done.7, bf16[256,1024]{1,0:T(8,128)(2,1)} %collective-permute-done.5, bf16[256,1024]{1,0:T(8,128)(2,1)} %get-tuple-element.16), kind=kLoop, calls=%fused_computation.13 | loop fusion | flops 10485504 | bytes 2098176 | tf_op jit(solution)/shard_map/reduce_sum | solution.py:120
  56.1 3.5 %convolution_convert_fusion.4 = bf16[256,512]{1,0:T(8,128)(2,1)} fusion(bf16[1024,512]{1,0:T(8,128)(2,1)S(1)} %copy-done.9, bf16[1024,512]{1,0:T(8,128)(2,1)S(1)} %copy-done.10, bf16[1024,512]{1,0:T(8,128)(2,1)S(1)} %copy-done.8, bf16[1024,512]{1,0:T(8,128)(2,1)S(1)} %copy-done.7, f32[4096]{0:T(1024)S(1)} %pad_maximum_fusion.23, ...), kind=kOutput, calls=%fused_computation.65 | convolution fusion | flops 1102184448 | bytes 6571008 | tf_op jit(solution)/shard_map/dot_general | solution.py:174
  60.6 3.4 %convolution_convert_fusion.9 = bf16[256,256]{0,1:T(8,128)(2,1)S(1)} fusion(bf16[1024,256]{1,0:T(8,128)(2,1)} %get-tuple-element.41, bf16[1024,256]{1,0:T(8,128)(2,1)} %get-tuple-element.42, bf16[1024,256]{1,0:T(8,128)(2,1)} %get-tuple-element.40, bf16[1024,256]{1,0:T(8,128)(2,1)} %get-tuple-element.39, f32[4096]{0:T(1024)S(1)} %pad_maximum_fusion.23, ...), kind=kOutput, calls=%fused_computation.70 | convolution fusion | flops 556859392 | bytes 4342784 | tf_op jit(solution)/shard_map/dot_general | solution.py:175
  64.1 2.7 %convolution_convert_fusion.8 = bf16[256,256]{0,1:T(8,128)(2,1)S(1)} fusion(bf16[1024,256]{1,0:T(8,128)(2,1)S(1)} %copy-done.17, bf16[1024,256]{1,0:T(8,128)(2,1)S(1)} %copy-done.15, bf16[1024,256]{1,0:T(8,128)(2,1)S(1)} %copy-done.19, bf16[1024,256]{1,0:T(8,128)(2,1)S(1)} %copy-done.21, f32[4096]{0:T(1024)S(1)} %pad_maximum_fusion.23, ...), kind=kOutput, calls=%fused_computation.69 | convolution fusion | flops 556859392 | bytes 4342784 | tf_op jit(solution)/shard_map/dot_general | solution.py:176
  68.9 2.8 %fusion.24 = bf16[256,1024]{1,0:T(8,128)(2,1)} fusion(f32[256,1024]{1,0:T(8,128)} %collective-permute-done.4, bf16[256,512]{0,1:T(8,128)(2,1)S(1)} %bitcast.114, bf16[512,4096]{1,0:T(8,128)(2,1)} %param.17, s32[]{:T(128)S(6)} %select_n.167), kind=kOutput, calls=%fused_computation.52 | convolution fusion | flops 268959744 | bytes 2883588 | tf_op jit(solution)/shard_map/dot_general | solution.py:59
  73.9 2.7 %fusion.63 = f32[256,1024]{1,0:T(8,128)} fusion(bf16[256,512]{0,1:T(8,128)(2,1)S(1)} %bitcast.116, bf16[512,4096]{1,0:T(8,128)(2,1)} %param.17, s32[]{:T(128)S(6)} %select_n.171), kind=kOutput, calls=%fused_computation.101 | convolution fusion | flops 268435456 | bytes 2359300 | tf_op jit(solution)/shard_map/dot_general | solution.py:59
  76.8 9.3 %collective-permute-done.6 = bf16[256,1024]{1,0:T(8,128)(2,1)S(1)} collective-permute-done((bf16[256,1024]{1,0:T(8,128)(2,1)}, bf16[256,1024]{1,0:T(8,128)(2,1)S(1)}, u32[]{:S(2)}, u32[]{:S(2)}) %collective-permute-start.6) | collective-permute-done | bytes 524320 | tf_op jit(solution)/shard_map/ppermute | solution.py:38
  86.1 2.1 %add_convert_fusion.3 = bf16[256,1024]{1,0:T(8,128)(2,1)S(1)} fusion(bf16[256,1024]{1,0:T(8,128)(2,1)S(1)} %collective-permute-done.6, f32[256,1024]{1,0:T(8,128)} %collective-permute-done.9, bf16[256,512]{0,1:T(8,128)(2,1)S(1)} %bitcast.115, bf16[512,4096]{1,0:T(8,128)(2,1)} %param.17, s32[]{:T(128)S(6)} %select_n.174, bf16[512,1024]{1,0:T(8,128)(2,1)S(1)} %copy-done.2), kind=kOutput, calls=%fused_computation.82 | convolution fusion | flops 270008320 | bytes 3932164 | tf_op jit(solution)/shard_map/dot_general | solution.py:59
  91.1 10.4 %collective-permute-done.10 = bf16[256,1024]{1,0:T(8,128)(2,1)S(1)} collective-permute-done((bf16[256,1024]{1,0:T(8,128)(2,1)S(1)}, bf16[256,1024]{1,0:T(8,128)(2,1)S(1)}, u32[]{:S(2)}, u32[]{:S(2)}) %collective-permute-start.10) | collective-permute-done | bytes 524320 | tf_op jit(solution)/shard_map/ppermute | solution.py:38
  103.1 10.9 %collective-permute-done.14 = bf16[256,1024]{1,0:T(8,128)(2,1)S(1)} collective-permute-done((bf16[256,1024]{1,0:T(8,128)(2,1)S(1)}, bf16[256,1024]{1,0:T(8,128)(2,1)S(1)}, u32[]{:S(2)}, u32[]{:S(2)}) %collective-permute-start.14) | collective-permute-done | bytes 524320 | tf_op jit(solution)/shard_map/ppermute | solution.py:38
  118.2 11.0 %collective-permute-done.16 = bf16[256,1024]{1,0:T(8,128)(2,1)S(1)} collective-permute-done((bf16[256,1024]{1,0:T(8,128)(2,1)S(1)}, bf16[256,1024]{1,0:T(8,128)(2,1)S(1)}, u32[]{:S(2)}, u32[]{:S(2)}) %collective-permute-start.16) | collective-permute-done | bytes 524320 | tf_op jit(solution)/shard_map/ppermute | solution.py:38
  142.2 3.8 %collective-permute-done.19 = bf16[2,273,256]{2,1,0:T(8,128)(2,1)S(1)} collective-permute-done((bf16[2,273,256]{2,1,0:T(8,128)(2,1)S(1)}, bf16[2,273,256]{2,1,0:T(8,128)(2,1)S(1)}, u32[]{:S(2)}, u32[]{:S(2)}) %collective-permute-start.19) | collective-permute-done | bytes 279584 | tf_op jit(solution)/shard_map/ppermute | solution.py:114
  145.9 18.3 %collective-permute-done.20 = bf16[2,273,256]{2,1,0:T(8,128)(2,1)S(1)} collective-permute-done((bf16[2,273,256]{2,1,0:T(8,128)(2,1)S(1)}, bf16[2,273,256]{2,1,0:T(8,128)(2,1)S(1)}, u32[]{:S(2)}, u32[]{:S(2)}) %collective-permute-start.20) | collective-permute-done | bytes 279584 | tf_op jit(solution)/shard_map/ppermute | solution.py:114
  173.0 12.4 %collective-permute-done.23 = bf16[256,1024]{1,0:T(8,128)(2,1)S(1)} collective-permute-done((bf16[256,1024]{1,0:T(8,128)(2,1)S(1)}, bf16[256,1024]{1,0:T(8,128)(2,1)S(1)}, u32[]{:S(2)}, u32[]{:S(2)}) %collective-permute-start.23) | collective-permute-done | bytes 524320 | tf_op jit(solution)/shard_map/ppermute | solution.py:38
  186.5 12.0 %collective-permute-done.26 = bf16[256,1024]{1,0:T(8,128)(2,1)S(1)} collective-permute-done((bf16[256,1024]{1,0:T(8,128)(2,1)S(1)}, bf16[256,1024]{1,0:T(8,128)(2,1)S(1)}, u32[]{:S(2)}, u32[]{:S(2)}) %collective-permute-start.26) | collective-permute-done | bytes 524320 | tf_op jit(solution)/shard_map/ppermute | solution.py:38
  (186 shorter events, 58.8 us)
Async XLA Ops:
  0.9 7.1 %collective-permute-start = (bf16[64,1024]{1,0:T(8,128)(2,1)S(1)}, bf16[64,1024]{1,0:T(8,128)(2,1)S(1)}, u32[]{:S(2)}, u32[]{:S(2)}) collective-permute-start(bf16[64,1024]{1,0:T(8,128)(2,1)S(1)} %slice.34), channel_id=1, source_target_pairs={{0,4},{4,8},{8,12},{1,5},{5,9},{9,13},{2,6},{6,10},{10,14},{3,7},{... | collective-permute-start | bytes 393224 | tf_op jit(solution)/shard_map/ppermute | solution.py:17
  4.3 49.1 %collective-permute-start.7 = (bf16[256,1024]{1,0:T(8,128)(2,1)}, bf16[256,1024]{1,0:T(8,128)(2,1)}, u32[]{:S(2)}, u32[]{:S(2)}) collective-permute-start(bf16[256,1024]{1,0:T(8,128)(2,1)} %get-tuple-element.16), channel_id=1, source_target_pairs={{0,1},{1,0},{2,3},{3,2},{4,5},{5,4},{6,7},{7,6},{8,9},{9,8},{10,11... | collective-permute-start | bytes 1572872 | tf_op jit(solution)/shard_map/ppermute | solution.py:27
  8.1 15.7 %collective-permute-start.1 = (bf16[320,1024]{1,0:T(8,128)(2,1)S(1)}, bf16[320,1024]{1,0:T(8,128)(2,1)S(1)}, u32[]{:S(2)}, u32[]{:S(2)}) collective-permute-start(bf16[320,1024]{1,0:T(8,128)(2,1)S(1)} %pad_maximum_fusion.13), channel_id=1, source_target_pairs={{0,2},{1,3},{2,0},{3,1},{4,6},{5,7},{6,4},{7,5},{8,10},{9,11},{10,... | collective-permute-start | bytes 1966088 | tf_op jit(solution)/shard_map/ppermute | solution.py:38
  15.5 12.9 %collective-permute-start.2 = (bf16[320,1024]{1,0:T(8,128)(2,1)S(1)}, bf16[320,1024]{1,0:T(8,128)(2,1)S(1)}, u32[]{:S(2)}, u32[]{:S(2)}) collective-permute-start(bf16[320,1024]{1,0:T(8,128)(2,1)S(1)} %pad_maximum_fusion.13), channel_id=1, source_target_pairs={{0,1},{1,0},{2,3},{3,2},{4,5},{5,4},{6,7},{7,6},{8,9},{9,8},{10,11... | collective-permute-start | bytes 1966088 | tf_op jit(solution)/shard_map/ppermute | solution.py:27
  27.0 17.7 %collective-permute-start.5 = (bf16[256,1024]{1,0:T(8,128)(2,1)}, bf16[256,1024]{1,0:T(8,128)(2,1)}, u32[]{:S(2)}, u32[]{:S(2)}) collective-permute-start(bf16[256,1024]{1,0:T(8,128)(2,1)} %get-tuple-element.16), channel_id=1, source_target_pairs={{0,2},{1,3},{2,0},{3,1},{4,6},{5,7},{6,4},{7,5},{8,10},{9,11},{10,... | collective-permute-start | bytes 1572872 | tf_op jit(solution)/shard_map/ppermute | solution.py:38
  44.7 8.7 %collective-permute-start.8 = (bf16[256,1024]{1,0:T(8,128)(2,1)}, bf16[256,1024]{1,0:T(8,128)(2,1)}, u32[]{:S(2)}, u32[]{:S(2)}) collective-permute-start(bf16[256,1024]{1,0:T(8,128)(2,1)} %collective-permute-done.5), channel_id=1, source_target_pairs={{0,1},{1,0},{2,3},{3,2},{4,5},{5,4},{6,7},{7,6},{8,9},{9,8},{10,11... | collective-permute-start | bytes 1572872 | tf_op jit(solution)/shard_map/ppermute | solution.py:27
  50.2 18.6 %collective-permute-start.4 = (f32[256,1024]{1,0:T(8,128)}, f32[256,1024]{1,0:T(8,128)}, u32[]{:S(2)}, u32[]{:S(2)}) collective-permute-start(f32[256,1024]{1,0:T(8,128)} %fusion.65), channel_id=1, source_target_pairs={{0,1},{1,0},{2,3},{3,2},{4,5},{5,4},{6,7},{7,6},{8,9},{9,8},{10,11... | collective-permute-start | bytes 3145736 | tf_op jit(solution)/shard_map/ppermute | solution.py:27
  53.3 32.8 %collective-permute-start.9 = (f32[256,1024]{1,0:T(8,128)}, f32[256,1024]{1,0:T(8,128)}, u32[]{:S(2)}, u32[]{:S(2)}) collective-permute-start(f32[256,1024]{1,0:T(8,128)} %fusion.55), channel_id=1, source_target_pairs={{0,1},{1,0},{2,3},{3,2},{4,5},{5,4},{6,7},{7,6},{8,9},{9,8},{10,11... | collective-permute-start | bytes 3145736 | tf_op jit(solution)/shard_map/ppermute | solution.py:27
  71.7 14.4 %collective-permute-start.6 = (bf16[256,1024]{1,0:T(8,128)(2,1)}, bf16[256,1024]{1,0:T(8,128)(2,1)S(1)}, u32[]{:S(2)}, u32[]{:S(2)}) collective-permute-start(bf16[256,1024]{1,0:T(8,128)(2,1)} %fusion.24), channel_id=1, source_target_pairs={{0,2},{1,3},{2,0},{3,1},{4,6},{5,7},{6,4},{7,5},{8,10},{9,11},{10,... | collective-permute-start | bytes 1572872 | tf_op jit(solution)/shard_map/ppermute | solution.py:38
  76.6 14.1 %collective-permute-start.13 = (f32[256,1024]{1,0:T(8,128)}, f32[256,1024]{1,0:T(8,128)S(1)}, u32[]{:S(2)}, u32[]{:S(2)}) collective-permute-start(f32[256,1024]{1,0:T(8,128)} %fusion.63), channel_id=1, source_target_pairs={{0,1},{1,0},{2,3},{3,2},{4,5},{5,4},{6,7},{7,6},{8,9},{9,8},{10,11... | collective-permute-start | bytes 3145736 | tf_op jit(solution)/shard_map/ppermute | solution.py:27
  88.2 13.4 %collective-permute-start.10 = (bf16[256,1024]{1,0:T(8,128)(2,1)S(1)}, bf16[256,1024]{1,0:T(8,128)(2,1)S(1)}, u32[]{:S(2)}, u32[]{:S(2)}) collective-permute-start(bf16[256,1024]{1,0:T(8,128)(2,1)S(1)} %add_convert_fusion.3), channel_id=1, source_target_pairs={{0,2},{1,3},{2,0},{3,1},{4,6},{5,7},{6,4},{7,5},{8,10},{9,11},{10,... | collective-permute-start | bytes 1572872 | tf_op jit(solution)/shard_map/ppermute | solution.py:38
  90.5 23.5 %collective-permute-start.15 = (f32[256,1024]{1,0:T(8,128)S(1)}, f32[256,1024]{1,0:T(8,128)S(1)}, u32[]{:S(2)}, u32[]{:S(2)}) collective-permute-start(f32[256,1024]{1,0:T(8,128)S(1)} %fusion.53), channel_id=1, source_target_pairs={{0,1},{1,0},{2,3},{3,2},{4,5},{5,4},{6,7},{7,6},{8,9},{9,8},{10,11... | collective-permute-start | bytes 3145736 | tf_op jit(solution)/shard_map/ppermute | solution.py:27
  101.6 12.4 %collective-permute-start.14 = (bf16[256,1024]{1,0:T(8,128)(2,1)S(1)}, bf16[256,1024]{1,0:T(8,128)(2,1)S(1)}, u32[]{:S(2)}, u32[]{:S(2)}) collective-permute-start(bf16[256,1024]{1,0:T(8,128)(2,1)S(1)} %fusion.25), channel_id=1, source_target_pairs={{0,2},{1,3},{2,0},{3,1},{4,6},{5,7},{6,4},{7,5},{8,10},{9,11},{10,... | collective-permute-start | bytes 1572872 | tf_op jit(solution)/shard_map/ppermute | solution.py:38
  102.4 13.1 %collective-permute-start.11 = (bf16[256,1024]{1,0:T(8,128)(2,1)S(1)}, bf16[256,1024]{1,0:T(8,128)(2,1)S(1)}, u32[]{:S(2)}, u32[]{:S(2)}) collective-permute-start(bf16[256,1024]{1,0:T(8,128)(2,1)S(1)} %add_convert_fusion.3), channel_id=1, source_target_pairs={{0,1},{1,0},{2,3},{3,2},{4,5},{5,4},{6,7},{7,6},{8,9},{9,8},{10,11... | collective-permute-start | bytes 1572872 | tf_op jit(solution)/shard_map/ppermute | solution.py:27
  102.5 13.0 %collective-permute-start.12 = (bf16[256,1024]{1,0:T(8,128)(2,1)S(1)}, bf16[256,1024]{1,0:T(8,128)(2,1)S(1)}, u32[]{:S(2)}, u32[]{:S(2)}) collective-permute-start(bf16[256,1024]{1,0:T(8,128)(2,1)S(1)} %collective-permute-done.10), channel_id=1, source_target_pairs={{0,1},{1,0},{2,3},{3,2},{4,5},{5,4},{6,7},{7,6},{8,9},{9,8},{10,11... | collective-permute-start | bytes 1572872 | tf_op jit(solution)/shard_map/ppermute | solution.py:27
  114.8 14.5 %collective-permute-start.17 = (bf16[256,1024]{1,0:T(8,128)(2,1)S(1)}, bf16[256,1024]{1,0:T(8,128)(2,1)S(1)}, u32[]{:S(2)}, u32[]{:S(2)}) collective-permute-start(bf16[256,1024]{1,0:T(8,128)(2,1)S(1)} %add_convert_fusion.2), channel_id=1, source_target_pairs={{0,1},{1,0},{2,3},{3,2},{4,5},{5,4},{6,7},{7,6},{8,9},{9,8},{10,11... | collective-permute-start | bytes 1572872 | tf_op jit(solution)/shard_map/ppermute | solution.py:27
  114.9 14.3 %collective-permute-start.16 = (bf16[256,1024]{1,0:T(8,128)(2,1)S(1)}, bf16[256,1024]{1,0:T(8,128)(2,1)S(1)}, u32[]{:S(2)}, u32[]{:S(2)}) collective-permute-start(bf16[256,1024]{1,0:T(8,128)(2,1)S(1)} %add_convert_fusion.2), channel_id=1, source_target_pairs={{0,2},{1,3},{2,0},{3,1},{4,6},{5,7},{6,4},{7,5},{8,10},{9,11},{10,... | collective-permute-start | bytes 1572872 | tf_op jit(solution)/shard_map/ppermute | solution.py:38
  134.8 11.1 %collective-permute-start.19 = (bf16[2,273,256]{2,1,0:T(8,128)(2,1)S(1)}, bf16[2,273,256]{2,1,0:T(8,128)(2,1)S(1)}, u32[]{:S(2)}, u32[]{:S(2)}) collective-permute-start(bf16[2,273,256]{2,1,0:T(8,128)(2,1)S(1)} %convolution_convert_fusion), channel_id=1, source_target_pairs={{0,4},{4,8},{8,12},{1,5},{5,9},{9,13},{2,6},{6,10},{10,14},{3,7},{... | collective-permute-start | bytes 838664 | tf_op jit(solution)/shard_map/ppermute | solution.py:114
  136.2 28.0 %collective-permute-start.20 = (bf16[2,273,256]{2,1,0:T(8,128)(2,1)S(1)}, bf16[2,273,256]{2,1,0:T(8,128)(2,1)S(1)}, u32[]{:S(2)}, u32[]{:S(2)}) collective-permute-start(bf16[2,273,256]{2,1,0:T(8,128)(2,1)S(1)} %convolution_convert_fusion), channel_id=1, source_target_pairs={{0,8},{4,12},{1,9},{5,13},{2,10},{6,14},{3,11},{7,15},{16,24},{20,... | collective-permute-start | bytes 838664 | tf_op jit(solution)/shard_map/ppermute | solution.py:114
  137.5 26.7 %collective-permute-start.21 = (bf16[2,273,256]{2,1,0:T(8,128)(2,1)S(1)}, bf16[2,273,256]{2,1,0:T(8,128)(2,1)S(1)}, u32[]{:S(2)}, u32[]{:S(2)}) collective-permute-start(bf16[2,273,256]{2,1,0:T(8,128)(2,1)S(1)} %convolution_convert_fusion), channel_id=1, source_target_pairs={{0,12},{1,13},{2,14},{3,15},{16,28},{17,29},{18,30},{19,31}} | collective-permute-start | bytes 838664 | tf_op jit(solution)/shard_map/ppermute | solution.py:114
  169.8 16.2 %collective-permute-start.24 = (f32[256,1024]{1,0:T(8,128)S(1)}, f32[256,1024]{1,0:T(8,128)S(1)}, u32[]{:S(2)}, u32[]{:S(2)}) collective-permute-start(f32[256,1024]{1,0:T(8,128)S(1)} %fusion.39), channel_id=1, source_target_pairs={{0,1},{1,0},{2,3},{3,2},{4,5},{5,4},{6,7},{7,6},{8,9},{9,8},{10,11... | collective-permute-start | bytes 3145736 | tf_op jit(solution)/shard_map/ppermute | solution.py:27
  171.4 14.0 %collective-permute-start.23 = (bf16[256,1024]{1,0:T(8,128)(2,1)S(1)}, bf16[256,1024]{1,0:T(8,128)(2,1)S(1)}, u32[]{:S(2)}, u32[]{:S(2)}) collective-permute-start(bf16[256,1024]{1,0:T(8,128)(2,1)S(1)} %fusion.26), channel_id=1, source_target_pairs={{0,2},{1,3},{2,0},{3,1},{4,6},{5,7},{6,4},{7,5},{8,10},{9,11},{10,... | collective-permute-start | bytes 1572872 | tf_op jit(solution)/shard_map/ppermute | solution.py:38
  172.5 14.0 %collective-permute-start.27 = (f32[256,1024]{1,0:T(8,128)S(1)}, f32[256,1024]{1,0:T(8,128)S(1)}, u32[]{:S(2)}, u32[]{:S(2)}) collective-permute-start(f32[256,1024]{1,0:T(8,128)S(1)} %fusion.37), channel_id=1, source_target_pairs={{0,1},{1,0},{2,3},{3,2},{4,5},{5,4},{6,7},{7,6},{8,9},{9,8},{10,11... | collective-permute-start | bytes 3145736 | tf_op jit(solution)/shard_map/ppermute | solution.py:27
  185.4 13.1 %collective-permute-start.26 = (bf16[256,1024]{1,0:T(8,128)(2,1)S(1)}, bf16[256,1024]{1,0:T(8,128)(2,1)S(1)}, u32[]{:S(2)}, u32[]{:S(2)}) collective-permute-start(bf16[256,1024]{1,0:T(8,128)(2,1)S(1)} %fusion.27), channel_id=1, source_target_pairs={{0,2},{1,3},{2,0},{3,1},{4,6},{5,7},{6,4},{7,5},{8,10},{9,11},{10,... | collective-permute-start | bytes 1572872 | tf_op jit(solution)/shard_map/ppermute | solution.py:38
  (36 other events, 363.5 us)

commit v8 on v7

--- a/solution.py
+++ b/solution.py
@@ -215,56 +215,43 @@
         if i + 1 < CHUNKS:
             wholes.append(gather_finish(started[i + 1], attended_parts[i]))
 
-    after_parts = [None] * CHUNKS
-    qf_parts, kf_parts, lv_parts = [], [], []
-    dep = attended_parts[1] if CHUNKS > 1 else None
+    after_parts = []
     for i in range(CHUNKS):
+        dep = attended_parts[i + 1] if i + 1 < CHUNKS else None
         partial = head_reduce_scatter(attended_parts[i], wo_attn, dep)
-        after_parts[i] = (hidden_parts[i].astype(jnp.float32) + partial).astype(jnp.bfloat16)
-        normed2 = norm_rows(head_all_gather(after_parts[i]), lin_gain)
-        feats = jnp.dot(normed2, w_feature, preferred_element_type=jnp.float32)
-        lin_heads = feats.shape[1] // (2 * FEAT)
-        feats = feats.reshape(size, lin_heads, 2, FEAT)
-        qf_parts.append(feats[:, :, 0, :])
-        kf_parts.append(feats[:, :, 1, :])
-        lv_parts.append(
-            jnp.dot(normed2, wv_linear, preferred_element_type=jnp.float32)
-            .astype(jnp.bfloat16)
-            .reshape(size, lin_heads, VDIM)
-        )
-        dep = lv_parts[-1]
-    key_feat = jnp.concatenate(kf_parts, axis=0)
-    lvalues = jnp.concatenate(lv_parts, axis=0)
-    lin_heads = key_feat.shape[1]
+        after_parts.append((hidden_parts[i].astype(jnp.float32) + partial).astype(jnp.bfloat16))
+    after_window = jnp.concatenate(after_parts, axis=0)
+
+    normed2 = norm_rows(head_all_gather(after_window), lin_gain)
+    feats = jnp.dot(normed2, w_feature, preferred_element_type=jnp.float32)
+    lin_heads = feats.shape[1] // (2 * FEAT)
+    feats = feats.reshape(tok_rows, lin_heads, 2, FEAT)
+    query_feat = feats[:, :, 0, :]
+    key_feat = feats[:, :, 1, :]
+    lvalues = (
+        jnp.dot(normed2, wv_linear, preferred_element_type=jnp.float32)
+        .astype(jnp.bfloat16)
+        .reshape(tok_rows, lin_heads, VDIM)
+    )
     highest = lax.Precision.HIGHEST
     phi_key = taylor(key_feat)
     local_state = jnp.einsum(
         "thf,thv->hfv", phi_key, lvalues.astype(jnp.float32), precision=highest
     )
-    carried = entry_state + earlier_sum(local_state)
-
-    normed_parts = []
-    for i in range(CHUNKS):
-        query_feat = qf_parts[i]
-        phi_query = taylor(query_feat)
-        cross = jnp.einsum("thf,hfv->thv", phi_query, carried, precision=highest)
-        sims = jnp.einsum(
-            "thf,shf->hts", query_feat, key_feat, precision=highest
-        ) / math.sqrt(FEAT)
-        causal = (i * size + jnp.arange(size))[:, None] >= jnp.arange(tok_rows)[None, :]
-        weights = jnp.where(causal[None], 1.0 + sims + 0.5 * sims * sims, 0.0).astype(jnp.bfloat16)
-        intra = jnp.einsum("hts,shv->thv", weights, lvalues, preferred_element_type=jnp.float32)
-        lin_out = cross + intra
-        scale = lax.rsqrt(jnp.mean(lin_out * lin_out, axis=-1, keepdims=True) + 1e-05)
-        normed_parts.append(
-            (lin_out * scale * out_gain[None]).astype(jnp.bfloat16).reshape(size, lin_heads * VDIM)
-        )
-    outs = []
-    for i in range(CHUNKS):
-        dep = normed_parts[i + 1] if i + 1 < CHUNKS else None
-        lin_part = head_reduce_scatter(normed_parts[i], wo_linear, dep)
-        outs.append((after_parts[i].astype(jnp.float32) + lin_part).astype(jnp.bfloat16))
-    return jnp.concatenate(outs, axis=0)
+    prior = earlier_sum(local_state)
+    phi_query = taylor(query_feat)
+    sims = jnp.einsum("thf,shf->hts", query_feat, key_feat, precision=highest) / math.sqrt(FEAT)
+    causal = jnp.arange(tok_rows)[:, None] >= jnp.arange(tok_rows)[None, :]
+    weights = jnp.where(causal[None], 1.0 + sims + 0.5 * sims * sims, 0.0).astype(jnp.bfloat16)
+    intra = jnp.einsum("hts,shv->thv", weights, lvalues, preferred_element_type=jnp.float32)
+    own = jnp.einsum("thf,hfv->thv", phi_query, entry_state, precision=highest) + intra
+    lin_out = own + jnp.einsum("thf,hfv->thv", phi_query, prior, precision=highest)
+    scale = lax.rsqrt(jnp.mean(lin_out * lin_out, axis=-1, keepdims=True) + 1e-05)
+    lin_normed = (
+        (lin_out * scale * out_gain[None]).astype(jnp.bfloat16).reshape(tok_rows, lin_heads * VDIM)
+    )
+    lin_part = head_reduce_scatter(lin_normed, wo_linear)
+    return (after_window.astype(jnp.float32) + lin_part).astype(jnp.bfloat16)
 
 
 def solution(mesh):

time: 201 us -> 214 us (1.065)
  waiting for transfers between devices: 103 us -> 109 us
  matrix products: 53.8 us -> 58.7 us
  other arithmetic: 13.4 us -> 16.2 us
    ppermute x8 -> x6, waiting for transfers between devices: 74.3 us -> 80 us  [chip_shift(): moved = lax.ppermute(value, 'head', pairs)]
    reduce_sum x4 -> x3, other arithmetic: 6.4 us -> 9.33 us  [norm_rows(): scale = lax.rsqrt(jnp.mean(wide * wide, axis=-1, keepdims=True) + 1e-05)]
    ppermute x16 -> x12, waiting for transfers between devices: 2.91 us -> 5.76 us  [core_swap(): return lax.ppermute(value, 'head', [(h, h ^ 1) for h in range(devices)])]
    ppermute x3, waiting for transfers between devices: 22 us -> 19.9 us  [earlier_sum(): total = total + lax.ppermute(sent, 'ctx', pairs).astype(jnp.float32)]
    ppermute x8 -> x6, starting transfers between devices: 6.56 us -> 5.35 us  [chip_shift(): moved = lax.ppermute(value, 'head', pairs)]
    dot_general x16 -> x12, matrix products: 19.7 us -> 20.2 us  [block(): return jnp.dot(lhs, cols, preferred_element_type=jnp.float32)]
  transfers between devices with their start and end apart: 28 -> 22, of which waited for: 12 -> 11; matrix products, arithmetic and copies ran while one was open for 36% -> 34% of each run, Pallas kernels for 0% -> 0%
where the time goes in v8:
time: 214 us; the launch traced here: 213 us
  waiting for transfers between devices  109 us (51%)
  matrix products  58.7 us (27%)
  other arithmetic  16.2 us (8%)
  local copies, waits for them, and re-layouts  15.8 us (7%)
  starting transfers between devices  12.7 us (6%)
    ppermute x6, waiting for transfers between devices, chip_shift(): moved = lax.ppermute(value, 'head', pairs)  80 us
    dot_general x12, matrix products, block(): return jnp.dot(lhs, cols, preferred_element_type=jnp.float32)  20.2 us
    ppermute x3, waiting for transfers between devices, earlier_sum(): total = total + lax.ppermute(sent, 'ctx', pairs).astype(jnp.float32)  19.9 us
    reduce_sum x3, other arithmetic, norm_rows(): scale = lax.rsqrt(jnp.mean(wide * wide, axis=-1, keepdims=True) + 1e-05)  9.33 us
    dot_general x2, matrix products, project(): jnp.dot(query_rows, w_query, preferred_element_type=jnp.float32)  8.72 us
    dynamic_slice x5, local copies, waits for them, and re-layouts, gathered_rows(): lax.dynamic_slice_in_dim(weight, src * block, block, axis=0)  6.91 us
    dot_general x2, matrix products, project(): jnp.dot(normed, w_keys, preferred_element_type=jnp.float32)  6.58 us
    ppermute x12, waiting for transfers between devices, core_swap(): return lax.ppermute(value, 'head', [(h, h ^ 1) for h in range(devices)])  5.76 us
  transfers between devices with their start and end apart: 22, of which 11 were waited for; matrix products, arithmetic and copies ran while one was open for 34% of the time, Pallas kernels for 0%

profile of v8, /device:TPU:24, one launch (start us, length us, event | category | flops | bytes accessed | tf_op | source)
XLA Modules:
  0.0 213.4 jit_solution(5456368829360231128)
XLA Ops:
  4.4 3.7 %collective-permute-done = bf16[64,1024]{1,0:T(8,128)(2,1)S(1)} collective-permute-done((bf16[64,1024]{1,0:T(8,128)(2,1)S(1)}, bf16[64,1024]{1,0:T(8,128)(2,1)S(1)}, u32[]{:S(2)}, u32[]{:S(2)}) %collective-permute-start) | collective-permute-done | bytes 131104 | tf_op jit(solution)/shard_map/ppermute | solution.py:17
  11.3 12.6 %collective-permute-done.1 = bf16[320,1024]{1,0:T(8,128)(2,1)S(1)} collective-permute-done((bf16[320,1024]{1,0:T(8,128)(2,1)S(1)}, bf16[320,1024]{1,0:T(8,128)(2,1)S(1)}, u32[]{:S(2)}, u32[]{:S(2)}) %collective-permute-start.1) | collective-permute-done | bytes 655392 | tf_op jit(solution)/shard_map/ppermute | solution.py:38
  23.8 4.3 %constant_dynamic-slice_fusion.11 = (bf16[1024,512]{1,0:T(8,128)(2,1)}, bf16[1024,512]{1,0:T(8,128)(2,1)}, bf16[1024,512]{1,0:T(8,128)(2,1)}, bf16[1024,512]{1,0:T(8,128)(2,1)}) fusion(bf16[4096,512]{1,0:T(8,128)(2,1)} %param.14, s32[]{:T(128)S(6)} %select_n.145, s32[]{:T(128)S(6)} %select_n.149, s32[]{:T(128)S(6)} %select_n.151, s32[]{:T(128)S(6)} %select_n.150), kind=kLoop, calls=%fused_computation.156 | loop fusion | bytes 8388624 | tf_op jit(solution)/shard_map/dynamic_slice | solution.py:103
  32.0 3.4 %fusion.5 = f32[320]{0:T(512)S(1)} fusion(bf16[320,1024]{1,0:T(8,128)(2,1)S(1)} %collective-permute-done.3, bf16[320,1024]{1,0:T(8,128)(2,1)S(1)} %collective-permute-done.2, bf16[320,1024]{1,0:T(8,128)(2,1)S(1)} %collective-permute-done.1, bf16[256,1024]{1,0:T(8,128)(2,1)S(1)} %get-tuple-element.35, bf16[64,1024]{1,0:T(8,128)(2,1)S(1)} %collective-permute-done), kind=kLoop, calls=%fused_computation.11 | loop fusion | flops 15728320 | bytes 2622720 | tf_op jit(solution)/shard_map/reduce_sum | solution.py:120
  40.3 3.3 %convolution_convert_fusion.4 = bf16[320,256]{1,0:T(8,128)(2,1)S(1)} fusion(bf16[320,4096]{1,0:T(8,128)(2,1)} %copy-done.5, bf16[1024,256]{1,0:T(8,128)(2,1)} %get-tuple-element.29, bf16[1024,256]{1,0:T(8,128)(2,1)} %get-tuple-element.30, bf16[1024,256]{1,0:T(8,128)(2,1)} %get-tuple-element.28, bf16[1024,256]{1,0:T(8,128)(2,1)} %get-tuple-element.27), kind=kOutput, calls=%fused_computation.66 | convolution fusion | flops 679559168 | bytes 4882432 | tf_op jit(solution)/shard_map/dot_general | solution.py:175
  44.3 4.2 %fusion.39 = bf16[256,512]{1,0:T(8,128)(2,1)} fusion(bf16[320,4096]{1,0:T(8,128)(2,1)S(1)} %copy-done.6, bf16[1024,512]{1,0:T(8,128)(2,1)} %get-tuple-element.21, bf16[1024,512]{1,0:T(8,128)(2,1)} %get-tuple-element.22, bf16[1024,512]{1,0:T(8,128)(2,1)} %get-tuple-element.20, bf16[1024,512]{1,0:T(8,128)(2,1)} %get-tuple-element.19), kind=kOutput, calls=%fused_computation.62 | convolution fusion | flops 1090650112 | bytes 6553600 | tf_op jit(solution)/shard_map/dot_general | solution.py:174
  49.5 2.6 %fusion.137 = (f32[2,2,256]{2,1,0:T(2,128)S(1)}, f32[2,2,256,320]{2,3,1,0:T(8,128)}) fusion(pred[256,320]{0,1:T(8,128)(4,1)} %and_and_fusion.1, bf16[256,2,2,128]{3,2,1,0:T(2,128)(2,1)S(1)} %reshape.132, bf16[320,2,128,1]{2,1,0,3:T(2,128)(2,1)} %bitcast.110), kind=kOutput, calls=%fused_computation.198 | convolution fusion | flops 85197120 | bytes 1822720 | tf_op jit(solution)/shard_map/sub | solution.py:195
  55.0 2.7 %fusion.65 = f32[256,1024]{1,0:T(8,128)} fusion(bf16[256,512]{0,1:T(8,128)(2,1)S(1)} %bitcast.93, bf16[512,4096]{1,0:T(8,128)(2,1)} %param.17, s32[]{:T(128)S(6)} %select_n.153), kind=kOutput, calls=%fused_computation.98 | convolution fusion | flops 268435456 | bytes 2359300 | tf_op jit(solution)/shard_map/dot_general | solution.py:59
  60.8 4.5 %convolution_convert_fusion.2 = bf16[256,512]{1,0:T(8,128)(2,1)} fusion(bf16[1024,512]{1,0:T(8,128)(2,1)} %get-tuple-element.21, bf16[1024,512]{1,0:T(8,128)(2,1)} %get-tuple-element.22, bf16[1024,512]{1,0:T(8,128)(2,1)} %get-tuple-element.20, bf16[1024,512]{1,0:T(8,128)(2,1)S(1)} %copy-done.9, f32[4096]{0:T(1024)S(1)} %pad_maximum_fusion.18, ...), kind=kOutput, calls=%fused_computation.64 | convolution fusion | flops 1102184448 | bytes 6571008 | tf_op jit(solution)/shard_map/dot_general | solution.py:174
  66.4 3.3 %convolution_convert_fusion.7 = bf16[256,256]{0,1:T(8,128)(2,1)S(1)} fusion(bf16[1024,256]{1,0:T(8,128)(2,1)} %get-tuple-element.29, bf16[1024,256]{1,0:T(8,128)(2,1)} %get-tuple-element.30, bf16[1024,256]{1,0:T(8,128)(2,1)} %get-tuple-element.28, bf16[1024,256]{1,0:T(8,128)(2,1)S(1)} %copy-done.18, f32[4096]{0:T(1024)S(1)} %pad_maximum_fusion.18, ...), kind=kOutput, calls=%fused_computation.69 | convolution fusion | flops 556859392 | bytes 4342784 | tf_op jit(solution)/shard_map/dot_general | solution.py:175
  69.8 2.7 %convolution_convert_fusion.6 = bf16[256,256]{0,1:T(8,128)(2,1)S(1)} fusion(bf16[1024,256]{1,0:T(8,128)(2,1)S(1)} %copy-done.13, bf16[1024,256]{1,0:T(8,128)(2,1)S(1)} %copy-done.11, bf16[1024,256]{1,0:T(8,128)(2,1)S(1)} %copy-done.15, bf16[1024,256]{1,0:T(8,128)(2,1)S(1)} %copy-done.17, f32[4096]{0:T(1024)S(1)} %pad_maximum_fusion.18, ...), kind=kOutput, calls=%fused_computation.68 | convolution fusion | flops 556859392 | bytes 4342784 | tf_op jit(solution)/shard_map/dot_general | solution.py:176
  76.1 2.7 %fusion.63 = f32[256,1024]{1,0:T(8,128)} fusion(bf16[256,512]{0,1:T(8,128)(2,1)S(1)} %bitcast.97, bf16[512,4096]{1,0:T(8,128)(2,1)} %param.17, s32[]{:T(128)S(6)} %select_n.153), kind=kOutput, calls=%fused_computation.96 | convolution fusion | flops 268435456 | bytes 2359300 | tf_op jit(solution)/shard_map/dot_general | solution.py:59
  79.0 2.8 %fusion.55 = f32[256,1024]{1,0:T(8,128)} fusion(bf16[256,512]{0,1:T(8,128)(2,1)S(1)} %bitcast.94, bf16[512,4096]{1,0:T(8,128)(2,1)} %param.17, s32[]{:T(128)S(6)} %select_n.157), kind=kOutput, calls=%fused_computation.92 | convolution fusion | flops 268435456 | bytes 2359300 | tf_op jit(solution)/shard_map/dot_general | solution.py:59
  84.9 2.5 %fusion.35 = bf16[256,1024]{1,0:T(8,128)(2,1)} fusion(f32[256,1024]{1,0:T(8,128)} %collective-permute-done.10, bf16[256,512]{0,1:T(8,128)(2,1)S(1)} %bitcast.99, bf16[512,4096]{1,0:T(8,128)(2,1)S(1)} %copy-done.1, s32[]{:T(128)S(6)} %select_n.149), kind=kOutput, calls=%fused_computation.59 | convolution fusion | flops 268959744 | bytes 2883588 | tf_op jit(solution)/shard_map/dot_general | solution.py:59
  87.4 10.6 %collective-permute-done.6 = bf16[256,1024]{1,0:T(8,128)(2,1)} collective-permute-done((bf16[256,1024]{1,0:T(8,128)(2,1)S(1)}, bf16[256,1024]{1,0:T(8,128)(2,1)}, u32[]{:S(2)}, u32[]{:S(2)}) %collective-permute-start.6) | collective-permute-done | bytes 524320 | tf_op jit(solution)/shard_map/ppermute | solution.py:38
  98.6 2.3 %add_convert_fusion.3 = bf16[256,1024]{1,0:T(8,128)(2,1)S(1)} fusion(bf16[256,1024]{1,0:T(8,128)(2,1)} %collective-permute-done.6, f32[256,1024]{1,0:T(8,128)} %collective-permute-done.9, bf16[256,512]{0,1:T(8,128)(2,1)S(1)} %bitcast.96, bf16[512,4096]{1,0:T(8,128)(2,1)} %param.17, s32[]{:T(128)S(6)} %select_n.156, bf16[512,1024]{1,0:T(8,128)(2,1)S(1)} %copy-done.2), kind=kOutput, calls=%fused_computation.89 | convolution fusion | flops 270008320 | bytes 3932164 | tf_op jit(solution)/shard_map/dot_general | solution.py:59
  100.9 10.8 %collective-permute-done.11 = bf16[256,1024]{1,0:T(8,128)(2,1)} collective-permute-done((bf16[256,1024]{1,0:T(8,128)(2,1)}, bf16[256,1024]{1,0:T(8,128)(2,1)}, u32[]{:S(2)}, u32[]{:S(2)}) %collective-permute-start.11) | collective-permute-done | bytes 524320 | tf_op jit(solution)/shard_map/ppermute | solution.py:38
  114.6 23.1 %collective-permute-done.13 = bf16[512,1024]{1,0:T(8,128)(2,1)S(1)} collective-permute-done((bf16[512,1024]{1,0:T(8,128)(2,1)S(1)}, bf16[512,1024]{1,0:T(8,128)(2,1)S(1)}, u32[]{:S(2)}, u32[]{:S(2)}) %collective-permute-start.13) | collective-permute-done | bytes 1048608 | tf_op jit(solution)/shard_map/ppermute | solution.py:38
  140.3 3.9 %fusion.2 = f32[512]{0:T(512)S(1)} fusion(bf16[512,1024]{1,0:T(8,128)(2,1)S(1)} %collective-permute-done.15, bf16[512,1024]{1,0:T(8,128)(2,1)S(1)} %collective-permute-done.14, bf16[512,1024]{1,0:T(8,128)(2,1)S(1)} %collective-permute-done.13, bf16[256,1024]{1,0:T(8,128)(2,1)S(1)} %add_convert_fusion.2, bf16[256,1024]{1,0:T(8,128)(2,1)S(1)} %add_convert_fusion.3), kind=kLoop, calls=%fused_computation.4 | loop fusion | flops 25165312 | bytes 4196352 | tf_op jit(solution)/shard_map/reduce_sum | solution.py:120
  145.9 2.6 %fusion.31 = bf16[512,512]{0,1:T(8,128)(2,1)S(1)} fusion(bf16[1024,512]{1,0:T(8,128)(2,1)S(1)} %get-tuple-element.25, bf16[1024,512]{1,0:T(8,128)(2,1)S(1)} %get-tuple-element.26, bf16[1024,512]{1,0:T(8,128)(2,1)S(1)} %get-tuple-element.24, bf16[1024,512]{1,0:T(8,128)(2,1)S(1)} %get-tuple-element.23, f32[4096]{0:T(1024)S(1)} %pad_maximum_fusion.19, ...), kind=kOutput, calls=%fused_computation.57 | convolution fusion | flops 2191785984 | bytes 8931328 | tf_op jit(solution)/shard_map/dot_general | solution.py:232
  153.5 2.3 %select_convert_fusion = bf16[2,512,512]{2,1,0:T(8,128)(2,1)S(1)} fusion(pred[512,512]{1,0:T(8,128)(4,1)S(1)} %iota_compare_fusion, f32[512,2,2,16]{0,3,2,1:T(8,128)S(1)} %bitcast.106), kind=kOutput, calls=%fused_computation.35 | convolution fusion | flops 104333312 | bytes 1441792 | tf_op jit(solution)/shard_map/thf,shf->hts/dot_general | solution.py:243
  160.3 18.0 %collective-permute-done.17 = bf16[2,273,256]{2,1,0:T(8,128)(2,1)S(1)} collective-permute-done((bf16[2,273,256]{2,1,0:T(8,128)(2,1)S(1)}, bf16[2,273,256]{2,1,0:T(8,128)(2,1)S(1)}, u32[]{:S(2)}, u32[]{:S(2)}) %collective-permute-start.17) | collective-permute-done | bytes 279584 | tf_op jit(solution)/shard_map/ppermute | solution.py:114
  182.8 2.9 %collective-permute-done.19 = f32[512,1024]{1,0:T(8,128)S(1)} collective-permute-done((f32[512,1024]{1,0:T(8,128)S(1)}, f32[512,1024]{1,0:T(8,128)S(1)}, u32[]{:S(2)}, u32[]{:S(2)}) %collective-permute-start.19) | collective-permute-done | bytes 2097184 | tf_op jit(solution)/shard_map/ppermute | solution.py:27
  188.6 23.0 %collective-permute-done.20 = bf16[512,1024]{1,0:T(8,128)(2,1)S(1)} collective-permute-done((bf16[512,1024]{1,0:T(8,128)(2,1)S(1)}, bf16[512,1024]{1,0:T(8,128)(2,1)S(1)}, u32[]{:S(2)}, u32[]{:S(2)}) %collective-permute-start.20) | collective-permute-done | bytes 1048608 | tf_op jit(solution)/shard_map/ppermute | solution.py:38
  (140 shorter events, 58.0 us)
Async XLA Ops:
  0.0 156.4 %copy-start = (f32[2,273,256]{2,0,1:T(2,128)S(1)}, f32[2,273,256]{2,0,1:T(2,128)}, u32[]{:S(2)}) copy-start(f32[2,273,256]{2,0,1:T(2,128)} %param.23) | copy-start | bytes 1677316
  1.0 7.1 %collective-permute-start = (bf16[64,1024]{1,0:T(8,128)(2,1)S(1)}, bf16[64,1024]{1,0:T(8,128)(2,1)S(1)}, u32[]{:S(2)}, u32[]{:S(2)}) collective-permute-start(bf16[64,1024]{1,0:T(8,128)(2,1)S(1)} %slice.28), channel_id=1, source_target_pairs={{0,4},{4,8},{8,12},{1,5},{5,9},{9,13},{2,6},{6,10},{10,14},{3,7},{... | collective-permute-start | bytes 393224 | tf_op jit(solution)/shard_map/ppermute | solution.py:17
  4.4 54.4 %collective-permute-start.7 = (bf16[256,1024]{1,0:T(8,128)(2,1)}, bf16[256,1024]{1,0:T(8,128)(2,1)}, u32[]{:S(2)}, u32[]{:S(2)}) collective-permute-start(bf16[256,1024]{1,0:T(8,128)(2,1)} %get-tuple-element.12), channel_id=1, source_target_pairs={{0,1},{1,0},{2,3},{3,2},{4,5},{5,4},{6,7},{7,6},{8,9},{9,8},{10,11... | collective-permute-start | bytes 1572872 | tf_op jit(solution)/shard_map/ppermute | solution.py:27
  8.2 15.7 %collective-permute-start.1 = (bf16[320,1024]{1,0:T(8,128)(2,1)S(1)}, bf16[320,1024]{1,0:T(8,128)(2,1)S(1)}, u32[]{:S(2)}, u32[]{:S(2)}) collective-permute-start(bf16[320,1024]{1,0:T(8,128)(2,1)S(1)} %pad_maximum_fusion.12), channel_id=1, source_target_pairs={{0,2},{1,3},{2,0},{3,1},{4,6},{5,7},{6,4},{7,5},{8,10},{9,11},{10,... | collective-permute-start | bytes 1966088 | tf_op jit(solution)/shard_map/ppermute | solution.py:38
  11.2 20.8 %collective-permute-start.2 = (bf16[320,1024]{1,0:T(8,128)(2,1)S(1)}, bf16[320,1024]{1,0:T(8,128)(2,1)S(1)}, u32[]{:S(2)}, u32[]{:S(2)}) collective-permute-start(bf16[320,1024]{1,0:T(8,128)(2,1)S(1)} %pad_maximum_fusion.12), channel_id=1, source_target_pairs={{0,1},{1,0},{2,3},{3,2},{4,5},{5,4},{6,7},{7,6},{8,9},{9,8},{10,11... | collective-permute-start | bytes 1966088 | tf_op jit(solution)/shard_map/ppermute | solution.py:27
  23.8 8.2 %collective-permute-start.3 = (bf16[320,1024]{1,0:T(8,128)(2,1)S(1)}, bf16[320,1024]{1,0:T(8,128)(2,1)S(1)}, u32[]{:S(2)}, u32[]{:S(2)}) collective-permute-start(bf16[320,1024]{1,0:T(8,128)(2,1)S(1)} %collective-permute-done.1), channel_id=1, source_target_pairs={{0,1},{1,0},{2,3},{3,2},{4,5},{5,4},{6,7},{7,6},{8,9},{9,8},{10,11... | collective-permute-start | bytes 1966088 | tf_op jit(solution)/shard_map/ppermute | solution.py:27
  30.5 23.4 %collective-permute-start.5 = (bf16[256,1024]{1,0:T(8,128)(2,1)}, bf16[256,1024]{1,0:T(8,128)(2,1)}, u32[]{:S(2)}, u32[]{:S(2)}) collective-permute-start(bf16[256,1024]{1,0:T(8,128)(2,1)} %get-tuple-element.12), channel_id=1, source_target_pairs={{0,2},{1,3},{2,0},{3,1},{4,6},{5,7},{6,4},{7,5},{8,10},{9,11},{10,... | collective-permute-start | bytes 1572872 | tf_op jit(solution)/shard_map/ppermute | solution.py:38
  53.9 4.8 %collective-permute-start.8 = (bf16[256,1024]{1,0:T(8,128)(2,1)}, bf16[256,1024]{1,0:T(8,128)(2,1)}, u32[]{:S(2)}, u32[]{:S(2)}) collective-permute-start(bf16[256,1024]{1,0:T(8,128)(2,1)} %collective-permute-done.5), channel_id=1, source_target_pairs={{0,1},{1,0},{2,3},{3,2},{4,5},{5,4},{6,7},{7,6},{8,9},{9,8},{10,11... | collective-permute-start | bytes 1572872 | tf_op jit(solution)/shard_map/ppermute | solution.py:27
  57.7 24.4 %collective-permute-start.4 = (f32[256,1024]{1,0:T(8,128)}, f32[256,1024]{1,0:T(8,128)S(1)}, u32[]{:S(2)}, u32[]{:S(2)}) collective-permute-start(f32[256,1024]{1,0:T(8,128)} %fusion.65), channel_id=1, source_target_pairs={{0,1},{1,0},{2,3},{3,2},{4,5},{5,4},{6,7},{7,6},{8,9},{9,8},{10,11... | collective-permute-start | bytes 3145736 | tf_op jit(solution)/shard_map/ppermute | solution.py:27
  78.7 6.2 %collective-permute-start.10 = (f32[256,1024]{1,0:T(8,128)}, f32[256,1024]{1,0:T(8,128)}, u32[]{:S(2)}, u32[]{:S(2)}) collective-permute-start(f32[256,1024]{1,0:T(8,128)} %fusion.63), channel_id=1, source_target_pairs={{0,1},{1,0},{2,3},{3,2},{4,5},{5,4},{6,7},{7,6},{8,9},{9,8},{10,11... | collective-permute-start | bytes 3145736 | tf_op jit(solution)/shard_map/ppermute | solution.py:27
  81.8 16.8 %collective-permute-start.9 = (f32[256,1024]{1,0:T(8,128)}, f32[256,1024]{1,0:T(8,128)}, u32[]{:S(2)}, u32[]{:S(2)}) collective-permute-start(f32[256,1024]{1,0:T(8,128)} %fusion.55), channel_id=1, source_target_pairs={{0,1},{1,0},{2,3},{3,2},{4,5},{5,4},{6,7},{7,6},{8,9},{9,8},{10,11... | collective-permute-start | bytes 3145736 | tf_op jit(solution)/shard_map/ppermute | solution.py:27
  83.8 14.3 %collective-permute-start.6 = (bf16[256,1024]{1,0:T(8,128)(2,1)S(1)}, bf16[256,1024]{1,0:T(8,128)(2,1)}, u32[]{:S(2)}, u32[]{:S(2)}) collective-permute-start(bf16[256,1024]{1,0:T(8,128)(2,1)S(1)} %fusion.34), channel_id=1, source_target_pairs={{0,2},{1,3},{2,0},{3,1},{4,6},{5,7},{6,4},{7,5},{8,10},{9,11},{10,... | collective-permute-start | bytes 1572872 | tf_op jit(solution)/shard_map/ppermute | solution.py:38
  84.8 16.1 %collective-permute-start.12 = (f32[256,1024]{1,0:T(8,128)S(1)}, f32[256,1024]{1,0:T(8,128)}, u32[]{:S(2)}, u32[]{:S(2)}) collective-permute-start(f32[256,1024]{1,0:T(8,128)S(1)} %fusion.53), channel_id=1, source_target_pairs={{0,1},{1,0},{2,3},{3,2},{4,5},{5,4},{6,7},{7,6},{8,9},{9,8},{10,11... | collective-permute-start | bytes 3145736 | tf_op jit(solution)/shard_map/ppermute | solution.py:27
  98.1 13.6 %collective-permute-start.11 = (bf16[256,1024]{1,0:T(8,128)(2,1)}, bf16[256,1024]{1,0:T(8,128)(2,1)}, u32[]{:S(2)}, u32[]{:S(2)}) collective-permute-start(bf16[256,1024]{1,0:T(8,128)(2,1)} %fusion.35), channel_id=1, source_target_pairs={{0,2},{1,3},{2,0},{3,1},{4,6},{5,7},{6,4},{7,5},{8,10},{9,11},{10,... | collective-permute-start | bytes 1572872 | tf_op jit(solution)/shard_map/ppermute | solution.py:38
  98.6 39.4 %copy-start.19 = (bf16[4096,64]{0,1:T(8,128)(2,1)S(1)}, bf16[4096,64]{0,1:T(8,128)(2,1)}, u32[]{:S(2)}) copy-start(bf16[4096,64]{0,1:T(8,128)(2,1)} %param.19) | copy-start | bytes 1572868
  114.0 23.7 %collective-permute-start.13 = (bf16[512,1024]{1,0:T(8,128)(2,1)S(1)}, bf16[512,1024]{1,0:T(8,128)(2,1)S(1)}, u32[]{:S(2)}, u32[]{:S(2)}) collective-permute-start(bf16[512,1024]{1,0:T(8,128)(2,1)S(1)} %pad_maximum_fusion.7), channel_id=1, source_target_pairs={{0,2},{1,3},{2,0},{3,1},{4,6},{5,7},{6,4},{7,5},{8,10},{9,11},{10,... | collective-permute-start | bytes 3145736 | tf_op jit(solution)/shard_map/ppermute | solution.py:38
  114.6 23.8 %collective-permute-start.14 = (bf16[512,1024]{1,0:T(8,128)(2,1)S(1)}, bf16[512,1024]{1,0:T(8,128)(2,1)S(1)}, u32[]{:S(2)}, u32[]{:S(2)}) collective-permute-start(bf16[512,1024]{1,0:T(8,128)(2,1)S(1)} %pad_maximum_fusion.7), channel_id=1, source_target_pairs={{0,1},{1,0},{2,3},{3,2},{4,5},{5,4},{6,7},{7,6},{8,9},{9,8},{10,11... | collective-permute-start | bytes 3145736 | tf_op jit(solution)/shard_map/ppermute | solution.py:27
  137.6 2.7 %collective-permute-start.15 = (bf16[512,1024]{1,0:T(8,128)(2,1)S(1)}, bf16[512,1024]{1,0:T(8,128)(2,1)S(1)}, u32[]{:S(2)}, u32[]{:S(2)}) collective-permute-start(bf16[512,1024]{1,0:T(8,128)(2,1)S(1)} %collective-permute-done.13), channel_id=1, source_target_pairs={{0,1},{1,0},{2,3},{3,2},{4,5},{5,4},{6,7},{7,6},{8,9},{9,8},{10,11... | collective-permute-start | bytes 3145736 | tf_op jit(solution)/shard_map/ppermute | solution.py:27
  149.3 11.0 %collective-permute-start.16 = (bf16[2,273,256]{2,1,0:T(8,128)(2,1)S(1)}, bf16[2,273,256]{2,1,0:T(8,128)(2,1)S(1)}, u32[]{:S(2)}, u32[]{:S(2)}) collective-permute-start(bf16[2,273,256]{2,1,0:T(8,128)(2,1)S(1)} %convolution_convert_fusion), channel_id=1, source_target_pairs={{0,4},{4,8},{8,12},{1,5},{5,9},{9,13},{2,6},{6,10},{10,14},{3,7},{... | collective-permute-start | bytes 838664 | tf_op jit(solution)/shard_map/ppermute | solution.py:114
  150.6 27.8 %collective-permute-start.17 = (bf16[2,273,256]{2,1,0:T(8,128)(2,1)S(1)}, bf16[2,273,256]{2,1,0:T(8,128)(2,1)S(1)}, u32[]{:S(2)}, u32[]{:S(2)}) collective-permute-start(bf16[2,273,256]{2,1,0:T(8,128)(2,1)S(1)} %convolution_convert_fusion), channel_id=1, source_target_pairs={{0,8},{4,12},{1,9},{5,13},{2,10},{6,14},{3,11},{7,15},{16,24},{20,... | collective-permute-start | bytes 838664 | tf_op jit(solution)/shard_map/ppermute | solution.py:114
  151.9 26.5 %collective-permute-start.18 = (bf16[2,273,256]{2,1,0:T(8,128)(2,1)S(1)}, bf16[2,273,256]{2,1,0:T(8,128)(2,1)S(1)}, u32[]{:S(2)}, u32[]{:S(2)}) collective-permute-start(bf16[2,273,256]{2,1,0:T(8,128)(2,1)S(1)} %convolution_convert_fusion), channel_id=1, source_target_pairs={{0,12},{1,13},{2,14},{3,15},{16,28},{17,29},{18,30},{19,31}} | collective-permute-start | bytes 838664 | tf_op jit(solution)/shard_map/ppermute | solution.py:114
  181.4 4.2 %collective-permute-start.19 = (f32[512,1024]{1,0:T(8,128)S(1)}, f32[512,1024]{1,0:T(8,128)S(1)}, u32[]{:S(2)}, u32[]{:S(2)}) collective-permute-start(f32[512,1024]{1,0:T(8,128)S(1)} %fusion.50), channel_id=1, source_target_pairs={{0,1},{1,0},{2,3},{3,2},{4,5},{5,4},{6,7},{7,6},{8,9},{9,8},{10,11... | collective-permute-start | bytes 6291464 | tf_op jit(solution)/shard_map/ppermute | solution.py:27
  182.2 6.4 %collective-permute-start.21 = (f32[512,1024]{1,0:T(8,128)S(1)}, f32[512,1024]{1,0:T(8,128)S(1)}, u32[]{:S(2)}, u32[]{:S(2)}) collective-permute-start(f32[512,1024]{1,0:T(8,128)S(1)} %fusion.46), channel_id=1, source_target_pairs={{0,1},{1,0},{2,3},{3,2},{4,5},{5,4},{6,7},{7,6},{8,9},{9,8},{10,11... | collective-permute-start | bytes 6291464 | tf_op jit(solution)/shard_map/ppermute | solution.py:27
  186.4 25.3 %collective-permute-start.20 = (bf16[512,1024]{1,0:T(8,128)(2,1)S(1)}, bf16[512,1024]{1,0:T(8,128)(2,1)S(1)}, u32[]{:S(2)}, u32[]{:S(2)}) collective-permute-start(bf16[512,1024]{1,0:T(8,128)(2,1)S(1)} %add_convert_fusion.1), channel_id=1, source_target_pairs={{0,2},{1,3},{2,0},{3,1},{4,6},{5,7},{6,4},{7,5},{8,10},{9,11},{10,... | collective-permute-start | bytes 3145736 | tf_op jit(solution)/shard_map/ppermute | solution.py:38
  (22 other events, 223.7 us)

commit v9 on v6

--- a/solution.py
+++ b/solution.py
@@ -33,25 +33,30 @@
     return lax.ppermute(value, "head", pairs)
 
 
+def after(value, dep):
+    value, _ = lax.optimization_barrier((value, dep))
+    return value
+
+
 def head_reduce_scatter(lhs, weight):
     devices, chips = head_layout()
     me = lax.axis_index("head")
     core, chip = me % 2, me // 2
     width = weight.shape[1] // devices
 
-    def block(which, offset):
-        col = (((chip + offset) % chips) * 2 + which) * width
-        cols = lax.dynamic_slice_in_dim(weight, col, width, axis=1)
-        return jnp.dot(lhs, cols, preferred_element_type=jnp.float32)
-
-    order = [chips - 1 - j for j in range(chips)]
-    on_chip = {}
-    for offset in order:
-        on_chip[offset] = block(core, offset) + core_swap(block(1 - core, offset))
-    acc = on_chip[chips - 1]
+    def on_chip_sum(source, offset):
+        sums = []
+        for which in (core, 1 - core):
+            col = (((chip + offset) % chips) * 2 + which) * width
+            cols = lax.dynamic_slice_in_dim(weight, col, width, axis=1)
+            sums.append(jnp.dot(source, cols, preferred_element_type=jnp.float32))
+        return sums[0] + core_swap(sums[1])
+
+    acc = on_chip_sum(lhs, chips - 1)
     for step in range(chips - 1):
-        got = chip_shift(acc.astype(jnp.bfloat16), 1).astype(jnp.float32)
-        acc = got + on_chip[(chips - step - 2) % chips]
+        sent = acc.astype(jnp.bfloat16)
+        got = chip_shift(sent, 1).astype(jnp.float32)
+        acc = got + on_chip_sum(after(lhs, sent), (chips - step - 2) % chips)
     return acc
 
 

time: 190 us -> 195 us (1.026)
  waiting for transfers between devices: 123 us -> 131 us
  other arithmetic: 10.9 us -> 6.76 us
    ppermute x8, waiting for transfers between devices: 5.71 us -> 10.8 us  [core_swap(): return lax.ppermute(value, 'head', [(h, h ^ 1) for h in range(devices)])]
    convert_element_type x2 -> x0, other arithmetic: 4.14 us -> none  [the longest x1 2.41 us: body(): (hidden_parts[i].astype(jnp.float32) + partial_out).astype(jnp.bfloat16)]
    ppermute x4, waiting for transfers between devices: 91.4 us -> 94.7 us  [chip_shift(): return lax.ppermute(value, 'head', pairs)]
  transfers between devices with their start and end apart: 16 -> 16, of which waited for: 10 -> 10; matrix products, arithmetic and copies ran while one was open for 11% -> 5% of each run, Pallas kernels for 0% -> 0%
where the time goes in v9:
time: 195 us; the launch traced here: 194 us
  waiting for transfers between devices  131 us (67%)
  matrix products  38 us (19%)
  starting transfers between devices  12.2 us (6%)
  other arithmetic  6.76 us (3%)
  local copies, waits for them, and re-layouts  5.53 us (3%)
    ppermute x4, waiting for transfers between devices, chip_shift(): return lax.ppermute(value, 'head', pairs)  94.7 us
    ppermute x3, waiting for transfers between devices, earlier_sum(): total = total + lax.ppermute(sent, 'ctx', pairs).astype(jnp.float32)  21.9 us
    dot_general x8, matrix products, on_chip_sum(): sums.append(jnp.dot(source, cols, preferred_element_type=jnp.float32))  16.3 us
    ppermute x8, waiting for transfers between devices, core_swap(): return lax.ppermute(value, 'head', [(h, h ^ 1) for h in range(devices)])  10.8 us
    ppermute x4, starting transfers between devices, chip_shift(): return lax.ppermute(value, 'head', pairs)  6.05 us
    ppermute x3, starting transfers between devices, earlier_sum(): total = total + lax.ppermute(sent, 'ctx', pairs).astype(jnp.float32)  4.27 us
    dynamic_slice x6, local copies, waits for them, and re-layouts, gathered_rows(): lax.dynamic_slice_in_dim(weight, src * block, block, axis=0)  4.05 us
    sub x1, matrix products, body(): expd = jnp.exp(scores - top)  3.95 us
  transfers between devices with their start and end apart: 16, of which 10 were waited for; matrix products, arithmetic and copies ran while one was open for 5% of the time, Pallas kernels for 0%

profile of v9, /device:TPU:24, one launch (start us, length us, event | category | flops | bytes accessed | tf_op | source)
XLA Modules:
  0.0 194.4 jit_solution(5662507993142736442)
XLA Ops:
  1.5 23.6 %collective-permute-done = bf16[512,1024]{1,0:T(8,128)(2,1)S(1)} collective-permute-done((bf16[512,1024]{1,0:T(8,128)(2,1)}, bf16[512,1024]{1,0:T(8,128)(2,1)S(1)}, u32[]{:S(2)}, u32[]{:S(2)}) %collective-permute-start) | collective-permute-done | bytes 1048608 | tf_op jit(solution)/shard_map/ppermute | solution.py:33
  26.0 2.6 %constant_dynamic-slice_fusion.11 = (bf16[1024,512]{1,0:T(8,128)(2,1)S(1)}, bf16[1024,512]{1,0:T(8,128)(2,1)S(1)}, bf16[1024,512]{1,0:T(8,128)(2,1)S(1)}, bf16[1024,512]{1,0:T(8,128)(2,1)S(1)}) fusion(bf16[4096,512]{1,0:T(8,128)(2,1)} %param.14, s32[]{:T(128)S(6)} %select_n.127, s32[]{:T(128)S(6)} %select_n.131, s32[]{:T(128)S(6)} %select_n.133, ...), kind=kLoop, calls=%fused_computation.136 | loop fusion | bytes 8388624 | tf_op jit(solution)/shard_map/dynamic_slice | solution.py:87
  30.7 2.0 %fusion.1 = f32[512]{0:T(512)S(1)} fusion(bf16[512,1024]{1,0:T(8,128)(2,1)} %collective-permute-done.2, bf16[512,1024]{1,0:T(8,128)(2,1)S(1)} %collective-permute-done.1, bf16[512,1024]{1,0:T(8,128)(2,1)S(1)} %collective-permute-done, bf16[512,1024]{1,0:T(8,128)(2,1)S(1)} %copy-done), kind=kLoop, calls=%fused_computation.5 | loop fusion | flops 20971008 | bytes 4196352 | tf_op jit(solution)/shard_map/reduce_sum | solution.py:104
  32.7 2.4 %fusion.3 = bf16[512,4096]{1,0:T(8,128)(2,1)S(1)} fusion(f32[4096]{0:T(1024)S(1)} %pad_maximum_fusion.3, f32[512]{0:T(512)S(1)} %add_rsqrt_fusion.2, bf16[512,1024]{1,0:T(8,128)(2,1)} %collective-permute-done.2, bf16[512,1024]{1,0:T(8,128)(2,1)S(1)} %collective-permute-done.1, bf16[512,1024]{1,0:T(8,128)(2,1)S(1)} %collective-permute-done, ...), kind=kLoop, calls=%fused_computation.7 | loop fusion | flops 23068672 | bytes 8407040 | tf_op jit(solution)/shard_map/convert_element_type | solution.py:105
  39.4 2.4 %fusion.48 = bf16[512,512]{0,1:T(8,128)(2,1)S(1)} fusion(bf16[512,4096]{1,0:T(8,128)(2,1)S(1)} %fusion.3, bf16[1024,512]{1,0:T(8,128)(2,1)S(1)} %get-tuple-element.11, bf16[1024,512]{1,0:T(8,128)(2,1)S(1)} %get-tuple-element.12, bf16[1024,512]{1,0:T(8,128)(2,1)S(1)} %get-tuple-element.10, bf16[1024,512]{1,0:T(8,128)(2,1)S(1)} %get-tuple-element.9), kind=kOutput, calls=%fused_computation.61 | convolution fusion | flops 2164523008 | bytes 8912896 | tf_op jit(solution)/shard_map/dot_general | solution.py:154
  41.7 3.9 %collective-permute-done.3 = bf16[64,512]{0,1:T(8,128)(2,1)S(1)} collective-permute-done((bf16[64,512]{0,1:T(8,128)(2,1)S(1)}, bf16[64,512]{0,1:T(8,128)(2,1)S(1)}, u32[]{:S(2)}, u32[]{:S(2)}) %collective-permute-start.3) | collective-permute-done | bytes 65568 | tf_op jit(solution)/shard_map/ppermute | solution.py:17
  46.0 3.9 %fusion.117 = (f32[2,2,512]{2,1,0:T(2,128)S(1)}, f32[2,2,512,576]{2,3,1,0:T(8,128)}) fusion(pred[512,576]{0,1:T(8,128)(4,1)S(1)} %and_and_fusion, bf16[576,2,128,1]{0,2,3,1:T(8,128)(2,1)S(1)} %bitcast.82, bf16[512,2,2,128]{0,3,2,1:T(8,128)(2,1)S(1)} %bitcast.83), kind=kOutput, calls=%fused_computation.164 | convolution fusion | flops 306709056 | bytes 5840896 | tf_op jit(solution)/shard_map/sub | solution.py:181
  50.0 2.9 %fusion.51 = bf16[2,128,2,512]{3,1,2,0:T(8,128)(2,1)S(1)} fusion(bf16[576,2,128,1]{0,2,3,1:T(8,128)(2,1)S(1)} %bitcast.81, f32[2,2,512,576]{2,3,1,0:T(8,128)} %get-tuple-element.44, f32[2,2,512]{2,1,0:T(2,128)S(1)} %get-tuple-element.43), kind=kOutput, calls=%fused_computation.62 | convolution fusion | flops 304611328 | bytes 5545984 | tf_op jit(solution)/shard_map/kgts,skd->tkgd/dot_general | solution.py:183
  52.9 3.3 %fusion.78 = f32[512,1024]{1,0:T(8,128)} fusion(bf16[512,512]{0,1:T(8,128)(2,1)S(1)} %bitcast.70, bf16[512,4096]{1,0:T(8,128)(2,1)} %param.17, s32[]{:T(128)S(6)} %select_n.135), kind=kOutput, calls=%fused_computation.90 | convolution fusion | flops 536870912 | bytes 3670020 | tf_op jit(solution)/shard_map/dot_general | solution.py:52
  56.2 4.5 %collective-permute-done.4 = f32[512,1024]{1,0:T(8,128)} collective-permute-done((f32[512,1024]{1,0:T(8,128)}, f32[512,1024]{1,0:T(8,128)}, u32[]{:S(2)}, u32[]{:S(2)}) %collective-permute-start.4) | collective-permute-done | bytes 2097184 | tf_op jit(solution)/shard_map/ppermute | solution.py:27
  60.7 2.7 %add_convert_fusion.3 = bf16[512,1024]{1,0:T(8,128)(2,1)S(1)} fusion(f32[512,1024]{1,0:T(8,128)} %collective-permute-done.4, bf16[512,512]{0,1:T(8,128)(2,1)S(1)} %bitcast.71, bf16[512,4096]{1,0:T(8,128)(2,1)} %param.17, s32[]{:T(128)S(6)} %select_n.131), kind=kOutput, calls=%fused_computation.57 | convolution fusion | flops 537919488 | bytes 4718596 | tf_op jit(solution)/shard_map/dot_general | solution.py:52
  63.3 3.3 %fusion.75 = f32[512,1024]{1,0:T(8,128)} fusion(bf16[512,512]{0,1:T(8,128)(2,1)S(1)} %bitcast.72, bf16[512,4096]{1,0:T(8,128)(2,1)} %param.17, s32[]{:T(128)S(6)} %select_n.138), kind=kOutput, calls=%fused_computation.87 | convolution fusion | flops 536870912 | bytes 3670020 | tf_op jit(solution)/shard_map/dot_general | solution.py:52
  68.3 24.0 %collective-permute-done.5 = bf16[512,1024]{1,0:T(8,128)(2,1)} collective-permute-done((bf16[512,1024]{1,0:T(8,128)(2,1)S(1)}, bf16[512,1024]{1,0:T(8,128)(2,1)}, u32[]{:S(2)}, u32[]{:S(2)}) %collective-permute-start.5) | collective-permute-done | bytes 1048608 | tf_op jit(solution)/shard_map/ppermute | solution.py:33
  92.3 3.0 %add_convert_fusion.2 = bf16[512,1024]{1,0:T(8,128)(2,1)S(1)} fusion(f32[512,1024]{1,0:T(8,128)} %collective-permute-done.6, bf16[512,1024]{1,0:T(8,128)(2,1)} %collective-permute-done.5, bf16[512,1024]{1,0:T(8,128)(2,1)S(1)} %copy-done, bf16[512,512]{0,1:T(8,128)(2,1)S(1)} %bitcast.73, bf16[512,4096]{1,0:T(8,128)(2,1)} %param.17, s32[]{:T(128)S(6)} %select_n.137), kind=kOutput, calls=%fused_computation.56 | convolution fusion | flops 540016640 | bytes 6815748 | tf_op jit(solution)/shard_map/dot_general | solution.py:52
  96.9 23.1 %collective-permute-done.7 = bf16[512,1024]{1,0:T(8,128)(2,1)S(1)} collective-permute-done((bf16[512,1024]{1,0:T(8,128)(2,1)S(1)}, bf16[512,1024]{1,0:T(8,128)(2,1)S(1)}, u32[]{:S(2)}, u32[]{:S(2)}) %collective-permute-start.7) | collective-permute-done | bytes 1048608 | tf_op jit(solution)/shard_map/ppermute | solution.py:33
  120.6 2.1 %collective-permute-done.9 = bf16[512,1024]{1,0:T(8,128)(2,1)S(1)} collective-permute-done((bf16[512,1024]{1,0:T(8,128)(2,1)S(1)}, bf16[512,1024]{1,0:T(8,128)(2,1)S(1)}, u32[]{:S(2)}, u32[]{:S(2)}) %collective-permute-start.9) | collective-permute-done | bytes 1048608 | tf_op jit(solution)/shard_map/ppermute | solution.py:27
  125.4 2.6 %fusion.45 = bf16[512,512]{0,1:T(8,128)(2,1)S(1)} fusion(bf16[1024,512]{1,0:T(8,128)(2,1)S(1)} %get-tuple-element.15, bf16[1024,512]{1,0:T(8,128)(2,1)S(1)} %get-tuple-element.16, bf16[1024,512]{1,0:T(8,128)(2,1)S(1)} %get-tuple-element.14, bf16[1024,512]{1,0:T(8,128)(2,1)S(1)} %get-tuple-element.13, f32[4096]{0:T(1024)S(1)} %pad_maximum_fusion.4, ...), kind=kOutput, calls=%fused_computation.60 | convolution fusion | flops 2187591680 | bytes 8931328 | tf_op jit(solution)/shard_map/dot_general | solution.py:201
  133.1 2.3 %select_convert_fusion = bf16[2,512,512]{2,1,0:T(8,128)(2,1)S(1)} fusion(pred[512,512]{1,0:T(8,128)(4,1)S(1)} %iota_compare_fusion, f32[512,2,2,16]{0,3,2,1:T(8,128)S(1)} %bitcast.80), kind=kOutput, calls=%fused_computation.55 | convolution fusion | flops 104333312 | bytes 1441792 | tf_op jit(solution)/shard_map/thf,shf->hts/dot_general | solution.py:220
  136.1 3.9 %collective-permute-done.10 = bf16[2,273,256]{2,1,0:T(8,128)(2,1)S(1)} collective-permute-done((bf16[2,273,256]{2,1,0:T(8,128)(2,1)S(1)}, bf16[2,273,256]{2,1,0:T(8,128)(2,1)S(1)}, u32[]{:S(2)}, u32[]{:S(2)}) %collective-permute-start.10) | collective-permute-done | bytes 279584 | tf_op jit(solution)/shard_map/ppermute | solution.py:98
  140.0 18.0 %collective-permute-done.11 = bf16[2,273,256]{2,1,0:T(8,128)(2,1)S(1)} collective-permute-done((bf16[2,273,256]{2,1,0:T(8,128)(2,1)S(1)}, bf16[2,273,256]{2,1,0:T(8,128)(2,1)S(1)}, u32[]{:S(2)}, u32[]{:S(2)}) %collective-permute-start.11) | collective-permute-done | bytes 279584 | tf_op jit(solution)/shard_map/ppermute | solution.py:98
  158.0 2.2 %multiply_reduce_fusion = (f32[512,2]{0,1:T(2,128)S(1)}, f32[512,2,256]{0,2,1:T(8,128)S(1)}) fusion(f32[2,256,512]{2,1,0:T(8,128)S(1)} %fusion.118, f32[512,2,256]{0,2,1:T(8,128)S(1)} %bitcast.74, f32[512,2,16]{0,2,1:T(8,128)S(1)} %get-tuple-element.32, f32[273]{0:T(512)S(1)} %pad.7.clone, f32[2,273,256]{2,0,1:T(2,128)S(1)} %copy-done.5, ...), kind=kOutput, calls=%fused_computation.83 | convolution fusion | flops 860966912 | bytes 4614212 | tf_op jit(solution)/shard_map/thf,hfv->thv/dot_general | solution.py:219
  161.2 4.1 %collective-permute-done.13 = f32[512,1024]{1,0:T(8,128)S(1)} collective-permute-done((f32[512,1024]{1,0:T(8,128)S(1)}, f32[512,1024]{1,0:T(8,128)S(1)}, u32[]{:S(2)}, u32[]{:S(2)}) %collective-permute-start.13) | collective-permute-done | bytes 2097184 | tf_op jit(solution)/shard_map/ppermute | solution.py:27
  168.5 23.9 %collective-permute-done.14 = bf16[512,1024]{1,0:T(8,128)(2,1)S(1)} collective-permute-done((bf16[512,1024]{1,0:T(8,128)(2,1)S(1)}, bf16[512,1024]{1,0:T(8,128)(2,1)S(1)}, u32[]{:S(2)}, u32[]{:S(2)}) %collective-permute-start.14) | collective-permute-done | bytes 1048608 | tf_op jit(solution)/shard_map/ppermute | solution.py:33
  192.5 1.9 add_convert_fusion
  (73 shorter events, 25.0 us)
Async XLA Ops:
  0.0 25.1 %collective-permute-start = (bf16[512,1024]{1,0:T(8,128)(2,1)}, bf16[512,1024]{1,0:T(8,128)(2,1)S(1)}, u32[]{:S(2)}, u32[]{:S(2)}) collective-permute-start(bf16[512,1024]{1,0:T(8,128)(2,1)} %param.12), channel_id=1, source_target_pairs={{0,2},{1,3},{2,0},{3,1},{4,6},{5,7},{6,4},{7,5},{8,10},{9,11},{10,... | collective-permute-start | bytes 3145736 | tf_op jit(solution)/shard_map/ppermute | solution.py:33
  1.5 28.6 %collective-permute-start.1 = (bf16[512,1024]{1,0:T(8,128)(2,1)}, bf16[512,1024]{1,0:T(8,128)(2,1)S(1)}, u32[]{:S(2)}, u32[]{:S(2)}) collective-permute-start(bf16[512,1024]{1,0:T(8,128)(2,1)} %param.12), channel_id=1, source_target_pairs={{0,1},{1,0},{2,3},{3,2},{4,5},{5,4},{6,7},{7,6},{8,9},{9,8},{10,11... | collective-permute-start | bytes 3145736 | tf_op jit(solution)/shard_map/ppermute | solution.py:27
  25.1 5.0 %collective-permute-start.2 = (bf16[512,1024]{1,0:T(8,128)(2,1)S(1)}, bf16[512,1024]{1,0:T(8,128)(2,1)}, u32[]{:S(2)}, u32[]{:S(2)}) collective-permute-start(bf16[512,1024]{1,0:T(8,128)(2,1)S(1)} %collective-permute-done), channel_id=1, source_target_pairs={{0,1},{1,0},{2,3},{3,2},{4,5},{5,4},{6,7},{7,6},{8,9},{9,8},{10,11... | collective-permute-start | bytes 3145736 | tf_op jit(solution)/shard_map/ppermute | solution.py:27
  26.0 2.9 %copy-start.3 = (bf16[4096,256]{1,0:T(8,128)(2,1)S(1)}, bf16[4096,256]{1,0:T(8,128)(2,1)}, u32[]{:S(2)}) copy-start(bf16[4096,256]{1,0:T(8,128)(2,1)} %param.16) | copy-start | bytes 6291460
  26.0 3.5 %copy-start.4 = (bf16[4096,256]{1,0:T(8,128)(2,1)S(1)}, bf16[4096,256]{1,0:T(8,128)(2,1)}, u32[]{:S(2)}) copy-start(bf16[4096,256]{1,0:T(8,128)(2,1)} %param.15) | copy-start | bytes 6291460
  37.9 7.7 %collective-permute-start.3 = (bf16[64,512]{0,1:T(8,128)(2,1)S(1)}, bf16[64,512]{0,1:T(8,128)(2,1)S(1)}, u32[]{:S(2)}, u32[]{:S(2)}) collective-permute-start(bf16[64,512]{0,1:T(8,128)(2,1)S(1)} %pad_maximum_fusion.2), channel_id=1, source_target_pairs={{0,4},{4,8},{8,12},{1,5},{5,9},{9,13},{2,6},{6,10},{10,14},{3,7},{... | collective-permute-start | bytes 196616 | tf_op jit(solution)/shard_map/ppermute | solution.py:17
  56.2 4.5 %collective-permute-start.4 = (f32[512,1024]{1,0:T(8,128)}, f32[512,1024]{1,0:T(8,128)}, u32[]{:S(2)}, u32[]{:S(2)}) collective-permute-start(f32[512,1024]{1,0:T(8,128)} %fusion.78), channel_id=1, source_target_pairs={{0,1},{1,0},{2,3},{3,2},{4,5},{5,4},{6,7},{7,6},{8,9},{9,8},{10,11... | collective-permute-start | bytes 6291464 | tf_op jit(solution)/shard_map/ppermute | solution.py:27
  66.6 53.4 %copy-start.7 = (f32[4096]{0:T(1024)S(1)}, f32[4096]{0:T(1024)}, u32[]{:S(2)}) copy-start(f32[4096]{0:T(1024)} %param.18) | copy-start | bytes 49156
  66.6 53.5 %copy-start.6 = (bf16[4096,64]{0,1:T(8,128)(2,1)S(1)}, bf16[4096,64]{0,1:T(8,128)(2,1)}, u32[]{:S(2)}) copy-start(bf16[4096,64]{0,1:T(8,128)(2,1)} %param.19) | copy-start | bytes 1572868
  66.6 25.7 %collective-permute-start.6 = (f32[512,1024]{1,0:T(8,128)}, f32[512,1024]{1,0:T(8,128)}, u32[]{:S(2)}, u32[]{:S(2)}) collective-permute-start(f32[512,1024]{1,0:T(8,128)} %fusion.75), channel_id=1, source_target_pairs={{0,1},{1,0},{2,3},{3,2},{4,5},{5,4},{6,7},{7,6},{8,9},{9,8},{10,11... | collective-permute-start | bytes 6291464 | tf_op jit(solution)/shard_map/ppermute | solution.py:27
  66.8 25.5 %collective-permute-start.5 = (bf16[512,1024]{1,0:T(8,128)(2,1)S(1)}, bf16[512,1024]{1,0:T(8,128)(2,1)}, u32[]{:S(2)}, u32[]{:S(2)}) collective-permute-start(bf16[512,1024]{1,0:T(8,128)(2,1)S(1)} %add_convert_fusion.3), channel_id=1, source_target_pairs={{0,2},{1,3},{2,0},{3,1},{4,6},{5,7},{6,4},{7,5},{8,10},{9,11},{10,... | collective-permute-start | bytes 3145736 | tf_op jit(solution)/shard_map/ppermute | solution.py:33
  68.3 52.0 %copy-start.1 = (bf16[4096,512]{1,0:T(8,128)(2,1)S(1)}, bf16[4096,512]{1,0:T(8,128)(2,1)}, u32[]{:S(2)}) copy-start(bf16[4096,512]{1,0:T(8,128)(2,1)} %param.20) | copy-start | bytes 12582916
  95.3 24.7 %collective-permute-start.7 = (bf16[512,1024]{1,0:T(8,128)(2,1)S(1)}, bf16[512,1024]{1,0:T(8,128)(2,1)S(1)}, u32[]{:S(2)}, u32[]{:S(2)}) collective-permute-start(bf16[512,1024]{1,0:T(8,128)(2,1)S(1)} %add_convert_fusion.2), channel_id=1, source_target_pairs={{0,2},{1,3},{2,0},{3,1},{4,6},{5,7},{6,4},{7,5},{8,10},{9,11},{10,... | collective-permute-start | bytes 3145736 | tf_op jit(solution)/shard_map/ppermute | solution.py:33
  96.9 23.6 %collective-permute-start.8 = (bf16[512,1024]{1,0:T(8,128)(2,1)S(1)}, bf16[512,1024]{1,0:T(8,128)(2,1)S(1)}, u32[]{:S(2)}, u32[]{:S(2)}) collective-permute-start(bf16[512,1024]{1,0:T(8,128)(2,1)S(1)} %add_convert_fusion.2), channel_id=1, source_target_pairs={{0,1},{1,0},{2,3},{3,2},{4,5},{5,4},{6,7},{7,6},{8,9},{9,8},{10,11... | collective-permute-start | bytes 3145736 | tf_op jit(solution)/shard_map/ppermute | solution.py:27
  120.0 2.7 %collective-permute-start.9 = (bf16[512,1024]{1,0:T(8,128)(2,1)S(1)}, bf16[512,1024]{1,0:T(8,128)(2,1)S(1)}, u32[]{:S(2)}, u32[]{:S(2)}) collective-permute-start(bf16[512,1024]{1,0:T(8,128)(2,1)S(1)} %collective-permute-done.7), channel_id=1, source_target_pairs={{0,1},{1,0},{2,3},{3,2},{4,5},{5,4},{6,7},{7,6},{8,9},{9,8},{10,11... | collective-permute-start | bytes 3145736 | tf_op jit(solution)/shard_map/ppermute | solution.py:27
  128.8 29.2 %copy-start.5 = (f32[2,273,256]{2,0,1:T(2,128)S(1)}, f32[2,273,256]{2,0,1:T(2,128)}, u32[]{:S(2)}) copy-start(f32[2,273,256]{2,0,1:T(2,128)} %param.23) | copy-start | bytes 1677316
  128.8 11.2 %collective-permute-start.10 = (bf16[2,273,256]{2,1,0:T(8,128)(2,1)S(1)}, bf16[2,273,256]{2,1,0:T(8,128)(2,1)S(1)}, u32[]{:S(2)}, u32[]{:S(2)}) collective-permute-start(bf16[2,273,256]{2,1,0:T(8,128)(2,1)S(1)} %convolution_convert_fusion), channel_id=1, source_target_pairs={{0,4},{4,8},{8,12},{1,5},{5,9},{9,13},{2,6},{6,10},{10,14},{3,7},{... | collective-permute-start | bytes 838664 | tf_op jit(solution)/shard_map/ppermute | solution.py:98
  130.2 27.8 %collective-permute-start.11 = (bf16[2,273,256]{2,1,0:T(8,128)(2,1)S(1)}, bf16[2,273,256]{2,1,0:T(8,128)(2,1)S(1)}, u32[]{:S(2)}, u32[]{:S(2)}) collective-permute-start(bf16[2,273,256]{2,1,0:T(8,128)(2,1)S(1)} %convolution_convert_fusion), channel_id=1, source_target_pairs={{0,8},{4,12},{1,9},{5,13},{2,10},{6,14},{3,11},{7,15},{16,24},{20,... | collective-permute-start | bytes 838664 | tf_op jit(solution)/shard_map/ppermute | solution.py:98
  131.5 26.5 %collective-permute-start.12 = (bf16[2,273,256]{2,1,0:T(8,128)(2,1)S(1)}, bf16[2,273,256]{2,1,0:T(8,128)(2,1)S(1)}, u32[]{:S(2)}, u32[]{:S(2)}) collective-permute-start(bf16[2,273,256]{2,1,0:T(8,128)(2,1)S(1)} %convolution_convert_fusion), channel_id=1, source_target_pairs={{0,12},{1,13},{2,14},{3,15},{16,28},{17,29},{18,30},{19,31}} | collective-permute-start | bytes 838664 | tf_op jit(solution)/shard_map/ppermute | solution.py:98
  135.4 24.8 %copy-start.8 = (f32[2,256]{1,0:T(2,128)S(1)}, f32[2,256]{1,0:T(2,128)}, u32[]{:S(2)}) copy-start(f32[2,256]{1,0:T(2,128)} %param.21) | copy-start | bytes 6148
  135.6 24.8 %copy-start.2 = (bf16[512,4096]{1,0:T(8,128)(2,1)S(1)}, bf16[512,4096]{1,0:T(8,128)(2,1)}, u32[]{:S(2)}) copy-start(bf16[512,4096]{1,0:T(8,128)(2,1)} %param.22) | copy-start | bytes 12582916
  161.1 4.2 %collective-permute-start.13 = (f32[512,1024]{1,0:T(8,128)S(1)}, f32[512,1024]{1,0:T(8,128)S(1)}, u32[]{:S(2)}, u32[]{:S(2)}) collective-permute-start(f32[512,1024]{1,0:T(8,128)S(1)} %fusion.72), channel_id=1, source_target_pairs={{0,1},{1,0},{2,3},{3,2},{4,5},{5,4},{6,7},{7,6},{8,9},{9,8},{10,11... | collective-permute-start | bytes 6291464 | tf_op jit(solution)/shard_map/ppermute | solution.py:27
  166.8 25.6 %collective-permute-start.15 = (f32[512,1024]{1,0:T(8,128)S(1)}, f32[512,1024]{1,0:T(8,128)S(1)}, u32[]{:S(2)}, u32[]{:S(2)}) collective-permute-start(f32[512,1024]{1,0:T(8,128)S(1)} %fusion.69), channel_id=1, source_target_pairs={{0,1},{1,0},{2,3},{3,2},{4,5},{5,4},{6,7},{7,6},{8,9},{9,8},{10,11... | collective-permute-start | bytes 6291464 | tf_op jit(solution)/shard_map/ppermute | solution.py:27
  167.0 25.4 %collective-permute-start.14 = (bf16[512,1024]{1,0:T(8,128)(2,1)S(1)}, bf16[512,1024]{1,0:T(8,128)(2,1)S(1)}, u32[]{:S(2)}, u32[]{:S(2)}) collective-permute-start(bf16[512,1024]{1,0:T(8,128)(2,1)S(1)} %add_convert_fusion.1), channel_id=1, source_target_pairs={{0,2},{1,3},{2,0},{3,1},{4,6},{5,7},{6,4},{7,5},{8,10},{9,11},{10,... | collective-permute-start | bytes 3145736 | tf_op jit(solution)/shard_map/ppermute | solution.py:33
  (1 other events, 1.2 us)

commit v10 on v6

--- a/solution.py
+++ b/solution.py
@@ -158,25 +158,34 @@
     after_parts, after_whole_parts = [], []
     for i in range(CHUNKS):
         kv_win = kv_all[i * size : i * size + size + WINDOW]
-        key_win = kv_win[:, :kv_cols].reshape(size + WINDOW, kv_heads, HEAD)
-        value_win = kv_win[:, kv_cols:].reshape(size + WINDOW, kv_heads, HEAD)
-        query_heads = query_parts[i].reshape(size, kv_heads, group, HEAD)
+        blocks = size // WINDOW
+        kv_blocks = jnp.concatenate(
+            [
+                kv_win[:-WINDOW].reshape(blocks, WINDOW, 2 * kv_cols),
+                kv_win[WINDOW:].reshape(blocks, WINDOW, 2 * kv_cols),
+            ],
+            axis=1,
+        )
+        key_blocks = kv_blocks[..., :kv_cols].reshape(blocks, 2 * WINDOW, kv_heads, HEAD)
+        value_blocks = kv_blocks[..., kv_cols:].reshape(blocks, 2 * WINDOW, kv_heads, HEAD)
+        query_blocks = query_parts[i].reshape(blocks, WINDOW, kv_heads, group, HEAD)
         scores = jnp.einsum(
-            "tkgd,skd->kgts", query_heads, key_win, preferred_element_type=jnp.float32
+            "bqkgd,bskd->bkgqs", query_blocks, key_blocks, preferred_element_type=jnp.float32
         ) / math.sqrt(HEAD)
-        qpos = start + i * size + jnp.arange(size, dtype=jnp.int32)
-        kpos = start + i * size - WINDOW + jnp.arange(size + WINDOW, dtype=jnp.int32)
+        base = start + i * size + WINDOW * jnp.arange(blocks, dtype=jnp.int32)
+        qpos = base[:, None] + jnp.arange(WINDOW, dtype=jnp.int32)[None, :]
+        kpos = base[:, None] - WINDOW + jnp.arange(2 * WINDOW, dtype=jnp.int32)[None, :]
         visible = (
-            (kpos[None, :] <= qpos[:, None])
-            & (kpos[None, :] > qpos[:, None] - WINDOW)
-            & (kpos[None, :] >= 0)
-        )
-        scores = jnp.where(visible, scores, -jnp.inf)
+            (kpos[:, None, :] <= qpos[:, :, None])
+            & (kpos[:, None, :] > qpos[:, :, None] - WINDOW)
+            & (kpos[:, None, :] >= 0)
+        )
+        scores = jnp.where(visible[:, None, None], scores, -jnp.inf)
         top = jnp.max(scores, axis=-1, keepdims=True)
         expd = jnp.exp(scores - top)
         probs = (expd / jnp.sum(expd, axis=-1, keepdims=True)).astype(jnp.bfloat16)
         attended = jnp.einsum(
-            "kgts,skd->tkgd", probs, value_win, preferred_element_type=jnp.float32
+            "bkgqs,bskd->bqkgd", probs, value_blocks, preferred_element_type=jnp.float32
         )
         attended = attended.astype(jnp.bfloat16).reshape(size, -1)
         partial_out = head_reduce_scatter(attended, wo_attn)

time: 190 us -> 193 us (1.016)
  local copies, waits for them, and re-layouts: 5.54 us -> 12.5 us
  waiting for transfers between devices: 123 us -> 118 us
    ppermute x4, waiting for transfers between devices: 91.4 us -> 84.2 us  [chip_shift(): return lax.ppermute(value, 'head', pairs)]
    sub x1 -> x0, matrix products: 3.95 us -> none  [body(): expd = jnp.exp(scores - top)]
    dynamic_slice x6, local copies, waits for them, and re-layouts: 4.02 us -> 7.57 us  [gathered_rows(): lax.dynamic_slice_in_dim(weight, src * block, block, axis=0)]
    dot_general x1 -> x2, matrix products: 2.92 us -> 5.76 us  [the longest x1 4.43 us: body(): jnp.einsum('bkgqs,bskd->bqkgd', probs, value_blocks, preferred_element_ty...]
    slice x1 -> x3, local copies, waits for them, and re-layouts: 0.06 us -> 2.54 us  [the longest x1 2.06 us: body(): kv_blocks[..., :kv_cols].reshape(blocks, 2 * WINDOW, kv_heads, HEAD)]
    ppermute x8, waiting for transfers between devices: 5.71 us -> 8.03 us  [core_swap(): return lax.ppermute(value, 'head', [(h, h ^ 1) for h in range(devices)])]
  transfers between devices with their start and end apart: 16 -> 16, of which waited for: 10 -> 11; matrix products, arithmetic and copies ran while one was open for 11% -> 13% of each run, Pallas kernels for 0% -> 0%
where the time goes in v10:
time: 193 us; the launch traced here: 192 us
  waiting for transfers between devices  118 us (61%)
  matrix products  35.9 us (19%)
  starting transfers between devices  12.7 us (7%)
  other arithmetic  12.7 us (7%)
  local copies, waits for them, and re-layouts  12.5 us (6%)
    ppermute x4, waiting for transfers between devices, chip_shift(): return lax.ppermute(value, 'head', pairs)  84.2 us
    ppermute x3, waiting for transfers between devices, earlier_sum(): total = total + lax.ppermute(sent, 'ctx', pairs).astype(jnp.float32)  22.2 us
    dot_general x8, matrix products, block(): return jnp.dot(lhs, cols, preferred_element_type=jnp.float32)  15.1 us
    ppermute x8, waiting for transfers between devices, core_swap(): return lax.ppermute(value, 'head', [(h, h ^ 1) for h in range(devices)])  8.03 us
    dynamic_slice x6, local copies, waits for them, and re-layouts, gathered_rows(): lax.dynamic_slice_in_dim(weight, src * block, block, axis=0)  7.57 us
    ppermute x4, starting transfers between devices, chip_shift(): return lax.ppermute(value, 'head', pairs)  6.09 us
    dot_general x1, matrix products, body(): jnp.einsum('bkgqs,bskd->bqkgd', probs, value_blocks, preferred_element_ty...  4.43 us
    ppermute x3, starting transfers between devices, earlier_sum(): total = total + lax.ppermute(sent, 'ctx', pairs).astype(jnp.float32)  4.01 us
  transfers between devices with their start and end apart: 16, of which 11 were waited for; matrix products, arithmetic and copies ran while one was open for 13% of the time, Pallas kernels for 0%

profile of v10, /device:TPU:24, one launch (start us, length us, event | category | flops | bytes accessed | tf_op | source)
XLA Modules:
  0.0 192.0 jit_solution(44044670837544282)
XLA Ops:
  2.2 4.4 %constant_dynamic-slice_fusion.11 = (bf16[1024,512]{1,0:T(8,128)(2,1)}, bf16[1024,512]{1,0:T(8,128)(2,1)}, bf16[1024,512]{1,0:T(8,128)(2,1)}, bf16[1024,512]{1,0:T(8,128)(2,1)}) fusion(bf16[4096,512]{1,0:T(8,128)(2,1)} %param.14, s32[]{:T(128)S(6)} %select_n.127, s32[]{:T(128)S(6)} %select_n.131, s32[]{:T(128)S(6)} %select_n.133, s32[]{:T(128)S(6)} %select_n.132), kind=kLoop, calls=%fused_computation.146 | loop fusion | bytes 8388624 | tf_op jit(solution)/shard_map/dynamic_slice | solution.py:82
  6.7 2.1 %constant_dynamic-slice_fusion.15 = (bf16[1024,256]{1,0:T(8,128)(2,1)}, bf16[1024,256]{1,0:T(8,128)(2,1)}, bf16[1024,256]{1,0:T(8,128)(2,1)}, bf16[1024,256]{1,0...) fusion(bf16[4096,256]{1,0:T(8,128)(2,1)S(1)} %copy-done.3, ...), kind=kLoop, calls=%fused_computation.150 | loop fusion | bytes 8388624 | tf_op jit(solution)/shard_map/dynamic_slice | solution.py:82
  8.7 16.4 %collective-permute-done = bf16[512,1024]{1,0:T(8,128)(2,1)S(1)} collective-permute-done((bf16[512,1024]{1,0:T(8,128)(2,1)}, bf16[512,1024]{1,0:T(8,128)(2,1)S(1)}, u32[]{:S(2)}, u32[]{:S(2)}) %collective-permute-start) | collective-permute-done | bytes 1048608 | tf_op jit(solution)/shard_map/ppermute | solution.py:33
  25.6 2.3 %collective-permute-done.2 = bf16[512,1024]{1,0:T(8,128)(2,1)} collective-permute-done((bf16[512,1024]{1,0:T(8,128)(2,1)S(1)}, bf16[512,1024]{1,0:T(8,128)(2,1)}, u32[]{:S(2)}, u32[]{:S(2)}) %collective-permute-start.2) | collective-permute-done | bytes 1048608 | tf_op jit(solution)/shard_map/ppermute | solution.py:27
  27.9 2.0 %fusion.1 = f32[512]{0:T(512)S(1)} fusion(bf16[512,1024]{1,0:T(8,128)(2,1)} %collective-permute-done.2, bf16[512,1024]{1,0:T(8,128)(2,1)S(1)} %collective-permute-done.1, bf16[512,1024]{1,0:T(8,128)(2,1)S(1)} %collective-permute-done, bf16[512,1024]{1,0:T(8,128)(2,1)S(1)} %copy-done), kind=kLoop, calls=%fused_computation.5 | loop fusion | flops 20971008 | bytes 4196352 | tf_op jit(solution)/shard_map/reduce_sum | solution.py:99
  30.0 2.6 %fusion.3 = bf16[512,4096]{1,0:T(8,128)(2,1)S(1)} fusion(f32[4096]{0:T(1024)S(1)} %pad_maximum_fusion.6, f32[512]{0:T(512)S(1)} %add_rsqrt_fusion.2, bf16[512,1024]{1,0:T(8,128)(2,1)} %collective-permute-done.2, bf16[512,1024]{1,0:T(8,128)(2,1)S(1)} %collective-permute-done.1, bf16[512,1024]{1,0:T(8,128)(2,1)S(1)} %collective-permute-done, ...), kind=kLoop, calls=%fused_computation.7 | loop fusion | flops 23068672 | bytes 8407040 | tf_op jit(solution)/shard_map/convert_element_type | solution.py:100
  37.1 2.6 %fusion.47 = bf16[512,512]{1,0:T(8,128)(2,1)S(1)} fusion(bf16[512,4096]{1,0:T(8,128)(2,1)S(1)} %fusion.3, bf16[1024,512]{1,0:T(8,128)(2,1)S(1)} %copy-done.7, bf16[1024,512]{1,0:T(8,128)(2,1)S(1)} %copy-done.8, bf16[1024,512]{1,0:T(8,128)(2,1)S(1)} %copy-done.6, bf16[1024,512]{1,0:T(8,128)(2,1)S(1)} %copy-done.5), kind=kOutput, calls=%fused_computation.58 | convolution fusion | flops 2164523008 | bytes 8912896 | tf_op jit(solution)/shard_map/dot_general | solution.py:149
  39.8 3.2 %collective-permute-done.3 = bf16[64,512]{0,1:T(8,128)(2,1)S(1)} collective-permute-done((bf16[64,512]{0,1:T(8,128)(2,1)S(1)}, bf16[64,512]{0,1:T(8,128)(2,1)S(1)}, u32[]{:S(2)}, u32[]{:S(2)}) %collective-permute-start.3) | collective-permute-done | bytes 65568 | tf_op jit(solution)/shard_map/ppermute | solution.py:17
  44.6 2.1 %copy.21 = bf16[8,128,256]{1,2,0:T(8,128)(2,1)} copy(bf16[8,128,256]{2,1,0:T(8,128)(2,1)} %get-tuple-element.21) | data formatting | bytes 1048576 | tf_op jit(solution)/shard_map/slice | solution.py:169
  48.9 4.4 %fusion.50 = bf16[8,64,2,2,128]{4,1,3,2,0:T(8,128)(2,1)} fusion(bf16[8,128,2,128,1]{1,3,4,2,0:T(8,128)(2,1)S(1)} %bitcast.69, f32[8,2,2,64]{3,2,1,0:T(2,128)S(1)} %fusion.118, f32[8,2,2,64,128]{4,3,2,1,0:T(8,128)S(1)} %fusion.43), kind=kOutput, calls=%fused_computation.60 | convolution fusion | flops 68159616 | bytes 2105344 | tf_op jit(solution)/shard_map/bkgqs,bskd->bqkgd/dot_general | solution.py:187
  55.1 3.3 %fusion.79 = f32[512,1024]{1,0:T(8,128)} fusion(bf16[512,512]{1,0:T(8,128)(2,1)S(1)} %reshape.174, bf16[512,4096]{1,0:T(8,128)(2,1)} %param.17, s32[]{:T(128)S(6)} %select_n.135), kind=kOutput, calls=%fused_computation.91 | convolution fusion | flops 536870912 | bytes 3670020 | tf_op jit(solution)/shard_map/dot_general | solution.py:45
  58.4 3.3 %fusion.75 = f32[512,1024]{1,0:T(8,128)} fusion(bf16[512,512]{1,0:T(8,128)(2,1)S(1)} %reshape.174, bf16[512,4096]{1,0:T(8,128)(2,1)} %param.17, s32[]{:T(128)S(6)} %select_n.138), kind=kOutput, calls=%fused_computation.87 | convolution fusion | flops 536870912 | bytes 3670020 | tf_op jit(solution)/shard_map/dot_general | solution.py:45
  62.9 3.6 %add_convert_fusion.3 = bf16[512,1024]{1,0:T(8,128)(2,1)} fusion(f32[512,1024]{1,0:T(8,128)} %collective-permute-done.4, bf16[512,512]{1,0:T(8,128)(2,1)S(1)} %reshape.174, bf16[512,4096]{1,0:T(8,128)(2,1)} %param.17, s32[]{:T(128)S(6)} %select_n.131), kind=kOutput, calls=%fused_computation.49 | convolution fusion | flops 537919488 | bytes 4718596 | tf_op jit(solution)/shard_map/dot_general | solution.py:45
  70.0 21.9 %collective-permute-done.5 = bf16[512,1024]{1,0:T(8,128)(2,1)S(1)} collective-permute-done((bf16[512,1024]{1,0:T(8,128)(2,1)}, bf16[512,1024]{1,0:T(8,128)(2,1)S(1)}, u32[]{:S(2)}, u32[]{:S(2)}) %collective-permute-start.5) | collective-permute-done | bytes 1048608 | tf_op jit(solution)/shard_map/ppermute | solution.py:33
  92.0 2.3 %add_convert_fusion.2 = bf16[512,1024]{1,0:T(8,128)(2,1)S(1)} fusion(f32[512,1024]{1,0:T(8,128)S(1)} %fusion.77, f32[512,1024]{1,0:T(8,128)} %collective-permute-done.6, bf16[512,1024]{1,0:T(8,128)(2,1)S(1)} %collective-permute-done.5, bf16[512,1024]{1,0:T(8,128)(2,1)S(1)} %copy-done), kind=kLoop, calls=%fused_computation.48 | loop fusion | flops 3145728 | bytes 7340032 | tf_op jit(solution)/shard_map/convert_element_type | solution.py:192
  95.9 22.9 %collective-permute-done.7 = bf16[512,1024]{1,0:T(8,128)(2,1)S(1)} collective-permute-done((bf16[512,1024]{1,0:T(8,128)(2,1)S(1)}, bf16[512,1024]{1,0:T(8,128)(2,1)S(1)}, u32[]{:S(2)}, u32[]{:S(2)}) %collective-permute-start.7) | collective-permute-done | bytes 1048608 | tf_op jit(solution)/shard_map/ppermute | solution.py:33
  119.3 2.1 %collective-permute-done.9 = bf16[512,1024]{1,0:T(8,128)(2,1)S(1)} collective-permute-done((bf16[512,1024]{1,0:T(8,128)(2,1)S(1)}, bf16[512,1024]{1,0:T(8,128)(2,1)S(1)}, u32[]{:S(2)}, u32[]{:S(2)}) %collective-permute-start.9) | collective-permute-done | bytes 1048608 | tf_op jit(solution)/shard_map/ppermute | solution.py:27
  124.3 2.6 %fusion.44 = bf16[512,512]{0,1:T(8,128)(2,1)S(1)} fusion(bf16[1024,512]{1,0:T(8,128)(2,1)S(1)} %get-tuple-element.11, bf16[1024,512]{1,0:T(8,128)(2,1)S(1)} %get-tuple-element.12, bf16[1024,512]{1,0:T(8,128)(2,1)S(1)} %get-tuple-element.10, bf16[1024,512]{1,0:T(8,128)(2,1)S(1)} %get-tuple-element.9, f32[4096]{0:T(1024)S(1)} %pad_maximum_fusion.7, ...), kind=kOutput, calls=%fused_computation.57 | convolution fusion | flops 2187591680 | bytes 8931328 | tf_op jit(solution)/shard_map/dot_general | solution.py:205
  131.8 2.3 %select_convert_fusion = bf16[2,512,512]{2,1,0:T(8,128)(2,1)S(1)} fusion(pred[512,512]{1,0:T(8,128)(4,1)S(1)} %iota_compare_fusion, f32[512,2,2,16]{0,3,2,1:T(8,128)S(1)} %bitcast.72), kind=kOutput, calls=%fused_computation.47 | convolution fusion | flops 104333312 | bytes 1441792 | tf_op jit(solution)/shard_map/thf,shf->hts/dot_general | solution.py:224
  134.8 4.2 %collective-permute-done.10 = bf16[2,273,256]{2,1,0:T(8,128)(2,1)S(1)} collective-permute-done((bf16[2,273,256]{2,1,0:T(8,128)(2,1)S(1)}, bf16[2,273,256]{2,1,0:T(8,128)(2,1)S(1)}, u32[]{:S(2)}, u32[]{:S(2)}) %collective-permute-start.10) | collective-permute-done | bytes 279584 | tf_op jit(solution)/shard_map/ppermute | solution.py:93
  138.9 18.0 %collective-permute-done.11 = bf16[2,273,256]{2,1,0:T(8,128)(2,1)S(1)} collective-permute-done((bf16[2,273,256]{2,1,0:T(8,128)(2,1)S(1)}, bf16[2,273,256]{2,1,0:T(8,128)(2,1)S(1)}, u32[]{:S(2)}, u32[]{:S(2)}) %collective-permute-start.11) | collective-permute-done | bytes 279584 | tf_op jit(solution)/shard_map/ppermute | solution.py:93
  157.0 2.2 %multiply_reduce_fusion = (f32[512,2]{0,1:T(2,128)S(1)}, f32[512,2,256]{0,2,1:T(8,128)S(1)}) fusion(f32[2,256,512]{2,1,0:T(8,128)S(1)} %fusion.119, f32[512,2,256]{0,2,1:T(8,128)S(1)} %bitcast.62, f32[512,2,16]{0,2,1:T(8,128)S(1)} %get-tuple-element.30, f32[273]{0:T(512)S(1)} %pad.7.clone, f32[2,273,256]{2,0,1:T(2,128)S(1)} %copy-done.9, ...), kind=kOutput, calls=%fused_computation.83 | convolution fusion | flops 860966912 | bytes 4614212 | tf_op jit(solution)/shard_map/thf,hfv->thv/dot_general | solution.py:223
  161.5 2.9 %collective-permute-done.13 = f32[512,1024]{1,0:T(8,128)S(1)} collective-permute-done((f32[512,1024]{1,0:T(8,128)S(1)}, f32[512,1024]{1,0:T(8,128)S(1)}, u32[]{:S(2)}, u32[]{:S(2)}) %collective-permute-start.13) | collective-permute-done | bytes 2097184 | tf_op jit(solution)/shard_map/ppermute | solution.py:27
  167.3 23.0 %collective-permute-done.14 = bf16[512,1024]{1,0:T(8,128)(2,1)S(1)} collective-permute-done((bf16[512,1024]{1,0:T(8,128)(2,1)S(1)}, bf16[512,1024]{1,0:T(8,128)(2,1)S(1)}, u32[]{:S(2)}, u32[]{:S(2)}) %collective-permute-start.14) | collective-permute-done | bytes 1048608 | tf_op jit(solution)/shard_map/ppermute | solution.py:33
  (108 shorter events, 34.7 us)
Async XLA Ops:
  0.0 25.1 %collective-permute-start = (bf16[512,1024]{1,0:T(8,128)(2,1)}, bf16[512,1024]{1,0:T(8,128)(2,1)S(1)}, u32[]{:S(2)}, u32[]{:S(2)}) collective-permute-start(bf16[512,1024]{1,0:T(8,128)(2,1)} %param.12), channel_id=1, source_target_pairs={{0,2},{1,3},{2,0},{3,1},{4,6},{5,7},{6,4},{7,5},{8,10},{9,11},{10,... | collective-permute-start | bytes 3145736 | tf_op jit(solution)/shard_map/ppermute | solution.py:33
  1.5 24.1 %collective-permute-start.1 = (bf16[512,1024]{1,0:T(8,128)(2,1)}, bf16[512,1024]{1,0:T(8,128)(2,1)S(1)}, u32[]{:S(2)}, u32[]{:S(2)}) collective-permute-start(bf16[512,1024]{1,0:T(8,128)(2,1)} %param.12), channel_id=1, source_target_pairs={{0,1},{1,0},{2,3},{3,2},{4,5},{5,4},{6,7},{7,6},{8,9},{9,8},{10,11... | collective-permute-start | bytes 3145736 | tf_op jit(solution)/shard_map/ppermute | solution.py:27
  2.2 4.4 %copy-start.4 = (bf16[4096,256]{1,0:T(8,128)(2,1)S(1)}, bf16[4096,256]{1,0:T(8,128)(2,1)}, u32[]{:S(2)}) copy-start(bf16[4096,256]{1,0:T(8,128)(2,1)} %param.15) | copy-start | bytes 6291460
  6.7 21.2 %copy-start = (bf16[512,1024]{1,0:T(8,128)(2,1)S(1)}, bf16[512,1024]{1,0:T(8,128)(2,1)}, u32[]{:S(2)}) copy-start(bf16[512,1024]{1,0:T(8,128)(2,1)} %param.12) | copy-start | bytes 3145732
  25.1 2.8 %collective-permute-start.2 = (bf16[512,1024]{1,0:T(8,128)(2,1)S(1)}, bf16[512,1024]{1,0:T(8,128)(2,1)}, u32[]{:S(2)}, u32[]{:S(2)}) collective-permute-start(bf16[512,1024]{1,0:T(8,128)(2,1)S(1)} %collective-permute-done), channel_id=1, source_target_pairs={{0,1},{1,0},{2,3},{3,2},{4,5},{5,4},{6,7},{7,6},{8,9},{9,8},{10,11... | collective-permute-start | bytes 3145736 | tf_op jit(solution)/shard_map/ppermute | solution.py:27
  35.5 7.4 %collective-permute-start.3 = (bf16[64,512]{0,1:T(8,128)(2,1)S(1)}, bf16[64,512]{0,1:T(8,128)(2,1)S(1)}, u32[]{:S(2)}, u32[]{:S(2)}) collective-permute-start(bf16[64,512]{0,1:T(8,128)(2,1)S(1)} %fusion.99), channel_id=1, source_target_pairs={{0,4},{4,8},{8,12},{1,5},{5,9},{9,13},{2,6},{6,10},{10,14},{3,7},{... | collective-permute-start | bytes 196616 | tf_op jit(solution)/shard_map/ppermute | solution.py:17
  58.4 4.5 %collective-permute-start.4 = (f32[512,1024]{1,0:T(8,128)}, f32[512,1024]{1,0:T(8,128)}, u32[]{:S(2)}, u32[]{:S(2)}) collective-permute-start(f32[512,1024]{1,0:T(8,128)} %fusion.79), channel_id=1, source_target_pairs={{0,1},{1,0},{2,3},{3,2},{4,5},{5,4},{6,7},{7,6},{8,9},{9,8},{10,11... | collective-permute-start | bytes 6291464 | tf_op jit(solution)/shard_map/ppermute | solution.py:27
  61.7 8.3 %collective-permute-start.6 = (f32[512,1024]{1,0:T(8,128)}, f32[512,1024]{1,0:T(8,128)}, u32[]{:S(2)}, u32[]{:S(2)}) collective-permute-start(f32[512,1024]{1,0:T(8,128)} %fusion.75), channel_id=1, source_target_pairs={{0,1},{1,0},{2,3},{3,2},{4,5},{5,4},{6,7},{7,6},{8,9},{9,8},{10,11... | collective-permute-start | bytes 6291464 | tf_op jit(solution)/shard_map/ppermute | solution.py:27
  66.6 25.4 %collective-permute-start.5 = (bf16[512,1024]{1,0:T(8,128)(2,1)}, bf16[512,1024]{1,0:T(8,128)(2,1)S(1)}, u32[]{:S(2)}, u32[]{:S(2)}) collective-permute-start(bf16[512,1024]{1,0:T(8,128)(2,1)} %add_convert_fusion.3), channel_id=1, source_target_pairs={{0,2},{1,3},{2,0},{3,1},{4,6},{5,7},{6,4},{7,5},{8,10},{9,11},{10,... | collective-permute-start | bytes 3145736 | tf_op jit(solution)/shard_map/ppermute | solution.py:33
  70.0 48.8 %copy-start.19 = (f32[4096]{0:T(1024)S(1)}, f32[4096]{0:T(1024)}, u32[]{:S(2)}) copy-start(f32[4096]{0:T(1024)} %param.18) | copy-start | bytes 49156
  70.0 48.9 %copy-start.18 = (bf16[4096,64]{0,1:T(8,128)(2,1)S(1)}, bf16[4096,64]{0,1:T(8,128)(2,1)}, u32[]{:S(2)}) copy-start(bf16[4096,64]{0,1:T(8,128)(2,1)} %param.19) | copy-start | bytes 1572868
  70.0 49.0 %copy-start.2 = (bf16[4096,512]{1,0:T(8,128)(2,1)S(1)}, bf16[4096,512]{1,0:T(8,128)(2,1)}, u32[]{:S(2)}) copy-start(bf16[4096,512]{1,0:T(8,128)(2,1)} %param.20) | copy-start | bytes 12582916
  94.3 24.4 %collective-permute-start.7 = (bf16[512,1024]{1,0:T(8,128)(2,1)S(1)}, bf16[512,1024]{1,0:T(8,128)(2,1)S(1)}, u32[]{:S(2)}, u32[]{:S(2)}) collective-permute-start(bf16[512,1024]{1,0:T(8,128)(2,1)S(1)} %add_convert_fusion.2), channel_id=1, source_target_pairs={{0,2},{1,3},{2,0},{3,1},{4,6},{5,7},{6,4},{7,5},{8,10},{9,11},{10,... | collective-permute-start | bytes 3145736 | tf_op jit(solution)/shard_map/ppermute | solution.py:33
  95.9 23.4 %collective-permute-start.8 = (bf16[512,1024]{1,0:T(8,128)(2,1)S(1)}, bf16[512,1024]{1,0:T(8,128)(2,1)S(1)}, u32[]{:S(2)}, u32[]{:S(2)}) collective-permute-start(bf16[512,1024]{1,0:T(8,128)(2,1)S(1)} %add_convert_fusion.2), channel_id=1, source_target_pairs={{0,1},{1,0},{2,3},{3,2},{4,5},{5,4},{6,7},{7,6},{8,9},{9,8},{10,11... | collective-permute-start | bytes 3145736 | tf_op jit(solution)/shard_map/ppermute | solution.py:27
  118.8 2.7 %collective-permute-start.9 = (bf16[512,1024]{1,0:T(8,128)(2,1)S(1)}, bf16[512,1024]{1,0:T(8,128)(2,1)S(1)}, u32[]{:S(2)}, u32[]{:S(2)}) collective-permute-start(bf16[512,1024]{1,0:T(8,128)(2,1)S(1)} %collective-permute-done.7), channel_id=1, source_target_pairs={{0,1},{1,0},{2,3},{3,2},{4,5},{5,4},{6,7},{7,6},{8,9},{9,8},{10,11... | collective-permute-start | bytes 3145736 | tf_op jit(solution)/shard_map/ppermute | solution.py:27
  127.7 29.2 %copy-start.9 = (f32[2,273,256]{2,0,1:T(2,128)S(1)}, f32[2,273,256]{2,0,1:T(2,128)}, u32[]{:S(2)}) copy-start(f32[2,273,256]{2,0,1:T(2,128)} %param.23) | copy-start | bytes 1677316
  127.7 11.2 %collective-permute-start.10 = (bf16[2,273,256]{2,1,0:T(8,128)(2,1)S(1)}, bf16[2,273,256]{2,1,0:T(8,128)(2,1)S(1)}, u32[]{:S(2)}, u32[]{:S(2)}) collective-permute-start(bf16[2,273,256]{2,1,0:T(8,128)(2,1)S(1)} %convolution_convert_fusion.1), channel_id=1, source_target_pairs={{0,4},{4,8},{8,12},{1,5},{5,9},{9,13},{2,6},{6,10},{10,14},{3,7},{... | collective-permute-start | bytes 838664 | tf_op jit(solution)/shard_map/ppermute | solution.py:93
  129.2 27.8 %collective-permute-start.11 = (bf16[2,273,256]{2,1,0:T(8,128)(2,1)S(1)}, bf16[2,273,256]{2,1,0:T(8,128)(2,1)S(1)}, u32[]{:S(2)}, u32[]{:S(2)}) collective-permute-start(bf16[2,273,256]{2,1,0:T(8,128)(2,1)S(1)} %convolution_convert_fusion.1), channel_id=1, source_target_pairs={{0,8},{4,12},{1,9},{5,13},{2,10},{6,14},{3,11},{7,15},{16,24},{20,... | collective-permute-start | bytes 838664 | tf_op jit(solution)/shard_map/ppermute | solution.py:93
  130.5 26.5 %collective-permute-start.12 = (bf16[2,273,256]{2,1,0:T(8,128)(2,1)S(1)}, bf16[2,273,256]{2,1,0:T(8,128)(2,1)S(1)}, u32[]{:S(2)}, u32[]{:S(2)}) collective-permute-start(bf16[2,273,256]{2,1,0:T(8,128)(2,1)S(1)} %convolution_convert_fusion.1), channel_id=1, source_target_pairs={{0,12},{1,13},{2,14},{3,15},{16,28},{17,29},{18,30},{19,31}} | collective-permute-start | bytes 838664 | tf_op jit(solution)/shard_map/ppermute | solution.py:93
  134.1 25.0 %copy-start.20 = (f32[2,256]{1,0:T(2,128)S(1)}, f32[2,256]{1,0:T(2,128)}, u32[]{:S(2)}) copy-start(f32[2,256]{1,0:T(2,128)} %param.21) | copy-start | bytes 6148
  134.3 25.1 %copy-start.1 = (bf16[512,4096]{1,0:T(8,128)(2,1)S(1)}, bf16[512,4096]{1,0:T(8,128)(2,1)}, u32[]{:S(2)}) copy-start(bf16[512,4096]{1,0:T(8,128)(2,1)} %param.22) | copy-start | bytes 12582916
  160.1 4.2 %collective-permute-start.13 = (f32[512,1024]{1,0:T(8,128)S(1)}, f32[512,1024]{1,0:T(8,128)S(1)}, u32[]{:S(2)}, u32[]{:S(2)}) collective-permute-start(f32[512,1024]{1,0:T(8,128)S(1)} %fusion.72), channel_id=1, source_target_pairs={{0,1},{1,0},{2,3},{3,2},{4,5},{5,4},{6,7},{7,6},{8,9},{9,8},{10,11... | collective-permute-start | bytes 6291464 | tf_op jit(solution)/shard_map/ppermute | solution.py:27
  160.9 6.4 %collective-permute-start.15 = (f32[512,1024]{1,0:T(8,128)S(1)}, f32[512,1024]{1,0:T(8,128)S(1)}, u32[]{:S(2)}, u32[]{:S(2)}) collective-permute-start(f32[512,1024]{1,0:T(8,128)S(1)} %fusion.68), channel_id=1, source_target_pairs={{0,1},{1,0},{2,3},{3,2},{4,5},{5,4},{6,7},{7,6},{8,9},{9,8},{10,11... | collective-permute-start | bytes 6291464 | tf_op jit(solution)/shard_map/ppermute | solution.py:27
  165.0 25.3 %collective-permute-start.14 = (bf16[512,1024]{1,0:T(8,128)(2,1)S(1)}, bf16[512,1024]{1,0:T(8,128)(2,1)S(1)}, u32[]{:S(2)}, u32[]{:S(2)}) collective-permute-start(bf16[512,1024]{1,0:T(8,128)(2,1)S(1)} %add_convert_fusion.1), channel_id=1, source_target_pairs={{0,2},{1,3},{2,0},{3,1},{4,6},{5,7},{6,4},{7,5},{8,10},{9,11},{10,... | collective-permute-start | bytes 3145736 | tf_op jit(solution)/shard_map/ppermute | solution.py:33
  (13 other events, 32.1 us)

commit v11 on v6

--- a/solution.py
+++ b/solution.py
@@ -53,6 +53,31 @@
         got = chip_shift(acc.astype(jnp.bfloat16), 1).astype(jnp.float32)
         acc = got + on_chip[(chips - step - 2) % chips]
     return acc
+
+
+def residual_exchange(lhs, weight, whole, piece):
+    devices, chips = head_layout()
+    me = lax.axis_index("head")
+    core, chip = me % 2, me // 2
+    width = weight.shape[1] // devices
+
+    def on_chip_sum(offset):
+        sums = []
+        for which in (core, 1 - core):
+            col = (((chip + offset) % chips) * 2 + which) * width
+            cols = lax.dynamic_slice_in_dim(weight, col, width, axis=1)
+            sums.append(jnp.dot(lhs, cols, preferred_element_type=jnp.float32))
+        return sums[0] + core_swap(sums[1])
+
+    there, here = on_chip_sum(1), on_chip_sum(0)
+    sent = jnp.concatenate([there, here], axis=1).astype(jnp.bfloat16)
+    got = chip_shift(sent, 1).astype(jnp.float32)
+    mine = (piece.astype(jnp.float32) + here + got[:, :width]).astype(jnp.bfloat16)
+    other = (whole[:, width : 2 * width].astype(jnp.float32) + there + got[:, width:]).astype(
+        jnp.bfloat16
+    )
+    pair = jnp.concatenate([mine, other], axis=1)
+    return mine, jnp.concatenate([pair, core_swap(pair)], axis=1)
 
 
 def gather_sources():
@@ -143,8 +168,10 @@
     wv_linear = gathered_rows(wv_linear)
 
     query_parts, kv_parts = [], []
+    hidden_wholes = []
     for part in hidden_parts:
-        normed = norm_rows(head_all_gather(part), attn_gain)
+        hidden_wholes.append(head_all_gather(part))
+        normed = norm_rows(hidden_wholes[-1], attn_gain)
         query_parts.append(
             jnp.dot(normed, w_query, preferred_element_type=jnp.float32).astype(jnp.bfloat16)
         )
@@ -179,10 +206,16 @@
             "kgts,skd->tkgd", probs, value_win, preferred_element_type=jnp.float32
         )
         attended = attended.astype(jnp.bfloat16).reshape(size, -1)
-        partial_out = head_reduce_scatter(attended, wo_attn)
-        after_window = (hidden_parts[i].astype(jnp.float32) + partial_out).astype(jnp.bfloat16)
+        if head_layout()[1] == 2:
+            after_window, after_whole = residual_exchange(
+                attended, wo_attn, hidden_wholes[i], hidden_parts[i]
+            )
+        else:
+            partial_out = head_reduce_scatter(attended, wo_attn)
+            after_window = (hidden_parts[i].astype(jnp.float32) + partial_out).astype(jnp.bfloat16)
+            after_whole = head_all_gather(after_window)
         after_parts.append(after_window)
-        after_whole_parts.append(head_all_gather(after_window))
+        after_whole_parts.append(after_whole)
 
     qf_parts, kf_parts, lv_parts = [], [], []
     for i in range(CHUNKS):

time: 190 us -> 194 us (1.021)
  waiting for transfers between devices: 123 us -> 125 us
    dot_general x8 -> x4, matrix products: 15.1 us -> 2.99 us  [block(): return jnp.dot(lhs, cols, preferred_element_type=jnp.float32)]
    dot_general x0 -> x4, matrix products: none -> 11.9 us  [on_chip_sum(): sums.append(jnp.dot(lhs, cols, preferred_element_type=jnp.float32))]
    ppermute x4 -> x3, waiting for transfers between devices: 91.4 us -> 93 us  [chip_shift(): return lax.ppermute(value, 'head', pairs)]
    ppermute x4 -> x3, starting transfers between devices: 6.09 us -> 4.61 us  [chip_shift(): return lax.ppermute(value, 'head', pairs)]
    ppermute x8 -> x7, waiting for transfers between devices: 5.71 us -> 6.25 us  [core_swap(): return lax.ppermute(value, 'head', [(h, h ^ 1) for h in range(devices)])]
    dynamic_slice x6 -> x5, local copies, waits for them, and re-layouts: 4.02 us -> 4.05 us  [gathered_rows(): lax.dynamic_slice_in_dim(weight, src * block, block, axis=0)]
  transfers between devices with their start and end apart: 16 -> 14, of which waited for: 10 -> 11; matrix products, arithmetic and copies ran while one was open for 11% -> 10% of each run, Pallas kernels for 0% -> 0%
where the time goes in v11:
time: 194 us
  waiting for transfers between devices  125 us (64%)
  matrix products  38.6 us (20%)
  starting transfers between devices  11.3 us (6%)
  other arithmetic  10.9 us (6%)
  local copies, waits for them, and re-layouts  7.31 us (4%)
    ppermute x3, waiting for transfers between devices, chip_shift(): return lax.ppermute(value, 'head', pairs)  93 us
    ppermute x3, waiting for transfers between devices, earlier_sum(): total = total + lax.ppermute(sent, 'ctx', pairs).astype(jnp.float32)  22.9 us
    dot_general x4, matrix products, on_chip_sum(): sums.append(jnp.dot(lhs, cols, preferred_element_type=jnp.float32))  11.9 us
    ppermute x7, waiting for transfers between devices, core_swap(): return lax.ppermute(value, 'head', [(h, h ^ 1) for h in range(devices)])  6.25 us
    sub x1, matrix products, body(): expd = jnp.exp(scores - top)  4.98 us
    ppermute x3, starting transfers between devices, chip_shift(): return lax.ppermute(value, 'head', pairs)  4.61 us
    dynamic_slice x5, local copies, waits for them, and re-layouts, gathered_rows(): lax.dynamic_slice_in_dim(weight, src * block, block, axis=0)  4.05 us
    ppermute x3, starting transfers between devices, earlier_sum(): total = total + lax.ppermute(sent, 'ctx', pairs).astype(jnp.float32)  4.01 us
  transfers between devices with their start and end apart: 14, of which 11 were waited for; matrix products, arithmetic and copies ran while one was open for 10% of the time, Pallas kernels for 0%

profile of v11, /device:TPU:24, one launch (start us, length us, event | category | flops | bytes accessed | tf_op | source)
XLA Modules:
  0.0 193.6 jit_solution(9833717300495528003)
XLA Ops:
  1.5 23.6 %collective-permute-done = bf16[512,1024]{1,0:T(8,128)(2,1)S(1)} collective-permute-done((bf16[512,1024]{1,0:T(8,128)(2,1)}, bf16[512,1024]{1,0:T(8,128)(2,1)S(1)}, u32[]{:S(2)}, u32[]{:S(2)}) %collective-permute-start) | collective-permute-done | bytes 1048608 | tf_op jit(solution)/shard_map/ppermute | solution.py:33
  26.0 2.6 %constant_dynamic-slice_fusion.11 = (bf16[1024,512]{1,0:T(8,128)(2,1)S(1)}, bf16[1024,512]{1,0:T(8,128)(2,1)S(1)}, bf16[1024,512]{1,0:T(8,128)(2,1)S(1)}, bf16[1024,512]{1,0:T(8,128)(2,1)S(1)}) fusion(bf16[4096,512]{1,0:T(8,128)(2,1)} %param.14, s32[]{:T(128)S(6)} %select_n.127, s32[]{:T(128)S(6)} %select_n.131, s32[]{:T(128)S(6)} %select_n.133, ...), kind=kLoop, calls=%fused_computation.143 | loop fusion | bytes 8388624 | tf_op jit(solution)/shard_map/dynamic_slice | solution.py:107
  30.7 2.0 %fusion.1 = f32[512]{0:T(512)S(1)} fusion(bf16[512,1024]{1,0:T(8,128)(2,1)} %collective-permute-done.2, bf16[512,1024]{1,0:T(8,128)(2,1)S(1)} %collective-permute-done.1, bf16[512,1024]{1,0:T(8,128)(2,1)S(1)} %collective-permute-done, bf16[512,1024]{1,0:T(8,128)(2,1)S(1)} %copy-done), kind=kLoop, calls=%fused_computation.5 | loop fusion | flops 20971008 | bytes 4196352 | tf_op jit(solution)/shard_map/reduce_sum | solution.py:124
  32.8 2.4 %fusion.3 = bf16[512,4096]{1,0:T(8,128)(2,1)S(1)} fusion(f32[4096]{0:T(1024)S(1)} %pad_maximum_fusion.5, f32[512]{0:T(512)S(1)} %add_rsqrt_fusion.2, bf16[512,1024]{1,0:T(8,128)(2,1)} %collective-permute-done.2, bf16[512,1024]{1,0:T(8,128)(2,1)S(1)} %collective-permute-done.1, bf16[512,1024]{1,0:T(8,128)(2,1)S(1)} %collective-permute-done, ...), kind=kLoop, calls=%fused_computation.7 | loop fusion | flops 23068672 | bytes 8407040 | tf_op jit(solution)/shard_map/convert_element_type | solution.py:125
  39.4 3.4 %fusion.50 = bf16[512,512]{0,1:T(8,128)(2,1)} fusion(bf16[512,4096]{1,0:T(8,128)(2,1)S(1)} %fusion.3, bf16[1024,512]{1,0:T(8,128)(2,1)S(1)} %get-tuple-element.9, bf16[1024,512]{1,0:T(8,128)(2,1)S(1)} %get-tuple-element.10, bf16[1024,512]{1,0:T(8,128)(2,1)S(1)} %get-tuple-element.8, bf16[1024,512]{1,0:T(8,128)(2,1)S(1)} %get-tuple-element.7), kind=kOutput, calls=%fused_computation.67 | convolution fusion | flops 2164523008 | bytes 8912896 | tf_op jit(solution)/shard_map/dot_general | solution.py:176
  42.8 2.9 %collective-permute-done.3 = bf16[64,512]{0,1:T(8,128)(2,1)S(1)} collective-permute-done((bf16[64,512]{0,1:T(8,128)(2,1)S(1)}, bf16[64,512]{0,1:T(8,128)(2,1)S(1)}, u32[]{:S(2)}, u32[]{:S(2)}) %collective-permute-start.3) | collective-permute-done | bytes 65568 | tf_op jit(solution)/shard_map/ppermute | solution.py:17
  46.1 5.0 %fusion.120 = (f32[2,2,512]{2,1,0:T(2,128)S(1)}, f32[2,2,512,576]{2,3,1,0:T(8,128)}) fusion(pred[512,576]{0,1:T(8,128)(4,1)S(1)} %and_and_fusion, bf16[576,2,128,1]{0,2,3,1:T(8,128)(2,1)S(1)} %bitcast.82, bf16[512,2,2,128]{0,3,2,1:T(8,128)(2,1)} %bitcast.83), kind=kOutput, calls=%fused_computation.171 | convolution fusion | flops 306709056 | bytes 5840896 | tf_op jit(solution)/shard_map/sub | solution.py:203
  51.1 2.9 %fusion.53 = bf16[2,128,2,512]{3,1,2,0:T(8,128)(2,1)S(1)} fusion(bf16[576,2,128,1]{0,2,3,1:T(8,128)(2,1)S(1)} %bitcast.81, f32[2,2,512,576]{2,3,1,0:T(8,128)} %get-tuple-element.42, f32[2,2,512]{2,1,0:T(2,128)S(1)} %get-tuple-element.41), kind=kOutput, calls=%fused_computation.68 | convolution fusion | flops 304611328 | bytes 5545984 | tf_op jit(solution)/shard_map/kgts,skd->tkgd/dot_general | solution.py:205
  54.0 3.3 %fusion.75 = f32[512,1024]{1,0:T(8,128)} fusion(bf16[512,512]{0,1:T(8,128)(2,1)S(1)} %bitcast.70, bf16[512,4096]{1,0:T(8,128)(2,1)} %param.17, s32[]{:T(128)S(6)} %select_n.138), kind=kOutput, calls=%fused_computation.93 | convolution fusion | flops 536870912 | bytes 3670020 | tf_op jit(solution)/shard_map/dot_general | solution.py:69
  57.3 3.3 %fusion.78 = f32[512,1024]{1,0:T(8,128)} fusion(bf16[512,512]{0,1:T(8,128)(2,1)S(1)} %bitcast.71, bf16[512,4096]{1,0:T(8,128)(2,1)} %param.17, s32[]{:T(128)S(6)} %select_n.137), kind=kOutput, calls=%fused_computation.96 | convolution fusion | flops 536870912 | bytes 3670020 | tf_op jit(solution)/shard_map/dot_general | solution.py:69
  61.8 2.7 %fusion.122 = (bf16[512,1024]{1,0:T(8,128)(2,1)S(1)}, f32[512,1024]{1,0:T(8,128)S(1)}) fusion(f32[512,1024]{1,0:T(8,128)} %collective-permute-done.5, bf16[512,512]{0,1:T(8,128)(2,1)S(1)} %bitcast.72, bf16[512,4096]{1,0:T(8,128)(2,1)} %param.17, s32[]{:T(128)S(6)} %select_n.131), kind=kOutput, calls=%fused_computation.173 | convolution fusion | flops 537919488 | bytes 6815748 | tf_op jit(solution)/shard_map/dot_general | solution.py:69
  65.2 2.7 %fusion.121 = (bf16[512,1024]{1,0:T(8,128)(2,1)S(1)}, f32[512,1024]{1,0:T(8,128)S(1)}) fusion(f32[512,1024]{1,0:T(8,128)} %collective-permute-done.4, bf16[512,512]{0,1:T(8,128)(2,1)S(1)} %bitcast.73, bf16[512,4096]{1,0:T(8,128)(2,1)} %param.17, s32[]{:T(128)S(6)} %select_n.136), kind=kOutput, calls=%fused_computation.172 | convolution fusion | flops 537919488 | bytes 6815748 | tf_op jit(solution)/shard_map/dot_general | solution.py:69
  69.7 46.4 %collective-permute-done.6 = bf16[512,2048]{1,0:T(8,128)(2,1)S(1)} collective-permute-done((bf16[512,2048]{1,0:T(8,128)(2,1)S(1)}, bf16[512,2048]{1,0:T(8,128)(2,1)S(1)}, u32[]{:S(2)}, u32[]{:S(2)}) %collective-permute-start.6) | collective-permute-done | bytes 2097184 | tf_op jit(solution)/shard_map/ppermute | solution.py:33
  118.4 1.8 copy-done.2
  120.5 1.9 collective-permute-done.7
  125.3 2.6 %fusion.47 = bf16[512,512]{0,1:T(8,128)(2,1)S(1)} fusion(bf16[1024,512]{1,0:T(8,128)(2,1)S(1)} %get-tuple-element.13, bf16[1024,512]{1,0:T(8,128)(2,1)S(1)} %get-tuple-element.14, bf16[1024,512]{1,0:T(8,128)(2,1)S(1)} %get-tuple-element.12, bf16[1024,512]{1,0:T(8,128)(2,1)S(1)} %get-tuple-element.11, f32[4096]{0:T(1024)S(1)} %pad_maximum_fusion.6, ...), kind=kOutput, calls=%fused_computation.66 | convolution fusion | flops 2183397376 | bytes 8931328 | tf_op jit(solution)/shard_map/dot_general | solution.py:229
  132.7 2.3 %select_convert_fusion = bf16[2,512,512]{2,1,0:T(8,128)(2,1)S(1)} fusion(pred[512,512]{1,0:T(8,128)(4,1)S(1)} %iota_compare_fusion, f32[512,2,2,16]{0,3,2,1:T(8,128)S(1)} %bitcast.80), kind=kOutput, calls=%fused_computation.61 | convolution fusion | flops 104333312 | bytes 1441792 | tf_op jit(solution)/shard_map/thf,shf->hts/dot_general | solution.py:248
  135.7 6.5 %collective-permute-done.10 = bf16[2,273,256]{2,1,0:T(8,128)(2,1)S(1)} collective-permute-done((bf16[2,273,256]{2,1,0:T(8,128)(2,1)S(1)}, bf16[2,273,256]{2,1,0:T(8,128)(2,1)S(1)}, u32[]{:S(2)}, u32[]{:S(2)}) %collective-permute-start.10) | collective-permute-done | bytes 279584 | tf_op jit(solution)/shard_map/ppermute | solution.py:118
  142.2 6.0 %collective-permute-done.8 = bf16[2,273,256]{2,1,0:T(8,128)(2,1)S(1)} collective-permute-done((bf16[2,273,256]{2,1,0:T(8,128)(2,1)S(1)}, bf16[2,273,256]{2,1,0:T(8,128)(2,1)S(1)}, u32[]{:S(2)}, u32[]{:S(2)}) %collective-permute-start.8) | collective-permute-done | bytes 279584 | tf_op jit(solution)/shard_map/ppermute | solution.py:118
  148.2 10.4 %collective-permute-done.9 = bf16[2,273,256]{2,1,0:T(8,128)(2,1)S(1)} collective-permute-done((bf16[2,273,256]{2,1,0:T(8,128)(2,1)S(1)}, bf16[2,273,256]{2,1,0:T(8,128)(2,1)S(1)}, u32[]{:S(2)}, u32[]{:S(2)}) %collective-permute-start.9) | collective-permute-done | bytes 279584 | tf_op jit(solution)/shard_map/ppermute | solution.py:118
  158.6 2.2 %multiply_reduce_fusion = (f32[512,2]{0,1:T(2,128)S(1)}, f32[512,2,256]{0,2,1:T(8,128)S(1)}) fusion(f32[2,256,512]{2,1,0:T(8,128)S(1)} %fusion.123, f32[512,2,256]{0,2,1:T(8,128)S(1)} %bitcast.74, f32[512,2,16]{0,2,1:T(8,128)S(1)} %get-tuple-element.30, f32[273]{0:T(512)S(1)} %pad.7.clone, f32[2,273,256]{2,0,1:T(2,128)S(1)} %copy-done.5, ...), kind=kOutput, calls=%fused_computation.89 | convolution fusion | flops 860966912 | bytes 4614212 | tf_op jit(solution)/shard_map/thf,hfv->thv/dot_general | solution.py:247
  163.1 2.8 %collective-permute-done.11 = f32[512,1024]{1,0:T(8,128)S(1)} collective-permute-done((f32[512,1024]{1,0:T(8,128)S(1)}, f32[512,1024]{1,0:T(8,128)S(1)}, u32[]{:S(2)}, u32[]{:S(2)}) %collective-permute-start.11) | collective-permute-done | bytes 2097184 | tf_op jit(solution)/shard_map/ppermute | solution.py:27
  169.0 23.0 %collective-permute-done.12 = bf16[512,1024]{1,0:T(8,128)(2,1)S(1)} collective-permute-done((bf16[512,1024]{1,0:T(8,128)(2,1)S(1)}, bf16[512,1024]{1,0:T(8,128)(2,1)S(1)}, u32[]{:S(2)}, u32[]{:S(2)}) %collective-permute-start.12) | collective-permute-done | bytes 1048608 | tf_op jit(solution)/shard_map/ppermute | solution.py:33
  192.0 1.7 add_convert_fusion
  (71 shorter events, 28.8 us)
Async XLA Ops:
  0.0 25.1 %collective-permute-start = (bf16[512,1024]{1,0:T(8,128)(2,1)}, bf16[512,1024]{1,0:T(8,128)(2,1)S(1)}, u32[]{:S(2)}, u32[]{:S(2)}) collective-permute-start(bf16[512,1024]{1,0:T(8,128)(2,1)} %param.12), channel_id=1, source_target_pairs={{0,2},{1,3},{2,0},{3,1},{4,6},{5,7},{6,4},{7,5},{8,10},{9,11},{10,... | collective-permute-start | bytes 3145736 | tf_op jit(solution)/shard_map/ppermute | solution.py:33
  1.5 28.7 %collective-permute-start.1 = (bf16[512,1024]{1,0:T(8,128)(2,1)}, bf16[512,1024]{1,0:T(8,128)(2,1)S(1)}, u32[]{:S(2)}, u32[]{:S(2)}) collective-permute-start(bf16[512,1024]{1,0:T(8,128)(2,1)} %param.12), channel_id=1, source_target_pairs={{0,1},{1,0},{2,3},{3,2},{4,5},{5,4},{6,7},{7,6},{8,9},{9,8},{10,11... | collective-permute-start | bytes 3145736 | tf_op jit(solution)/shard_map/ppermute | solution.py:27
  25.1 5.1 %collective-permute-start.2 = (bf16[512,1024]{1,0:T(8,128)(2,1)S(1)}, bf16[512,1024]{1,0:T(8,128)(2,1)}, u32[]{:S(2)}, u32[]{:S(2)}) collective-permute-start(bf16[512,1024]{1,0:T(8,128)(2,1)S(1)} %collective-permute-done), channel_id=1, source_target_pairs={{0,1},{1,0},{2,3},{3,2},{4,5},{5,4},{6,7},{7,6},{8,9},{9,8},{10,11... | collective-permute-start | bytes 3145736 | tf_op jit(solution)/shard_map/ppermute | solution.py:27
  26.0 2.9 %copy-start.3 = (bf16[4096,256]{1,0:T(8,128)(2,1)S(1)}, bf16[4096,256]{1,0:T(8,128)(2,1)}, u32[]{:S(2)}) copy-start(bf16[4096,256]{1,0:T(8,128)(2,1)} %param.16) | copy-start | bytes 6291460
  26.0 3.5 %copy-start.4 = (bf16[4096,256]{1,0:T(8,128)(2,1)S(1)}, bf16[4096,256]{1,0:T(8,128)(2,1)}, u32[]{:S(2)}) copy-start(bf16[4096,256]{1,0:T(8,128)(2,1)} %param.15) | copy-start | bytes 6291460
  29.5 1.2 copy-start
  38.0 7.7 %collective-permute-start.3 = (bf16[64,512]{0,1:T(8,128)(2,1)S(1)}, bf16[64,512]{0,1:T(8,128)(2,1)S(1)}, u32[]{:S(2)}, u32[]{:S(2)}) collective-permute-start(bf16[64,512]{0,1:T(8,128)(2,1)S(1)} %pad_maximum_fusion.4), channel_id=1, source_target_pairs={{0,4},{4,8},{8,12},{1,5},{5,9},{9,13},{2,6},{6,10},{10,14},{3,7},{... | collective-permute-start | bytes 196616 | tf_op jit(solution)/shard_map/ppermute | solution.py:17
  57.3 4.5 %collective-permute-start.5 = (f32[512,1024]{1,0:T(8,128)}, f32[512,1024]{1,0:T(8,128)}, u32[]{:S(2)}, u32[]{:S(2)}) collective-permute-start(f32[512,1024]{1,0:T(8,128)} %fusion.75), channel_id=1, source_target_pairs={{0,1},{1,0},{2,3},{3,2},{4,5},{5,4},{6,7},{7,6},{8,9},{9,8},{10,11... | collective-permute-start | bytes 6291464 | tf_op jit(solution)/shard_map/ppermute | solution.py:27
  60.6 4.6 %collective-permute-start.4 = (f32[512,1024]{1,0:T(8,128)}, f32[512,1024]{1,0:T(8,128)}, u32[]{:S(2)}, u32[]{:S(2)}) collective-permute-start(f32[512,1024]{1,0:T(8,128)} %fusion.78), channel_id=1, source_target_pairs={{0,1},{1,0},{2,3},{3,2},{4,5},{5,4},{6,7},{7,6},{8,9},{9,8},{10,11... | collective-permute-start | bytes 6291464 | tf_op jit(solution)/shard_map/ppermute | solution.py:27
  68.1 48.0 %collective-permute-start.6 = (bf16[512,2048]{1,0:T(8,128)(2,1)S(1)}, bf16[512,2048]{1,0:T(8,128)(2,1)S(1)}, u32[]{:S(2)}, u32[]{:S(2)}) collective-permute-start(bf16[512,2048]{1,0:T(8,128)(2,1)S(1)} %pad_maximum_fusion.2), channel_id=1, source_target_pairs={{0,2},{1,3},{2,0},{3,1},{4,6},{5,7},{6,4},{7,5},{8,10},{9,11},{10,... | collective-permute-start | bytes 6291464 | tf_op jit(solution)/shard_map/ppermute | solution.py:33
  116.6 1.8 copy-start.6
  118.0 2.2 %copy-start.2 = (bf16[4096,512]{1,0:T(8,128)(2,1)S(1)}, bf16[4096,512]{1,0:T(8,128)(2,1)}, u32[]{:S(2)}) copy-start(bf16[4096,512]{1,0:T(8,128)(2,1)} %param.20) | copy-start | bytes 12582916
  118.2 4.2 %collective-permute-start.7 = (bf16[512,2048]{1,0:T(8,128)(2,1)S(1)}, bf16[512,2048]{1,0:T(8,128)(2,1)S(1)}, u32[]{:S(2)}, u32[]{:S(2)}) collective-permute-start(bf16[512,2048]{1,0:T(8,128)(2,1)S(1)} %pad_maximum_fusion.3), channel_id=1, source_target_pairs={{0,1},{1,0},{2,3},{3,2},{4,5},{5,4},{6,7},{7,6},{8,9},{9,8},{10,11... | collective-permute-start | bytes 6291464 | tf_op jit(solution)/shard_map/ppermute | solution.py:27
  128.7 29.9 %copy-start.5 = (f32[2,273,256]{2,0,1:T(2,128)S(1)}, f32[2,273,256]{2,0,1:T(2,128)}, u32[]{:S(2)}) copy-start(f32[2,273,256]{2,0,1:T(2,128)} %param.23) | copy-start | bytes 1677316
  128.7 13.6 %collective-permute-start.10 = (bf16[2,273,256]{2,1,0:T(8,128)(2,1)S(1)}, bf16[2,273,256]{2,1,0:T(8,128)(2,1)S(1)}, u32[]{:S(2)}, u32[]{:S(2)}) collective-permute-start(bf16[2,273,256]{2,1,0:T(8,128)(2,1)S(1)} %convolution_convert_fusion), channel_id=1, source_target_pairs={{0,12},{1,13},{2,14},{3,15},{16,28},{17,29},{18,30},{19,31}} | collective-permute-start | bytes 838664 | tf_op jit(solution)/shard_map/ppermute | solution.py:118
  130.1 18.1 %collective-permute-start.8 = (bf16[2,273,256]{2,1,0:T(8,128)(2,1)S(1)}, bf16[2,273,256]{2,1,0:T(8,128)(2,1)S(1)}, u32[]{:S(2)}, u32[]{:S(2)}) collective-permute-start(bf16[2,273,256]{2,1,0:T(8,128)(2,1)S(1)} %convolution_convert_fusion), channel_id=1, source_target_pairs={{0,4},{4,8},{8,12},{1,5},{5,9},{9,13},{2,6},{6,10},{10,14},{3,7},{... | collective-permute-start | bytes 838664 | tf_op jit(solution)/shard_map/ppermute | solution.py:118
  131.4 27.2 %collective-permute-start.9 = (bf16[2,273,256]{2,1,0:T(8,128)(2,1)S(1)}, bf16[2,273,256]{2,1,0:T(8,128)(2,1)S(1)}, u32[]{:S(2)}, u32[]{:S(2)}) collective-permute-start(bf16[2,273,256]{2,1,0:T(8,128)(2,1)S(1)} %convolution_convert_fusion), channel_id=1, source_target_pairs={{0,8},{4,12},{1,9},{5,13},{2,10},{6,14},{3,11},{7,15},{16,24},{20,... | collective-permute-start | bytes 838664 | tf_op jit(solution)/shard_map/ppermute | solution.py:118
  135.1 25.7 %copy-start.7 = (f32[2,256]{1,0:T(2,128)S(1)}, f32[2,256]{1,0:T(2,128)}, u32[]{:S(2)}) copy-start(f32[2,256]{1,0:T(2,128)} %param.21) | copy-start | bytes 6148
  135.2 25.7 %copy-start.1 = (bf16[512,4096]{1,0:T(8,128)(2,1)S(1)}, bf16[512,4096]{1,0:T(8,128)(2,1)}, u32[]{:S(2)}) copy-start(bf16[512,4096]{1,0:T(8,128)(2,1)} %param.22) | copy-start | bytes 12582916
  161.7 4.2 %collective-permute-start.11 = (f32[512,1024]{1,0:T(8,128)S(1)}, f32[512,1024]{1,0:T(8,128)S(1)}, u32[]{:S(2)}, u32[]{:S(2)}) collective-permute-start(f32[512,1024]{1,0:T(8,128)S(1)} %fusion.72), channel_id=1, source_target_pairs={{0,1},{1,0},{2,3},{3,2},{4,5},{5,4},{6,7},{7,6},{8,9},{9,8},{10,11... | collective-permute-start | bytes 6291464 | tf_op jit(solution)/shard_map/ppermute | solution.py:27
  162.5 6.5 %collective-permute-start.13 = (f32[512,1024]{1,0:T(8,128)S(1)}, f32[512,1024]{1,0:T(8,128)S(1)}, u32[]{:S(2)}, u32[]{:S(2)}) collective-permute-start(f32[512,1024]{1,0:T(8,128)S(1)} %fusion.68), channel_id=1, source_target_pairs={{0,1},{1,0},{2,3},{3,2},{4,5},{5,4},{6,7},{7,6},{8,9},{9,8},{10,11... | collective-permute-start | bytes 6291464 | tf_op jit(solution)/shard_map/ppermute | solution.py:27
  166.7 25.3 %collective-permute-start.12 = (bf16[512,1024]{1,0:T(8,128)(2,1)S(1)}, bf16[512,1024]{1,0:T(8,128)(2,1)S(1)}, u32[]{:S(2)}, u32[]{:S(2)}) collective-permute-start(bf16[512,1024]{1,0:T(8,128)(2,1)S(1)} %add_convert_fusion.1), channel_id=1, source_target_pairs={{0,2},{1,3},{2,0},{3,1},{4,6},{5,7},{6,4},{7,5},{8,10},{9,11},{10,... | collective-permute-start | bytes 3145736 | tf_op jit(solution)/shard_map/ppermute | solution.py:33

commit v12 on v6

--- a/solution.py
+++ b/solution.py
@@ -86,11 +86,15 @@
 
 def earlier_sum(local):
     count = lax.axis_size("ctx")
-    sent = local.astype(jnp.bfloat16)
+    running = local
     total = jnp.zeros(local.shape, jnp.float32)
-    for by in range(1, count):
+    by = 1
+    while by < count:
         pairs = [(i, i + by) for i in range(count - by)]
-        total = total + lax.ppermute(sent, "ctx", pairs).astype(jnp.float32)
+        got = lax.ppermute(running.astype(jnp.bfloat16), "ctx", pairs).astype(jnp.float32)
+        total = total + got
+        running = running + got
+        by *= 2
     return total
 
 

time: 190 us -> 189 us (level)
    ppermute x3 -> x2, starting transfers between devices: 4.27 us -> 3.11 us  [earlier_sum(): lax.ppermute(running.astype(jnp.bfloat16), 'ctx', pairs).astype(jnp.float32)]
    ppermute x3 -> x2, waiting for transfers between devices: 21.9 us -> 21.8 us  [earlier_sum(): lax.ppermute(running.astype(jnp.bfloat16), 'ctx', pairs).astype(jnp.float32)]
  transfers between devices with their start and end apart: 16 -> 15, of which waited for: 10 -> 10; matrix products, arithmetic and copies ran while one was open for 11% -> 11% of each run, Pallas kernels for 0% -> 0%
where the time goes in v12:
time: 189 us; the launch traced here: 188 us
  waiting for transfers between devices  123 us (65%)
  matrix products  36.8 us (19%)
  starting transfers between devices  11.8 us (6%)
  other arithmetic  11 us (6%)
  local copies, waits for them, and re-layouts  5.54 us (3%)
    ppermute x4, waiting for transfers between devices, chip_shift(): return lax.ppermute(value, 'head', pairs)  91.4 us
    ppermute x2, waiting for transfers between devices, earlier_sum(): lax.ppermute(running.astype(jnp.bfloat16), 'ctx', pairs).astype(jnp.float32)  21.8 us
    dot_general x8, matrix products, block(): return jnp.dot(lhs, cols, preferred_element_type=jnp.float32)  15.1 us
    ppermute x4, starting transfers between devices, chip_shift(): return lax.ppermute(value, 'head', pairs)  6.09 us
    ppermute x8, waiting for transfers between devices, core_swap(): return lax.ppermute(value, 'head', [(h, h ^ 1) for h in range(devices)])  5.71 us
    dynamic_slice x6, local copies, waits for them, and re-layouts, gathered_rows(): lax.dynamic_slice_in_dim(weight, src * block, block, axis=0)  4.02 us
    sub x1, matrix products, body(): expd = jnp.exp(scores - top)  3.95 us
    ppermute x1, waiting for transfers between devices, from_behind(): return lax.ppermute(value, axis, pairs)  3.88 us
  transfers between devices with their start and end apart: 15, of which 10 were waited for; matrix products, arithmetic and copies ran while one was open for 11% of the time, Pallas kernels for 0%

profile of v12, /device:TPU:24, one launch (start us, length us, event | category | flops | bytes accessed | tf_op | source)
XLA Modules:
  0.0 188.4 jit_solution(14688136072426426186)
XLA Ops:
  1.5 23.6 %collective-permute-done = bf16[512,1024]{1,0:T(8,128)(2,1)S(1)} collective-permute-done((bf16[512,1024]{1,0:T(8,128)(2,1)}, bf16[512,1024]{1,0:T(8,128)(2,1)S(1)}, u32[]{:S(2)}, u32[]{:S(2)}) %collective-permute-start) | collective-permute-done | bytes 1048608 | tf_op jit(solution)/shard_map/ppermute | solution.py:33
  26.0 2.6 %constant_dynamic-slice_fusion.11 = (bf16[1024,512]{1,0:T(8,128)(2,1)S(1)}, bf16[1024,512]{1,0:T(8,128)(2,1)S(1)}, bf16[1024,512]{1,0:T(8,128)(2,1)S(1)}, bf16[1024,512]{1,0:T(8,128)(2,1)S(1)}) fusion(bf16[4096,512]{1,0:T(8,128)(2,1)} %param.14, s32[]{:T(128)S(6)} %select_n.127, s32[]{:T(128)S(6)} %select_n.131, s32[]{:T(128)S(6)} %select_n.133, ...), kind=kLoop, calls=%fused_computation.138 | loop fusion | bytes 8388624 | tf_op jit(solution)/shard_map/dynamic_slice | solution.py:82
  30.7 2.0 %fusion.1 = f32[512]{0:T(512)S(1)} fusion(bf16[512,1024]{1,0:T(8,128)(2,1)} %collective-permute-done.2, bf16[512,1024]{1,0:T(8,128)(2,1)S(1)} %collective-permute-done.1, bf16[512,1024]{1,0:T(8,128)(2,1)S(1)} %collective-permute-done, bf16[512,1024]{1,0:T(8,128)(2,1)S(1)} %copy-done), kind=kLoop, calls=%fused_computation.5 | loop fusion | flops 20971008 | bytes 4196352 | tf_op jit(solution)/shard_map/reduce_sum | solution.py:103
  32.7 2.4 %fusion.3 = bf16[512,4096]{1,0:T(8,128)(2,1)S(1)} fusion(f32[4096]{0:T(1024)S(1)} %pad_maximum_fusion.3, f32[512]{0:T(512)S(1)} %add_rsqrt_fusion.2, bf16[512,1024]{1,0:T(8,128)(2,1)} %collective-permute-done.2, bf16[512,1024]{1,0:T(8,128)(2,1)S(1)} %collective-permute-done.1, bf16[512,1024]{1,0:T(8,128)(2,1)S(1)} %collective-permute-done, ...), kind=kLoop, calls=%fused_computation.7 | loop fusion | flops 23068672 | bytes 8407040 | tf_op jit(solution)/shard_map/convert_element_type | solution.py:104
  39.4 2.4 %fusion.48 = bf16[512,512]{0,1:T(8,128)(2,1)S(1)} fusion(bf16[512,4096]{1,0:T(8,128)(2,1)S(1)} %fusion.3, bf16[1024,512]{1,0:T(8,128)(2,1)S(1)} %get-tuple-element.7, bf16[1024,512]{1,0:T(8,128)(2,1)S(1)} %get-tuple-element.8, bf16[1024,512]{1,0:T(8,128)(2,1)S(1)} %get-tuple-element.6, bf16[1024,512]{1,0:T(8,128)(2,1)S(1)} %get-tuple-element.5), kind=kOutput, calls=%fused_computation.61 | convolution fusion | flops 2164523008 | bytes 8912896 | tf_op jit(solution)/shard_map/dot_general | solution.py:153
  41.8 3.9 %collective-permute-done.3 = bf16[64,512]{0,1:T(8,128)(2,1)S(1)} collective-permute-done((bf16[64,512]{0,1:T(8,128)(2,1)S(1)}, bf16[64,512]{0,1:T(8,128)(2,1)S(1)}, u32[]{:S(2)}, u32[]{:S(2)}) %collective-permute-start.3) | collective-permute-done | bytes 65568 | tf_op jit(solution)/shard_map/ppermute | solution.py:17
  46.0 3.9 %fusion.120 = (f32[2,2,512]{2,1,0:T(2,128)S(1)}, f32[2,2,512,576]{2,3,1,0:T(8,128)}) fusion(pred[512,576]{0,1:T(8,128)(4,1)S(1)} %and_and_fusion, bf16[576,2,128,1]{0,2,3,1:T(8,128)(2,1)S(1)} %bitcast.82, bf16[512,2,2,128]{0,3,2,1:T(8,128)(2,1)S(1)} %bitcast.83), kind=kOutput, calls=%fused_computation.166 | convolution fusion | flops 306709056 | bytes 5840896 | tf_op jit(solution)/shard_map/sub | solution.py:180
  50.0 2.9 %fusion.51 = bf16[2,128,2,512]{3,1,2,0:T(8,128)(2,1)S(1)} fusion(bf16[576,2,128,1]{0,2,3,1:T(8,128)(2,1)S(1)} %bitcast.81, f32[2,2,512,576]{2,3,1,0:T(8,128)} %get-tuple-element.40, f32[2,2,512]{2,1,0:T(2,128)S(1)} %get-tuple-element.39), kind=kOutput, calls=%fused_computation.62 | convolution fusion | flops 304611328 | bytes 5545984 | tf_op jit(solution)/shard_map/kgts,skd->tkgd/dot_general | solution.py:182
  52.9 3.3 %fusion.81 = f32[512,1024]{1,0:T(8,128)} fusion(bf16[512,512]{0,1:T(8,128)(2,1)S(1)} %bitcast.70, bf16[512,4096]{1,0:T(8,128)(2,1)} %param.17, s32[]{:T(128)S(6)} %select_n.135), kind=kOutput, calls=%fused_computation.92 | convolution fusion | flops 536870912 | bytes 3670020 | tf_op jit(solution)/shard_map/dot_general | solution.py:45
  56.2 3.3 %fusion.77 = f32[512,1024]{1,0:T(8,128)} fusion(bf16[512,512]{0,1:T(8,128)(2,1)S(1)} %bitcast.71, bf16[512,4096]{1,0:T(8,128)(2,1)} %param.17, s32[]{:T(128)S(6)} %select_n.138), kind=kOutput, calls=%fused_computation.88 | convolution fusion | flops 536870912 | bytes 3670020 | tf_op jit(solution)/shard_map/dot_general | solution.py:45
  60.7 3.6 %add_convert_fusion.3 = bf16[512,1024]{1,0:T(8,128)(2,1)} fusion(f32[512,1024]{1,0:T(8,128)} %collective-permute-done.4, bf16[512,512]{0,1:T(8,128)(2,1)S(1)} %bitcast.72, bf16[512,4096]{1,0:T(8,128)(2,1)} %param.17, s32[]{:T(128)S(6)} %select_n.131), kind=kOutput, calls=%fused_computation.57 | convolution fusion | flops 537919488 | bytes 4718596 | tf_op jit(solution)/shard_map/dot_general | solution.py:45
  65.8 1.9 %fusion.79 = f32[512,1024]{1,0:T(8,128)S(1)} fusion(bf16[512,512]{0,1:T(8,128)(2,1)S(1)} %bitcast.73, bf16[512,4096]{1,0:T(8,128)(2,1)} %param.17, s32[]{:T(128)S(6)} %select_n.137), kind=kOutput, calls=%fused_computation.90 | convolution fusion | flops 536870912 | bytes 3670020 | tf_op jit(solution)/shard_map/dot_general | solution.py:45
  67.8 21.9 %collective-permute-done.5 = bf16[512,1024]{1,0:T(8,128)(2,1)S(1)} collective-permute-done((bf16[512,1024]{1,0:T(8,128)(2,1)}, bf16[512,1024]{1,0:T(8,128)(2,1)S(1)}, u32[]{:S(2)}, u32[]{:S(2)}) %collective-permute-start.5) | collective-permute-done | bytes 1048608 | tf_op jit(solution)/shard_map/ppermute | solution.py:33
  89.8 2.4 %add_convert_fusion.2 = bf16[512,1024]{1,0:T(8,128)(2,1)S(1)} fusion(f32[512,1024]{1,0:T(8,128)S(1)} %fusion.79, f32[512,1024]{1,0:T(8,128)} %collective-permute-done.6, bf16[512,1024]{1,0:T(8,128)(2,1)S(1)} %collective-permute-done.5, bf16[512,1024]{1,0:T(8,128)(2,1)S(1)} %copy-done), kind=kLoop, calls=%fused_computation.56 | loop fusion | flops 3145728 | bytes 7340032 | tf_op jit(solution)/shard_map/convert_element_type | solution.py:187
  93.7 22.9 %collective-permute-done.7 = bf16[512,1024]{1,0:T(8,128)(2,1)S(1)} collective-permute-done((bf16[512,1024]{1,0:T(8,128)(2,1)S(1)}, bf16[512,1024]{1,0:T(8,128)(2,1)S(1)}, u32[]{:S(2)}, u32[]{:S(2)}) %collective-permute-start.7) | collective-permute-done | bytes 1048608 | tf_op jit(solution)/shard_map/ppermute | solution.py:33
  117.1 2.1 %collective-permute-done.9 = bf16[512,1024]{1,0:T(8,128)(2,1)S(1)} collective-permute-done((bf16[512,1024]{1,0:T(8,128)(2,1)S(1)}, bf16[512,1024]{1,0:T(8,128)(2,1)S(1)}, u32[]{:S(2)}, u32[]{:S(2)}) %collective-permute-start.9) | collective-permute-done | bytes 1048608 | tf_op jit(solution)/shard_map/ppermute | solution.py:27
  122.0 2.6 %fusion.45 = bf16[512,512]{0,1:T(8,128)(2,1)S(1)} fusion(bf16[1024,512]{1,0:T(8,128)(2,1)S(1)} %get-tuple-element.11, bf16[1024,512]{1,0:T(8,128)(2,1)S(1)} %get-tuple-element.12, bf16[1024,512]{1,0:T(8,128)(2,1)S(1)} %get-tuple-element.10, bf16[1024,512]{1,0:T(8,128)(2,1)S(1)} %get-tuple-element.9, f32[4096]{0:T(1024)S(1)} %pad_maximum_fusion.4, ...), kind=kOutput, calls=%fused_computation.60 | convolution fusion | flops 2187591680 | bytes 8931328 | tf_op jit(solution)/shard_map/dot_general | solution.py:200
  126.8 2.3 %select_convert_fusion = bf16[2,512,512]{2,1,0:T(8,128)(2,1)S(1)} fusion(pred[512,512]{1,0:T(8,128)(4,1)S(1)} %iota_compare_fusion, f32[512,2,2,16]{0,3,2,1:T(8,128)S(1)} %bitcast.80), kind=kOutput, calls=%fused_computation.55 | convolution fusion | flops 104333312 | bytes 1441792 | tf_op jit(solution)/shard_map/thf,shf->hts/dot_general | solution.py:219
  129.2 7.0 %collective-permute-done.10 = bf16[2,273,256]{2,1,0:T(8,128)(2,1)S(1)} collective-permute-done((bf16[2,273,256]{2,1,0:T(8,128)(2,1)S(1)}, bf16[2,273,256]{2,1,0:T(8,128)(2,1)S(1)}, u32[]{:S(2)}, u32[]{:S(2)}) %collective-permute-start.10) | collective-permute-done | bytes 279584 | tf_op jit(solution)/shard_map/ppermute | solution.py:94
  136.2 1.8 collective-permute-start.11
  138.5 14.8 %collective-permute-done.11 = bf16[2,273,256]{2,1,0:T(8,128)(2,1)S(1)} collective-permute-done((bf16[2,273,256]{2,1,0:T(8,128)(2,1)S(1)}, bf16[2,273,256]{2,1,0:T(8,128)(2,1)S(1)}, u32[]{:S(2)}, u32[]{:S(2)}) %collective-permute-start.11) | collective-permute-done | bytes 279584 | tf_op jit(solution)/shard_map/ppermute | solution.py:94
  153.4 2.2 %multiply_reduce_fusion = (f32[512,2]{0,1:T(2,128)S(1)}, f32[512,2,256]{0,2,1:T(8,128)S(1)}) fusion(f32[2,256,512]{2,1,0:T(8,128)S(1)} %fusion.122, f32[512,2,256]{0,2,1:T(8,128)S(1)} %bitcast.74, f32[512,2,16]{0,2,1:T(8,128)S(1)} %get-tuple-element.28, f32[273]{0:T(512)S(1)} %pad.7.clone, bf16[2,273,256]{2,1,0:T(8,128)(2,1)S(1)} %collective-permute-done.10, ...), kind=kOutput, calls=%fused_computation.84 | convolution fusion | flops 860687360 | bytes 4334660 | tf_op jit(solution)/shard_map/thf,hfv->thv/dot_general | solution.py:218
  157.8 2.9 %collective-permute-done.12 = f32[512,1024]{1,0:T(8,128)S(1)} collective-permute-done((f32[512,1024]{1,0:T(8,128)S(1)}, f32[512,1024]{1,0:T(8,128)S(1)}, u32[]{:S(2)}, u32[]{:S(2)}) %collective-permute-start.12) | collective-permute-done | bytes 2097184 | tf_op jit(solution)/shard_map/ppermute | solution.py:27
  163.7 23.0 %collective-permute-done.13 = bf16[512,1024]{1,0:T(8,128)(2,1)S(1)} collective-permute-done((bf16[512,1024]{1,0:T(8,128)(2,1)S(1)}, bf16[512,1024]{1,0:T(8,128)(2,1)S(1)}, u32[]{:S(2)}, u32[]{:S(2)}) %collective-permute-start.13) | collective-permute-done | bytes 1048608 | tf_op jit(solution)/shard_map/ppermute | solution.py:33
  (74 shorter events, 26.1 us)
Async XLA Ops:
  0.0 25.1 %collective-permute-start = (bf16[512,1024]{1,0:T(8,128)(2,1)}, bf16[512,1024]{1,0:T(8,128)(2,1)S(1)}, u32[]{:S(2)}, u32[]{:S(2)}) collective-permute-start(bf16[512,1024]{1,0:T(8,128)(2,1)} %param.12), channel_id=1, source_target_pairs={{0,2},{1,3},{2,0},{3,1},{4,6},{5,7},{6,4},{7,5},{8,10},{9,11},{10,... | collective-permute-start | bytes 3145736 | tf_op jit(solution)/shard_map/ppermute | solution.py:33
  1.5 28.6 %collective-permute-start.1 = (bf16[512,1024]{1,0:T(8,128)(2,1)}, bf16[512,1024]{1,0:T(8,128)(2,1)S(1)}, u32[]{:S(2)}, u32[]{:S(2)}) collective-permute-start(bf16[512,1024]{1,0:T(8,128)(2,1)} %param.12), channel_id=1, source_target_pairs={{0,1},{1,0},{2,3},{3,2},{4,5},{5,4},{6,7},{7,6},{8,9},{9,8},{10,11... | collective-permute-start | bytes 3145736 | tf_op jit(solution)/shard_map/ppermute | solution.py:27
  25.1 5.0 %collective-permute-start.2 = (bf16[512,1024]{1,0:T(8,128)(2,1)S(1)}, bf16[512,1024]{1,0:T(8,128)(2,1)}, u32[]{:S(2)}, u32[]{:S(2)}) collective-permute-start(bf16[512,1024]{1,0:T(8,128)(2,1)S(1)} %collective-permute-done), channel_id=1, source_target_pairs={{0,1},{1,0},{2,3},{3,2},{4,5},{5,4},{6,7},{7,6},{8,9},{9,8},{10,11... | collective-permute-start | bytes 3145736 | tf_op jit(solution)/shard_map/ppermute | solution.py:27
  26.0 2.9 %copy-start.3 = (bf16[4096,256]{1,0:T(8,128)(2,1)S(1)}, bf16[4096,256]{1,0:T(8,128)(2,1)}, u32[]{:S(2)}) copy-start(bf16[4096,256]{1,0:T(8,128)(2,1)} %param.16) | copy-start | bytes 6291460
  26.0 3.5 %copy-start.4 = (bf16[4096,256]{1,0:T(8,128)(2,1)S(1)}, bf16[4096,256]{1,0:T(8,128)(2,1)}, u32[]{:S(2)}) copy-start(bf16[4096,256]{1,0:T(8,128)(2,1)} %param.15) | copy-start | bytes 6291460
  29.4 1.2 copy-start
  37.9 7.7 %collective-permute-start.3 = (bf16[64,512]{0,1:T(8,128)(2,1)S(1)}, bf16[64,512]{0,1:T(8,128)(2,1)S(1)}, u32[]{:S(2)}, u32[]{:S(2)}) collective-permute-start(bf16[64,512]{0,1:T(8,128)(2,1)S(1)} %pad_maximum_fusion.2), channel_id=1, source_target_pairs={{0,4},{4,8},{8,12},{1,5},{5,9},{9,13},{2,6},{6,10},{10,14},{3,7},{... | collective-permute-start | bytes 196616 | tf_op jit(solution)/shard_map/ppermute | solution.py:17
  56.2 4.5 %collective-permute-start.4 = (f32[512,1024]{1,0:T(8,128)}, f32[512,1024]{1,0:T(8,128)}, u32[]{:S(2)}, u32[]{:S(2)}) collective-permute-start(f32[512,1024]{1,0:T(8,128)} %fusion.81), channel_id=1, source_target_pairs={{0,1},{1,0},{2,3},{3,2},{4,5},{5,4},{6,7},{7,6},{8,9},{9,8},{10,11... | collective-permute-start | bytes 6291464 | tf_op jit(solution)/shard_map/ppermute | solution.py:27
  59.5 8.3 %collective-permute-start.6 = (f32[512,1024]{1,0:T(8,128)}, f32[512,1024]{1,0:T(8,128)}, u32[]{:S(2)}, u32[]{:S(2)}) collective-permute-start(f32[512,1024]{1,0:T(8,128)} %fusion.77), channel_id=1, source_target_pairs={{0,1},{1,0},{2,3},{3,2},{4,5},{5,4},{6,7},{7,6},{8,9},{9,8},{10,11... | collective-permute-start | bytes 6291464 | tf_op jit(solution)/shard_map/ppermute | solution.py:27
  64.4 25.4 %collective-permute-start.5 = (bf16[512,1024]{1,0:T(8,128)(2,1)}, bf16[512,1024]{1,0:T(8,128)(2,1)S(1)}, u32[]{:S(2)}, u32[]{:S(2)}) collective-permute-start(bf16[512,1024]{1,0:T(8,128)(2,1)} %add_convert_fusion.3), channel_id=1, source_target_pairs={{0,2},{1,3},{2,0},{3,1},{4,6},{5,7},{6,4},{7,5},{8,10},{9,11},{10,... | collective-permute-start | bytes 3145736 | tf_op jit(solution)/shard_map/ppermute | solution.py:33
  67.8 48.8 %copy-start.7 = (f32[4096]{0:T(1024)S(1)}, f32[4096]{0:T(1024)}, u32[]{:S(2)}) copy-start(f32[4096]{0:T(1024)} %param.18) | copy-start | bytes 49156
  67.8 48.9 %copy-start.6 = (bf16[4096,64]{0,1:T(8,128)(2,1)S(1)}, bf16[4096,64]{0,1:T(8,128)(2,1)}, u32[]{:S(2)}) copy-start(bf16[4096,64]{0,1:T(8,128)(2,1)} %param.19) | copy-start | bytes 1572868
  67.8 49.0 %copy-start.2 = (bf16[4096,512]{1,0:T(8,128)(2,1)S(1)}, bf16[4096,512]{1,0:T(8,128)(2,1)}, u32[]{:S(2)}) copy-start(bf16[4096,512]{1,0:T(8,128)(2,1)} %param.20) | copy-start | bytes 12582916
  92.2 24.4 %collective-permute-start.7 = (bf16[512,1024]{1,0:T(8,128)(2,1)S(1)}, bf16[512,1024]{1,0:T(8,128)(2,1)S(1)}, u32[]{:S(2)}, u32[]{:S(2)}) collective-permute-start(bf16[512,1024]{1,0:T(8,128)(2,1)S(1)} %add_convert_fusion.2), channel_id=1, source_target_pairs={{0,2},{1,3},{2,0},{3,1},{4,6},{5,7},{6,4},{7,5},{8,10},{9,11},{10,... | collective-permute-start | bytes 3145736 | tf_op jit(solution)/shard_map/ppermute | solution.py:33
  93.7 23.4 %collective-permute-start.8 = (bf16[512,1024]{1,0:T(8,128)(2,1)S(1)}, bf16[512,1024]{1,0:T(8,128)(2,1)S(1)}, u32[]{:S(2)}, u32[]{:S(2)}) collective-permute-start(bf16[512,1024]{1,0:T(8,128)(2,1)S(1)} %add_convert_fusion.2), channel_id=1, source_target_pairs={{0,1},{1,0},{2,3},{3,2},{4,5},{5,4},{6,7},{7,6},{8,9},{9,8},{10,11... | collective-permute-start | bytes 3145736 | tf_op jit(solution)/shard_map/ppermute | solution.py:27
  116.6 2.7 %collective-permute-start.9 = (bf16[512,1024]{1,0:T(8,128)(2,1)S(1)}, bf16[512,1024]{1,0:T(8,128)(2,1)S(1)}, u32[]{:S(2)}, u32[]{:S(2)}) collective-permute-start(bf16[512,1024]{1,0:T(8,128)(2,1)S(1)} %collective-permute-done.7), channel_id=1, source_target_pairs={{0,1},{1,0},{2,3},{3,2},{4,5},{5,4},{6,7},{7,6},{8,9},{9,8},{10,11... | collective-permute-start | bytes 3145736 | tf_op jit(solution)/shard_map/ppermute | solution.py:27
  125.4 10.8 %collective-permute-start.10 = (bf16[2,273,256]{2,1,0:T(8,128)(2,1)S(1)}, bf16[2,273,256]{2,1,0:T(8,128)(2,1)S(1)}, u32[]{:S(2)}, u32[]{:S(2)}) collective-permute-start(bf16[2,273,256]{2,1,0:T(8,128)(2,1)S(1)} %get-tuple-element.41), channel_id=1, source_target_pairs={{0,4},{4,8},{8,12},{1,5},{5,9},{9,13},{2,6},{6,10},{10,14},{3,7},{... | collective-permute-start | bytes 838664 | tf_op jit(solution)/shard_map/ppermute | solution.py:94
  126.8 26.6 %copy-start.5 = (f32[2,273,256]{2,0,1:T(2,128)S(1)}, f32[2,273,256]{2,0,1:T(2,128)}, u32[]{:S(2)}) copy-start(f32[2,273,256]{2,0,1:T(2,128)} %param.23) | copy-start | bytes 1677316
  129.2 26.4 %copy-start.8 = (f32[2,256]{1,0:T(2,128)S(1)}, f32[2,256]{1,0:T(2,128)}, u32[]{:S(2)}) copy-start(f32[2,256]{1,0:T(2,128)} %param.21) | copy-start | bytes 6148
  136.2 19.5 %copy-start.1 = (bf16[512,4096]{1,0:T(8,128)(2,1)S(1)}, bf16[512,4096]{1,0:T(8,128)(2,1)}, u32[]{:S(2)}) copy-start(bf16[512,4096]{1,0:T(8,128)(2,1)} %param.22) | copy-start | bytes 12582916
  136.2 17.1 %collective-permute-start.11 = (bf16[2,273,256]{2,1,0:T(8,128)(2,1)S(1)}, bf16[2,273,256]{2,1,0:T(8,128)(2,1)S(1)}, u32[]{:S(2)}, u32[]{:S(2)}) collective-permute-start(bf16[2,273,256]{2,1,0:T(8,128)(2,1)S(1)} %fusion.84), channel_id=1, source_target_pairs={{0,8},{4,12},{1,9},{5,13},{2,10},{6,14},{3,11},{7,15},{16,24},{20,... | collective-permute-start | bytes 838664 | tf_op jit(solution)/shard_map/ppermute | solution.py:94
  156.5 4.2 %collective-permute-start.12 = (f32[512,1024]{1,0:T(8,128)S(1)}, f32[512,1024]{1,0:T(8,128)S(1)}, u32[]{:S(2)}, u32[]{:S(2)}) collective-permute-start(f32[512,1024]{1,0:T(8,128)S(1)} %fusion.74), channel_id=1, source_target_pairs={{0,1},{1,0},{2,3},{3,2},{4,5},{5,4},{6,7},{7,6},{8,9},{9,8},{10,11... | collective-permute-start | bytes 6291464 | tf_op jit(solution)/shard_map/ppermute | solution.py:27
  157.3 6.4 %collective-permute-start.14 = (f32[512,1024]{1,0:T(8,128)S(1)}, f32[512,1024]{1,0:T(8,128)S(1)}, u32[]{:S(2)}, u32[]{:S(2)}) collective-permute-start(f32[512,1024]{1,0:T(8,128)S(1)} %fusion.70), channel_id=1, source_target_pairs={{0,1},{1,0},{2,3},{3,2},{4,5},{5,4},{6,7},{7,6},{8,9},{9,8},{10,11... | collective-permute-start | bytes 6291464 | tf_op jit(solution)/shard_map/ppermute | solution.py:27
  161.4 25.3 %collective-permute-start.13 = (bf16[512,1024]{1,0:T(8,128)(2,1)S(1)}, bf16[512,1024]{1,0:T(8,128)(2,1)S(1)}, u32[]{:S(2)}, u32[]{:S(2)}) collective-permute-start(bf16[512,1024]{1,0:T(8,128)(2,1)S(1)} %add_convert_fusion.1), channel_id=1, source_target_pairs={{0,2},{1,3},{2,0},{3,1},{4,6},{5,7},{6,4},{7,5},{8,10},{9,11},{10,... | collective-permute-start | bytes 3145736 | tf_op jit(solution)/shard_map/ppermute | solution.py:33

commit v13 on v12

--- a/solution.py
+++ b/solution.py
@@ -209,20 +209,20 @@
     local_state = jnp.einsum(
         "thf,thv->hfv", phi_key, lvalues.astype(jnp.float32), precision=highest
     )
-    carried = entry_state + earlier_sum(local_state)
+    prior = earlier_sum(local_state)
 
     outs = []
     for i in range(CHUNKS):
         query_feat = qf_parts[i]
         phi_query = taylor(query_feat)
-        cross = jnp.einsum("thf,hfv->thv", phi_query, carried, precision=highest)
+        own = jnp.einsum("thf,hfv->thv", phi_query, entry_state, precision=highest)
         sims = jnp.einsum(
             "thf,shf->hts", query_feat, key_feat, precision=highest
         ) / math.sqrt(FEAT)
         causal = (i * size + jnp.arange(size))[:, None] >= jnp.arange(tok_rows)[None, :]
         weights = jnp.where(causal[None], 1.0 + sims + 0.5 * sims * sims, 0.0).astype(jnp.bfloat16)
         intra = jnp.einsum("hts,shv->thv", weights, lvalues, preferred_element_type=jnp.float32)
-        lin_out = cross + intra
+        lin_out = (own + intra) + jnp.einsum("thf,hfv->thv", phi_query, prior, precision=highest)
         scale = lax.rsqrt(jnp.mean(lin_out * lin_out, axis=-1, keepdims=True) + 1e-05)
         lin_normed = (
             (lin_out * scale * out_gain[None]).astype(jnp.bfloat16).reshape(size, lin_heads * VDIM)

time: 189 us -> 190 us (level)
  matrix products: 36.8 us -> 38.9 us
  waiting for transfers between devices: 123 us -> 121 us
    ppermute x2, waiting for transfers between devices: 21.8 us -> 19.7 us  [earlier_sum(): lax.ppermute(running.astype(jnp.bfloat16), 'ctx', pairs).astype(jnp.float32)]
    dot_general x1 -> x2, matrix products: 2.16 us -> 4.12 us  [the longest x1 2.08 us: body(): jnp.einsum('thf,hfv->thv', phi_query, prior, precision=highest)]
  transfers between devices with their start and end apart: 15 -> 15, of which waited for: 10 -> 10; matrix products, arithmetic and copies ran while one was open for 11% -> 12% of each run, Pallas kernels for 0% -> 0%
where the time goes in v13:
time: 190 us
  waiting for transfers between devices  121 us (64%)
  matrix products  38.9 us (20%)
  other arithmetic  12.5 us (7%)
  starting transfers between devices  11.6 us (6%)
  local copies, waits for them, and re-layouts  5.54 us (3%)
    ppermute x4, waiting for transfers between devices, chip_shift(): return lax.ppermute(value, 'head', pairs)  91.4 us
    ppermute x2, waiting for transfers between devices, earlier_sum(): lax.ppermute(running.astype(jnp.bfloat16), 'ctx', pairs).astype(jnp.float32)  19.7 us
    dot_general x8, matrix products, block(): return jnp.dot(lhs, cols, preferred_element_type=jnp.float32)  15.2 us
    ppermute x4, starting transfers between devices, chip_shift(): return lax.ppermute(value, 'head', pairs)  6.1 us
    ppermute x8, waiting for transfers between devices, core_swap(): return lax.ppermute(value, 'head', [(h, h ^ 1) for h in range(devices)])  5.69 us
    reduce_sum x2, other arithmetic, norm_rows(): scale = lax.rsqrt(jnp.mean(wide * wide, axis=-1, keepdims=True) + 1e-05)  4.51 us
    dynamic_slice x6, local copies, waits for them, and re-layouts, gathered_rows(): lax.dynamic_slice_in_dim(weight, src * block, block, axis=0)  4.05 us
    sub x1, matrix products, body(): expd = jnp.exp(scores - top)  3.97 us
  transfers between devices with their start and end apart: 15, of which 10 were waited for; matrix products, arithmetic and copies ran while one was open for 12% of the time, Pallas kernels for 0%

profile of v13, /device:TPU:24, one launch (start us, length us, event | category | flops | bytes accessed | tf_op | source)
XLA Modules:
  0.0 189.6 jit_solution(10339306351678957235)
XLA Ops:
  1.5 23.6 %collective-permute-done = bf16[512,1024]{1,0:T(8,128)(2,1)S(1)} collective-permute-done((bf16[512,1024]{1,0:T(8,128)(2,1)}, bf16[512,1024]{1,0:T(8,128)(2,1)S(1)}, u32[]{:S(2)}, u32[]{:S(2)}) %collective-permute-start) | collective-permute-done | bytes 1048608 | tf_op jit(solution)/shard_map/ppermute | solution.py:33
  26.0 2.6 %constant_dynamic-slice_fusion.11 = (bf16[1024,512]{1,0:T(8,128)(2,1)S(1)}, bf16[1024,512]{1,0:T(8,128)(2,1)S(1)}, bf16[1024,512]{1,0:T(8,128)(2,1)S(1)}, bf16[1024,512]{1,0:T(8,128)(2,1)S(1)}) fusion(bf16[4096,512]{1,0:T(8,128)(2,1)} %param.14, s32[]{:T(128)S(6)} %select_n.127, s32[]{:T(128)S(6)} %select_n.131, s32[]{:T(128)S(6)} %select_n.133, ...), kind=kLoop, calls=%fused_computation.138 | loop fusion | bytes 8388624 | tf_op jit(solution)/shard_map/dynamic_slice | solution.py:82
  30.7 3.5 %fusion.1 = f32[512]{0:T(512)S(1)} fusion(bf16[512,1024]{1,0:T(8,128)(2,1)} %collective-permute-done.2, bf16[512,1024]{1,0:T(8,128)(2,1)} %collective-permute-done.1, bf16[512,1024]{1,0:T(8,128)(2,1)S(1)} %collective-permute-done, bf16[512,1024]{1,0:T(8,128)(2,1)S(1)} %copy-done.1), kind=kLoop, calls=%fused_computation.5 | loop fusion | flops 20971008 | bytes 4196352 | tf_op jit(solution)/shard_map/reduce_sum | solution.py:103
  34.2 2.6 %fusion.3 = bf16[512,4096]{1,0:T(8,128)(2,1)S(1)} fusion(f32[4096]{0:T(1024)S(1)} %pad_maximum_fusion.6, f32[512]{0:T(512)S(1)} %add_rsqrt_fusion.2, bf16[512,1024]{1,0:T(8,128)(2,1)} %collective-permute-done.2, bf16[512,1024]{1,0:T(8,128)(2,1)} %collective-permute-done.1, bf16[512,1024]{1,0:T(8,128)(2,1)S(1)} %collective-permute-done, ...), kind=kLoop, calls=%fused_computation.7 | loop fusion | flops 23068672 | bytes 8407040 | tf_op jit(solution)/shard_map/convert_element_type | solution.py:104
  41.0 2.4 %fusion.49 = bf16[512,512]{0,1:T(8,128)(2,1)S(1)} fusion(bf16[512,4096]{1,0:T(8,128)(2,1)S(1)} %fusion.3, bf16[1024,512]{1,0:T(8,128)(2,1)S(1)} %get-tuple-element.7, bf16[1024,512]{1,0:T(8,128)(2,1)S(1)} %get-tuple-element.8, bf16[1024,512]{1,0:T(8,128)(2,1)S(1)} %get-tuple-element.6, bf16[1024,512]{1,0:T(8,128)(2,1)S(1)} %get-tuple-element.5), kind=kOutput, calls=%fused_computation.64 | convolution fusion | flops 2164523008 | bytes 8912896 | tf_op jit(solution)/shard_map/dot_general | solution.py:153
  43.4 3.9 %collective-permute-done.3 = bf16[64,512]{0,1:T(8,128)(2,1)S(1)} collective-permute-done((bf16[64,512]{0,1:T(8,128)(2,1)S(1)}, bf16[64,512]{0,1:T(8,128)(2,1)S(1)}, u32[]{:S(2)}, u32[]{:S(2)}) %collective-permute-start.3) | collective-permute-done | bytes 65568 | tf_op jit(solution)/shard_map/ppermute | solution.py:17
  47.6 4.0 %fusion.117 = (f32[2,2,512]{2,1,0:T(2,128)S(1)}, f32[2,2,512,576]{2,3,1,0:T(8,128)}) fusion(pred[512,576]{0,1:T(8,128)(4,1)S(1)} %and_and_fusion, bf16[576,2,128,1]{0,2,3,1:T(8,128)(2,1)S(1)} %bitcast.91, bf16[512,2,2,128]{0,3,2,1:T(8,128)(2,1)S(1)} %bitcast.92), kind=kOutput, calls=%fused_computation.167 | convolution fusion | flops 306709056 | bytes 5840896 | tf_op jit(solution)/shard_map/sub | solution.py:180
  51.6 3.0 %fusion.52 = bf16[2,128,2,512]{3,1,2,0:T(8,128)(2,1)S(1)} fusion(bf16[576,2,128,1]{0,2,3,1:T(8,128)(2,1)S(1)} %bitcast.90, f32[2,2,512,576]{2,3,1,0:T(8,128)} %get-tuple-element.40, f32[2,2,512]{2,1,0:T(2,128)S(1)} %get-tuple-element.39), kind=kOutput, calls=%fused_computation.65 | convolution fusion | flops 304611328 | bytes 5545984 | tf_op jit(solution)/shard_map/kgts,skd->tkgd/dot_general | solution.py:182
  54.6 3.3 %fusion.78 = f32[512,1024]{1,0:T(8,128)} fusion(bf16[512,512]{0,1:T(8,128)(2,1)S(1)} %bitcast.78, bf16[512,4096]{1,0:T(8,128)(2,1)} %param.17, s32[]{:T(128)S(6)} %select_n.135), kind=kOutput, calls=%fused_computation.92 | convolution fusion | flops 536870912 | bytes 3670020 | tf_op jit(solution)/shard_map/dot_general | solution.py:45
  57.9 3.3 %fusion.74 = f32[512,1024]{1,0:T(8,128)} fusion(bf16[512,512]{0,1:T(8,128)(2,1)S(1)} %bitcast.79, bf16[512,4096]{1,0:T(8,128)(2,1)} %param.17, s32[]{:T(128)S(6)} %select_n.138), kind=kOutput, calls=%fused_computation.88 | convolution fusion | flops 536870912 | bytes 3670020 | tf_op jit(solution)/shard_map/dot_general | solution.py:45
  62.4 3.6 %add_convert_fusion.3 = bf16[512,1024]{1,0:T(8,128)(2,1)} fusion(f32[512,1024]{1,0:T(8,128)} %collective-permute-done.4, bf16[512,512]{0,1:T(8,128)(2,1)S(1)} %bitcast.80, bf16[512,4096]{1,0:T(8,128)(2,1)} %param.17, s32[]{:T(128)S(6)} %select_n.131), kind=kOutput, calls=%fused_computation.57 | convolution fusion | flops 537919488 | bytes 4718596 | tf_op jit(solution)/shard_map/dot_general | solution.py:45
  67.6 2.0 %fusion.76 = f32[512,1024]{1,0:T(8,128)S(1)} fusion(bf16[512,512]{0,1:T(8,128)(2,1)S(1)} %bitcast.81, bf16[512,4096]{1,0:T(8,128)(2,1)} %param.17, s32[]{:T(128)S(6)} %select_n.137), kind=kOutput, calls=%fused_computation.90 | convolution fusion | flops 536870912 | bytes 3670020 | tf_op jit(solution)/shard_map/dot_general | solution.py:45
  69.6 21.9 %collective-permute-done.5 = bf16[512,1024]{1,0:T(8,128)(2,1)S(1)} collective-permute-done((bf16[512,1024]{1,0:T(8,128)(2,1)}, bf16[512,1024]{1,0:T(8,128)(2,1)S(1)}, u32[]{:S(2)}, u32[]{:S(2)}) %collective-permute-start.5) | collective-permute-done | bytes 1048608 | tf_op jit(solution)/shard_map/ppermute | solution.py:33
  91.5 2.3 %add_convert_fusion.2 = bf16[512,1024]{1,0:T(8,128)(2,1)S(1)} fusion(f32[512,1024]{1,0:T(8,128)S(1)} %fusion.76, f32[512,1024]{1,0:T(8,128)} %collective-permute-done.6, bf16[512,1024]{1,0:T(8,128)(2,1)S(1)} %collective-permute-done.5, bf16[512,1024]{1,0:T(8,128)(2,1)S(1)} %copy-done.1), kind=kLoop, calls=%fused_computation.56 | loop fusion | flops 3145728 | bytes 7340032 | tf_op jit(solution)/shard_map/convert_element_type | solution.py:187
  95.3 22.9 %collective-permute-done.7 = bf16[512,1024]{1,0:T(8,128)(2,1)S(1)} collective-permute-done((bf16[512,1024]{1,0:T(8,128)(2,1)S(1)}, bf16[512,1024]{1,0:T(8,128)(2,1)S(1)}, u32[]{:S(2)}, u32[]{:S(2)}) %collective-permute-start.7) | collective-permute-done | bytes 1048608 | tf_op jit(solution)/shard_map/ppermute | solution.py:33
  118.7 2.1 %collective-permute-done.9 = bf16[512,1024]{1,0:T(8,128)(2,1)S(1)} collective-permute-done((bf16[512,1024]{1,0:T(8,128)(2,1)S(1)}, bf16[512,1024]{1,0:T(8,128)(2,1)S(1)}, u32[]{:S(2)}, u32[]{:S(2)}) %collective-permute-start.9) | collective-permute-done | bytes 1048608 | tf_op jit(solution)/shard_map/ppermute | solution.py:27
  123.5 2.6 %fusion.46 = bf16[512,512]{0,1:T(8,128)(2,1)S(1)} fusion(bf16[1024,512]{1,0:T(8,128)(2,1)S(1)} %get-tuple-element.11, bf16[1024,512]{1,0:T(8,128)(2,1)S(1)} %get-tuple-element.12, bf16[1024,512]{1,0:T(8,128)(2,1)S(1)} %get-tuple-element.10, bf16[1024,512]{1,0:T(8,128)(2,1)S(1)} %get-tuple-element.9, f32[4096]{0:T(1024)S(1)} %pad_maximum_fusion.7, ...), kind=kOutput, calls=%fused_computation.63 | convolution fusion | flops 2187591680 | bytes 8931328 | tf_op jit(solution)/shard_map/dot_general | solution.py:200
  128.2 2.3 %select_convert_fusion = bf16[2,512,512]{2,1,0:T(8,128)(2,1)S(1)} fusion(pred[512,512]{1,0:T(8,128)(4,1)S(1)} %iota_compare_fusion, f32[512,2,2,16]{0,3,2,1:T(8,128)S(1)} %bitcast.89), kind=kOutput, calls=%fused_computation.55 | convolution fusion | flops 104333312 | bytes 1441792 | tf_op jit(solution)/shard_map/thf,shf->hts/dot_general | solution.py:219
  131.2 6.5 %collective-permute-done.10 = bf16[2,273,256]{2,1,0:T(8,128)(2,1)S(1)} collective-permute-done((bf16[2,273,256]{2,1,0:T(8,128)(2,1)S(1)}, bf16[2,273,256]{2,1,0:T(8,128)(2,1)S(1)}, u32[]{:S(2)}, u32[]{:S(2)}) %collective-permute-start.10) | collective-permute-done | bytes 279584 | tf_op jit(solution)/shard_map/ppermute | solution.py:94
  139.4 2.0 %fusion.45 = f32[512,2,256]{0,2,1:T(8,128)S(1)} fusion(f32[512,2,256]{0,2,1:T(8,128)S(1)} %convolution_bitcast_fusion.2, f32[512,2,256]{0,2,1:T(8,128)S(1)} %bitcast.82, f32[512,2,16]{0,2,1:T(8,128)S(1)} %get-tuple-element.28, f32[273]{0:T(512)S(1)} %pad.7.clone, f32[2,273,256]{2,0,1:T(2,128)S(1)} %copy-done), kind=kOutput, calls=%fused_computation.61 | convolution fusion | flops 859604992 | bytes 3771460 | tf_op jit(solution)/shard_map/thf,hfv->thv/dot_general | solution.py:218
  141.4 13.2 %collective-permute-done.11 = bf16[2,273,256]{2,1,0:T(8,128)(2,1)S(1)} collective-permute-done((bf16[2,273,256]{2,1,0:T(8,128)(2,1)S(1)}, bf16[2,273,256]{2,1,0:T(8,128)(2,1)S(1)}, u32[]{:S(2)}, u32[]{:S(2)}) %collective-permute-start.11) | collective-permute-done | bytes 279584 | tf_op jit(solution)/shard_map/ppermute | solution.py:94
  154.6 2.1 %multiply_reduce_fusion = (f32[512,2]{0,1:T(2,128)S(1)}, f32[512,2,256]{0,2,1:T(8,128)S(1)}) fusion(f32[512,2,256]{0,2,1:T(8,128)S(1)} %fusion.45, f32[512,2,256]{0,2,1:T(8,128)S(1)} %bitcast.83, f32[512,2,16]{0,2,1:T(8,128)S(1)} %get-tuple-element.28, f32[273]{0:T(512)S(1)} %pad.7.clone, bf16[2,273,256]{2,1,0:T(8,128)(2,1)S(1)} %collective-permute-done.10, ...), kind=kOutput, calls=%fused_computation.84 | convolution fusion | flops 860547584 | bytes 3775556 | tf_op jit(solution)/shard_map/thf,hfv->thv/dot_general | solution.py:225
  159.0 2.9 %collective-permute-done.12 = f32[512,1024]{1,0:T(8,128)S(1)} collective-permute-done((f32[512,1024]{1,0:T(8,128)S(1)}, f32[512,1024]{1,0:T(8,128)S(1)}, u32[]{:S(2)}, u32[]{:S(2)}) %collective-permute-start.12) | collective-permute-done | bytes 2097184 | tf_op jit(solution)/shard_map/ppermute | solution.py:27
  164.9 23.0 %collective-permute-done.13 = bf16[512,1024]{1,0:T(8,128)(2,1)S(1)} collective-permute-done((bf16[512,1024]{1,0:T(8,128)(2,1)S(1)}, bf16[512,1024]{1,0:T(8,128)(2,1)S(1)}, u32[]{:S(2)}, u32[]{:S(2)}) %collective-permute-start.13) | collective-permute-done | bytes 1048608 | tf_op jit(solution)/shard_map/ppermute | solution.py:33
  (75 shorter events, 27.6 us)
Async XLA Ops:
  0.0 139.3 %copy-start = (f32[2,273,256]{2,0,1:T(2,128)S(1)}, f32[2,273,256]{2,0,1:T(2,128)}, u32[]{:S(2)}) copy-start(f32[2,273,256]{2,0,1:T(2,128)} %param.23) | copy-start | bytes 1677316
  0.0 25.1 %collective-permute-start = (bf16[512,1024]{1,0:T(8,128)(2,1)}, bf16[512,1024]{1,0:T(8,128)(2,1)S(1)}, u32[]{:S(2)}, u32[]{:S(2)}) collective-permute-start(bf16[512,1024]{1,0:T(8,128)(2,1)} %param.12), channel_id=1, source_target_pairs={{0,2},{1,3},{2,0},{3,1},{4,6},{5,7},{6,4},{7,5},{8,10},{9,11},{10,... | collective-permute-start | bytes 3145736 | tf_op jit(solution)/shard_map/ppermute | solution.py:33
  1.5 28.6 %collective-permute-start.1 = (bf16[512,1024]{1,0:T(8,128)(2,1)}, bf16[512,1024]{1,0:T(8,128)(2,1)}, u32[]{:S(2)}, u32[]{:S(2)}) collective-permute-start(bf16[512,1024]{1,0:T(8,128)(2,1)} %param.12), channel_id=1, source_target_pairs={{0,1},{1,0},{2,3},{3,2},{4,5},{5,4},{6,7},{7,6},{8,9},{9,8},{10,11... | collective-permute-start | bytes 3145736 | tf_op jit(solution)/shard_map/ppermute | solution.py:27
  25.1 5.0 %collective-permute-start.2 = (bf16[512,1024]{1,0:T(8,128)(2,1)S(1)}, bf16[512,1024]{1,0:T(8,128)(2,1)}, u32[]{:S(2)}, u32[]{:S(2)}) collective-permute-start(bf16[512,1024]{1,0:T(8,128)(2,1)S(1)} %collective-permute-done), channel_id=1, source_target_pairs={{0,1},{1,0},{2,3},{3,2},{4,5},{5,4},{6,7},{7,6},{8,9},{9,8},{10,11... | collective-permute-start | bytes 3145736 | tf_op jit(solution)/shard_map/ppermute | solution.py:27
  26.0 2.9 %copy-start.4 = (bf16[4096,256]{1,0:T(8,128)(2,1)S(1)}, bf16[4096,256]{1,0:T(8,128)(2,1)}, u32[]{:S(2)}) copy-start(bf16[4096,256]{1,0:T(8,128)(2,1)} %param.16) | copy-start | bytes 6291460
  26.0 3.5 %copy-start.5 = (bf16[4096,256]{1,0:T(8,128)(2,1)S(1)}, bf16[4096,256]{1,0:T(8,128)(2,1)}, u32[]{:S(2)}) copy-start(bf16[4096,256]{1,0:T(8,128)(2,1)} %param.15) | copy-start | bytes 6291460
  29.4 1.2 copy-start.1
  39.5 7.7 %collective-permute-start.3 = (bf16[64,512]{0,1:T(8,128)(2,1)S(1)}, bf16[64,512]{0,1:T(8,128)(2,1)S(1)}, u32[]{:S(2)}, u32[]{:S(2)}) collective-permute-start(bf16[64,512]{0,1:T(8,128)(2,1)S(1)} %pad_maximum_fusion.5), channel_id=1, source_target_pairs={{0,4},{4,8},{8,12},{1,5},{5,9},{9,13},{2,6},{6,10},{10,14},{3,7},{... | collective-permute-start | bytes 196616 | tf_op jit(solution)/shard_map/ppermute | solution.py:17
  57.9 4.5 %collective-permute-start.4 = (f32[512,1024]{1,0:T(8,128)}, f32[512,1024]{1,0:T(8,128)}, u32[]{:S(2)}, u32[]{:S(2)}) collective-permute-start(f32[512,1024]{1,0:T(8,128)} %fusion.78), channel_id=1, source_target_pairs={{0,1},{1,0},{2,3},{3,2},{4,5},{5,4},{6,7},{7,6},{8,9},{9,8},{10,11... | collective-permute-start | bytes 6291464 | tf_op jit(solution)/shard_map/ppermute | solution.py:27
  61.2 8.3 %collective-permute-start.6 = (f32[512,1024]{1,0:T(8,128)}, f32[512,1024]{1,0:T(8,128)}, u32[]{:S(2)}, u32[]{:S(2)}) collective-permute-start(f32[512,1024]{1,0:T(8,128)} %fusion.74), channel_id=1, source_target_pairs={{0,1},{1,0},{2,3},{3,2},{4,5},{5,4},{6,7},{7,6},{8,9},{9,8},{10,11... | collective-permute-start | bytes 6291464 | tf_op jit(solution)/shard_map/ppermute | solution.py:27
  66.1 25.4 %collective-permute-start.5 = (bf16[512,1024]{1,0:T(8,128)(2,1)}, bf16[512,1024]{1,0:T(8,128)(2,1)S(1)}, u32[]{:S(2)}, u32[]{:S(2)}) collective-permute-start(bf16[512,1024]{1,0:T(8,128)(2,1)} %add_convert_fusion.3), channel_id=1, source_target_pairs={{0,2},{1,3},{2,0},{3,1},{4,6},{5,7},{6,4},{7,5},{8,10},{9,11},{10,... | collective-permute-start | bytes 3145736 | tf_op jit(solution)/shard_map/ppermute | solution.py:33
  69.5 48.7 %copy-start.7 = (f32[4096]{0:T(1024)S(1)}, f32[4096]{0:T(1024)}, u32[]{:S(2)}) copy-start(f32[4096]{0:T(1024)} %param.18) | copy-start | bytes 49156
  69.5 48.8 %copy-start.6 = (bf16[4096,64]{0,1:T(8,128)(2,1)S(1)}, bf16[4096,64]{0,1:T(8,128)(2,1)}, u32[]{:S(2)}) copy-start(bf16[4096,64]{0,1:T(8,128)(2,1)} %param.19) | copy-start | bytes 1572868
  69.6 48.8 %copy-start.3 = (bf16[4096,512]{1,0:T(8,128)(2,1)S(1)}, bf16[4096,512]{1,0:T(8,128)(2,1)}, u32[]{:S(2)}) copy-start(bf16[4096,512]{1,0:T(8,128)(2,1)} %param.20) | copy-start | bytes 12582916
  93.8 24.4 %collective-permute-start.7 = (bf16[512,1024]{1,0:T(8,128)(2,1)S(1)}, bf16[512,1024]{1,0:T(8,128)(2,1)S(1)}, u32[]{:S(2)}, u32[]{:S(2)}) collective-permute-start(bf16[512,1024]{1,0:T(8,128)(2,1)S(1)} %add_convert_fusion.2), channel_id=1, source_target_pairs={{0,2},{1,3},{2,0},{3,1},{4,6},{5,7},{6,4},{7,5},{8,10},{9,11},{10,... | collective-permute-start | bytes 3145736 | tf_op jit(solution)/shard_map/ppermute | solution.py:33
  95.3 23.4 %collective-permute-start.8 = (bf16[512,1024]{1,0:T(8,128)(2,1)S(1)}, bf16[512,1024]{1,0:T(8,128)(2,1)S(1)}, u32[]{:S(2)}, u32[]{:S(2)}) collective-permute-start(bf16[512,1024]{1,0:T(8,128)(2,1)S(1)} %add_convert_fusion.2), channel_id=1, source_target_pairs={{0,1},{1,0},{2,3},{3,2},{4,5},{5,4},{6,7},{7,6},{8,9},{9,8},{10,11... | collective-permute-start | bytes 3145736 | tf_op jit(solution)/shard_map/ppermute | solution.py:27
  118.2 2.7 %collective-permute-start.9 = (bf16[512,1024]{1,0:T(8,128)(2,1)S(1)}, bf16[512,1024]{1,0:T(8,128)(2,1)S(1)}, u32[]{:S(2)}, u32[]{:S(2)}) collective-permute-start(bf16[512,1024]{1,0:T(8,128)(2,1)S(1)} %collective-permute-done.7), channel_id=1, source_target_pairs={{0,1},{1,0},{2,3},{3,2},{4,5},{5,4},{6,7},{7,6},{8,9},{9,8},{10,11... | collective-permute-start | bytes 3145736 | tf_op jit(solution)/shard_map/ppermute | solution.py:27
  126.9 10.8 %collective-permute-start.10 = (bf16[2,273,256]{2,1,0:T(8,128)(2,1)S(1)}, bf16[2,273,256]{2,1,0:T(8,128)(2,1)S(1)}, u32[]{:S(2)}, u32[]{:S(2)}) collective-permute-start(bf16[2,273,256]{2,1,0:T(8,128)(2,1)S(1)} %get-tuple-element.41), channel_id=1, source_target_pairs={{0,4},{4,8},{8,12},{1,5},{5,9},{9,13},{2,6},{6,10},{10,14},{3,7},{... | collective-permute-start | bytes 838664 | tf_op jit(solution)/shard_map/ppermute | solution.py:94
  137.7 19.1 %copy-start.8 = (f32[2,256]{1,0:T(2,128)S(1)}, f32[2,256]{1,0:T(2,128)}, u32[]{:S(2)}) copy-start(f32[2,256]{1,0:T(2,128)} %param.21) | copy-start | bytes 6148
  137.8 16.9 %collective-permute-start.11 = (bf16[2,273,256]{2,1,0:T(8,128)(2,1)S(1)}, bf16[2,273,256]{2,1,0:T(8,128)(2,1)S(1)}, u32[]{:S(2)}, u32[]{:S(2)}) collective-permute-start(bf16[2,273,256]{2,1,0:T(8,128)(2,1)S(1)} %fusion.81), channel_id=1, source_target_pairs={{0,8},{4,12},{1,9},{5,13},{2,10},{6,14},{3,11},{7,15},{16,24},{20,... | collective-permute-start | bytes 838664 | tf_op jit(solution)/shard_map/ppermute | solution.py:94
  139.3 17.6 %copy-start.2 = (bf16[512,4096]{1,0:T(8,128)(2,1)S(1)}, bf16[512,4096]{1,0:T(8,128)(2,1)}, u32[]{:S(2)}) copy-start(bf16[512,4096]{1,0:T(8,128)(2,1)} %param.22) | copy-start | bytes 12582916
  157.6 4.2 %collective-permute-start.12 = (f32[512,1024]{1,0:T(8,128)S(1)}, f32[512,1024]{1,0:T(8,128)S(1)}, u32[]{:S(2)}, u32[]{:S(2)}) collective-permute-start(f32[512,1024]{1,0:T(8,128)S(1)} %fusion.71), channel_id=1, source_target_pairs={{0,1},{1,0},{2,3},{3,2},{4,5},{5,4},{6,7},{7,6},{8,9},{9,8},{10,11... | collective-permute-start | bytes 6291464 | tf_op jit(solution)/shard_map/ppermute | solution.py:27
  158.5 6.4 %collective-permute-start.14 = (f32[512,1024]{1,0:T(8,128)S(1)}, f32[512,1024]{1,0:T(8,128)S(1)}, u32[]{:S(2)}, u32[]{:S(2)}) collective-permute-start(f32[512,1024]{1,0:T(8,128)S(1)} %fusion.67), channel_id=1, source_target_pairs={{0,1},{1,0},{2,3},{3,2},{4,5},{5,4},{6,7},{7,6},{8,9},{9,8},{10,11... | collective-permute-start | bytes 6291464 | tf_op jit(solution)/shard_map/ppermute | solution.py:27
  162.6 25.3 %collective-permute-start.13 = (bf16[512,1024]{1,0:T(8,128)(2,1)S(1)}, bf16[512,1024]{1,0:T(8,128)(2,1)S(1)}, u32[]{:S(2)}, u32[]{:S(2)}) collective-permute-start(bf16[512,1024]{1,0:T(8,128)(2,1)S(1)} %add_convert_fusion.1), channel_id=1, source_target_pairs={{0,2},{1,3},{2,0},{3,1},{4,6},{5,7},{6,4},{7,5},{8,10},{9,11},{10,... | collective-permute-start | bytes 3145736 | tf_op jit(solution)/shard_map/ppermute | solution.py:33

commit v14 on v12

--- a/solution.py
+++ b/solution.py
@@ -63,7 +63,7 @@
     return [me] + [r + core for r in ring] + [me ^ 1] + [r + 1 - core for r in ring]
 
 
-def head_all_gather(piece):
+def head_all_gather(piece, dep=None):
     devices, chips = head_layout()
     pieces = [piece, None]
     pieces[1] = core_swap(piece)
@@ -71,6 +71,8 @@
     for step in range(chips - 1):
         cur = chip_shift(cur, 1)
         ring.append(cur)
+    if dep is not None:
+        ring = [lax.optimization_barrier((r, dep))[0] for r in ring]
     forwarded = [core_swap(r) for r in ring]
     return jnp.concatenate([piece] + ring + [pieces[1]] + forwarded, axis=1)
 
@@ -148,7 +150,8 @@
 
     query_parts, kv_parts = [], []
     for part in hidden_parts:
-        normed = norm_rows(head_all_gather(part), attn_gain)
+        ready = (attn_gain, w_query, w_keys, w_values, lin_gain, w_feature, wv_linear)
+        normed = norm_rows(head_all_gather(part, ready), attn_gain)
         query_parts.append(
             jnp.dot(normed, w_query, preferred_element_type=jnp.float32).astype(jnp.bfloat16)
         )

time: 189 us -> 188 us (level)
    dynamic_slice x6 -> x5, local copies, waits for them, and re-layouts: 4.02 us -> 4.06 us  [gathered_rows(): lax.dynamic_slice_in_dim(weight, src * block, block, axis=0)]
where the time goes in v14:
time: 188 us; the launch traced here: 187 us
  waiting for transfers between devices  122 us (65%)
  matrix products  36.8 us (20%)
  starting transfers between devices  11.8 us (6%)
  other arithmetic  10.8 us (6%)
  local copies, waits for them, and re-layouts  5.56 us (3%)
    ppermute x4, waiting for transfers between devices, chip_shift(): return lax.ppermute(value, 'head', pairs)  90.5 us
    ppermute x2, waiting for transfers between devices, earlier_sum(): lax.ppermute(running.astype(jnp.bfloat16), 'ctx', pairs).astype(jnp.float32)  21.8 us
    dot_general x8, matrix products, block(): return jnp.dot(lhs, cols, preferred_element_type=jnp.float32)  15.2 us
    ppermute x4, starting transfers between devices, chip_shift(): return lax.ppermute(value, 'head', pairs)  6.1 us
    ppermute x8, waiting for transfers between devices, core_swap(): return lax.ppermute(value, 'head', [(h, h ^ 1) for h in range(devices)])  5.73 us
    dynamic_slice x5, local copies, waits for them, and re-layouts, gathered_rows(): lax.dynamic_slice_in_dim(weight, src * block, block, axis=0)  4.06 us
    ppermute x1, waiting for transfers between devices, from_behind(): return lax.ppermute(value, axis, pairs)  3.93 us
    sub x1, matrix products, body(): expd = jnp.exp(scores - top)  3.92 us
  transfers between devices with their start and end apart: 15, of which 10 were waited for; matrix products, arithmetic and copies ran while one was open for 11% of the time, Pallas kernels for 0%

profile of v14, /device:TPU:24, one launch (start us, length us, event | category | flops | bytes accessed | tf_op | source)
XLA Modules:
  0.0 187.5 jit_solution(15127266920417252124)
XLA Ops:
  2.3 22.8 %collective-permute-done = bf16[512,1024]{1,0:T(8,128)(2,1)S(1)} collective-permute-done((bf16[512,1024]{1,0:T(8,128)(2,1)}, bf16[512,1024]{1,0:T(8,128)(2,1)S(1)}, u32[]{:S(2)}, u32[]{:S(2)}) %collective-permute-start) | collective-permute-done | bytes 1048608 | tf_op jit(solution)/shard_map/ppermute | solution.py:33
  25.2 2.6 %constant_dynamic-slice_fusion.19 = (bf16[1024,512]{1,0:T(8,128)(2,1)S(1)}, bf16[1024,512]{1,0:T(8,128)(2,1)S(1)}, bf16[1024,512]{1,0:T(8,128)(2,1)S(1)}, bf16[1024,512]{1,0:T(8,128)(2,1)S(1)}) fusion(bf16[4096,512]{1,0:T(8,128)(2,1)} %param.14, s32[]{:T(128)S(6)} %select_n.127, s32[]{:T(128)S(6)} %select_n.131, s32[]{:T(128)S(6)} %select_n.133, ...), kind=kLoop, calls=%fused_computation.112 | loop fusion | bytes 8388624 | tf_op jit(solution)/shard_map/dynamic_slice | solution.py:84
  29.9 2.0 %fusion.1 = f32[512]{0:T(512)S(1)} fusion(bf16[512,1024]{1,0:T(8,128)(2,1)} %collective-permute-done.2, bf16[512,1024]{1,0:T(8,128)(2,1)S(1)} %collective-permute-done.1, bf16[512,1024]{1,0:T(8,128)(2,1)S(1)} %collective-permute-done, bf16[512,1024]{1,0:T(8,128)(2,1)S(1)} %copy-done), kind=kLoop, calls=%fused_computation.5 | loop fusion | flops 20971008 | bytes 4196352 | tf_op jit(solution)/shard_map/reduce_sum | solution.py:105
  31.9 2.4 %fusion.3 = bf16[512,4096]{1,0:T(8,128)(2,1)S(1)} fusion(f32[4096]{0:T(1024)S(1)} %pad_maximum_fusion.8, f32[512]{0:T(512)S(1)} %add_rsqrt_fusion.2, bf16[512,1024]{1,0:T(8,128)(2,1)} %collective-permute-done.2, bf16[512,1024]{1,0:T(8,128)(2,1)S(1)} %collective-permute-done.1, bf16[512,1024]{1,0:T(8,128)(2,1)S(1)} %collective-permute-done, ...), kind=kLoop, calls=%fused_computation.7 | loop fusion | flops 23068672 | bytes 8407040 | tf_op jit(solution)/shard_map/convert_element_type | solution.py:106
  38.6 2.4 %convolution_convert_fusion.1 = bf16[512,512]{0,1:T(8,128)(2,1)S(1)} fusion(bf16[512,4096]{1,0:T(8,128)(2,1)S(1)} %fusion.3, bf16[1024,512]{1,0:T(8,128)(2,1)S(1)} %get-tuple-element.13, bf16[1024,512]{1,0:T(8,128)(2,1)S(1)} %get-tuple-element.14, bf16[1024,512]{1,0:T(8,128)(2,1)S(1)} %get-tuple-element.12, bf16[1024,512]{1,0:T(8,128)(2,1)S(1)} %get-tuple-element.11), kind=kOutput, calls=%fused_computation.33 | convolution fusion | flops 2164523008 | bytes 8912896 | tf_op jit(solution)/shard_map/dot_general | solution.py:156
  40.9 3.9 %collective-permute-done.3 = bf16[64,512]{0,1:T(8,128)(2,1)S(1)} collective-permute-done((bf16[64,512]{0,1:T(8,128)(2,1)S(1)}, bf16[64,512]{0,1:T(8,128)(2,1)S(1)}, u32[]{:S(2)}, u32[]{:S(2)}) %collective-permute-start.3) | collective-permute-done | bytes 65568 | tf_op jit(solution)/shard_map/ppermute | solution.py:17
  45.3 3.9 %fusion.64 = (f32[2,2,512]{2,1,0:T(2,128)S(1)}, f32[2,2,512,576]{2,3,1,0:T(8,128)}) fusion(pred[512,576]{0,1:T(8,128)(4,1)S(1)} %and_and_fusion, bf16[576,2,128,1]{0,2,3,1:T(8,128)(2,1)S(1)} %bitcast.82, bf16[512,2,2,128]{0,3,2,1:T(8,128)(2,1)S(1)} %bitcast.83), kind=kOutput, calls=%fused_computation.127 | convolution fusion | flops 306709056 | bytes 5840896 | tf_op jit(solution)/shard_map/sub | solution.py:183
  49.2 2.9 %fusion.13 = bf16[2,128,2,512]{3,1,2,0:T(8,128)(2,1)S(1)} fusion(bf16[576,2,128,1]{0,2,3,1:T(8,128)(2,1)S(1)} %bitcast.81, f32[2,2,512,576]{2,3,1,0:T(8,128)} %get-tuple-element.42, f32[2,2,512]{2,1,0:T(2,128)S(1)} %get-tuple-element.41), kind=kOutput, calls=%fused_computation.34 | convolution fusion | flops 304611328 | bytes 5545984 | tf_op jit(solution)/shard_map/kgts,skd->tkgd/dot_general | solution.py:185
  52.1 3.3 %fusion.37 = f32[512,1024]{1,0:T(8,128)} fusion(bf16[512,512]{0,1:T(8,128)(2,1)S(1)} %bitcast.70, bf16[512,4096]{1,0:T(8,128)(2,1)} %param.17, s32[]{:T(128)S(6)} %select_n.135), kind=kOutput, calls=%fused_computation.64 | convolution fusion | flops 536870912 | bytes 3670020 | tf_op jit(solution)/shard_map/dot_general | solution.py:45
  55.4 3.3 %fusion.33 = f32[512,1024]{1,0:T(8,128)} fusion(bf16[512,512]{0,1:T(8,128)(2,1)S(1)} %bitcast.71, bf16[512,4096]{1,0:T(8,128)(2,1)} %param.17, s32[]{:T(128)S(6)} %select_n.138), kind=kOutput, calls=%fused_computation.60 | convolution fusion | flops 536870912 | bytes 3670020 | tf_op jit(solution)/shard_map/dot_general | solution.py:45
  59.9 3.6 %add_convert_fusion.3 = bf16[512,1024]{1,0:T(8,128)(2,1)} fusion(f32[512,1024]{1,0:T(8,128)} %collective-permute-done.4, bf16[512,512]{0,1:T(8,128)(2,1)S(1)} %bitcast.72, bf16[512,4096]{1,0:T(8,128)(2,1)} %param.17, s32[]{:T(128)S(6)} %select_n.131), kind=kOutput, calls=%fused_computation.29 | convolution fusion | flops 537919488 | bytes 4718596 | tf_op jit(solution)/shard_map/dot_general | solution.py:45
  65.0 1.9 %fusion.35 = f32[512,1024]{1,0:T(8,128)S(1)} fusion(bf16[512,512]{0,1:T(8,128)(2,1)S(1)} %bitcast.73, bf16[512,4096]{1,0:T(8,128)(2,1)} %param.17, s32[]{:T(128)S(6)} %select_n.137), kind=kOutput, calls=%fused_computation.62 | convolution fusion | flops 536870912 | bytes 3670020 | tf_op jit(solution)/shard_map/dot_general | solution.py:45
  67.0 21.9 %collective-permute-done.5 = bf16[512,1024]{1,0:T(8,128)(2,1)S(1)} collective-permute-done((bf16[512,1024]{1,0:T(8,128)(2,1)}, bf16[512,1024]{1,0:T(8,128)(2,1)S(1)}, u32[]{:S(2)}, u32[]{:S(2)}) %collective-permute-start.5) | collective-permute-done | bytes 1048608 | tf_op jit(solution)/shard_map/ppermute | solution.py:33
  89.0 2.3 %add_convert_fusion.2 = bf16[512,1024]{1,0:T(8,128)(2,1)S(1)} fusion(f32[512,1024]{1,0:T(8,128)S(1)} %fusion.35, f32[512,1024]{1,0:T(8,128)} %collective-permute-done.6, bf16[512,1024]{1,0:T(8,128)(2,1)S(1)} %collective-permute-done.5, bf16[512,1024]{1,0:T(8,128)(2,1)S(1)} %copy-done), kind=kLoop, calls=%fused_computation.28 | loop fusion | flops 3145728 | bytes 7340032 | tf_op jit(solution)/shard_map/convert_element_type | solution.py:190
  92.8 22.9 %collective-permute-done.7 = bf16[512,1024]{1,0:T(8,128)(2,1)S(1)} collective-permute-done((bf16[512,1024]{1,0:T(8,128)(2,1)S(1)}, bf16[512,1024]{1,0:T(8,128)(2,1)S(1)}, u32[]{:S(2)}, u32[]{:S(2)}) %collective-permute-start.7) | collective-permute-done | bytes 1048608 | tf_op jit(solution)/shard_map/ppermute | solution.py:33
  116.2 2.2 %collective-permute-done.9 = bf16[512,1024]{1,0:T(8,128)(2,1)S(1)} collective-permute-done((bf16[512,1024]{1,0:T(8,128)(2,1)S(1)}, bf16[512,1024]{1,0:T(8,128)(2,1)S(1)}, u32[]{:S(2)}, u32[]{:S(2)}) %collective-permute-start.9) | collective-permute-done | bytes 1048608 | tf_op jit(solution)/shard_map/ppermute | solution.py:27
  121.0 2.6 %convolution_convert_fusion = bf16[512,512]{0,1:T(8,128)(2,1)S(1)} fusion(f32[4096]{0:T(1024)S(1)} %pad_maximum_fusion.9, f32[512]{0:T(512)S(1)} %add_rsqrt_fusion.1, bf16[512,1024]{1,0:T(8,128)(2,1)S(1)} %collective-permute-done.9, bf16[512,1024]{1,0:T(8,128)(2,1)S(1)} %collective-permute-done.8, bf16[512,1024]{1,0:T(8,128)(2,1)S(1)} %collective-permute-done.7, ...), kind=kOutput, calls=%fused_computation.32 | convolution fusion | flops 2187591680 | bytes 8931328 | tf_op jit(solution)/shard_map/dot_general | solution.py:203
  125.9 2.3 %select_convert_fusion = bf16[2,512,512]{2,1,0:T(8,128)(2,1)S(1)} fusion(pred[512,512]{1,0:T(8,128)(4,1)S(1)} %iota_compare_fusion, f32[512,2,2,16]{0,3,2,1:T(8,128)S(1)} %bitcast.80), kind=kOutput, calls=%fused_computation.27 | convolution fusion | flops 104333312 | bytes 1441792 | tf_op jit(solution)/shard_map/thf,shf->hts/dot_general | solution.py:222
  128.2 7.0 %collective-permute-done.10 = bf16[2,273,256]{2,1,0:T(8,128)(2,1)S(1)} collective-permute-done((bf16[2,273,256]{2,1,0:T(8,128)(2,1)S(1)}, bf16[2,273,256]{2,1,0:T(8,128)(2,1)S(1)}, u32[]{:S(2)}, u32[]{:S(2)}) %collective-permute-start.10) | collective-permute-done | bytes 279584 | tf_op jit(solution)/shard_map/ppermute | solution.py:96
  135.3 1.8 collective-permute-start.11
  137.6 14.8 %collective-permute-done.11 = bf16[2,273,256]{2,1,0:T(8,128)(2,1)S(1)} collective-permute-done((bf16[2,273,256]{2,1,0:T(8,128)(2,1)S(1)}, bf16[2,273,256]{2,1,0:T(8,128)(2,1)S(1)}, u32[]{:S(2)}, u32[]{:S(2)}) %collective-permute-start.11) | collective-permute-done | bytes 279584 | tf_op jit(solution)/shard_map/ppermute | solution.py:96
  152.4 2.1 %multiply_reduce_fusion = (f32[512,2]{0,1:T(2,128)S(1)}, f32[512,2,256]{0,2,1:T(8,128)S(1)}) fusion(f32[2,256,512]{2,1,0:T(8,128)S(1)} %fusion.66, f32[512,2,256]{0,2,1:T(8,128)S(1)} %bitcast.74, f32[512,2,16]{0,2,1:T(8,128)S(1)} %get-tuple-element.30, f32[273]{0:T(512)S(1)} %pad.3.clone, bf16[2,273,256]{2,1,0:T(8,128)(2,1)S(1)} %collective-permute-done.10, ...), kind=kOutput, calls=%fused_computation.56 | convolution fusion | flops 860687360 | bytes 4334660 | tf_op jit(solution)/shard_map/thf,hfv->thv/dot_general | solution.py:221
  156.9 2.8 %collective-permute-done.12 = f32[512,1024]{1,0:T(8,128)S(1)} collective-permute-done((f32[512,1024]{1,0:T(8,128)S(1)}, f32[512,1024]{1,0:T(8,128)S(1)}, u32[]{:S(2)}, u32[]{:S(2)}) %collective-permute-start.12) | collective-permute-done | bytes 2097184 | tf_op jit(solution)/shard_map/ppermute | solution.py:27
  162.8 23.0 %collective-permute-done.13 = bf16[512,1024]{1,0:T(8,128)(2,1)S(1)} collective-permute-done((bf16[512,1024]{1,0:T(8,128)(2,1)S(1)}, bf16[512,1024]{1,0:T(8,128)(2,1)S(1)}, u32[]{:S(2)}, u32[]{:S(2)}) %collective-permute-start.13) | collective-permute-done | bytes 1048608 | tf_op jit(solution)/shard_map/ppermute | solution.py:33
  (71 shorter events, 26.1 us)
Async XLA Ops:
  0.0 25.1 %collective-permute-start = (bf16[512,1024]{1,0:T(8,128)(2,1)}, bf16[512,1024]{1,0:T(8,128)(2,1)S(1)}, u32[]{:S(2)}, u32[]{:S(2)}) collective-permute-start(bf16[512,1024]{1,0:T(8,128)(2,1)} %param.12), channel_id=1, source_target_pairs={{0,2},{1,3},{2,0},{3,1},{4,6},{5,7},{6,4},{7,5},{8,10},{9,11},{10,... | collective-permute-start | bytes 3145736 | tf_op jit(solution)/shard_map/ppermute | solution.py:33
  1.5 27.8 %collective-permute-start.1 = (bf16[512,1024]{1,0:T(8,128)(2,1)}, bf16[512,1024]{1,0:T(8,128)(2,1)S(1)}, u32[]{:S(2)}, u32[]{:S(2)}) collective-permute-start(bf16[512,1024]{1,0:T(8,128)(2,1)} %param.12), channel_id=1, source_target_pairs={{0,1},{1,0},{2,3},{3,2},{4,5},{5,4},{6,7},{7,6},{8,9},{9,8},{10,11... | collective-permute-start | bytes 3145736 | tf_op jit(solution)/shard_map/ppermute | solution.py:27
  25.1 4.2 %collective-permute-start.2 = (bf16[512,1024]{1,0:T(8,128)(2,1)S(1)}, bf16[512,1024]{1,0:T(8,128)(2,1)}, u32[]{:S(2)}, u32[]{:S(2)}) collective-permute-start(bf16[512,1024]{1,0:T(8,128)(2,1)S(1)} %collective-permute-done), channel_id=1, source_target_pairs={{0,1},{1,0},{2,3},{3,2},{4,5},{5,4},{6,7},{7,6},{8,9},{9,8},{10,11... | collective-permute-start | bytes 3145736 | tf_op jit(solution)/shard_map/ppermute | solution.py:27
  25.1 2.9 %copy-start.3 = (bf16[4096,256]{1,0:T(8,128)(2,1)S(1)}, bf16[4096,256]{1,0:T(8,128)(2,1)}, u32[]{:S(2)}) copy-start(bf16[4096,256]{1,0:T(8,128)(2,1)} %param.16) | copy-start | bytes 6291460
  25.2 3.5 %copy-start.4 = (bf16[4096,256]{1,0:T(8,128)(2,1)S(1)}, bf16[4096,256]{1,0:T(8,128)(2,1)}, u32[]{:S(2)}) copy-start(bf16[4096,256]{1,0:T(8,128)(2,1)} %param.15) | copy-start | bytes 6291460
  28.6 1.2 copy-start
  37.1 7.8 %collective-permute-start.3 = (bf16[64,512]{0,1:T(8,128)(2,1)S(1)}, bf16[64,512]{0,1:T(8,128)(2,1)S(1)}, u32[]{:S(2)}, u32[]{:S(2)}) collective-permute-start(bf16[64,512]{0,1:T(8,128)(2,1)S(1)} %pad_maximum_fusion.7), channel_id=1, source_target_pairs={{0,4},{4,8},{8,12},{1,5},{5,9},{9,13},{2,6},{6,10},{10,14},{3,7},{... | collective-permute-start | bytes 196616 | tf_op jit(solution)/shard_map/ppermute | solution.py:17
  55.4 4.5 %collective-permute-start.4 = (f32[512,1024]{1,0:T(8,128)}, f32[512,1024]{1,0:T(8,128)}, u32[]{:S(2)}, u32[]{:S(2)}) collective-permute-start(f32[512,1024]{1,0:T(8,128)} %fusion.37), channel_id=1, source_target_pairs={{0,1},{1,0},{2,3},{3,2},{4,5},{5,4},{6,7},{7,6},{8,9},{9,8},{10,11... | collective-permute-start | bytes 6291464 | tf_op jit(solution)/shard_map/ppermute | solution.py:27
  58.7 8.3 %collective-permute-start.6 = (f32[512,1024]{1,0:T(8,128)}, f32[512,1024]{1,0:T(8,128)}, u32[]{:S(2)}, u32[]{:S(2)}) collective-permute-start(f32[512,1024]{1,0:T(8,128)} %fusion.33), channel_id=1, source_target_pairs={{0,1},{1,0},{2,3},{3,2},{4,5},{5,4},{6,7},{7,6},{8,9},{9,8},{10,11... | collective-permute-start | bytes 6291464 | tf_op jit(solution)/shard_map/ppermute | solution.py:27
  63.5 25.4 %collective-permute-start.5 = (bf16[512,1024]{1,0:T(8,128)(2,1)}, bf16[512,1024]{1,0:T(8,128)(2,1)S(1)}, u32[]{:S(2)}, u32[]{:S(2)}) collective-permute-start(bf16[512,1024]{1,0:T(8,128)(2,1)} %add_convert_fusion.3), channel_id=1, source_target_pairs={{0,2},{1,3},{2,0},{3,1},{4,6},{5,7},{6,4},{7,5},{8,10},{9,11},{10,... | collective-permute-start | bytes 3145736 | tf_op jit(solution)/shard_map/ppermute | solution.py:33
  67.0 48.8 %copy-start.6 = (bf16[4096,64]{0,1:T(8,128)(2,1)S(1)}, bf16[4096,64]{0,1:T(8,128)(2,1)}, u32[]{:S(2)}) copy-start(bf16[4096,64]{0,1:T(8,128)(2,1)} %param.19) | copy-start | bytes 1572868
  67.0 48.8 %copy-start.2 = (bf16[4096,512]{1,0:T(8,128)(2,1)S(1)}, bf16[4096,512]{1,0:T(8,128)(2,1)}, u32[]{:S(2)}) copy-start(bf16[4096,512]{1,0:T(8,128)(2,1)} %param.20) | copy-start | bytes 12582916
  91.2 24.4 %collective-permute-start.7 = (bf16[512,1024]{1,0:T(8,128)(2,1)S(1)}, bf16[512,1024]{1,0:T(8,128)(2,1)S(1)}, u32[]{:S(2)}, u32[]{:S(2)}) collective-permute-start(bf16[512,1024]{1,0:T(8,128)(2,1)S(1)} %add_convert_fusion.2), channel_id=1, source_target_pairs={{0,2},{1,3},{2,0},{3,1},{4,6},{5,7},{6,4},{7,5},{8,10},{9,11},{10,... | collective-permute-start | bytes 3145736 | tf_op jit(solution)/shard_map/ppermute | solution.py:33
  92.8 23.3 %collective-permute-start.8 = (bf16[512,1024]{1,0:T(8,128)(2,1)S(1)}, bf16[512,1024]{1,0:T(8,128)(2,1)S(1)}, u32[]{:S(2)}, u32[]{:S(2)}) collective-permute-start(bf16[512,1024]{1,0:T(8,128)(2,1)S(1)} %add_convert_fusion.2), channel_id=1, source_target_pairs={{0,1},{1,0},{2,3},{3,2},{4,5},{5,4},{6,7},{7,6},{8,9},{9,8},{10,11... | collective-permute-start | bytes 3145736 | tf_op jit(solution)/shard_map/ppermute | solution.py:27
  115.7 2.7 %collective-permute-start.9 = (bf16[512,1024]{1,0:T(8,128)(2,1)S(1)}, bf16[512,1024]{1,0:T(8,128)(2,1)S(1)}, u32[]{:S(2)}, u32[]{:S(2)}) collective-permute-start(bf16[512,1024]{1,0:T(8,128)(2,1)S(1)} %collective-permute-done.7), channel_id=1, source_target_pairs={{0,1},{1,0},{2,3},{3,2},{4,5},{5,4},{6,7},{7,6},{8,9},{9,8},{10,11... | collective-permute-start | bytes 3145736 | tf_op jit(solution)/shard_map/ppermute | solution.py:27
  124.4 10.8 %collective-permute-start.10 = (bf16[2,273,256]{2,1,0:T(8,128)(2,1)S(1)}, bf16[2,273,256]{2,1,0:T(8,128)(2,1)S(1)}, u32[]{:S(2)}, u32[]{:S(2)}) collective-permute-start(bf16[2,273,256]{2,1,0:T(8,128)(2,1)S(1)} %get-tuple-element.43), channel_id=1, source_target_pairs={{0,4},{4,8},{8,12},{1,5},{5,9},{9,13},{2,6},{6,10},{10,14},{3,7},{... | collective-permute-start | bytes 838664 | tf_op jit(solution)/shard_map/ppermute | solution.py:96
  125.9 26.6 %copy-start.5 = (f32[2,273,256]{2,0,1:T(2,128)S(1)}, f32[2,273,256]{2,0,1:T(2,128)}, u32[]{:S(2)}) copy-start(f32[2,273,256]{2,0,1:T(2,128)} %param.23) | copy-start | bytes 1677316
  128.2 26.4 %copy-start.7 = (f32[2,256]{1,0:T(2,128)S(1)}, f32[2,256]{1,0:T(2,128)}, u32[]{:S(2)}) copy-start(f32[2,256]{1,0:T(2,128)} %param.21) | copy-start | bytes 6148
  135.3 19.5 %copy-start.1 = (bf16[512,4096]{1,0:T(8,128)(2,1)S(1)}, bf16[512,4096]{1,0:T(8,128)(2,1)}, u32[]{:S(2)}) copy-start(bf16[512,4096]{1,0:T(8,128)(2,1)} %param.22) | copy-start | bytes 12582916
  135.3 17.1 %collective-permute-start.11 = (bf16[2,273,256]{2,1,0:T(8,128)(2,1)S(1)}, bf16[2,273,256]{2,1,0:T(8,128)(2,1)S(1)}, u32[]{:S(2)}, u32[]{:S(2)}) collective-permute-start(bf16[2,273,256]{2,1,0:T(8,128)(2,1)S(1)} %fusion.40), channel_id=1, source_target_pairs={{0,8},{4,12},{1,9},{5,13},{2,10},{6,14},{3,11},{7,15},{16,24},{20,... | collective-permute-start | bytes 838664 | tf_op jit(solution)/shard_map/ppermute | solution.py:96
  155.5 4.2 %collective-permute-start.12 = (f32[512,1024]{1,0:T(8,128)S(1)}, f32[512,1024]{1,0:T(8,128)S(1)}, u32[]{:S(2)}, u32[]{:S(2)}) collective-permute-start(f32[512,1024]{1,0:T(8,128)S(1)} %fusion.30), channel_id=1, source_target_pairs={{0,1},{1,0},{2,3},{3,2},{4,5},{5,4},{6,7},{7,6},{8,9},{9,8},{10,11... | collective-permute-start | bytes 6291464 | tf_op jit(solution)/shard_map/ppermute | solution.py:27
  156.3 6.5 %collective-permute-start.14 = (f32[512,1024]{1,0:T(8,128)S(1)}, f32[512,1024]{1,0:T(8,128)S(1)}, u32[]{:S(2)}, u32[]{:S(2)}) collective-permute-start(f32[512,1024]{1,0:T(8,128)S(1)} %fusion.26), channel_id=1, source_target_pairs={{0,1},{1,0},{2,3},{3,2},{4,5},{5,4},{6,7},{7,6},{8,9},{9,8},{10,11... | collective-permute-start | bytes 6291464 | tf_op jit(solution)/shard_map/ppermute | solution.py:27
  160.5 25.3 %collective-permute-start.13 = (bf16[512,1024]{1,0:T(8,128)(2,1)S(1)}, bf16[512,1024]{1,0:T(8,128)(2,1)S(1)}, u32[]{:S(2)}, u32[]{:S(2)}) collective-permute-start(bf16[512,1024]{1,0:T(8,128)(2,1)S(1)} %add_convert_fusion.1), channel_id=1, source_target_pairs={{0,2},{1,3},{2,0},{3,1},{4,6},{5,7},{6,4},{7,5},{8,10},{9,11},{10,... | collective-permute-start | bytes 3145736 | tf_op jit(solution)/shard_map/ppermute | solution.py:33

commit v15 on v14

--- a/solution.py
+++ b/solution.py
@@ -152,13 +152,22 @@
     for part in hidden_parts:
         ready = (attn_gain, w_query, w_keys, w_values, lin_gain, w_feature, wv_linear)
         normed = norm_rows(head_all_gather(part, ready), attn_gain)
+        last_normed = normed
         query_parts.append(
             jnp.dot(normed, w_query, preferred_element_type=jnp.float32).astype(jnp.bfloat16)
         )
         keys = jnp.dot(normed, w_keys, preferred_element_type=jnp.float32).astype(jnp.bfloat16)
         values = jnp.dot(normed, w_values, preferred_element_type=jnp.float32).astype(jnp.bfloat16)
         kv_parts.append(jnp.concatenate([keys, values], axis=1))
-    rim = from_behind(kv_parts[-1][size - WINDOW :], "ctx", 1)
+    tail_normed = last_normed[size - WINDOW :]
+    tail_kv = jnp.concatenate(
+        [
+            jnp.dot(tail_normed, w_keys, preferred_element_type=jnp.float32).astype(jnp.bfloat16),
+            jnp.dot(tail_normed, w_values, preferred_element_type=jnp.float32).astype(jnp.bfloat16),
+        ],
+        axis=1,
+    )
+    rim = from_behind(tail_kv, "ctx", 1)
     kv_all = jnp.concatenate([rim] + kv_parts, axis=0)
     start = lax.axis_index("ctx") * tok_rows
 

time: 188 us -> 185 us (0.984)
  waiting for transfers between devices: 122 us -> 114 us
  other arithmetic: 10.8 us -> 13.9 us
    ppermute x4, waiting for transfers between devices: 90.5 us -> 85.2 us  [chip_shift(): return lax.ppermute(value, 'head', pairs)]
    concatenate x2 -> x4, other arithmetic: 0.01 us -> 2.93 us  [gathered_rows(): jnp.concatenate([lax.dynamic_slice_in_dim(weight, src * block, block, axi...]
    ppermute x1, waiting for transfers between devices: 3.93 us -> 1.23 us  [from_behind(): return lax.ppermute(value, axis, pairs)]
    dynamic_slice x5, local copies, waits for them, and re-layouts: 4.06 us -> 6.1 us  [gathered_rows(): lax.dynamic_slice_in_dim(weight, src * block, block, axis=0)]
  transfers between devices with their start and end apart: 15 -> 15, of which waited for: 10 -> 10; matrix products, arithmetic and copies ran while one was open for 11% -> 15% of each run, Pallas kernels for 0% -> 0%
where the time goes in v15:
time: 185 us; the launch traced here: 184 us
  waiting for transfers between devices  114 us (62%)
  matrix products  37.7 us (20%)
  other arithmetic  13.9 us (8%)
  starting transfers between devices  11.8 us (6%)
  local copies, waits for them, and re-layouts  6.34 us (3%)
    ppermute x4, waiting for transfers between devices, chip_shift(): return lax.ppermute(value, 'head', pairs)  85.2 us
    ppermute x2, waiting for transfers between devices, earlier_sum(): lax.ppermute(running.astype(jnp.bfloat16), 'ctx', pairs).astype(jnp.float32)  21.9 us
    dot_general x8, matrix products, block(): return jnp.dot(lhs, cols, preferred_element_type=jnp.float32)  15.1 us
    dynamic_slice x5, local copies, waits for them, and re-layouts, gathered_rows(): lax.dynamic_slice_in_dim(weight, src * block, block, axis=0)  6.1 us
    ppermute x4, starting transfers between devices, chip_shift(): return lax.ppermute(value, 'head', pairs)  6.09 us
    ppermute x8, waiting for transfers between devices, core_swap(): return lax.ppermute(value, 'head', [(h, h ^ 1) for h in range(devices)])  5.75 us
    sub x1, matrix products, body(): expd = jnp.exp(scores - top)  3.92 us
  transfers between devices with their start and end apart: 15, of which 10 were waited for; matrix products, arithmetic and copies ran while one was open for 15% of the time, Pallas kernels for 0%

profile of v15, /device:TPU:24, one launch (start us, length us, event | category | flops | bytes accessed | tf_op | source)
XLA Modules:
  0.0 184.3 jit_solution(4389069274689688641)
XLA Ops:
  2.3 2.4 %constant_dynamic-slice_fusion.11 = (bf16[1024,256]{1,0:T(8,128)(2,1)S(1)}, bf16[1024,256]{1,0:T(8,128)(2,1)S(1)}, bf16[1024,256]{1,0:T(8,128)(2,1)S(1)}, bf16[1...) fusion(bf16[4096,256]{1,0:T(8,128)(2,1)} %param.16, ...), kind=kLoop, calls=%fused_computation.108 | loop fusion | bytes 8388624 | tf_op jit(solution)/shard_map/dynamic_slice | solution.py:84
  7.7 17.4 %collective-permute-done = bf16[512,1024]{1,0:T(8,128)(2,1)S(1)} collective-permute-done((bf16[512,1024]{1,0:T(8,128)(2,1)}, bf16[512,1024]{1,0:T(8,128)(2,1)S(1)}, u32[]{:S(2)}, u32[]{:S(2)}) %collective-permute-start) | collective-permute-done | bytes 1048608 | tf_op jit(solution)/shard_map/ppermute | solution.py:33
  25.2 2.5 %constant_dynamic-slice_fusion.19 = (bf16[1024,512]{1,0:T(8,128)(2,1)S(1)}, bf16[1024,512]{1,0:T(8,128)(2,1)S(1)}, bf16[1024,512]{1,0:T(8,128)(2,1)S(1)}, bf16[1024,512]{1,0:T(8,128)(2,1)S(1)}) fusion(bf16[4096,512]{1,0:T(8,128)(2,1)} %param.14, s32[]{:T(128)S(6)} %select_n.127, s32[]{:T(128)S(6)} %select_n.131, s32[]{:T(128)S(6)} %select_n.133, ...), kind=kLoop, calls=%fused_computation.116 | loop fusion | bytes 8388624 | tf_op jit(solution)/shard_map/dynamic_slice | solution.py:84
  28.1 2.0 %fusion.1 = f32[512]{0:T(512)S(1)} fusion(bf16[512,1024]{1,0:T(8,128)(2,1)} %collective-permute-done.2, bf16[512,1024]{1,0:T(8,128)(2,1)S(1)} %collective-permute-done.1, bf16[512,1024]{1,0:T(8,128)(2,1)S(1)} %collective-permute-done, bf16[512,1024]{1,0:T(8,128)(2,1)S(1)} %copy-done), kind=kLoop, calls=%fused_computation.5 | loop fusion | flops 20971008 | bytes 4196352 | tf_op jit(solution)/shard_map/reduce_sum | solution.py:105
  30.1 2.6 %fusion.3 = bf16[512,4096]{1,0:T(8,128)(2,1)S(1)} fusion(f32[4096]{0:T(1024)S(1)} %pad_maximum_fusion.8, f32[512]{0:T(512)S(1)} %add_rsqrt_fusion.2, bf16[512,1024]{1,0:T(8,128)(2,1)} %collective-permute-done.2, bf16[512,1024]{1,0:T(8,128)(2,1)S(1)} %collective-permute-done.1, bf16[512,1024]{1,0:T(8,128)(2,1)S(1)} %collective-permute-done, ...), kind=kLoop, calls=%fused_computation.7 | loop fusion | flops 23068672 | bytes 8407040 | tf_op jit(solution)/shard_map/convert_element_type | solution.py:106
  36.5 2.4 %convolution_convert_fusion.1 = bf16[512,512]{0,1:T(8,128)(2,1)S(1)} fusion(bf16[512,4096]{1,0:T(8,128)(2,1)S(1)} %fusion.3, bf16[1024,512]{1,0:T(8,128)(2,1)S(1)} %get-tuple-element.13, bf16[1024,512]{1,0:T(8,128)(2,1)S(1)} %get-tuple-element.14, bf16[1024,512]{1,0:T(8,128)(2,1)S(1)} %get-tuple-element.12, bf16[1024,512]{1,0:T(8,128)(2,1)S(1)} %get-tuple-element.11), kind=kOutput, calls=%fused_computation.33 | convolution fusion | flops 2164523008 | bytes 8912896 | tf_op jit(solution)/shard_map/dot_general | solution.py:157
  41.9 3.9 %fusion.66 = (f32[2,2,512]{2,1,0:T(2,128)S(1)}, f32[2,2,512,576]{2,3,1,0:T(8,128)}) fusion(pred[512,576]{0,1:T(8,128)(4,1)S(1)} %and_and_fusion, bf16[576,2,128,1]{0,2,3,1:T(8,128)(2,1)S(1)} %bitcast.86, bf16[512,2,2,128]{0,3,2,1:T(8,128)(2,1)S(1)} %bitcast.87), kind=kOutput, calls=%fused_computation.131 | convolution fusion | flops 306709056 | bytes 5840896 | tf_op jit(solution)/shard_map/sub | solution.py:192
  45.8 2.9 %fusion.13 = bf16[2,128,2,512]{3,1,2,0:T(8,128)(2,1)S(1)} fusion(bf16[576,2,128,1]{0,2,3,1:T(8,128)(2,1)S(1)} %bitcast.85, f32[2,2,512,576]{2,3,1,0:T(8,128)} %get-tuple-element.42, f32[2,2,512]{2,1,0:T(2,128)S(1)} %get-tuple-element.41), kind=kOutput, calls=%fused_computation.34 | convolution fusion | flops 304611328 | bytes 5545984 | tf_op jit(solution)/shard_map/kgts,skd->tkgd/dot_general | solution.py:194
  48.7 3.3 %fusion.37 = f32[512,1024]{1,0:T(8,128)} fusion(bf16[512,512]{0,1:T(8,128)(2,1)S(1)} %bitcast.74, bf16[512,4096]{1,0:T(8,128)(2,1)} %param.17, s32[]{:T(128)S(6)} %select_n.135), kind=kOutput, calls=%fused_computation.66 | convolution fusion | flops 536870912 | bytes 3670020 | tf_op jit(solution)/shard_map/dot_general | solution.py:45
  52.1 3.3 %fusion.33 = f32[512,1024]{1,0:T(8,128)} fusion(bf16[512,512]{0,1:T(8,128)(2,1)S(1)} %bitcast.75, bf16[512,4096]{1,0:T(8,128)(2,1)} %param.17, s32[]{:T(128)S(6)} %select_n.138), kind=kOutput, calls=%fused_computation.62 | convolution fusion | flops 536870912 | bytes 3670020 | tf_op jit(solution)/shard_map/dot_general | solution.py:45
  56.6 3.6 %add_convert_fusion.3 = bf16[512,1024]{1,0:T(8,128)(2,1)} fusion(f32[512,1024]{1,0:T(8,128)} %collective-permute-done.4, bf16[512,512]{0,1:T(8,128)(2,1)S(1)} %bitcast.76, bf16[512,4096]{1,0:T(8,128)(2,1)} %param.17, s32[]{:T(128)S(6)} %select_n.131), kind=kOutput, calls=%fused_computation.29 | convolution fusion | flops 537919488 | bytes 4718596 | tf_op jit(solution)/shard_map/dot_general | solution.py:45
  61.7 1.9 %fusion.35 = f32[512,1024]{1,0:T(8,128)S(1)} fusion(bf16[512,512]{0,1:T(8,128)(2,1)S(1)} %bitcast.77, bf16[512,4096]{1,0:T(8,128)(2,1)} %param.17, s32[]{:T(128)S(6)} %select_n.137), kind=kOutput, calls=%fused_computation.64 | convolution fusion | flops 536870912 | bytes 3670020 | tf_op jit(solution)/shard_map/dot_general | solution.py:45
  63.7 21.9 %collective-permute-done.5 = bf16[512,1024]{1,0:T(8,128)(2,1)S(1)} collective-permute-done((bf16[512,1024]{1,0:T(8,128)(2,1)}, bf16[512,1024]{1,0:T(8,128)(2,1)S(1)}, u32[]{:S(2)}, u32[]{:S(2)}) %collective-permute-start.5) | collective-permute-done | bytes 1048608 | tf_op jit(solution)/shard_map/ppermute | solution.py:33
  85.6 2.3 %add_convert_fusion.2 = bf16[512,1024]{1,0:T(8,128)(2,1)S(1)} fusion(f32[512,1024]{1,0:T(8,128)S(1)} %fusion.35, f32[512,1024]{1,0:T(8,128)} %collective-permute-done.6, bf16[512,1024]{1,0:T(8,128)(2,1)S(1)} %collective-permute-done.5, bf16[512,1024]{1,0:T(8,128)(2,1)S(1)} %copy-done), kind=kLoop, calls=%fused_computation.28 | loop fusion | flops 3145728 | bytes 7340032 | tf_op jit(solution)/shard_map/convert_element_type | solution.py:199
  89.5 22.9 %collective-permute-done.7 = bf16[512,1024]{1,0:T(8,128)(2,1)S(1)} collective-permute-done((bf16[512,1024]{1,0:T(8,128)(2,1)S(1)}, bf16[512,1024]{1,0:T(8,128)(2,1)S(1)}, u32[]{:S(2)}, u32[]{:S(2)}) %collective-permute-start.7) | collective-permute-done | bytes 1048608 | tf_op jit(solution)/shard_map/ppermute | solution.py:33
  112.9 2.2 %collective-permute-done.9 = bf16[512,1024]{1,0:T(8,128)(2,1)S(1)} collective-permute-done((bf16[512,1024]{1,0:T(8,128)(2,1)S(1)}, bf16[512,1024]{1,0:T(8,128)(2,1)S(1)}, u32[]{:S(2)}, u32[]{:S(2)}) %collective-permute-start.9) | collective-permute-done | bytes 1048608 | tf_op jit(solution)/shard_map/ppermute | solution.py:27
  117.7 2.6 %convolution_convert_fusion = bf16[512,512]{0,1:T(8,128)(2,1)S(1)} fusion(f32[4096]{0:T(1024)S(1)} %pad_maximum_fusion.9, f32[512]{0:T(512)S(1)} %add_rsqrt_fusion.1, bf16[512,1024]{1,0:T(8,128)(2,1)S(1)} %collective-permute-done.9, bf16[512,1024]{1,0:T(8,128)(2,1)S(1)} %collective-permute-done.8, bf16[512,1024]{1,0:T(8,128)(2,1)S(1)} %collective-permute-done.7, ...), kind=kOutput, calls=%fused_computation.32 | convolution fusion | flops 2187591680 | bytes 8931328 | tf_op jit(solution)/shard_map/dot_general | solution.py:212
  122.6 2.3 %select_convert_fusion = bf16[2,512,512]{2,1,0:T(8,128)(2,1)S(1)} fusion(pred[512,512]{1,0:T(8,128)(4,1)S(1)} %iota_compare_fusion, f32[512,2,2,16]{0,3,2,1:T(8,128)S(1)} %bitcast.84), kind=kOutput, calls=%fused_computation.27 | convolution fusion | flops 104333312 | bytes 1441792 | tf_op jit(solution)/shard_map/thf,shf->hts/dot_general | solution.py:231
  125.0 6.9 %collective-permute-done.10 = bf16[2,273,256]{2,1,0:T(8,128)(2,1)S(1)} collective-permute-done((bf16[2,273,256]{2,1,0:T(8,128)(2,1)S(1)}, bf16[2,273,256]{2,1,0:T(8,128)(2,1)S(1)}, u32[]{:S(2)}, u32[]{:S(2)}) %collective-permute-start.10) | collective-permute-done | bytes 279584 | tf_op jit(solution)/shard_map/ppermute | solution.py:96
  132.0 1.8 collective-permute-start.11
  134.3 15.0 %collective-permute-done.11 = bf16[2,273,256]{2,1,0:T(8,128)(2,1)S(1)} collective-permute-done((bf16[2,273,256]{2,1,0:T(8,128)(2,1)S(1)}, bf16[2,273,256]{2,1,0:T(8,128)(2,1)S(1)}, u32[]{:S(2)}, u32[]{:S(2)}) %collective-permute-start.11) | collective-permute-done | bytes 279584 | tf_op jit(solution)/shard_map/ppermute | solution.py:96
  149.3 2.1 %multiply_reduce_fusion = (f32[512,2]{0,1:T(2,128)S(1)}, f32[512,2,256]{0,2,1:T(8,128)S(1)}) fusion(f32[2,256,512]{2,1,0:T(8,128)S(1)} %fusion.68, f32[512,2,256]{0,2,1:T(8,128)S(1)} %bitcast.78, f32[512,2,16]{0,2,1:T(8,128)S(1)} %get-tuple-element.30, f32[273]{0:T(512)S(1)} %pad.3.clone, bf16[2,273,256]{2,1,0:T(8,128)(2,1)S(1)} %collective-permute-done.10, ...), kind=kOutput, calls=%fused_computation.58 | convolution fusion | flops 860687360 | bytes 4334660 | tf_op jit(solution)/shard_map/thf,hfv->thv/dot_general | solution.py:230
  153.7 2.9 %collective-permute-done.12 = f32[512,1024]{1,0:T(8,128)S(1)} collective-permute-done((f32[512,1024]{1,0:T(8,128)S(1)}, f32[512,1024]{1,0:T(8,128)S(1)}, u32[]{:S(2)}, u32[]{:S(2)}) %collective-permute-start.12) | collective-permute-done | bytes 2097184 | tf_op jit(solution)/shard_map/ppermute | solution.py:27
  159.6 23.0 %collective-permute-done.13 = bf16[512,1024]{1,0:T(8,128)(2,1)S(1)} collective-permute-done((bf16[512,1024]{1,0:T(8,128)(2,1)S(1)}, bf16[512,1024]{1,0:T(8,128)(2,1)S(1)}, u32[]{:S(2)}, u32[]{:S(2)}) %collective-permute-start.13) | collective-permute-done | bytes 1048608 | tf_op jit(solution)/shard_map/ppermute | solution.py:33
  (76 shorter events, 29.5 us)
Async XLA Ops:
  0.0 25.1 %collective-permute-start = (bf16[512,1024]{1,0:T(8,128)(2,1)}, bf16[512,1024]{1,0:T(8,128)(2,1)S(1)}, u32[]{:S(2)}, u32[]{:S(2)}) collective-permute-start(bf16[512,1024]{1,0:T(8,128)(2,1)} %param.12), channel_id=1, source_target_pairs={{0,2},{1,3},{2,0},{3,1},{4,6},{5,7},{6,4},{7,5},{8,10},{9,11},{10,... | collective-permute-start | bytes 3145736 | tf_op jit(solution)/shard_map/ppermute | solution.py:33
  1.5 26.6 %collective-permute-start.1 = (bf16[512,1024]{1,0:T(8,128)(2,1)}, bf16[512,1024]{1,0:T(8,128)(2,1)S(1)}, u32[]{:S(2)}, u32[]{:S(2)}) collective-permute-start(bf16[512,1024]{1,0:T(8,128)(2,1)} %param.12), channel_id=1, source_target_pairs={{0,1},{1,0},{2,3},{3,2},{4,5},{5,4},{6,7},{7,6},{8,9},{9,8},{10,11... | collective-permute-start | bytes 3145736 | tf_op jit(solution)/shard_map/ppermute | solution.py:27
  25.1 3.0 %collective-permute-start.2 = (bf16[512,1024]{1,0:T(8,128)(2,1)S(1)}, bf16[512,1024]{1,0:T(8,128)(2,1)}, u32[]{:S(2)}, u32[]{:S(2)}) collective-permute-start(bf16[512,1024]{1,0:T(8,128)(2,1)S(1)} %collective-permute-done), channel_id=1, source_target_pairs={{0,1},{1,0},{2,3},{3,2},{4,5},{5,4},{6,7},{7,6},{8,9},{9,8},{10,11... | collective-permute-start | bytes 3145736 | tf_op jit(solution)/shard_map/ppermute | solution.py:27
  25.1 2.9 %copy-start = (bf16[512,1024]{1,0:T(8,128)(2,1)S(1)}, bf16[512,1024]{1,0:T(8,128)(2,1)}, u32[]{:S(2)}) copy-start(bf16[512,1024]{1,0:T(8,128)(2,1)} %param.12) | copy-start | bytes 3145732
  30.1 2.6 %copy-start.2 = (bf16[4096,256]{1,0:T(8,128)(2,1)S(1)}, bf16[4096,256]{1,0:T(8,128)(2,1)}, u32[]{:S(2)}) copy-start(bf16[4096,256]{1,0:T(8,128)(2,1)} %pad_maximum_fusion.5) | copy-start | bytes 6291460
  32.7 1.8 copy-start.1
  35.0 6.4 %collective-permute-start.3 = (bf16[64,512]{1,0:T(8,128)(2,1)S(1)}, bf16[64,512]{1,0:T(8,128)(2,1)S(1)}, u32[]{:S(2)}, u32[]{:S(2)}) collective-permute-start(bf16[64,512]{1,0:T(8,128)(2,1)S(1)} %pad_maximum_fusion.7), channel_id=1, source_target_pairs={{0,4},{4,8},{8,12},{1,5},{5,9},{9,13},{2,6},{6,10},{10,14},{3,7},{... | collective-permute-start | bytes 196616 | tf_op jit(solution)/shard_map/ppermute | solution.py:17
  52.1 4.5 %collective-permute-start.4 = (f32[512,1024]{1,0:T(8,128)}, f32[512,1024]{1,0:T(8,128)}, u32[]{:S(2)}, u32[]{:S(2)}) collective-permute-start(f32[512,1024]{1,0:T(8,128)} %fusion.37), channel_id=1, source_target_pairs={{0,1},{1,0},{2,3},{3,2},{4,5},{5,4},{6,7},{7,6},{8,9},{9,8},{10,11... | collective-permute-start | bytes 6291464 | tf_op jit(solution)/shard_map/ppermute | solution.py:27
  55.4 8.3 %collective-permute-start.6 = (f32[512,1024]{1,0:T(8,128)}, f32[512,1024]{1,0:T(8,128)}, u32[]{:S(2)}, u32[]{:S(2)}) collective-permute-start(f32[512,1024]{1,0:T(8,128)} %fusion.33), channel_id=1, source_target_pairs={{0,1},{1,0},{2,3},{3,2},{4,5},{5,4},{6,7},{7,6},{8,9},{9,8},{10,11... | collective-permute-start | bytes 6291464 | tf_op jit(solution)/shard_map/ppermute | solution.py:27
  60.2 25.4 %collective-permute-start.5 = (bf16[512,1024]{1,0:T(8,128)(2,1)}, bf16[512,1024]{1,0:T(8,128)(2,1)S(1)}, u32[]{:S(2)}, u32[]{:S(2)}) collective-permute-start(bf16[512,1024]{1,0:T(8,128)(2,1)} %add_convert_fusion.3), channel_id=1, source_target_pairs={{0,2},{1,3},{2,0},{3,1},{4,6},{5,7},{6,4},{7,5},{8,10},{9,11},{10,... | collective-permute-start | bytes 3145736 | tf_op jit(solution)/shard_map/ppermute | solution.py:33
  63.6 48.9 %copy-start.6 = (bf16[4096,64]{0,1:T(8,128)(2,1)S(1)}, bf16[4096,64]{0,1:T(8,128)(2,1)}, u32[]{:S(2)}) copy-start(bf16[4096,64]{0,1:T(8,128)(2,1)} %param.19) | copy-start | bytes 1572868
  63.6 48.9 %copy-start.4 = (bf16[4096,512]{1,0:T(8,128)(2,1)S(1)}, bf16[4096,512]{1,0:T(8,128)(2,1)}, u32[]{:S(2)}) copy-start(bf16[4096,512]{1,0:T(8,128)(2,1)} %param.20) | copy-start | bytes 12582916
  87.9 24.4 %collective-permute-start.7 = (bf16[512,1024]{1,0:T(8,128)(2,1)S(1)}, bf16[512,1024]{1,0:T(8,128)(2,1)S(1)}, u32[]{:S(2)}, u32[]{:S(2)}) collective-permute-start(bf16[512,1024]{1,0:T(8,128)(2,1)S(1)} %add_convert_fusion.2), channel_id=1, source_target_pairs={{0,2},{1,3},{2,0},{3,1},{4,6},{5,7},{6,4},{7,5},{8,10},{9,11},{10,... | collective-permute-start | bytes 3145736 | tf_op jit(solution)/shard_map/ppermute | solution.py:33
  89.5 23.4 %collective-permute-start.8 = (bf16[512,1024]{1,0:T(8,128)(2,1)S(1)}, bf16[512,1024]{1,0:T(8,128)(2,1)S(1)}, u32[]{:S(2)}, u32[]{:S(2)}) collective-permute-start(bf16[512,1024]{1,0:T(8,128)(2,1)S(1)} %add_convert_fusion.2), channel_id=1, source_target_pairs={{0,1},{1,0},{2,3},{3,2},{4,5},{5,4},{6,7},{7,6},{8,9},{9,8},{10,11... | collective-permute-start | bytes 3145736 | tf_op jit(solution)/shard_map/ppermute | solution.py:27
  112.4 2.7 %collective-permute-start.9 = (bf16[512,1024]{1,0:T(8,128)(2,1)S(1)}, bf16[512,1024]{1,0:T(8,128)(2,1)S(1)}, u32[]{:S(2)}, u32[]{:S(2)}) collective-permute-start(bf16[512,1024]{1,0:T(8,128)(2,1)S(1)} %collective-permute-done.7), channel_id=1, source_target_pairs={{0,1},{1,0},{2,3},{3,2},{4,5},{5,4},{6,7},{7,6},{8,9},{9,8},{10,11... | collective-permute-start | bytes 3145736 | tf_op jit(solution)/shard_map/ppermute | solution.py:27
  121.2 10.8 %collective-permute-start.10 = (bf16[2,273,256]{2,1,0:T(8,128)(2,1)S(1)}, bf16[2,273,256]{2,1,0:T(8,128)(2,1)S(1)}, u32[]{:S(2)}, u32[]{:S(2)}) collective-permute-start(bf16[2,273,256]{2,1,0:T(8,128)(2,1)S(1)} %get-tuple-element.43), channel_id=1, source_target_pairs={{0,4},{4,8},{8,12},{1,5},{5,9},{9,13},{2,6},{6,10},{10,14},{3,7},{... | collective-permute-start | bytes 838664 | tf_op jit(solution)/shard_map/ppermute | solution.py:96
  122.6 26.7 %copy-start.5 = (f32[2,273,256]{2,0,1:T(2,128)S(1)}, f32[2,273,256]{2,0,1:T(2,128)}, u32[]{:S(2)}) copy-start(f32[2,273,256]{2,0,1:T(2,128)} %param.23) | copy-start | bytes 1677316
  125.0 26.5 %copy-start.7 = (f32[2,256]{1,0:T(2,128)S(1)}, f32[2,256]{1,0:T(2,128)}, u32[]{:S(2)}) copy-start(f32[2,256]{1,0:T(2,128)} %param.21) | copy-start | bytes 6148
  132.0 19.6 %copy-start.3 = (bf16[512,4096]{1,0:T(8,128)(2,1)S(1)}, bf16[512,4096]{1,0:T(8,128)(2,1)}, u32[]{:S(2)}) copy-start(bf16[512,4096]{1,0:T(8,128)(2,1)} %param.22) | copy-start | bytes 12582916
  132.0 17.2 %collective-permute-start.11 = (bf16[2,273,256]{2,1,0:T(8,128)(2,1)S(1)}, bf16[2,273,256]{2,1,0:T(8,128)(2,1)S(1)}, u32[]{:S(2)}, u32[]{:S(2)}) collective-permute-start(bf16[2,273,256]{2,1,0:T(8,128)(2,1)S(1)} %fusion.40), channel_id=1, source_target_pairs={{0,8},{4,12},{1,9},{5,13},{2,10},{6,14},{3,11},{7,15},{16,24},{20,... | collective-permute-start | bytes 838664 | tf_op jit(solution)/shard_map/ppermute | solution.py:96
  152.3 4.2 %collective-permute-start.12 = (f32[512,1024]{1,0:T(8,128)S(1)}, f32[512,1024]{1,0:T(8,128)S(1)}, u32[]{:S(2)}, u32[]{:S(2)}) collective-permute-start(f32[512,1024]{1,0:T(8,128)S(1)} %fusion.30), channel_id=1, source_target_pairs={{0,1},{1,0},{2,3},{3,2},{4,5},{5,4},{6,7},{7,6},{8,9},{9,8},{10,11... | collective-permute-start | bytes 6291464 | tf_op jit(solution)/shard_map/ppermute | solution.py:27
  153.2 6.4 %collective-permute-start.14 = (f32[512,1024]{1,0:T(8,128)S(1)}, f32[512,1024]{1,0:T(8,128)S(1)}, u32[]{:S(2)}, u32[]{:S(2)}) collective-permute-start(f32[512,1024]{1,0:T(8,128)S(1)} %fusion.26), channel_id=1, source_target_pairs={{0,1},{1,0},{2,3},{3,2},{4,5},{5,4},{6,7},{7,6},{8,9},{9,8},{10,11... | collective-permute-start | bytes 6291464 | tf_op jit(solution)/shard_map/ppermute | solution.py:27
  157.3 25.3 %collective-permute-start.13 = (bf16[512,1024]{1,0:T(8,128)(2,1)S(1)}, bf16[512,1024]{1,0:T(8,128)(2,1)S(1)}, u32[]{:S(2)}, u32[]{:S(2)}) collective-permute-start(bf16[512,1024]{1,0:T(8,128)(2,1)S(1)} %add_convert_fusion.1), channel_id=1, source_target_pairs={{0,2},{1,3},{2,0},{3,1},{4,6},{5,7},{6,4},{7,5},{8,10},{9,11},{10,... | collective-permute-start | bytes 3145736 | tf_op jit(solution)/shard_map/ppermute | solution.py:33

commit v16 on v15

--- a/solution.py
+++ b/solution.py
@@ -86,14 +86,15 @@
     )
 
 
-def earlier_sum(local):
+def earlier_sum(local, dep):
     count = lax.axis_size("ctx")
     running = local
     total = jnp.zeros(local.shape, jnp.float32)
     by = 1
     while by < count:
         pairs = [(i, i + by) for i in range(count - by)]
-        got = lax.ppermute(running.astype(jnp.bfloat16), "ctx", pairs).astype(jnp.float32)
+        got = lax.ppermute(running.astype(jnp.bfloat16), "ctx", pairs)
+        got = lax.optimization_barrier((got, dep))[0].astype(jnp.float32)
         total = total + got
         running = running + got
         by *= 2
@@ -221,19 +222,24 @@
     local_state = jnp.einsum(
         "thf,thv->hfv", phi_key, lvalues.astype(jnp.float32), precision=highest
     )
-    carried = entry_state + earlier_sum(local_state)
+    intra_parts = []
+    for i in range(CHUNKS):
+        sims = jnp.einsum(
+            "thf,shf->hts", qf_parts[i], key_feat, precision=highest
+        ) / math.sqrt(FEAT)
+        causal = (i * size + jnp.arange(size))[:, None] >= jnp.arange(tok_rows)[None, :]
+        weights = jnp.where(causal[None], 1.0 + sims + 0.5 * sims * sims, 0.0).astype(jnp.bfloat16)
+        intra_parts.append(
+            jnp.einsum("hts,shv->thv", weights, lvalues, preferred_element_type=jnp.float32)
+        )
+    carried = entry_state + earlier_sum(local_state, intra_parts)
 
     outs = []
     for i in range(CHUNKS):
         query_feat = qf_parts[i]
         phi_query = taylor(query_feat)
         cross = jnp.einsum("thf,hfv->thv", phi_query, carried, precision=highest)
-        sims = jnp.einsum(
-            "thf,shf->hts", query_feat, key_feat, precision=highest
-        ) / math.sqrt(FEAT)
-        causal = (i * size + jnp.arange(size))[:, None] >= jnp.arange(tok_rows)[None, :]
-        weights = jnp.where(causal[None], 1.0 + sims + 0.5 * sims * sims, 0.0).astype(jnp.bfloat16)
-        intra = jnp.einsum("hts,shv->thv", weights, lvalues, preferred_element_type=jnp.float32)
+        intra = intra_parts[i]
         lin_out = cross + intra
         scale = lax.rsqrt(jnp.mean(lin_out * lin_out, axis=-1, keepdims=True) + 1e-05)
         lin_normed = (

time: 185 us -> 187 us (1.011)
  waiting for transfers between devices: 114 us -> 116 us
    ppermute x2, waiting for transfers between devices: 21.9 us -> 24.3 us  [earlier_sum(): got = lax.ppermute(running.astype(jnp.bfloat16), 'ctx', pairs)]
  transfers between devices with their start and end apart: 15 -> 15, of which waited for: 10 -> 10; matrix products, arithmetic and copies ran while one was open for 15% -> 13% of each run, Pallas kernels for 0% -> 0%
where the time goes in v16:
time: 187 us; the launch traced here: 186 us
  waiting for transfers between devices  116 us (62%)
  matrix products  37.7 us (20%)
  other arithmetic  13.9 us (7%)
  starting transfers between devices  11.6 us (6%)
  local copies, waits for them, and re-layouts  6.34 us (3%)
    ppermute x4, waiting for transfers between devices, chip_shift(): return lax.ppermute(value, 'head', pairs)  85.2 us
    ppermute x2, waiting for transfers between devices, earlier_sum(): got = lax.ppermute(running.astype(jnp.bfloat16), 'ctx', pairs)  24.3 us
    dot_general x8, matrix products, block(): return jnp.dot(lhs, cols, preferred_element_type=jnp.float32)  15.1 us
    dynamic_slice x5, local copies, waits for them, and re-layouts, gathered_rows(): lax.dynamic_slice_in_dim(weight, src * block, block, axis=0)  6.1 us
    ppermute x4, starting transfers between devices, chip_shift(): return lax.ppermute(value, 'head', pairs)  6.09 us
    ppermute x8, waiting for transfers between devices, core_swap(): return lax.ppermute(value, 'head', [(h, h ^ 1) for h in range(devices)])  5.75 us
    sub x1, matrix products, body(): expd = jnp.exp(scores - top)  3.92 us
  transfers between devices with their start and end apart: 15, of which 10 were waited for; matrix products, arithmetic and copies ran while one was open for 13% of the time, Pallas kernels for 0%

profile of v16, /device:TPU:24, one launch (start us, length us, event | category | flops | bytes accessed | tf_op | source)
XLA Modules:
  0.0 186.4 jit_solution(7650786359471000846)
XLA Ops:
  2.3 2.4 %constant_dynamic-slice_fusion.11 = (bf16[1024,256]{1,0:T(8,128)(2,1)S(1)}, bf16[1024,256]{1,0:T(8,128)(2,1)S(1)}, bf16[1024,256]{1,0:T(8,128)(2,1)S(1)}, bf16[1...) fusion(bf16[4096,256]{1,0:T(8,128)(2,1)} %param.16, ...), kind=kLoop, calls=%fused_computation.109 | loop fusion | bytes 8388624 | tf_op jit(solution)/shard_map/dynamic_slice | solution.py:84
  7.7 17.4 %collective-permute-done = bf16[512,1024]{1,0:T(8,128)(2,1)S(1)} collective-permute-done((bf16[512,1024]{1,0:T(8,128)(2,1)}, bf16[512,1024]{1,0:T(8,128)(2,1)S(1)}, u32[]{:S(2)}, u32[]{:S(2)}) %collective-permute-start) | collective-permute-done | bytes 1048608 | tf_op jit(solution)/shard_map/ppermute | solution.py:33
  25.2 2.5 %constant_dynamic-slice_fusion.19 = (bf16[1024,512]{1,0:T(8,128)(2,1)S(1)}, bf16[1024,512]{1,0:T(8,128)(2,1)S(1)}, bf16[1024,512]{1,0:T(8,128)(2,1)S(1)}, bf16[1024,512]{1,0:T(8,128)(2,1)S(1)}) fusion(bf16[4096,512]{1,0:T(8,128)(2,1)} %param.14, s32[]{:T(128)S(6)} %select_n.127, s32[]{:T(128)S(6)} %select_n.131, s32[]{:T(128)S(6)} %select_n.133, ...), kind=kLoop, calls=%fused_computation.117 | loop fusion | bytes 8388624 | tf_op jit(solution)/shard_map/dynamic_slice | solution.py:84
  28.1 2.0 %fusion.1 = f32[512]{0:T(512)S(1)} fusion(bf16[512,1024]{1,0:T(8,128)(2,1)} %collective-permute-done.2, bf16[512,1024]{1,0:T(8,128)(2,1)S(1)} %collective-permute-done.1, bf16[512,1024]{1,0:T(8,128)(2,1)S(1)} %collective-permute-done, bf16[512,1024]{1,0:T(8,128)(2,1)S(1)} %copy-done), kind=kLoop, calls=%fused_computation.5 | loop fusion | flops 20971008 | bytes 4196352 | tf_op jit(solution)/shard_map/reduce_sum | solution.py:106
  30.1 2.6 %fusion.3 = bf16[512,4096]{1,0:T(8,128)(2,1)S(1)} fusion(f32[4096]{0:T(1024)S(1)} %pad_maximum_fusion.8, f32[512]{0:T(512)S(1)} %add_rsqrt_fusion.2, bf16[512,1024]{1,0:T(8,128)(2,1)} %collective-permute-done.2, bf16[512,1024]{1,0:T(8,128)(2,1)S(1)} %collective-permute-done.1, bf16[512,1024]{1,0:T(8,128)(2,1)S(1)} %collective-permute-done, ...), kind=kLoop, calls=%fused_computation.7 | loop fusion | flops 23068672 | bytes 8407040 | tf_op jit(solution)/shard_map/convert_element_type | solution.py:107
  36.5 2.4 %convolution_convert_fusion.1 = bf16[512,512]{0,1:T(8,128)(2,1)S(1)} fusion(bf16[512,4096]{1,0:T(8,128)(2,1)S(1)} %fusion.3, bf16[1024,512]{1,0:T(8,128)(2,1)S(1)} %get-tuple-element.17, bf16[1024,512]{1,0:T(8,128)(2,1)S(1)} %get-tuple-element.18, bf16[1024,512]{1,0:T(8,128)(2,1)S(1)} %get-tuple-element.16, bf16[1024,512]{1,0:T(8,128)(2,1)S(1)} %get-tuple-element.15), kind=kOutput, calls=%fused_computation.34 | convolution fusion | flops 2164523008 | bytes 8912896 | tf_op jit(solution)/shard_map/dot_general | solution.py:158
  41.9 3.9 %fusion.66 = (f32[2,2,512]{2,1,0:T(2,128)S(1)}, f32[2,2,512,576]{2,3,1,0:T(8,128)}) fusion(pred[512,576]{0,1:T(8,128)(4,1)S(1)} %and_and_fusion, bf16[576,2,128,1]{0,2,3,1:T(8,128)(2,1)S(1)} %bitcast.90, bf16[512,2,2,128]{0,3,2,1:T(8,128)(2,1)S(1)} %bitcast.91), kind=kOutput, calls=%fused_computation.132 | convolution fusion | flops 306709056 | bytes 5840896 | tf_op jit(solution)/shard_map/sub | solution.py:193
  45.8 2.9 %fusion.13 = bf16[2,128,2,512]{3,1,2,0:T(8,128)(2,1)S(1)} fusion(bf16[576,2,128,1]{0,2,3,1:T(8,128)(2,1)S(1)} %bitcast.89, f32[2,2,512,576]{2,3,1,0:T(8,128)} %get-tuple-element.46, f32[2,2,512]{2,1,0:T(2,128)S(1)} %get-tuple-element.45), kind=kOutput, calls=%fused_computation.35 | convolution fusion | flops 304611328 | bytes 5545984 | tf_op jit(solution)/shard_map/kgts,skd->tkgd/dot_general | solution.py:195
  48.7 3.3 %fusion.37 = f32[512,1024]{1,0:T(8,128)} fusion(bf16[512,512]{0,1:T(8,128)(2,1)S(1)} %bitcast.78, bf16[512,4096]{1,0:T(8,128)(2,1)} %param.17, s32[]{:T(128)S(6)} %select_n.135), kind=kOutput, calls=%fused_computation.67 | convolution fusion | flops 536870912 | bytes 3670020 | tf_op jit(solution)/shard_map/dot_general | solution.py:45
  52.1 3.3 %fusion.33 = f32[512,1024]{1,0:T(8,128)} fusion(bf16[512,512]{0,1:T(8,128)(2,1)S(1)} %bitcast.79, bf16[512,4096]{1,0:T(8,128)(2,1)} %param.17, s32[]{:T(128)S(6)} %select_n.138), kind=kOutput, calls=%fused_computation.63 | convolution fusion | flops 536870912 | bytes 3670020 | tf_op jit(solution)/shard_map/dot_general | solution.py:45
  56.6 3.6 %add_convert_fusion.3 = bf16[512,1024]{1,0:T(8,128)(2,1)} fusion(f32[512,1024]{1,0:T(8,128)} %collective-permute-done.4, bf16[512,512]{0,1:T(8,128)(2,1)S(1)} %bitcast.80, bf16[512,4096]{1,0:T(8,128)(2,1)} %param.17, s32[]{:T(128)S(6)} %select_n.131), kind=kOutput, calls=%fused_computation.29 | convolution fusion | flops 537919488 | bytes 4718596 | tf_op jit(solution)/shard_map/dot_general | solution.py:45
  61.7 1.9 %fusion.35 = f32[512,1024]{1,0:T(8,128)S(1)} fusion(bf16[512,512]{0,1:T(8,128)(2,1)S(1)} %bitcast.81, bf16[512,4096]{1,0:T(8,128)(2,1)} %param.17, s32[]{:T(128)S(6)} %select_n.137), kind=kOutput, calls=%fused_computation.65 | convolution fusion | flops 536870912 | bytes 3670020 | tf_op jit(solution)/shard_map/dot_general | solution.py:45
  63.7 21.9 %collective-permute-done.5 = bf16[512,1024]{1,0:T(8,128)(2,1)S(1)} collective-permute-done((bf16[512,1024]{1,0:T(8,128)(2,1)}, bf16[512,1024]{1,0:T(8,128)(2,1)S(1)}, u32[]{:S(2)}, u32[]{:S(2)}) %collective-permute-start.5) | collective-permute-done | bytes 1048608 | tf_op jit(solution)/shard_map/ppermute | solution.py:33
  85.6 2.3 %add_convert_fusion.2 = bf16[512,1024]{1,0:T(8,128)(2,1)S(1)} fusion(f32[512,1024]{1,0:T(8,128)S(1)} %fusion.35, f32[512,1024]{1,0:T(8,128)} %collective-permute-done.6, bf16[512,1024]{1,0:T(8,128)(2,1)S(1)} %collective-permute-done.5, bf16[512,1024]{1,0:T(8,128)(2,1)S(1)} %copy-done), kind=kLoop, calls=%fused_computation.28 | loop fusion | flops 3145728 | bytes 7340032 | tf_op jit(solution)/shard_map/convert_element_type | solution.py:200
  89.5 22.9 %collective-permute-done.7 = bf16[512,1024]{1,0:T(8,128)(2,1)S(1)} collective-permute-done((bf16[512,1024]{1,0:T(8,128)(2,1)S(1)}, bf16[512,1024]{1,0:T(8,128)(2,1)S(1)}, u32[]{:S(2)}, u32[]{:S(2)}) %collective-permute-start.7) | collective-permute-done | bytes 1048608 | tf_op jit(solution)/shard_map/ppermute | solution.py:33
  112.9 2.2 %collective-permute-done.9 = bf16[512,1024]{1,0:T(8,128)(2,1)S(1)} collective-permute-done((bf16[512,1024]{1,0:T(8,128)(2,1)S(1)}, bf16[512,1024]{1,0:T(8,128)(2,1)S(1)}, u32[]{:S(2)}, u32[]{:S(2)}) %collective-permute-start.9) | collective-permute-done | bytes 1048608 | tf_op jit(solution)/shard_map/ppermute | solution.py:27
  117.6 2.3 %select_convert_fusion = bf16[2,512,512]{2,1,0:T(8,128)(2,1)S(1)} fusion(pred[512,512]{1,0:T(8,128)(4,1)S(1)} %iota_compare_fusion, f32[512,2,2,16]{0,3,2,1:T(8,128)S(1)} %bitcast.88), kind=kOutput, calls=%fused_computation.27 | convolution fusion | flops 104333312 | bytes 1441792 | tf_op jit(solution)/shard_map/thf,shf->hts/dot_general | solution.py:227
  120.1 2.6 %convolution_convert_fusion = bf16[512,512]{0,1:T(8,128)(2,1)S(1)} fusion(f32[4096]{0:T(1024)S(1)} %pad_maximum_fusion.9, f32[512]{0:T(512)S(1)} %add_rsqrt_fusion.1, bf16[512,1024]{1,0:T(8,128)(2,1)S(1)} %collective-permute-done.9, bf16[512,1024]{1,0:T(8,128)(2,1)S(1)} %collective-permute-done.8, bf16[512,1024]{1,0:T(8,128)(2,1)S(1)} %collective-permute-done.7, ...), kind=kOutput, calls=%fused_computation.33 | convolution fusion | flops 2187591680 | bytes 8931328 | tf_op jit(solution)/shard_map/dot_general | solution.py:213
  125.3 9.0 %collective-permute-done.10 = bf16[2,273,256]{2,1,0:T(8,128)(2,1)S(1)} collective-permute-done((bf16[2,273,256]{2,1,0:T(8,128)(2,1)S(1)}, bf16[2,273,256]{2,1,0:T(8,128)(2,1)S(1)}, u32[]{:S(2)}, u32[]{:S(2)}) %collective-permute-start.10) | collective-permute-done | bytes 279584 | tf_op jit(solution)/shard_map/ppermute | solution.py:96
  136.1 15.3 %collective-permute-done.11 = bf16[2,273,256]{2,1,0:T(8,128)(2,1)S(1)} collective-permute-done((bf16[2,273,256]{2,1,0:T(8,128)(2,1)S(1)}, bf16[2,273,256]{2,1,0:T(8,128)(2,1)S(1)}, u32[]{:S(2)}, u32[]{:S(2)}) %collective-permute-start.11) | collective-permute-done | bytes 279584 | tf_op jit(solution)/shard_map/ppermute | solution.py:96
  151.4 2.1 %multiply_reduce_fusion = (f32[512,2]{0,1:T(2,128)S(1)}, f32[512,2,256]{0,2,1:T(8,128)S(1)}) fusion(f32[512,2,256]{0,2,1:T(8,128)S(1)} %convolution_bitcast_fusion.1, f32[512,2,256]{0,2,1:T(8,128)S(1)} %bitcast.82, f32[512,2,16]{0,2,1:T(8,128)S(1)} %get-tuple-element.34, f32[273]{0:T(512)S(1)} %pad.3.clone, ...), kind=kOutput, calls=%fused_computation.59 | convolution fusion | flops 860687360 | bytes 4334660 | tf_op jit(solution)/shard_map/thf,hfv->thv/dot_general | solution.py:241
  155.8 2.9 %collective-permute-done.12 = f32[512,1024]{1,0:T(8,128)S(1)} collective-permute-done((f32[512,1024]{1,0:T(8,128)S(1)}, f32[512,1024]{1,0:T(8,128)S(1)}, u32[]{:S(2)}, u32[]{:S(2)}) %collective-permute-start.12) | collective-permute-done | bytes 2097184 | tf_op jit(solution)/shard_map/ppermute | solution.py:27
  161.7 23.0 %collective-permute-done.13 = bf16[512,1024]{1,0:T(8,128)(2,1)S(1)} collective-permute-done((bf16[512,1024]{1,0:T(8,128)(2,1)S(1)}, bf16[512,1024]{1,0:T(8,128)(2,1)S(1)}, u32[]{:S(2)}, u32[]{:S(2)}) %collective-permute-start.13) | collective-permute-done | bytes 1048608 | tf_op jit(solution)/shard_map/ppermute | solution.py:33
  184.7 1.7 add_convert_fusion
  (76 shorter events, 29.3 us)
Async XLA Ops:
  0.0 25.1 %collective-permute-start = (bf16[512,1024]{1,0:T(8,128)(2,1)}, bf16[512,1024]{1,0:T(8,128)(2,1)S(1)}, u32[]{:S(2)}, u32[]{:S(2)}) collective-permute-start(bf16[512,1024]{1,0:T(8,128)(2,1)} %param.12), channel_id=1, source_target_pairs={{0,2},{1,3},{2,0},{3,1},{4,6},{5,7},{6,4},{7,5},{8,10},{9,11},{10,... | collective-permute-start | bytes 3145736 | tf_op jit(solution)/shard_map/ppermute | solution.py:33
  1.5 26.6 %collective-permute-start.1 = (bf16[512,1024]{1,0:T(8,128)(2,1)}, bf16[512,1024]{1,0:T(8,128)(2,1)S(1)}, u32[]{:S(2)}, u32[]{:S(2)}) collective-permute-start(bf16[512,1024]{1,0:T(8,128)(2,1)} %param.12), channel_id=1, source_target_pairs={{0,1},{1,0},{2,3},{3,2},{4,5},{5,4},{6,7},{7,6},{8,9},{9,8},{10,11... | collective-permute-start | bytes 3145736 | tf_op jit(solution)/shard_map/ppermute | solution.py:27
  25.1 3.0 %collective-permute-start.2 = (bf16[512,1024]{1,0:T(8,128)(2,1)S(1)}, bf16[512,1024]{1,0:T(8,128)(2,1)}, u32[]{:S(2)}, u32[]{:S(2)}) collective-permute-start(bf16[512,1024]{1,0:T(8,128)(2,1)S(1)} %collective-permute-done), channel_id=1, source_target_pairs={{0,1},{1,0},{2,3},{3,2},{4,5},{5,4},{6,7},{7,6},{8,9},{9,8},{10,11... | collective-permute-start | bytes 3145736 | tf_op jit(solution)/shard_map/ppermute | solution.py:27
  25.1 2.9 %copy-start = (bf16[512,1024]{1,0:T(8,128)(2,1)S(1)}, bf16[512,1024]{1,0:T(8,128)(2,1)}, u32[]{:S(2)}) copy-start(bf16[512,1024]{1,0:T(8,128)(2,1)} %param.12) | copy-start | bytes 3145732
  30.1 2.6 %copy-start.2 = (bf16[4096,256]{1,0:T(8,128)(2,1)S(1)}, bf16[4096,256]{1,0:T(8,128)(2,1)}, u32[]{:S(2)}) copy-start(bf16[4096,256]{1,0:T(8,128)(2,1)} %pad_maximum_fusion.5) | copy-start | bytes 6291460
  32.7 1.8 copy-start.1
  35.0 6.4 %collective-permute-start.3 = (bf16[64,512]{1,0:T(8,128)(2,1)S(1)}, bf16[64,512]{1,0:T(8,128)(2,1)S(1)}, u32[]{:S(2)}, u32[]{:S(2)}) collective-permute-start(bf16[64,512]{1,0:T(8,128)(2,1)S(1)} %pad_maximum_fusion.7), channel_id=1, source_target_pairs={{0,4},{4,8},{8,12},{1,5},{5,9},{9,13},{2,6},{6,10},{10,14},{3,7},{... | collective-permute-start | bytes 196616 | tf_op jit(solution)/shard_map/ppermute | solution.py:17
  52.1 4.5 %collective-permute-start.4 = (f32[512,1024]{1,0:T(8,128)}, f32[512,1024]{1,0:T(8,128)}, u32[]{:S(2)}, u32[]{:S(2)}) collective-permute-start(f32[512,1024]{1,0:T(8,128)} %fusion.37), channel_id=1, source_target_pairs={{0,1},{1,0},{2,3},{3,2},{4,5},{5,4},{6,7},{7,6},{8,9},{9,8},{10,11... | collective-permute-start | bytes 6291464 | tf_op jit(solution)/shard_map/ppermute | solution.py:27
  55.4 8.3 %collective-permute-start.6 = (f32[512,1024]{1,0:T(8,128)}, f32[512,1024]{1,0:T(8,128)}, u32[]{:S(2)}, u32[]{:S(2)}) collective-permute-start(f32[512,1024]{1,0:T(8,128)} %fusion.33), channel_id=1, source_target_pairs={{0,1},{1,0},{2,3},{3,2},{4,5},{5,4},{6,7},{7,6},{8,9},{9,8},{10,11... | collective-permute-start | bytes 6291464 | tf_op jit(solution)/shard_map/ppermute | solution.py:27
  60.2 25.4 %collective-permute-start.5 = (bf16[512,1024]{1,0:T(8,128)(2,1)}, bf16[512,1024]{1,0:T(8,128)(2,1)S(1)}, u32[]{:S(2)}, u32[]{:S(2)}) collective-permute-start(bf16[512,1024]{1,0:T(8,128)(2,1)} %add_convert_fusion.3), channel_id=1, source_target_pairs={{0,2},{1,3},{2,0},{3,1},{4,6},{5,7},{6,4},{7,5},{8,10},{9,11},{10,... | collective-permute-start | bytes 3145736 | tf_op jit(solution)/shard_map/ppermute | solution.py:33
  63.6 48.9 %copy-start.6 = (bf16[4096,64]{0,1:T(8,128)(2,1)S(1)}, bf16[4096,64]{0,1:T(8,128)(2,1)}, u32[]{:S(2)}) copy-start(bf16[4096,64]{0,1:T(8,128)(2,1)} %param.19) | copy-start | bytes 1572868
  63.6 48.9 %copy-start.4 = (bf16[4096,512]{1,0:T(8,128)(2,1)S(1)}, bf16[4096,512]{1,0:T(8,128)(2,1)}, u32[]{:S(2)}) copy-start(bf16[4096,512]{1,0:T(8,128)(2,1)} %param.20) | copy-start | bytes 12582916
  87.9 24.4 %collective-permute-start.7 = (bf16[512,1024]{1,0:T(8,128)(2,1)S(1)}, bf16[512,1024]{1,0:T(8,128)(2,1)S(1)}, u32[]{:S(2)}, u32[]{:S(2)}) collective-permute-start(bf16[512,1024]{1,0:T(8,128)(2,1)S(1)} %add_convert_fusion.2), channel_id=1, source_target_pairs={{0,2},{1,3},{2,0},{3,1},{4,6},{5,7},{6,4},{7,5},{8,10},{9,11},{10,... | collective-permute-start | bytes 3145736 | tf_op jit(solution)/shard_map/ppermute | solution.py:33
  89.5 23.4 %collective-permute-start.8 = (bf16[512,1024]{1,0:T(8,128)(2,1)S(1)}, bf16[512,1024]{1,0:T(8,128)(2,1)S(1)}, u32[]{:S(2)}, u32[]{:S(2)}) collective-permute-start(bf16[512,1024]{1,0:T(8,128)(2,1)S(1)} %add_convert_fusion.2), channel_id=1, source_target_pairs={{0,1},{1,0},{2,3},{3,2},{4,5},{5,4},{6,7},{7,6},{8,9},{9,8},{10,11... | collective-permute-start | bytes 3145736 | tf_op jit(solution)/shard_map/ppermute | solution.py:27
  112.4 2.7 %collective-permute-start.9 = (bf16[512,1024]{1,0:T(8,128)(2,1)S(1)}, bf16[512,1024]{1,0:T(8,128)(2,1)S(1)}, u32[]{:S(2)}, u32[]{:S(2)}) collective-permute-start(bf16[512,1024]{1,0:T(8,128)(2,1)S(1)} %collective-permute-done.7), channel_id=1, source_target_pairs={{0,1},{1,0},{2,3},{3,2},{4,5},{5,4},{6,7},{7,6},{8,9},{9,8},{10,11... | collective-permute-start | bytes 3145736 | tf_op jit(solution)/shard_map/ppermute | solution.py:27
  122.7 28.7 %copy-start.5 = (f32[2,273,256]{2,0,1:T(2,128)S(1)}, f32[2,273,256]{2,0,1:T(2,128)}, u32[]{:S(2)}) copy-start(f32[2,273,256]{2,0,1:T(2,128)} %param.23) | copy-start | bytes 1677316
  123.5 30.0 %copy-start.7 = (f32[2,256]{1,0:T(2,128)S(1)}, f32[2,256]{1,0:T(2,128)}, u32[]{:S(2)}) copy-start(f32[2,256]{1,0:T(2,128)} %param.21) | copy-start | bytes 6148
  123.5 10.8 %collective-permute-start.10 = (bf16[2,273,256]{2,1,0:T(8,128)(2,1)S(1)}, bf16[2,273,256]{2,1,0:T(8,128)(2,1)S(1)}, u32[]{:S(2)}, u32[]{:S(2)}) collective-permute-start(bf16[2,273,256]{2,1,0:T(8,128)(2,1)S(1)} %get-tuple-element.47), channel_id=1, source_target_pairs={{0,4},{4,8},{8,12},{1,5},{5,9},{9,13},{2,6},{6,10},{10,14},{3,7},{... | collective-permute-start | bytes 838664 | tf_op jit(solution)/shard_map/ppermute | solution.py:96
  125.3 28.4 %copy-start.3 = (bf16[512,4096]{1,0:T(8,128)(2,1)S(1)}, bf16[512,4096]{1,0:T(8,128)(2,1)}, u32[]{:S(2)}) copy-start(bf16[512,4096]{1,0:T(8,128)(2,1)} %param.22) | copy-start | bytes 12582916
  134.4 17.0 %collective-permute-start.11 = (bf16[2,273,256]{2,1,0:T(8,128)(2,1)S(1)}, bf16[2,273,256]{2,1,0:T(8,128)(2,1)S(1)}, u32[]{:S(2)}, u32[]{:S(2)}) collective-permute-start(bf16[2,273,256]{2,1,0:T(8,128)(2,1)S(1)} %fusion.40), channel_id=1, source_target_pairs={{0,8},{4,12},{1,9},{5,13},{2,10},{6,14},{3,11},{7,15},{16,24},{20,... | collective-permute-start | bytes 838664 | tf_op jit(solution)/shard_map/ppermute | solution.py:96
  154.4 4.2 %collective-permute-start.12 = (f32[512,1024]{1,0:T(8,128)S(1)}, f32[512,1024]{1,0:T(8,128)S(1)}, u32[]{:S(2)}, u32[]{:S(2)}) collective-permute-start(f32[512,1024]{1,0:T(8,128)S(1)} %fusion.30), channel_id=1, source_target_pairs={{0,1},{1,0},{2,3},{3,2},{4,5},{5,4},{6,7},{7,6},{8,9},{9,8},{10,11... | collective-permute-start | bytes 6291464 | tf_op jit(solution)/shard_map/ppermute | solution.py:27
  155.3 6.4 %collective-permute-start.14 = (f32[512,1024]{1,0:T(8,128)S(1)}, f32[512,1024]{1,0:T(8,128)S(1)}, u32[]{:S(2)}, u32[]{:S(2)}) collective-permute-start(f32[512,1024]{1,0:T(8,128)S(1)} %fusion.26), channel_id=1, source_target_pairs={{0,1},{1,0},{2,3},{3,2},{4,5},{5,4},{6,7},{7,6},{8,9},{9,8},{10,11... | collective-permute-start | bytes 6291464 | tf_op jit(solution)/shard_map/ppermute | solution.py:27
  159.4 25.3 %collective-permute-start.13 = (bf16[512,1024]{1,0:T(8,128)(2,1)S(1)}, bf16[512,1024]{1,0:T(8,128)(2,1)S(1)}, u32[]{:S(2)}, u32[]{:S(2)}) collective-permute-start(bf16[512,1024]{1,0:T(8,128)(2,1)S(1)} %add_convert_fusion.1), channel_id=1, source_target_pairs={{0,2},{1,3},{2,0},{3,1},{4,6},{5,7},{6,4},{7,5},{8,10},{9,11},{10,... | collective-permute-start | bytes 3145736 | tf_op jit(solution)/shard_map/ppermute | solution.py:33
